TPU v7x, 128 devices: a whole 4x4x4 slice. The times are simulated.
128 devices in a mesh: rows: 16 (over x, z), cols: 8 (over y, core).
Axes of the slice: x: 4, y: 4, z: 4, core: 2. Of those that a mesh axis runs over, the one named last changes fastest.
Arguments:
- features: bfloat16 [4, 128, 1024, 256], P(None, 'rows', 'cols'), may hold values from -27 to 27, as said below
- masks: int32 [4, 200, 128, 1024], P(None, None, 'rows', 'cols'), may hold values from 0 to 1, as said below
- queries: float32 [4, 200, 256], replicated, may hold values from -7 to 7
- conv_weight: bfloat16 [3, 3, 256, 256], replicated, may hold values from -0.125 to 0.125
- gn_gain: float32 [256], replicated, may hold values from 0.25 to 1.75
- gn_bias: float32 [256], replicated, may hold values from -0.5 to 0.5
- query_weight: bfloat16 [256, 256], replicated, may hold values from -7 to 7
- key_weight: bfloat16 [256, 256], replicated, may hold values from -0.375 to 0.375
- value_weight: bfloat16 [256, 256], replicated, may hold values from -0.375 to 0.375
- out_weight: bfloat16 [256, 256], replicated, may hold values from -0.375 to 0.375
- ln_gain: float32 [256], replicated, may hold values from 0.25 to 1.75
- ln_bias: float32 [256], replicated, may hold values from -0.5 to 0.5
- embed_one: bfloat16 [256, 256], replicated, may hold values from -0.375 to 0.375
- embed_two: bfloat16 [256, 256], replicated, may hold values from -0.375 to 0.375
Outputs:
- updated: float32 [4, 200, 256], replicated
- logits: bfloat16 [4, 200, 128, 1024], P(None, None, 'rows', 'cols')
Inputs may be any that keep to these rules, and one draw needn't show every extreme that they name: features have magnitudes that vary over the image. `masks`: each entry is 0 or 1; a query's foreground lies in one rectangle of the image, and a query may have none.
All inputs are finite; a program needn't handle non-finite values.
Results may differ from a plain program's by a relative error of at most 0.035.
Values may be sent and summed in bfloat16 or wider, within the bound.
No kernel may reach another device: no remote copies, remote signals or barrier semaphores. Data moves between devices by JAX's collectives and lax.ppermute only.
A program may use at most 256 MiB of HBM per device.

v0:
```python
import jax
import jax.numpy as jnp
from jax import lax
from jax.sharding import PartitionSpec as P

HEADS = 8
GROUPS = 32
QBLK = 8


def with_halo(cells, sides, width):
    for axis, dim in sides:
        count = lax.axis_size(axis)
        ends = count - 1
        head = lax.slice_in_dim(cells, 0, width, axis=dim)
        tail = lax.slice_in_dim(cells, cells.shape[dim] - width, cells.shape[dim], axis=dim)
        cells = jnp.concatenate(
            [
                lax.ppermute(tail, axis, [(i, (i + 1) % count) for i in range(ends)]),
                cells,
                lax.ppermute(head, axis, [((i + 1) % count, i) for i in range(ends)]),
            ],
            axis=dim,
        )
    return cells


def widen(factor, target):
    return jnp.repeat(factor, target.shape[-1] // factor.shape[-1], axis=-1)


def on_device(
    features,
    masks,
    queries,
    conv_weight,
    gn_gain,
    gn_bias,
    query_weight,
    key_weight,
    value_weight,
    out_weight,
    ln_gain,
    ln_bias,
    embed_one,
    embed_two,
):
    images, tile_rows, tile_cols, width = features.shape
    query_count = queries.shape[1]
    heads = HEADS
    head_size = width // heads
    pixels = tile_rows * tile_cols
    local_count = jnp.sum(masks, axis=(2, 3)).astype(jnp.float32)
    count = lax.psum(local_count, ("rows", "cols"))
    padded = with_halo(features, (("rows", 1), ("cols", 2)), 1)
    conv = lax.conv_general_dilated(
        padded,
        conv_weight,
        (1, 1),
        "VALID",
        dimension_numbers=("NHWC", "HWIO", "NHWC"),
        preferred_element_type=jnp.float32,
    )
    grouped = conv.reshape(images, pixels, GROUPS, width // GROUPS)
    first_sum = jnp.sum(grouped, axis=(1, 3))
    second_sum = jnp.sum(grouped * grouped, axis=(1, 3))
    first_sum, second_sum = lax.psum((first_sum, second_sum), ("rows", "cols"))
    number = lax.axis_size("rows") * lax.axis_size("cols") * pixels * (width // GROUPS)
    mean = first_sum / number
    var = second_sum / number - mean * mean
    normed = (grouped - mean[:, None, :, None]) / jnp.sqrt(var[:, None, :, None] + 1e-05)
    mask_feat = jax.nn.relu(normed.reshape(images, pixels, width) * gn_gain + gn_bias).astype(
        jnp.bfloat16
    )
    keys = jnp.dot(mask_feat, key_weight, preferred_element_type=jnp.float32).astype(jnp.bfloat16)
    vals = jnp.dot(mask_feat, value_weight, preferred_element_type=jnp.float32).astype(jnp.bfloat16)
    qproj = jnp.dot(
        queries.astype(jnp.bfloat16), query_weight, preferred_element_type=jnp.float32
    ).astype(jnp.bfloat16)
    allowed = (masks.reshape(images, query_count, pixels) == 1) | (count == 0.0)[:, :, None]
    logit_scale = 1.0 / head_size**0.5

    def head_parts(query_block, allowed_block):

        def one_head(index):
            head_query_rows = lax.dynamic_slice_in_dim(query_block, index * head_size, head_size, 2)
            head_key_rows = lax.dynamic_slice_in_dim(keys, index * head_size, head_size, 2)
            head_value_rows = lax.dynamic_slice_in_dim(vals, index * head_size, head_size, 2)
            attention_scores = (
                jnp.einsum(
                    "iam,itm->iat",
                    head_query_rows,
                    head_key_rows,
                    preferred_element_type=jnp.float32,
                )
                * logit_scale
            )
            top = jnp.max(jnp.where(allowed_block, attention_scores, -1e30), axis=2)
            attention_weights = jnp.where(
                allowed_block, jnp.exp(attention_scores - top[:, :, None]), 0.0
            ).astype(jnp.bfloat16)
            total = jnp.sum(attention_weights.astype(jnp.float32), axis=2)
            weighted_total = jnp.einsum(
                "xsr,xry->xsy",
                attention_weights,
                head_value_rows,
                preferred_element_type=jnp.float32,
            )
            return (top, total, weighted_total)

        top, total, weighted_total = lax.map(one_head, jnp.arange(heads, dtype=jnp.int32))
        block_rows = query_block.shape[1]
        return (
            jnp.moveaxis(top, 0, 2),
            jnp.moveaxis(total, 0, 2),
            jnp.moveaxis(weighted_total, 0, 2).reshape(images, block_rows, width),
        )

    blocks = query_count // QBLK
    query_blocks = qproj.reshape(images, blocks, QBLK, width)
    allowed_blocks = allowed.reshape(images, blocks, QBLK, pixels)

    def one_block(index):
        query_block = lax.dynamic_index_in_dim(query_blocks, index, 1, False)
        allowed_block = lax.dynamic_index_in_dim(allowed_blocks, index, 1, False)
        return head_parts(query_block, allowed_block)

    top, total, weighted_total = lax.map(one_block, jnp.arange(blocks, dtype=jnp.int32))
    top = jnp.moveaxis(top, 0, 1).reshape(images, query_count, heads)
    total = jnp.moveaxis(total, 0, 1).reshape(images, query_count, heads)
    weighted_total = jnp.moveaxis(weighted_total, 0, 1).reshape(images, query_count, width)
    highest = lax.pmax(top, ("rows", "cols"))
    factor = jnp.exp(top - highest)
    total, weighted_total = lax.psum(
        (total * factor, weighted_total * widen(factor, weighted_total)), ("rows", "cols")
    )
    attn = (weighted_total / widen(total, weighted_total)).astype(jnp.bfloat16)
    mixed = queries + jnp.dot(attn, out_weight, preferred_element_type=jnp.float32)
    centre = jnp.mean(mixed, axis=2, keepdims=True)
    spread = jnp.mean((mixed - centre) ** 2, axis=2, keepdims=True)
    updated = (mixed - centre) / jnp.sqrt(spread + 1e-05) * ln_gain + ln_bias
    hidden = jax.nn.relu(
        jnp.dot(updated.astype(jnp.bfloat16), embed_one, preferred_element_type=jnp.float32)
    ).astype(jnp.bfloat16)
    embed = jnp.dot(hidden, embed_two, preferred_element_type=jnp.float32).astype(jnp.bfloat16)
    logits = jnp.einsum(
        "bqc,bpc->bqp", embed, mask_feat, preferred_element_type=jnp.float32
    ).astype(jnp.bfloat16)
    return (updated, logits.reshape(images, query_count, tile_rows, tile_cols))


def solution(mesh):
    return jax.shard_map(
        on_device,
        mesh=mesh,
        in_specs=(
            P(None, "rows", "cols", None),
            P(None, None, "rows", "cols"),
            P(),
            P(),
            P(),
            P(),
            P(),
            P(),
            P(),
            P(),
            P(),
            P(),
            P(),
            P(),
        ),
        out_specs=(P(), P(None, None, "rows", "cols")),
        check_vma=False,
    )
```

profile of v0, /device:TPU:1, one launch (start us, length us, event | category | flops | bytes accessed | tf_op | source)
XLA Modules:
  0.0 1147.9 jit_solution(17326337725463689929)
XLA Ops:
  8.5 4.4 collective-permute-start
  14.1 3.2 broadcast_compare_fusion
  18.0 4.0 collective-permute-done.1
  23.6 4.7 collective-permute-start.2
  31.3 16.1 %reduce_sum.68 = s32[4,200]{1,0:T(4,128)S(1)} reduce(s32[4,200,8,128]{3,2,1,0:T(8,128)} %param.19, s32[]{:T(128)} %constant.48.clone.1), dimensions={2,3}, to_apply=%region_0.0 | reduce | flops 818400 | bytes 3280004 | tf_op jit(solution)/shard_map/reduce_sum | solution.py:53
  49.4 3.4 maximum_bitcast_fusion
  57.0 7.6 fusion.33
  64.7 2.6 copy.39
  67.5 2.2 slice_bitcast_fusion
  69.8 4.8 copy.41
  75.2 66.6 %all-reduce = (f32[4,200]{1,0:T(4,128)S(1)}, f32[4,32]{1,0:T(4,128)S(1)}, f32[4,32]{1,0:T(4,128)S(1)}) all-reduce(f32[4,200]{1,0:T(4,128)S(1)} %convert_element_type.41, f32[4,32]{1,0:T(4,128)S(1)} %reduce_sum.74, f32[4,32]{1,0:T(4,128)S(1)} %reduce_sum.71), channel_id=1, replica_groups=mesh['rows'=16,'cols'=8] {'rows','cols'}, use_global_device_ids=true, to_apply=%region_1.0 | all-reduce | flops 1056 | bytes 8448 | tf_op jit(solution)/shard_map/psum | solution.py:54
  142.2 3.5 copy.40
  146.8 2.0 convolution_convert_fusion.1
  148.9 4.0 copy.44
  152.9 2.0 convolution_convert_fusion
  154.9 3.1 copy.45
  159.5 758.5 %while.29 = (s32[]{:T(128)}, f32[25,4,8,8]{2,1,3,0:T(4,128)}, f32[25,4,8,8]{2,1,3,0:T(4,128)}, f32[25,4,8,256]{3,2,0,1:T(8,128)}, s32[25]{0:T(128)S(1)}, /*index...) while((s32[]{:T(128)}, f32[25,4,8,8]{2,1,3,0:T(4,128)}, ...), condition=%wide.region_13.14_spmd, body=%wide.region_8.0_spmd.sunk | while | flops 4554699 | bytes 1383326 | solution.py:128
  163.7 24.7 %while.30 = (s32[]{:T(128)}, f32[8,4,8]{2,1,0:T(4,128)S(1)}, f32[8,4,8]{2,1,0:T(4,128)S(1)}, f32[8,4,8,32]{3,2,1,0:T(8,128)S(1)}, s32[8]{0:T(128)S(1)}, /*index=...) while((s32[]{:T(128)}, f32[8,4,8]{2,1,0:T(4,128)S(1)}, ...), condition=%wide.region_12.12_spmd, body=%wide.region_9.11_spmd.sunk | while | flops 4554694 | bytes 1052227 | solution.py:111
  194.1 24.7 %while.30 = (s32[]{:T(128)}, f32[8,4,8]{2,1,0:T(4,128)S(1)}, f32[8,4,8]{2,1,0:T(4,128)S(1)}, f32[8,4,8,32]{3,2,1,0:T(8,128)S(1)}, s32[8]{0:T(128)S(1)}, /*index=...) while((s32[]{:T(128)}, f32[8,4,8]{2,1,0:T(4,128)S(1)}, ...), condition=%wide.region_12.12_spmd, body=%wide.region_9.11_spmd.sunk | while | flops 4554694 | bytes 1052227 | solution.py:111
  224.4 24.7 %while.30 = (s32[]{:T(128)}, f32[8,4,8]{2,1,0:T(4,128)S(1)}, f32[8,4,8]{2,1,0:T(4,128)S(1)}, f32[8,4,8,32]{3,2,1,0:T(8,128)S(1)}, s32[8]{0:T(128)S(1)}, /*index=...) while((s32[]{:T(128)}, f32[8,4,8]{2,1,0:T(4,128)S(1)}, ...), condition=%wide.region_12.12_spmd, body=%wide.region_9.11_spmd.sunk | while | flops 4554694 | bytes 1052227 | solution.py:111
  254.7 24.7 %while.30 = (s32[]{:T(128)}, f32[8,4,8]{2,1,0:T(4,128)S(1)}, f32[8,4,8]{2,1,0:T(4,128)S(1)}, f32[8,4,8,32]{3,2,1,0:T(8,128)S(1)}, s32[8]{0:T(128)S(1)}, /*index=...) while((s32[]{:T(128)}, f32[8,4,8]{2,1,0:T(4,128)S(1)}, ...), condition=%wide.region_12.12_spmd, body=%wide.region_9.11_spmd.sunk | while | flops 4554694 | bytes 1052227 | solution.py:111
  285.1 24.7 %while.30 = (s32[]{:T(128)}, f32[8,4,8]{2,1,0:T(4,128)S(1)}, f32[8,4,8]{2,1,0:T(4,128)S(1)}, f32[8,4,8,32]{3,2,1,0:T(8,128)S(1)}, s32[8]{0:T(128)S(1)}, /*index=...) while((s32[]{:T(128)}, f32[8,4,8]{2,1,0:T(4,128)S(1)}, ...), condition=%wide.region_12.12_spmd, body=%wide.region_9.11_spmd.sunk | while | flops 4554694 | bytes 1052227 | solution.py:111
  315.4 24.7 %while.30 = (s32[]{:T(128)}, f32[8,4,8]{2,1,0:T(4,128)S(1)}, f32[8,4,8]{2,1,0:T(4,128)S(1)}, f32[8,4,8,32]{3,2,1,0:T(8,128)S(1)}, s32[8]{0:T(128)S(1)}, /*index=...) while((s32[]{:T(128)}, f32[8,4,8]{2,1,0:T(4,128)S(1)}, ...), condition=%wide.region_12.12_spmd, body=%wide.region_9.11_spmd.sunk | while | flops 4554694 | bytes 1052227 | solution.py:111
  345.8 24.7 %while.30 = (s32[]{:T(128)}, f32[8,4,8]{2,1,0:T(4,128)S(1)}, f32[8,4,8]{2,1,0:T(4,128)S(1)}, f32[8,4,8,32]{3,2,1,0:T(8,128)S(1)}, s32[8]{0:T(128)S(1)}, /*index=...) while((s32[]{:T(128)}, f32[8,4,8]{2,1,0:T(4,128)S(1)}, ...), condition=%wide.region_12.12_spmd, body=%wide.region_9.11_spmd.sunk | while | flops 4554694 | bytes 1052227 | solution.py:111
  376.1 24.7 %while.30 = (s32[]{:T(128)}, f32[8,4,8]{2,1,0:T(4,128)S(1)}, f32[8,4,8]{2,1,0:T(4,128)S(1)}, f32[8,4,8,32]{3,2,1,0:T(8,128)S(1)}, s32[8]{0:T(128)S(1)}, /*index=...) while((s32[]{:T(128)}, f32[8,4,8]{2,1,0:T(4,128)S(1)}, ...), condition=%wide.region_12.12_spmd, body=%wide.region_9.11_spmd.sunk | while | flops 4554694 | bytes 1052227 | solution.py:111
  406.4 24.7 %while.30 = (s32[]{:T(128)}, f32[8,4,8]{2,1,0:T(4,128)S(1)}, f32[8,4,8]{2,1,0:T(4,128)S(1)}, f32[8,4,8,32]{3,2,1,0:T(8,128)S(1)}, s32[8]{0:T(128)S(1)}, /*index=...) while((s32[]{:T(128)}, f32[8,4,8]{2,1,0:T(4,128)S(1)}, ...), condition=%wide.region_12.12_spmd, body=%wide.region_9.11_spmd.sunk | while | flops 4554694 | bytes 1052227 | solution.py:111
  436.8 24.7 %while.30 = (s32[]{:T(128)}, f32[8,4,8]{2,1,0:T(4,128)S(1)}, f32[8,4,8]{2,1,0:T(4,128)S(1)}, f32[8,4,8,32]{3,2,1,0:T(8,128)S(1)}, s32[8]{0:T(128)S(1)}, /*index=...) while((s32[]{:T(128)}, f32[8,4,8]{2,1,0:T(4,128)S(1)}, ...), condition=%wide.region_12.12_spmd, body=%wide.region_9.11_spmd.sunk | while | flops 4554694 | bytes 1052227 | solution.py:111
  467.1 24.7 %while.30 = (s32[]{:T(128)}, f32[8,4,8]{2,1,0:T(4,128)S(1)}, f32[8,4,8]{2,1,0:T(4,128)S(1)}, f32[8,4,8,32]{3,2,1,0:T(8,128)S(1)}, s32[8]{0:T(128)S(1)}, /*index=...) while((s32[]{:T(128)}, f32[8,4,8]{2,1,0:T(4,128)S(1)}, ...), condition=%wide.region_12.12_spmd, body=%wide.region_9.11_spmd.sunk | while | flops 4554694 | bytes 1052227 | solution.py:111
  497.5 24.7 %while.30 = (s32[]{:T(128)}, f32[8,4,8]{2,1,0:T(4,128)S(1)}, f32[8,4,8]{2,1,0:T(4,128)S(1)}, f32[8,4,8,32]{3,2,1,0:T(8,128)S(1)}, s32[8]{0:T(128)S(1)}, /*index=...) while((s32[]{:T(128)}, f32[8,4,8]{2,1,0:T(4,128)S(1)}, ...), condition=%wide.region_12.12_spmd, body=%wide.region_9.11_spmd.sunk | while | flops 4554694 | bytes 1052227 | solution.py:111
  527.8 24.7 %while.30 = (s32[]{:T(128)}, f32[8,4,8]{2,1,0:T(4,128)S(1)}, f32[8,4,8]{2,1,0:T(4,128)S(1)}, f32[8,4,8,32]{3,2,1,0:T(8,128)S(1)}, s32[8]{0:T(128)S(1)}, /*index=...) while((s32[]{:T(128)}, f32[8,4,8]{2,1,0:T(4,128)S(1)}, ...), condition=%wide.region_12.12_spmd, body=%wide.region_9.11_spmd.sunk | while | flops 4554694 | bytes 1052227 | solution.py:111
  558.1 24.7 %while.30 = (s32[]{:T(128)}, f32[8,4,8]{2,1,0:T(4,128)S(1)}, f32[8,4,8]{2,1,0:T(4,128)S(1)}, f32[8,4,8,32]{3,2,1,0:T(8,128)S(1)}, s32[8]{0:T(128)S(1)}, /*index=...) while((s32[]{:T(128)}, f32[8,4,8]{2,1,0:T(4,128)S(1)}, ...), condition=%wide.region_12.12_spmd, body=%wide.region_9.11_spmd.sunk | while | flops 4554694 | bytes 1052227 | solution.py:111
  588.5 24.7 %while.30 = (s32[]{:T(128)}, f32[8,4,8]{2,1,0:T(4,128)S(1)}, f32[8,4,8]{2,1,0:T(4,128)S(1)}, f32[8,4,8,32]{3,2,1,0:T(8,128)S(1)}, s32[8]{0:T(128)S(1)}, /*index=...) while((s32[]{:T(128)}, f32[8,4,8]{2,1,0:T(4,128)S(1)}, ...), condition=%wide.region_12.12_spmd, body=%wide.region_9.11_spmd.sunk | while | flops 4554694 | bytes 1052227 | solution.py:111
  618.8 24.7 %while.30 = (s32[]{:T(128)}, f32[8,4,8]{2,1,0:T(4,128)S(1)}, f32[8,4,8]{2,1,0:T(4,128)S(1)}, f32[8,4,8,32]{3,2,1,0:T(8,128)S(1)}, s32[8]{0:T(128)S(1)}, /*index=...) while((s32[]{:T(128)}, f32[8,4,8]{2,1,0:T(4,128)S(1)}, ...), condition=%wide.region_12.12_spmd, body=%wide.region_9.11_spmd.sunk | while | flops 4554694 | bytes 1052227 | solution.py:111
  649.2 24.7 %while.30 = (s32[]{:T(128)}, f32[8,4,8]{2,1,0:T(4,128)S(1)}, f32[8,4,8]{2,1,0:T(4,128)S(1)}, f32[8,4,8,32]{3,2,1,0:T(8,128)S(1)}, s32[8]{0:T(128)S(1)}, /*index=...) while((s32[]{:T(128)}, f32[8,4,8]{2,1,0:T(4,128)S(1)}, ...), condition=%wide.region_12.12_spmd, body=%wide.region_9.11_spmd.sunk | while | flops 4554694 | bytes 1052227 | solution.py:111
  679.5 24.7 %while.30 = (s32[]{:T(128)}, f32[8,4,8]{2,1,0:T(4,128)S(1)}, f32[8,4,8]{2,1,0:T(4,128)S(1)}, f32[8,4,8,32]{3,2,1,0:T(8,128)S(1)}, s32[8]{0:T(128)S(1)}, /*index=...) while((s32[]{:T(128)}, f32[8,4,8]{2,1,0:T(4,128)S(1)}, ...), condition=%wide.region_12.12_spmd, body=%wide.region_9.11_spmd.sunk | while | flops 4554694 | bytes 1052227 | solution.py:111
  709.8 24.7 %while.30 = (s32[]{:T(128)}, f32[8,4,8]{2,1,0:T(4,128)S(1)}, f32[8,4,8]{2,1,0:T(4,128)S(1)}, f32[8,4,8,32]{3,2,1,0:T(8,128)S(1)}, s32[8]{0:T(128)S(1)}, /*index=...) while((s32[]{:T(128)}, f32[8,4,8]{2,1,0:T(4,128)S(1)}, ...), condition=%wide.region_12.12_spmd, body=%wide.region_9.11_spmd.sunk | while | flops 4554694 | bytes 1052227 | solution.py:111
  740.2 24.7 %while.30 = (s32[]{:T(128)}, f32[8,4,8]{2,1,0:T(4,128)S(1)}, f32[8,4,8]{2,1,0:T(4,128)S(1)}, f32[8,4,8,32]{3,2,1,0:T(8,128)S(1)}, s32[8]{0:T(128)S(1)}, /*index=...) while((s32[]{:T(128)}, f32[8,4,8]{2,1,0:T(4,128)S(1)}, ...), condition=%wide.region_12.12_spmd, body=%wide.region_9.11_spmd.sunk | while | flops 4554694 | bytes 1052227 | solution.py:111
  770.5 24.7 %while.30 = (s32[]{:T(128)}, f32[8,4,8]{2,1,0:T(4,128)S(1)}, f32[8,4,8]{2,1,0:T(4,128)S(1)}, f32[8,4,8,32]{3,2,1,0:T(8,128)S(1)}, s32[8]{0:T(128)S(1)}, /*index=...) while((s32[]{:T(128)}, f32[8,4,8]{2,1,0:T(4,128)S(1)}, ...), condition=%wide.region_12.12_spmd, body=%wide.region_9.11_spmd.sunk | while | flops 4554694 | bytes 1052227 | solution.py:111
  800.8 24.7 %while.30 = (s32[]{:T(128)}, f32[8,4,8]{2,1,0:T(4,128)S(1)}, f32[8,4,8]{2,1,0:T(4,128)S(1)}, f32[8,4,8,32]{3,2,1,0:T(8,128)S(1)}, s32[8]{0:T(128)S(1)}, /*index=...) while((s32[]{:T(128)}, f32[8,4,8]{2,1,0:T(4,128)S(1)}, ...), condition=%wide.region_12.12_spmd, body=%wide.region_9.11_spmd.sunk | while | flops 4554694 | bytes 1052227 | solution.py:111
  831.2 24.7 %while.30 = (s32[]{:T(128)}, f32[8,4,8]{2,1,0:T(4,128)S(1)}, f32[8,4,8]{2,1,0:T(4,128)S(1)}, f32[8,4,8,32]{3,2,1,0:T(8,128)S(1)}, s32[8]{0:T(128)S(1)}, /*index=...) while((s32[]{:T(128)}, f32[8,4,8]{2,1,0:T(4,128)S(1)}, ...), condition=%wide.region_12.12_spmd, body=%wide.region_9.11_spmd.sunk | while | flops 4554694 | bytes 1052227 | solution.py:111
  861.5 24.7 %while.30 = (s32[]{:T(128)}, f32[8,4,8]{2,1,0:T(4,128)S(1)}, f32[8,4,8]{2,1,0:T(4,128)S(1)}, f32[8,4,8,32]{3,2,1,0:T(8,128)S(1)}, s32[8]{0:T(128)S(1)}, /*index=...) while((s32[]{:T(128)}, f32[8,4,8]{2,1,0:T(4,128)S(1)}, ...), condition=%wide.region_12.12_spmd, body=%wide.region_9.11_spmd.sunk | while | flops 4554694 | bytes 1052227 | solution.py:111
  891.9 24.7 %while.30 = (s32[]{:T(128)}, f32[8,4,8]{2,1,0:T(4,128)S(1)}, f32[8,4,8]{2,1,0:T(4,128)S(1)}, f32[8,4,8,32]{3,2,1,0:T(8,128)S(1)}, s32[8]{0:T(128)S(1)}, /*index=...) while((s32[]{:T(128)}, f32[8,4,8]{2,1,0:T(4,128)S(1)}, ...), condition=%wide.region_12.12_spmd, body=%wide.region_9.11_spmd.sunk | while | flops 4554694 | bytes 1052227 | solution.py:111
  919.5 63.6 %pmax.7 = f32[4,200,8]{1,2,0:T(8,128)S(1)} all-reduce(f32[4,200,8]{1,2,0:T(8,128)S(1)} %reshape.70), channel_id=1, replica_groups=mesh['rows'=16,'cols'=8] {'rows','cols'}, use_global_device_ids=true, to_apply=%region_14.15 | all-reduce | flops 6400 | bytes 51200 | tf_op jit(solution)/shard_map/pmax | solution.py:132
  986.1 63.1 %psum.39 = f32[4,200,8]{1,2,0:T(8,128)S(1)} all-reduce(f32[4,200,8]{1,2,0:T(8,128)S(1)} %get-tuple-element.169), channel_id=1, replica_groups=mesh['rows'=16,'cols'=8] {'rows','cols'}, use_global_device_ids=true, to_apply=%region_16.17 | all-reduce | flops 6400 | bytes 51200 | tf_op jit(solution)/shard_map/psum | solution.py:134
  1050.5 79.4 %all-reduce.3.cloned.1.call-done = f32[4,200,256]{2,1,0:T(8,128)} async-done(((f32[4,200,256]{2,1,0:T(8,128)}), f32[4,200,256]{2,1,0:T(8,128)}) %all-reduce.3.cloned.1.call-update) | async-done | bytes 819216 | tf_op jit(solution)/shard_map/psum | solution.py:134
  1129.9 2.1 fusion.34
  1134.7 3.1 convolution_convert_fusion.2
  1137.8 3.1 copy.62
  (1370 shorter events, 590.2 us)
Async XLA Ops:
  7.2 49.9 %copy-start = (bf16[3,3,256,256]{3,2,1,0:T(8,128)(2,1)S(1)}, bf16[3,3,256,256]{3,2,1,0:T(8,128)(2,1)}, u32[]{:S(2)}) copy-start(bf16[3,3,256,256]{3,2,1,0:T(8,128)(2,1)} %param.21) | copy-start | bytes 3538948
  7.2 10.6 copy-start.6
  7.2 1122.8 %all-reduce.3.cloned.1.call-start = ((), (), s32[]{:S(2)}) async-start(), calls=%async_computation | async-start | bytes 1638400 | tf_op jit(solution)/shard_map/psum | solution.py:134
  8.5 9.3 collective-permute-start
  12.8 9.1 collective-permute-start.1
  17.4 12.9 %copy-start.10 = (f32[4,200,256]{2,1,0:T(8,128)S(1)}, f32[4,200,256]{2,1,0:T(8,128)}, u32[]{:S(2)}) copy-start(f32[4,200,256]{2,1,0:T(8,128)} %param.20) | copy-start | bytes 2457604
  17.4 12.9 %copy-start.14 = (bf16[256,256]{1,0:T(8,128)(2,1)S(1)}, bf16[256,256]{1,0:T(8,128)(2,1)}, u32[]{:S(2)}) copy-start(bf16[256,256]{1,0:T(8,128)(2,1)} %param.24) | copy-start | bytes 393220
  18.0 29.5 %copy-start.8 = (pred[4,200,8,128]{3,2,1,0:T(8,128)(4,1)S(1)}, pred[4,200,8,128]{3,2,1,0:T(8,128)(4,1)}, u32[]{:S(2)}) copy-start(pred[4,200,8,128]{3,2,1,0:T(8,128)(4,1)} %broadcast_compare_fusion) | copy-start | bytes 2457604
  22.0 1.5 copy-start.4
  23.6 25.8 %collective-permute-start.2 = (bf16[4,10,1,256]{3,2,1,0:T(2,128)(2,1)S(1)}, bf16[4,10,1,256]{3,2,1,0:T(2,128)(2,1)S(1)}, u32[]{:S(2)}, u32[]{:S(2)}) collective-permute-start(bf16[4,10,1,256]{3,2,1,0:T(2,128)(2,1)S(1)} %get-tuple-element.177), channel_id=1, source_target_pairs={{0,1},{1,2},{2,3},{3,4},{4,5},{5,6},{6,7},{8,9},{9,10},{10,11},{11... | collective-permute-start | bytes 61448 | tf_op jit(solution)/shard_map/ppermute | solution.py:19
  28.3 21.1 %collective-permute-start.3 = (bf16[4,10,1,256]{3,2,1,0:T(2,128)(2,1)S(1)}, bf16[4,10,1,256]{3,2,1,0:T(2,128)(2,1)S(1)}, u32[]{:S(2)}, u32[]{:S(2)}) collective-permute-start(bf16[4,10,1,256]{3,2,1,0:T(2,128)(2,1)S(1)} %get-tuple-element.178), channel_id=1, source_target_pairs={{1,0},{2,1},{3,2},{4,3},{5,4},{6,5},{7,6},{9,8},{10,9},{11,10},{12... | collective-permute-start | bytes 61448 | tf_op jit(solution)/shard_map/ppermute | solution.py:21
  55.5 1.6 copy-start.20
  142.2 3.5 copy-start.16
  142.2 3.5 copy-start.17
  145.7 1.1 copy-start.11
  146.8 6.0 copy-start.2
  148.9 4.0 copy-start.12
  154.9 3.2 copy-start.5
  918.0 67.1 %copy-start.9 = (f32[25,4,8,256]{3,2,0,1:T(8,128)S(1)}, f32[25,4,8,256]{3,2,0,1:T(8,128)}, u32[]{:S(2)}) copy-start(f32[25,4,8,256]{3,2,0,1:T(8,128)} %get-tuple-element.100) | copy-start | bytes 2457604
  1049.3 83.1 %copy-start.18 = (f32[256]{0:T(256)S(1)}, f32[256]{0:T(256)}, u32[]{:S(2)}) copy-start(f32[256]{0:T(256)} %param.29) | copy-start | bytes 3076
  1049.3 83.1 %copy-start.19 = (f32[256]{0:T(256)S(1)}, f32[256]{0:T(256)}, u32[]{:S(2)}) copy-start(f32[256]{0:T(256)} %param.28) | copy-start | bytes 3076
  1050.5 83.1 %copy-start.15 = (bf16[256,256]{1,0:T(8,128)(2,1)S(1)}, bf16[256,256]{1,0:T(8,128)(2,1)}, u32[]{:S(2)}) copy-start(bf16[256,256]{1,0:T(8,128)(2,1)} %param.30) | copy-start | bytes 393220
  1050.5 84.1 %copy-start.3 = (bf16[4,1024,256]{2,1,0:T(8,128)(2,1)S(1)}, bf16[4,1024,256]{2,1,0:T(8,128)(2,1)}, u32[]{:S(2)}) copy-start(bf16[4,1024,256]{2,1,0:T(8,128)(2,1)} %copy-done.2) | copy-start | bytes 6291460
  1050.5 84.1 %copy-start.13 = (bf16[256,256]{1,0:T(8,128)(2,1)S(1)}, bf16[256,256]{1,0:T(8,128)(2,1)}, u32[]{:S(2)}) copy-start(bf16[256,256]{1,0:T(8,128)(2,1)} %param.31) | copy-start | bytes 393220
  1132.7 0.9 copy-start.7
  1133.6 7.2 copy-start.1
Sparse Core Ops, SparseCore 0:
  986.2 143.6 all-reduce.2
where the time goes:
time: 1170 us; the launch traced here: 1150 us
  matrix products  321 us (27%)
  local copies, waits for them, and re-layouts  261 us (22%)
  loops' own time  194 us (17%)
  blocking collectives  193 us (16%)
  waiting for transfers between devices  83.8 us (7%)
  other arithmetic  66.9 us (6%)
  between operations  14.7 us (1%)
  starting transfers between devices  12.4 us (1%)
    dot_general x200, matrix products, one_head(): jnp.einsum('iam,itm->iat', head_query_rows, head_key_rows, preferred_elem...  252 us
    another operation x25, loops' own time, head_parts(): lax.map(one_head, jnp.arange(heads, dtype=jnp.int32))  142 us
    dynamic_slice x200, local copies, waits for them, and re-layouts, head_parts(): lax.map(one_head, jnp.arange(heads, dtype=jnp.int32))  133 us
    psum x1, waiting for transfers between devices, on_device(): lax.psum((total * factor, weighted_total * widen(factor, weighted_total))...  79.4 us
    psum x1, blocking collectives, on_device(): count = lax.psum(local_count, ('rows', 'cols'))  66.6 us
    pmax x1, blocking collectives, on_device(): highest = lax.pmax(top, ('rows', 'cols'))  63.6 us
    psum x1, blocking collectives, on_device(): lax.psum((total * factor, weighted_total * widen(factor, weighted_total))...  63.1 us
    another operation x1, loops' own time, on_device(): lax.map(one_block, jnp.arange(blocks, dtype=jnp.int32))  52.3 us
  transfers between devices with their start and end apart: 5, of which 3 were waited for; matrix products, arithmetic and copies ran while one was open for 2% of the time, Pallas kernels for 0%

commit v1 on v0

v1 whole, which is shorter than its diff:
```python
import jax
import jax.numpy as jnp
from jax import lax
from jax.experimental import pallas as pl
from jax.sharding import PartitionSpec as P

HEADS = 8
GROUPS = 32
NEG = -1e30


def with_halo(cells, sides, width):
    for axis, dim in sides:
        count = lax.axis_size(axis)
        ends = count - 1
        head = lax.slice_in_dim(cells, 0, width, axis=dim)
        tail = lax.slice_in_dim(cells, cells.shape[dim] - width, cells.shape[dim], axis=dim)
        cells = jnp.concatenate(
            [
                lax.ppermute(tail, axis, [(i, (i + 1) % count) for i in range(ends)]),
                cells,
                lax.ppermute(head, axis, [((i + 1) % count, i) for i in range(ends)]),
            ],
            axis=dim,
        )
    return cells


def butterfly_sum(x):
    for axis in ("cols", "rows"):
        n = lax.axis_size(axis)
        if n & (n - 1):
            x = jax.tree.map(lambda v: lax.psum(v, axis), x)
            continue
        k = 1
        while k < n:
            got = lax.ppermute(x, axis, [(i, i ^ k) for i in range(n)])
            x = jax.tree.map(lambda a, b: a + b, x, got)
            k *= 2
    return x


def split_parts(x, span):
    return x[:, :span], x[:, span : span + span // 32], x[:, span + span // 32 :]


def merge(a, b, span):
    wa, ta, ma = split_parts(a, span)
    wb, tb, mb = split_parts(b, span)
    m = jnp.maximum(ma, mb)
    fa = jnp.exp(ma - m)
    fb = jnp.exp(mb - m)
    t = ta * fa + tb * fb
    w = wa * jnp.repeat(fa, 32, axis=1) + wb * jnp.repeat(fb, 32, axis=1)
    return jnp.concatenate([w, t, m], axis=1)


def halving_merge(x, span):
    for axis in ("cols", "rows"):
        n = lax.axis_size(axis)
        idx = lax.axis_index(axis)
        k = n // 2
        while k >= 1:
            h = x.shape[0] // 2
            lo, hi = x[:h], x[h:]
            upper = (idx // k) % 2 == 1
            keep = jnp.where(upper, hi, lo)
            send = jnp.where(upper, lo, hi)
            got = lax.ppermute(send, axis, [(i, i ^ k) for i in range(n)])
            x = merge(keep, got, span)
            k //= 2
    return x


def doubling_gather(a):
    for axis in ("rows", "cols"):
        n = lax.axis_size(axis)
        idx = lax.axis_index(axis)
        k = 1
        while k < n:
            got = lax.ppermute(a, axis, [(i, i ^ k) for i in range(n)])
            upper = (idx // k) % 2 == 1
            a = jnp.where(upper, jnp.concatenate([got, a]), jnp.concatenate([a, got]))
            k *= 2
    return a


def attention_kernel(q_ref, k_ref, v_ref, a_ref, top_ref, tot_ref, wv_ref, *, scale):
    q = q_ref[0, 0]
    k = k_ref[0, 0]
    s = lax.dot_general(q, k, (((1,), (1,)), ((), ())), preferred_element_type=jnp.float32) * scale
    allowed = a_ref[0] != 0
    top = jnp.max(jnp.where(allowed, s, NEG), axis=1, keepdims=True)
    w = jnp.where(allowed, jnp.exp(s - top), 0.0).astype(jnp.bfloat16)
    tot_ref[0, 0] = jnp.sum(w.astype(jnp.float32), axis=1, keepdims=True)
    top_ref[0, 0] = top
    wv_ref[0, 0] = jnp.dot(w, v_ref[0, 0], preferred_element_type=jnp.float32)


def attention(qh, kh, vh, allowed, scale):
    images, heads, queries, hd = qh.shape
    pixels = kh.shape[2]
    kernel = lambda *refs: attention_kernel(*refs, scale=scale)
    return pl.pallas_call(
        kernel,
        grid=(images, heads),
        in_specs=[
            pl.BlockSpec((1, 1, queries, hd), lambda i, h: (i, h, 0, 0)),
            pl.BlockSpec((1, 1, pixels, hd), lambda i, h: (i, h, 0, 0)),
            pl.BlockSpec((1, 1, pixels, hd), lambda i, h: (i, h, 0, 0)),
            pl.BlockSpec((1, queries, pixels), lambda i, h: (i, 0, 0)),
        ],
        out_specs=[
            pl.BlockSpec((1, 1, queries, 1), lambda i, h: (i, h, 0, 0)),
            pl.BlockSpec((1, 1, queries, 1), lambda i, h: (i, h, 0, 0)),
            pl.BlockSpec((1, 1, queries, hd), lambda i, h: (i, h, 0, 0)),
        ],
        out_shape=[
            jax.ShapeDtypeStruct((images, heads, queries, 1), jnp.float32),
            jax.ShapeDtypeStruct((images, heads, queries, 1), jnp.float32),
            jax.ShapeDtypeStruct((images, heads, queries, hd), jnp.float32),
        ],
    )(qh, kh, vh, allowed)


def on_device(
    features,
    masks,
    queries,
    conv_weight,
    gn_gain,
    gn_bias,
    query_weight,
    key_weight,
    value_weight,
    out_weight,
    ln_gain,
    ln_bias,
    embed_one,
    embed_two,
):
    images, tile_rows, tile_cols, width = features.shape
    query_count = queries.shape[1]
    heads = HEADS
    head_size = width // heads
    pixels = tile_rows * tile_cols
    devices = lax.axis_size("rows") * lax.axis_size("cols")
    local_count = jnp.sum(masks, axis=(2, 3)).astype(jnp.float32)
    padded = with_halo(features, (("rows", 1), ("cols", 2)), 1)
    conv = lax.conv_general_dilated(
        padded,
        conv_weight,
        (1, 1),
        "VALID",
        dimension_numbers=("NHWC", "HWIO", "NHWC"),
        preferred_element_type=jnp.float32,
    )
    grouped = conv.reshape(images, pixels, GROUPS, width // GROUPS)
    first_sum = jnp.sum(grouped, axis=(1, 3))
    second_sum = jnp.sum(grouped * grouped, axis=(1, 3))
    stats = butterfly_sum(jnp.concatenate([local_count, first_sum, second_sum], axis=1))
    count = stats[:, :query_count]
    first_sum = stats[:, query_count : query_count + GROUPS]
    second_sum = stats[:, query_count + GROUPS :]
    number = devices * pixels * (width // GROUPS)
    mean = first_sum / number
    var = second_sum / number - mean * mean
    normed = (grouped - mean[:, None, :, None]) / jnp.sqrt(var[:, None, :, None] + 1e-05)
    mask_feat = jax.nn.relu(normed.reshape(images, pixels, width) * gn_gain + gn_bias).astype(
        jnp.bfloat16
    )
    keys = jnp.dot(mask_feat, key_weight, preferred_element_type=jnp.float32).astype(jnp.bfloat16)
    vals = jnp.dot(mask_feat, value_weight, preferred_element_type=jnp.float32).astype(jnp.bfloat16)
    qproj = jnp.dot(
        queries.astype(jnp.bfloat16), query_weight, preferred_element_type=jnp.float32
    ).astype(jnp.bfloat16)
    allowed = (
        (masks.reshape(images, query_count, pixels) == 1) | (count == 0.0)[:, :, None]
    ).astype(jnp.int32)
    by_head = lambda x: x.reshape(images, -1, heads, head_size).transpose(0, 2, 1, 3)
    top, total, weighted = attention(
        by_head(qproj), by_head(keys), by_head(vals), allowed, 1.0 / head_size**0.5
    )
    span = images * query_count * width // devices
    packed = jnp.concatenate(
        [
            weighted.transpose(0, 2, 1, 3).reshape(devices, span),
            total[..., 0].transpose(0, 2, 1).reshape(devices, span // 32),
            top[..., 0].transpose(0, 2, 1).reshape(devices, span // 32),
        ],
        axis=1,
    )
    reduced = halving_merge(packed, span)
    sums, totals, _ = split_parts(reduced, span)
    attn_block = (sums / jnp.repeat(totals, 32, axis=1)).astype(jnp.bfloat16)
    attn = doubling_gather(attn_block).reshape(images, query_count, width)
    mixed = queries + jnp.dot(attn, out_weight, preferred_element_type=jnp.float32)
    centre = jnp.mean(mixed, axis=2, keepdims=True)
    spread = jnp.mean((mixed - centre) ** 2, axis=2, keepdims=True)
    updated = (mixed - centre) / jnp.sqrt(spread + 1e-05) * ln_gain + ln_bias
    hidden = jax.nn.relu(
        jnp.dot(updated.astype(jnp.bfloat16), embed_one, preferred_element_type=jnp.float32)
    ).astype(jnp.bfloat16)
    embed = jnp.dot(hidden, embed_two, preferred_element_type=jnp.float32).astype(jnp.bfloat16)
    logits = jnp.einsum(
        "bqc,bpc->bqp", embed, mask_feat, preferred_element_type=jnp.float32
    ).astype(jnp.bfloat16)
    return (updated, logits.reshape(images, query_count, tile_rows, tile_cols))


def solution(mesh):
    return jax.shard_map(
        on_device,
        mesh=mesh,
        in_specs=(
            P(None, "rows", "cols", None),
            P(None, None, "rows", "cols"),
            P(),
            P(),
            P(),
            P(),
            P(),
            P(),
            P(),
            P(),
            P(),
            P(),
            P(),
            P(),
        ),
        out_specs=(P(), P(None, None, "rows", "cols")),
        check_vma=False,
    )
```

time: 1170 us -> 255 us (0.22); the launches traced: 1150 us -> 250 us
  matrix products: 321 us -> 23.2 us
  local copies, waits for them, and re-layouts: 261 us -> 46.5 us
  loops' own time: 194 us -> 0 us
  blocking collectives: 193 us -> 0 us
  starting transfers between devices: 12.4 us -> 64.7 us
  waiting for transfers between devices: 83.8 us -> 45.6 us
  Pallas kernels: 0 us -> 32.3 us
  other arithmetic: 66.9 us -> 36.5 us
  between operations: 14.7 us -> 1.58 us
    dot_general x400 -> x0, matrix products: 302 us -> none  [the longest x200 252 us: one_head(): jnp.einsum('iam,itm->iat', head_query_rows, head_key_rows, preferred_elem...]
    another operation x26 -> x0, loops' own time: 194 us -> none  [the longest x25 142 us: head_parts(): lax.map(one_head, jnp.arange(heads, dtype=jnp.int32))]
    dynamic_slice x225 -> x0, local copies, waits for them, and re-layouts: 149 us -> none  [the longest x200 133 us: head_parts(): lax.map(one_head, jnp.arange(heads, dtype=jnp.int32))]
    psum x2 -> x0, blocking collectives: 130 us -> none  [the longest x1 66.6 us: on_device(): count = lax.psum(local_count, ('rows', 'cols'))]
    psum x1 -> x0, waiting for transfers between devices: 79.4 us -> none  [on_device(): lax.psum((total * factor, weighted_total * widen(factor, weighted_total))...]
    pmax x1 -> x0, blocking collectives: 63.6 us -> none  [on_device(): highest = lax.pmax(top, ('rows', 'cols'))]
    ppermute x0 -> x21, starting transfers between devices: none -> 51.9 us  [the longest x7 20 us: doubling_gather(): got = lax.ppermute(a, axis, [(i, i ^ k) for i in range(n)])]
    ppermute x0 -> x21, waiting for transfers between devices: none -> 39.6 us  [the longest x7 18.6 us: halving_merge(): got = lax.ppermute(send, axis, [(i, i ^ k) for i in range(n)])]
  transfers between devices with their start and end apart: 5 -> 25, of which waited for: 3 -> 21; matrix products, arithmetic and copies ran while one was open for 2% -> 9% of each run, Pallas kernels for 0% -> 0%
where the time goes in v1:
time: 255 us; the launch traced here: 250 us
  starting transfers between devices  64.7 us (25%)
  local copies, waits for them, and re-layouts  46.5 us (18%)
  waiting for transfers between devices  45.6 us (18%)
  other arithmetic  36.5 us (14%)
  Pallas kernels  32.3 us (13%)
  matrix products  23.2 us (9%)
    pallas_call x1, Pallas kernels, attention(): pl.pallas_call(kernel, grid=(images, heads), in_specs=[pl.BlockSpec((1, 1...  32.3 us
    ppermute x7, starting transfers between devices, doubling_gather(): got = lax.ppermute(a, axis, [(i, i ^ k) for i in range(n)])  20 us
    ppermute x7, waiting for transfers between devices, halving_merge(): got = lax.ppermute(send, axis, [(i, i ^ k) for i in range(n)])  18.6 us
    ppermute x7, starting transfers between devices, halving_merge(): got = lax.ppermute(send, axis, [(i, i ^ k) for i in range(n)])  18.6 us
    reshape x3, local copies, waits for them, and re-layouts, on_device(): x.reshape(images, -1, heads, head_size).transpose(0, 2, 1, 3)  17.2 us
    reduce_sum x1, other arithmetic, on_device(): local_count = jnp.sum(masks, axis=(2, 3)).astype(jnp.float32)  16.1 us
    ppermute x7, waiting for transfers between devices, doubling_gather(): got = lax.ppermute(a, axis, [(i, i ^ k) for i in range(n)])  15.8 us
    ppermute x7, starting transfers between devices, butterfly_sum(): got = lax.ppermute(x, axis, [(i, i ^ k) for i in range(n)])  13.3 us
  transfers between devices with their start and end apart: 25, of which 21 were waited for; matrix products, arithmetic and copies ran while one was open for 9% of the time, Pallas kernels for 0%

profile of v1, /device:TPU:1, one launch (start us, length us, event | category | flops | bytes accessed | tf_op | source)
XLA Modules:
  0.0 250.4 jit_solution(13307486363842566407)
XLA Ops:
  2.1 4.4 %collective-permute-start = (bf16[4,1,128,256]{3,0,2,1:T(4,128)(2,1)S(1)}, bf16[4,1,128,256]{3,0,2,1:T(4,128)(2,1)S(1)}, u32[]{:S(2)}, u32[]{:S(2)}) collective-permute-start(bf16[4,1,128,256]{3,0,2,1:T(4,128)(2,1)S(1)} %copy.56), channel_id=1, source_target_pairs={{0,8},{8,16},{16,24},{24,32},{32,40},{40,48},{48,56},{56,64},{64,7... | collective-permute-start | bytes 786440 | tf_op jit(solution)/shard_map/ppermute | solution.py:20
  8.0 3.4 %collective-permute-done = bf16[4,1,128,256]{3,0,2,1:T(4,128)(2,1)S(1)} collective-permute-done((bf16[4,1,128,256]{3,0,2,1:T(4,128)(2,1)S(1)}, bf16[4,1,128,256]{3,0,2,1:T(4,128)(2,1)S(1)}, u32[]{:S(2)}, u32[]{:S(2)}) %collective-permute-start) | collective-permute-done | bytes 262176 | tf_op jit(solution)/shard_map/ppermute | solution.py:20
  11.5 1.8 constant_dynamic-update-slice_fusion.1
  13.3 2.5 %collective-permute-done.1 = bf16[4,1,128,256]{3,0,2,1:T(4,128)(2,1)S(1)} collective-permute-done((bf16[4,1,128,256]{3,0,2,1:T(4,128)(2,1)S(1)}, bf16[4,1,128,256]{3,0,2,1:T(4,128)(2,1)S(1)}, u32[]{:S(2)}, u32[]{:S(2)}) %collective-permute-start.1) | collective-permute-done | bytes 262176 | tf_op jit(solution)/shard_map/ppermute | solution.py:22
  16.0 1.5 copy-done.13
  17.5 4.7 %collective-permute-start.2 = (bf16[4,10,1,256]{3,0,2,1:T(4,128)(2,1)S(1)}, bf16[4,10,1,256]{3,0,2,1:T(4,128)(2,1)S(1)}, u32[]{:S(2)}, u32[]{:S(2)}) collective-permute-start(bf16[4,10,1,256]{3,0,2,1:T(4,128)(2,1)S(1)} %get-tuple-element.34), channel_id=1, source_target_pairs={{0,1},{1,2},{2,3},{3,4},{4,5},{5,6},{6,7},{8,9},{9,10},{10,11},{11... | collective-permute-start | bytes 61448 | tf_op jit(solution)/shard_map/ppermute | solution.py:20
  22.2 2.4 collective-permute-start.3
  24.7 16.1 %reduce_sum.50 = s32[4,200]{1,0:T(4,128)S(1)} reduce(s32[4,200,8,128]{3,2,1,0:T(8,128)} %param.15, s32[]{:T(128)} %constant.144.clone.1), dimensions={2,3}, to_apply=%region_0.0 | reduce | flops 818400 | bytes 3280004 | tf_op jit(solution)/shard_map/reduce_sum | solution.py:148
  40.9 12.7 %fusion.46 = (f32[4,256]{1,0:T(4,128)S(1)}, f32[4,256]{1,0:T(4,128)S(1)}, f32[4,8,128,256]{3,0,2,1:T(4,128)}) fusion(bf16[3,3,256,256]{3,2,1,0:T(8,128)(2,1)S(1)} %copy-done, bf16[4,10,1,256]{3,0,2,1:T(4,128)(2,1)S(1)} %collective-permute-done.3, bf16[4,10,128,256]{3,0,2,1:T(4,128)(2,1)} %copy-done.13, bf16[4,10,1,256]{3,0,2,1:T(4,128)(2,1)S(1)} %collective-permute-done.2), kind=kOutput, calls=%fused_computation.136 | convolution fusion | flops 4842969088 | bytes 8044544 | tf_op jit(solution)/shard_map/conv_general_dilated | solution.py:150
  55.3 1.5 collective-permute-start.5
  57.9 3.1 %collective-permute-start.6 = (f32[4,264]{1,0:T(4,128)S(1)}, f32[4,264]{1,0:T(4,128)S(1)}, u32[]{:S(2)}, u32[]{:S(2)}) collective-permute-start(f32[4,264]{1,0:T(4,128)S(1)} %add.146), channel_id=1, source_target_pairs={{0,4},{1,5},{2,6},{3,7},{4,0},{5,1},{6,2},{7,3},{8,12},{9,13},{10,... | collective-permute-start | bytes 12680 | tf_op jit(solution)/shard_map/ppermute | solution.py:37
  64.5 3.8 %collective-permute-start.8 = (f32[4,264]{1,0:T(4,128)S(1)}, f32[4,264]{1,0:T(4,128)S(1)}, u32[]{:S(2)}, u32[]{:S(2)}) collective-permute-start(f32[4,264]{1,0:T(4,128)S(1)} %add.148), channel_id=1, source_target_pairs={{0,16},{8,24},{16,0},{24,8},{32,48},{40,56},{48,32},{56,40},{64,80... | collective-permute-start | bytes 12680 | tf_op jit(solution)/shard_map/ppermute | solution.py:37
  70.5 2.4 broadcast_compare_fusion
  72.8 2.2 collective-permute-start.10
  76.7 1.6 copy.23
  78.8 3.1 %fusion.4 = bf16[4,1024,256]{2,1,0:T(8,128)(2,1)S(1)} fusion(f32[4,1024,256]{2,0,1:T(4,128)} %bitcast.59, f32[256]{0:T(256)S(1)} %copy-done.14, f32[256]{0:T(256)S(1)} %copy-done.15, f32[4,256]{1,0:T(4,128)S(1)} %div.99, f32[4,256]{1,0:T(4,128)S(1)} %sub.101), kind=kLoop, calls=%fused_computation.6 | loop fusion | flops 6291456 | bytes 6301696 | tf_op jit(solution)/shard_map/convert_element_type | solution.py:169
  82.0 2.1 convolution_convert_fusion.1
  84.1 7.9 %copy.29 = bf16[4,1024,8,32]{3,1,2,0:T(8,128)(2,1)} copy(bf16[4,1024,8,32]{1,3,2,0:T(8,128)(2,1)} %bitcast.55) | data formatting | bytes 4194304 | tf_op jit(solution)/shard_map/reshape | solution.py:180
  92.0 2.1 convolution_convert_fusion
  94.1 7.7 %copy.31 = bf16[4,1024,8,32]{3,1,2,0:T(8,128)(2,1)} copy(bf16[4,1024,8,32]{1,3,2,0:T(8,128)(2,1)} %bitcast.56) | data formatting | bytes 4194304 | tf_op jit(solution)/shard_map/reshape | solution.py:180
  101.8 2.1 or_convert_fusion.refs_3_
  103.9 32.3 %shard_map.149 = (f32[4,8,200,1]{3,2,1,0:T(8,128)}, f32[4,8,200,1]{3,2,1,0:T(8,128)}, f32[4,8,200,32]{3,2,1,0:T(8,128)}) custom-call(bf16[4,8,200,32]{3,2,1,0:T(8,128)(2,1)} %bitcast.58, bf16[4,8,1024,32]{3,2,1,0:T(8,128)(2,1)} %bitcast.53, bf16[4,8,1024,32]{3,2,1,0:T(8,128)(2,1)} %bitcast.54, s32[4,200,1024]{2,1,0:T(8,128)} %or_convert_fusion.refs_3_), custom_call_target="tpu_custom_call" | custom-call | tf_op jit(solution)/shard_map/pallas_call | solution.py:104
  136.2 4.2 %copy.32 = f32[4,200,8,32]{3,2,1,0:T(8,128)} copy(f32[4,200,8,32]{3,1,2,0:T(8,128)} %bitcast.60) | data formatting | bytes 1638400 | tf_op jit(solution)/shard_map/transpose | solution.py:187
  140.4 3.1 %reshape.118 = f32[128,1600]{1,0:T(8,128)} reshape(f32[4,200,8,32]{3,2,1,0:T(8,128)} %copy.32) | data formatting | bytes 1638400 | tf_op jit(solution)/shard_map/reshape | solution.py:187
  143.6 3.1 %reduce.4 = f32[4,8,200]{2,1,0:T(8,128)S(1)} reduce(f32[4,8,200,1]{3,2,1,0:T(8,128)} %get-tuple-element.6, f32[]{:T(128)} %constant.157), dimensions={3}, to_apply=%get-tuple-element.6.reduce_sub_computation | reduce | bytes 51204 | tf_op jit(solution)/shard_map/pallas_call | solution.py:104
  147.0 3.1 %reduce.5 = f32[4,8,200]{2,1,0:T(8,128)S(1)} reduce(f32[4,8,200,1]{3,2,1,0:T(8,128)} %get-tuple-element.7, f32[]{:T(128)} %constant.157), dimensions={3}, to_apply=%get-tuple-element.7.reduce_sub_computation | reduce | bytes 51204 | tf_op jit(solution)/shard_map/pallas_call | solution.py:104
  152.7 3.0 %collective-permute-start.11 = (f32[64,1700]{1,0:T(8,128)}, f32[64,1700]{1,0:T(8,128)S(1)}, u32[]{:S(2)}, u32[]{:S(2)}) collective-permute-start(f32[64,1700]{1,0:T(8,128)} %get-tuple-element.39), channel_id=1, source_target_pairs={{0,4},{1,5},{2,6},{3,7},{4,0},{5,1},{6,2},{7,3},{8,12},{9,13},{10,... | collective-permute-start | bytes 1305608 | tf_op jit(solution)/shard_map/ppermute | solution.py:69
  155.7 6.1 %collective-permute-done.11 = f32[64,1700]{1,0:T(8,128)S(1)} collective-permute-done((f32[64,1700]{1,0:T(8,128)}, f32[64,1700]{1,0:T(8,128)S(1)}, u32[]{:S(2)}, u32[]{:S(2)}) %collective-permute-start.11) | collective-permute-done | bytes 435232 | tf_op jit(solution)/shard_map/ppermute | solution.py:69
  168.3 3.5 %collective-permute-done.12 = f32[32,1700]{1,0:T(8,128)S(1)} collective-permute-done((f32[32,1700]{1,0:T(8,128)S(1)}, f32[32,1700]{1,0:T(8,128)S(1)}, u32[]{:S(2)}, u32[]{:S(2)}) %collective-permute-start.12) | collective-permute-done | bytes 217632 | tf_op jit(solution)/shard_map/ppermute | solution.py:69
  175.5 7.6 %collective-permute-start.13 = (f32[16,1700]{1,0:T(8,128)S(1)}, f32[16,1700]{1,0:T(8,128)S(1)}, u32[]{:S(2)}, u32[]{:S(2)}) collective-permute-start(f32[16,1700]{1,0:T(8,128)S(1)} %get-tuple-element.43), channel_id=1, source_target_pairs={{0,1},{1,0},{2,3},{3,2},{4,5},{5,4},{6,7},{7,6},{8,9},{9,8},{10,11... | collective-permute-start | bytes 326408 | tf_op jit(solution)/shard_map/ppermute | solution.py:69
  184.9 1.9 collective-permute-start.14
  186.8 2.9 %collective-permute-done.14 = f32[8,1700]{1,0:T(8,128)S(1)} collective-permute-done((f32[8,1700]{1,0:T(8,128)S(1)}, f32[8,1700]{1,0:T(8,128)S(1)}, u32[]{:S(2)}, u32[]{:S(2)}) %collective-permute-start.14) | collective-permute-done | bytes 54432 | tf_op jit(solution)/shard_map/ppermute | solution.py:69
  190.8 2.4 collective-permute-done.15
  193.8 3.1 %collective-permute-start.16 = (f32[2,1700]{1,0:T(2,128)S(1)}, f32[2,1700]{1,0:T(2,128)S(1)}, u32[]{:S(2)}, u32[]{:S(2)}) collective-permute-start(f32[2,1700]{1,0:T(2,128)S(1)} %get-tuple-element.49), channel_id=1, source_target_pairs={{0,16},{8,24},{16,0},{24,8},{32,48},{40,56},{48,32},{56,40},{64,80... | collective-permute-start | bytes 40808 | tf_op jit(solution)/shard_map/ppermute | solution.py:69
  199.8 1.6 collective-permute-done.17
  203.0 1.5 collective-permute-done.18
  204.6 3.3 %collective-permute-start.19 = (bf16[2,1600]{1,0:T(2,128)(2,1)S(1)}, bf16[2,1600]{1,0:T(2,128)(2,1)S(1)}, u32[]{:S(2)}, u32[]{:S(2)}) collective-permute-start(bf16[2,1600]{1,0:T(2,128)(2,1)S(1)} %broadcast_select_fusion.4), channel_id=1, source_target_pairs={{0,16},{8,24},{16,0},{24,8},{32,48},{40,56},{48,32},{56,40},{64,80... | collective-permute-start | bytes 19208 | tf_op jit(solution)/shard_map/ppermute | solution.py:81
  209.2 2.5 collective-permute-done.20
  211.7 1.7 collective-permute-start.21
  213.4 2.6 %collective-permute-done.21 = bf16[8,1600]{1,0:T(8,128)(2,1)S(1)} collective-permute-done((bf16[8,1600]{1,0:T(8,128)(2,1)S(1)}, bf16[8,1600]{1,0:T(8,128)(2,1)S(1)}, u32[]{:S(2)}, u32[]{:S(2)}) %collective-permute-start.21) | collective-permute-done | bytes 25632 | tf_op jit(solution)/shard_map/ppermute | solution.py:81
  216.0 9.1 %collective-permute-start.22 = (bf16[16,1600]{1,0:T(8,128)(2,1)S(1)}, bf16[16,1600]{1,0:T(8,128)(2,1)S(1)}, u32[]{:S(2)}, u32[]{:S(2)}) collective-permute-start(bf16[16,1600]{1,0:T(8,128)(2,1)S(1)} %maximum_select_fusion.3), channel_id=1, source_target_pairs={{0,1},{1,0},{2,3},{3,2},{4,5},{5,4},{6,7},{7,6},{8,9},{9,8},{10,11... | collective-permute-start | bytes 153608 | tf_op jit(solution)/shard_map/ppermute | solution.py:81
  226.0 1.7 collective-permute-start.23
  227.7 2.9 %collective-permute-done.23 = bf16[32,1600]{1,0:T(8,128)(2,1)S(1)} collective-permute-done((bf16[32,1600]{1,0:T(8,128)(2,1)S(1)}, bf16[32,1600]{1,0:T(8,128)(2,1)S(1)}, u32[]{:S(2)}, u32[]{:S(2)}) %collective-permute-start.23) | collective-permute-done | bytes 102432 | tf_op jit(solution)/shard_map/ppermute | solution.py:81
  230.6 3.0 %collective-permute-start.24 = (bf16[64,1600]{1,0:T(8,128)(2,1)S(1)}, bf16[64,1600]{1,0:T(8,128)(2,1)S(1)}, u32[]{:S(2)}, u32[]{:S(2)}) collective-permute-start(bf16[64,1600]{1,0:T(8,128)(2,1)S(1)} %maximum_select_fusion.1), channel_id=1, source_target_pairs={{0,4},{1,5},{2,6},{3,7},{4,0},{5,1},{6,2},{7,3},{8,12},{9,13},{10,... | collective-permute-start | bytes 614408 | tf_op jit(solution)/shard_map/ppermute | solution.py:81
  233.6 4.4 %collective-permute-done.24 = bf16[64,1600]{1,0:T(8,128)(2,1)S(1)} collective-permute-done((bf16[64,1600]{1,0:T(8,128)(2,1)S(1)}, bf16[64,1600]{1,0:T(8,128)(2,1)S(1)}, u32[]{:S(2)}, u32[]{:S(2)}) %collective-permute-start.24) | collective-permute-done | bytes 204832 | tf_op jit(solution)/shard_map/ppermute | solution.py:81
  239.4 1.7 fusion.49
  243.8 3.2 %convolution_convert_fusion.2 = bf16[4,200,1024]{2,1,0:T(8,128)(2,1)} fusion(bf16[4,1024,256]{2,1,0:T(8,128)(2,1)S(1)} %fusion.4, bf16[4,200,256]{2,1,0:T(8,128)(2,1)} %fusion.11, bf16[256,256]{1,0:T(8,128)(2,1)S(1)} %copy-done.10), kind=kOutput, calls=%fused_computation.16 | convolution fusion | flops 525312000 | bytes 4276224 | tf_op jit(solution)/shard_map/bqc,bpc->bqp/dot_general | solution.py:205
  247.0 3.1 %copy.43 = bf16[100,8,8,128]{3,2,1,0:T(8,128)(2,1)} copy(bf16[100,8,8,128]{3,1,2,0:T(8,128)(2,1)} %bitcast.57) | data formatting | bytes 3276800
  (162 shorter events, 40.9 us)
Async XLA Ops:
  0.6 40.2 %copy-start = (bf16[3,3,256,256]{3,2,1,0:T(8,128)(2,1)S(1)}, bf16[3,3,256,256]{3,2,1,0:T(8,128)(2,1)}, u32[]{:S(2)}) copy-start(bf16[3,3,256,256]{3,2,1,0:T(8,128)(2,1)} %param.17) | copy-start | bytes 3538948
  0.6 10.9 %copy-start.2 = (bf16[4,8,128,256]{3,2,1,0:T(8,128)(2,1)S(1)}, bf16[4,8,128,256]{3,2,1,0:T(8,128)(2,1)}, u32[]{:S(2)}) copy-start(bf16[4,8,128,256]{3,2,1,0:T(8,128)(2,1)} %param.14) | copy-start | bytes 6291460
  2.1 9.3 %collective-permute-start = (bf16[4,1,128,256]{3,0,2,1:T(4,128)(2,1)S(1)}, bf16[4,1,128,256]{3,0,2,1:T(4,128)(2,1)S(1)}, u32[]{:S(2)}, u32[]{:S(2)}) collective-permute-start(bf16[4,1,128,256]{3,0,2,1:T(4,128)(2,1)S(1)} %copy.56), channel_id=1, source_target_pairs={{0,8},{8,16},{16,24},{24,32},{32,40},{40,48},{48,56},{56,64},{64,7... | collective-permute-start | bytes 786440 | tf_op jit(solution)/shard_map/ppermute | solution.py:20
  6.7 9.1 %collective-permute-start.1 = (bf16[4,1,128,256]{3,0,2,1:T(4,128)(2,1)S(1)}, bf16[4,1,128,256]{3,0,2,1:T(4,128)(2,1)S(1)}, u32[]{:S(2)}, u32[]{:S(2)}) collective-permute-start(bf16[4,1,128,256]{3,0,2,1:T(4,128)(2,1)S(1)} %copy.57), channel_id=1, source_target_pairs={{8,0},{16,8},{24,16},{32,24},{40,32},{48,40},{56,48},{64,56},{72,6... | collective-permute-start | bytes 786440 | tf_op jit(solution)/shard_map/ppermute | solution.py:22
  15.9 1.5 copy-start.13
  17.5 23.3 %collective-permute-start.2 = (bf16[4,10,1,256]{3,0,2,1:T(4,128)(2,1)S(1)}, bf16[4,10,1,256]{3,0,2,1:T(4,128)(2,1)S(1)}, u32[]{:S(2)}, u32[]{:S(2)}) collective-permute-start(bf16[4,10,1,256]{3,0,2,1:T(4,128)(2,1)S(1)} %get-tuple-element.34), channel_id=1, source_target_pairs={{0,1},{1,2},{2,3},{3,4},{4,5},{5,6},{6,7},{8,9},{9,10},{10,11},{11... | collective-permute-start | bytes 61448 | tf_op jit(solution)/shard_map/ppermute | solution.py:20
  22.2 18.6 %collective-permute-start.3 = (bf16[4,10,1,256]{3,0,2,1:T(4,128)(2,1)S(1)}, bf16[4,10,1,256]{3,0,2,1:T(4,128)(2,1)S(1)}, u32[]{:S(2)}, u32[]{:S(2)}) collective-permute-start(bf16[4,10,1,256]{3,0,2,1:T(4,128)(2,1)S(1)} %get-tuple-element.35), channel_id=1, source_target_pairs={{1,0},{2,1},{3,2},{4,3},{5,4},{6,5},{7,6},{9,8},{10,9},{11,10},{12... | collective-permute-start | bytes 61448 | tf_op jit(solution)/shard_map/ppermute | solution.py:22
  53.6 21.5 %copy-start.3 = (f32[4,200,256]{2,1,0:T(8,128)S(1)}, f32[4,200,256]{2,1,0:T(8,128)}, u32[]{:S(2)}) copy-start(f32[4,200,256]{2,1,0:T(8,128)} %param.16) | copy-start | bytes 2457604
  53.6 21.5 %copy-start.11 = (bf16[256,256]{1,0:T(8,128)(2,1)S(1)}, bf16[256,256]{1,0:T(8,128)(2,1)}, u32[]{:S(2)}) copy-start(bf16[256,256]{1,0:T(8,128)(2,1)} %param.20) | copy-start | bytes 393220
  54.1 1.2 collective-permute-start.4
  55.3 2.5 %collective-permute-start.5 = (f32[4,264]{1,0:T(4,128)S(1)}, f32[4,264]{1,0:T(4,128)S(1)}, u32[]{:S(2)}, u32[]{:S(2)}) collective-permute-start(f32[4,264]{1,0:T(4,128)S(1)} %fusion.56), channel_id=1, source_target_pairs={{0,2},{1,3},{2,0},{3,1},{4,6},{5,7},{6,4},{7,5},{8,10},{9,11},{10,... | collective-permute-start | bytes 12680 | tf_op jit(solution)/shard_map/ppermute | solution.py:37
  57.9 4.1 %collective-permute-start.6 = (f32[4,264]{1,0:T(4,128)S(1)}, f32[4,264]{1,0:T(4,128)S(1)}, u32[]{:S(2)}, u32[]{:S(2)}) collective-permute-start(f32[4,264]{1,0:T(4,128)S(1)} %add.146), channel_id=1, source_target_pairs={{0,4},{1,5},{2,6},{3,7},{4,0},{5,1},{6,2},{7,3},{8,12},{9,13},{10,... | collective-permute-start | bytes 12680 | tf_op jit(solution)/shard_map/ppermute | solution.py:37
  62.0 2.5 collective-permute-start.7
  64.5 4.8 %collective-permute-start.8 = (f32[4,264]{1,0:T(4,128)S(1)}, f32[4,264]{1,0:T(4,128)S(1)}, u32[]{:S(2)}, u32[]{:S(2)}) collective-permute-start(f32[4,264]{1,0:T(4,128)S(1)} %add.148), channel_id=1, source_target_pairs={{0,16},{8,24},{16,0},{24,8},{32,48},{40,56},{48,32},{56,40},{64,80... | collective-permute-start | bytes 12680 | tf_op jit(solution)/shard_map/ppermute | solution.py:37
  69.3 3.6 %collective-permute-start.9 = (f32[4,264]{1,0:T(4,128)S(1)}, f32[4,264]{1,0:T(4,128)S(1)}, u32[]{:S(2)}, u32[]{:S(2)}) collective-permute-start(f32[4,264]{1,0:T(4,128)S(1)} %add.149), channel_id=1, source_target_pairs={{0,32},{8,40},{16,48},{24,56},{32,0},{40,8},{48,16},{56,24},{64,96... | collective-permute-start | bytes 12680 | tf_op jit(solution)/shard_map/ppermute | solution.py:37
  72.8 5.5 %collective-permute-start.10 = (f32[4,264]{1,0:T(4,128)S(1)}, f32[4,264]{1,0:T(4,128)S(1)}, u32[]{:S(2)}, u32[]{:S(2)}) collective-permute-start(f32[4,264]{1,0:T(4,128)S(1)} %add.150), channel_id=1, source_target_pairs={{0,64},{8,72},{16,80},{24,88},{32,96},{40,104},{48,112},{56,120},{... | collective-permute-start | bytes 12680 | tf_op jit(solution)/shard_map/ppermute | solution.py:37
  75.3 3.4 %copy-start.14 = (f32[256]{0:T(256)S(1)}, f32[256]{0:T(256)}, u32[]{:S(2)}) copy-start(f32[256]{0:T(256)} %param.19) | copy-start | bytes 3076
  75.3 3.4 %copy-start.15 = (f32[256]{0:T(256)S(1)}, f32[256]{0:T(256)}, u32[]{:S(2)}) copy-start(f32[256]{0:T(256)} %param.18) | copy-start | bytes 3076
  78.8 3.2 %copy-start.7 = (bf16[256,256]{1,0:T(8,128)(2,1)S(1)}, bf16[256,256]{1,0:T(8,128)(2,1)}, u32[]{:S(2)}) copy-start(bf16[256,256]{1,0:T(8,128)(2,1)} %param.21) | copy-start | bytes 393220
  84.1 7.9 %copy-start.8 = (bf16[256,256]{1,0:T(8,128)(2,1)S(1)}, bf16[256,256]{1,0:T(8,128)(2,1)}, u32[]{:S(2)}) copy-start(bf16[256,256]{1,0:T(8,128)(2,1)} %param.22) | copy-start | bytes 393220
  152.7 9.1 %collective-permute-start.11 = (f32[64,1700]{1,0:T(8,128)}, f32[64,1700]{1,0:T(8,128)S(1)}, u32[]{:S(2)}, u32[]{:S(2)}) collective-permute-start(f32[64,1700]{1,0:T(8,128)} %get-tuple-element.39), channel_id=1, source_target_pairs={{0,4},{1,5},{2,6},{3,7},{4,0},{5,1},{6,2},{7,3},{8,12},{9,13},{10,... | collective-permute-start | bytes 1305608 | tf_op jit(solution)/shard_map/ppermute | solution.py:69
  161.8 1.0 copy-start.5
  166.9 5.0 %collective-permute-start.12 = (f32[32,1700]{1,0:T(8,128)S(1)}, f32[32,1700]{1,0:T(8,128)S(1)}, u32[]{:S(2)}, u32[]{:S(2)}) collective-permute-start(f32[32,1700]{1,0:T(8,128)S(1)} %get-tuple-element.41), channel_id=1, source_target_pairs={{0,2},{1,3},{2,0},{3,1},{4,6},{5,7},{6,4},{7,5},{8,10},{9,11},{10,... | collective-permute-start | bytes 652808 | tf_op jit(solution)/shard_map/ppermute | solution.py:69
  171.8 0.7 copy-start.6
  175.5 8.5 %collective-permute-start.13 = (f32[16,1700]{1,0:T(8,128)S(1)}, f32[16,1700]{1,0:T(8,128)S(1)}, u32[]{:S(2)}, u32[]{:S(2)}) collective-permute-start(f32[16,1700]{1,0:T(8,128)S(1)} %get-tuple-element.43), channel_id=1, source_target_pairs={{0,1},{1,0},{2,3},{3,2},{4,5},{5,4},{6,7},{7,6},{8,9},{9,8},{10,11... | collective-permute-start | bytes 326408 | tf_op jit(solution)/shard_map/ppermute | solution.py:69
  184.9 4.9 %collective-permute-start.14 = (f32[8,1700]{1,0:T(8,128)S(1)}, f32[8,1700]{1,0:T(8,128)S(1)}, u32[]{:S(2)}, u32[]{:S(2)}) collective-permute-start(f32[8,1700]{1,0:T(8,128)S(1)} %get-tuple-element.45), channel_id=1, source_target_pairs={{0,64},{8,72},{16,80},{24,88},{32,96},{40,104},{48,112},{56,120},{... | collective-permute-start | bytes 163208 | tf_op jit(solution)/shard_map/ppermute | solution.py:69
  189.9 49.5 %copy-start.9 = (bf16[256,256]{1,0:T(8,128)(2,1)S(1)}, bf16[256,256]{1,0:T(8,128)(2,1)}, u32[]{:S(2)}) copy-start(bf16[256,256]{1,0:T(8,128)(2,1)} %param.23) | copy-start | bytes 393220
  190.4 2.8 %collective-permute-start.15 = (f32[4,1700]{1,0:T(4,128)S(1)}, f32[4,1700]{1,0:T(4,128)S(1)}, u32[]{:S(2)}, u32[]{:S(2)}) collective-permute-start(f32[4,1700]{1,0:T(4,128)S(1)} %get-tuple-element.47), channel_id=1, source_target_pairs={{0,32},{8,40},{16,48},{24,56},{32,0},{40,8},{48,16},{56,24},{64,96... | collective-permute-start | bytes 81608 | tf_op jit(solution)/shard_map/ppermute | solution.py:69
  193.8 4.2 %collective-permute-start.16 = (f32[2,1700]{1,0:T(2,128)S(1)}, f32[2,1700]{1,0:T(2,128)S(1)}, u32[]{:S(2)}, u32[]{:S(2)}) collective-permute-start(f32[2,1700]{1,0:T(2,128)S(1)} %get-tuple-element.49), channel_id=1, source_target_pairs={{0,16},{8,24},{16,0},{24,8},{32,48},{40,56},{48,32},{56,40},{64,80... | collective-permute-start | bytes 40808 | tf_op jit(solution)/shard_map/ppermute | solution.py:69
  198.6 2.8 %collective-permute-start.17 = (f32[1,1700]{1,0:T(1,128)S(1)}, f32[1,1700]{1,0:T(1,128)S(1)}, u32[]{:S(2)}, u32[]{:S(2)}) collective-permute-start(f32[1,1700]{1,0:T(1,128)S(1)} %get-tuple-element.54), channel_id=1, source_target_pairs={{0,8},{8,0},{16,24},{24,16},{32,40},{40,32},{48,56},{56,48},{64,72... | collective-permute-start | bytes 20408 | tf_op jit(solution)/shard_map/ppermute | solution.py:69
  202.0 2.6 %collective-permute-start.18 = (bf16[1,1600]{1,0:T(2,128)(2,1)S(1)}, bf16[1,1600]{1,0:T(2,128)(2,1)S(1)}, u32[]{:S(2)}, u32[]{:S(2)}) collective-permute-start(bf16[1,1600]{1,0:T(2,128)(2,1)S(1)} %fusion.32), channel_id=1, source_target_pairs={{0,8},{8,0},{16,24},{24,16},{32,40},{40,32},{48,56},{56,48},{64,72... | collective-permute-start | bytes 9608 | tf_op jit(solution)/shard_map/ppermute | solution.py:81
  204.6 4.4 %collective-permute-start.19 = (bf16[2,1600]{1,0:T(2,128)(2,1)S(1)}, bf16[2,1600]{1,0:T(2,128)(2,1)S(1)}, u32[]{:S(2)}, u32[]{:S(2)}) collective-permute-start(bf16[2,1600]{1,0:T(2,128)(2,1)S(1)} %broadcast_select_fusion.4), channel_id=1, source_target_pairs={{0,16},{8,24},{16,0},{24,8},{32,48},{40,56},{48,32},{56,40},{64,80... | collective-permute-start | bytes 19208 | tf_op jit(solution)/shard_map/ppermute | solution.py:81
  209.0 2.6 %collective-permute-start.20 = (bf16[4,1600]{1,0:T(4,128)(2,1)S(1)}, bf16[4,1600]{1,0:T(4,128)(2,1)S(1)}, u32[]{:S(2)}, u32[]{:S(2)}) collective-permute-start(bf16[4,1600]{1,0:T(4,128)(2,1)S(1)} %maximum_select_fusion.5), channel_id=1, source_target_pairs={{0,32},{8,40},{16,48},{24,56},{32,0},{40,8},{48,16},{56,24},{64,96... | collective-permute-start | bytes 38408 | tf_op jit(solution)/shard_map/ppermute | solution.py:81
  211.7 4.3 %collective-permute-start.21 = (bf16[8,1600]{1,0:T(8,128)(2,1)S(1)}, bf16[8,1600]{1,0:T(8,128)(2,1)S(1)}, u32[]{:S(2)}, u32[]{:S(2)}) collective-permute-start(bf16[8,1600]{1,0:T(8,128)(2,1)S(1)} %maximum_select_fusion.4), channel_id=1, source_target_pairs={{0,64},{8,72},{16,80},{24,88},{32,96},{40,104},{48,112},{56,120},{... | collective-permute-start | bytes 76808 | tf_op jit(solution)/shard_map/ppermute | solution.py:81
  216.0 25.6 %copy-start.16 = (f32[256]{0:T(256)S(1)}, f32[256]{0:T(256)}, u32[]{:S(2)}) copy-start(f32[256]{0:T(256)} %param.25) | copy-start | bytes 3076
  216.0 25.6 %copy-start.17 = (f32[256]{0:T(256)S(1)}, f32[256]{0:T(256)}, u32[]{:S(2)}) copy-start(f32[256]{0:T(256)} %param.24) | copy-start | bytes 3076
  216.0 10.0 %collective-permute-start.22 = (bf16[16,1600]{1,0:T(8,128)(2,1)S(1)}, bf16[16,1600]{1,0:T(8,128)(2,1)S(1)}, u32[]{:S(2)}, u32[]{:S(2)}) collective-permute-start(bf16[16,1600]{1,0:T(8,128)(2,1)S(1)} %maximum_select_fusion.3), channel_id=1, source_target_pairs={{0,1},{1,0},{2,3},{3,2},{4,5},{5,4},{6,7},{7,6},{8,9},{9,8},{10,11... | collective-permute-start | bytes 153608 | tf_op jit(solution)/shard_map/ppermute | solution.py:81
  226.0 4.6 %collective-permute-start.23 = (bf16[32,1600]{1,0:T(8,128)(2,1)S(1)}, bf16[32,1600]{1,0:T(8,128)(2,1)S(1)}, u32[]{:S(2)}, u32[]{:S(2)}) collective-permute-start(bf16[32,1600]{1,0:T(8,128)(2,1)S(1)} %maximum_select_fusion.2), channel_id=1, source_target_pairs={{0,2},{1,3},{2,0},{3,1},{4,6},{5,7},{6,4},{7,5},{8,10},{9,11},{10,... | collective-permute-start | bytes 307208 | tf_op jit(solution)/shard_map/ppermute | solution.py:81
  230.6 7.4 %collective-permute-start.24 = (bf16[64,1600]{1,0:T(8,128)(2,1)S(1)}, bf16[64,1600]{1,0:T(8,128)(2,1)S(1)}, u32[]{:S(2)}, u32[]{:S(2)}) collective-permute-start(bf16[64,1600]{1,0:T(8,128)(2,1)S(1)} %maximum_select_fusion.1), channel_id=1, source_target_pairs={{0,4},{1,5},{2,6},{3,7},{4,0},{5,1},{6,2},{7,3},{8,12},{9,13},{10,... | collective-permute-start | bytes 614408 | tf_op jit(solution)/shard_map/ppermute | solution.py:81
  238.1 4.7 %copy-start.12 = (bf16[256,256]{1,0:T(8,128)(2,1)S(1)}, bf16[256,256]{1,0:T(8,128)(2,1)}, u32[]{:S(2)}) copy-start(bf16[256,256]{1,0:T(8,128)(2,1)} %param.26) | copy-start | bytes 393220
  239.4 4.3 %copy-start.10 = (bf16[256,256]{1,0:T(8,128)(2,1)S(1)}, bf16[256,256]{1,0:T(8,128)(2,1)}, u32[]{:S(2)}) copy-start(bf16[256,256]{1,0:T(8,128)(2,1)} %param.27) | copy-start | bytes 393220
  241.9 0.9 copy-start.4
  243.8 6.3 %copy-start.1 = (bf16[3,3,256,256]{3,2,1,0:T(8,128)(2,1)S(1)}, bf16[3,3,256,256]{3,2,1,0:T(8,128)(2,1)}, u32[]{:S(2)}) copy-start(bf16[3,3,256,256]{3,2,1,0:T(8,128)(2,1)} %param.17) | copy-start | bytes 3538948

commit v2 on v1

--- a/solution.py
+++ b/solution.py
@@ -85,42 +85,84 @@
     return a
 
 
-def attention_kernel(q_ref, k_ref, v_ref, a_ref, top_ref, tot_ref, wv_ref, *, scale):
-    q = q_ref[0, 0]
-    k = k_ref[0, 0]
-    s = lax.dot_general(q, k, (((1,), (1,)), ((), ())), preferred_element_type=jnp.float32) * scale
-    allowed = a_ref[0] != 0
-    top = jnp.max(jnp.where(allowed, s, NEG), axis=1, keepdims=True)
-    w = jnp.where(allowed, jnp.exp(s - top), 0.0).astype(jnp.bfloat16)
-    tot_ref[0, 0] = jnp.sum(w.astype(jnp.float32), axis=1, keepdims=True)
-    top_ref[0, 0] = top
-    wv_ref[0, 0] = jnp.dot(w, v_ref[0, 0], preferred_element_type=jnp.float32)
-
-
-def attention(qh, kh, vh, allowed, scale):
-    images, heads, queries, hd = qh.shape
-    pixels = kh.shape[2]
-    kernel = lambda *refs: attention_kernel(*refs, scale=scale)
+def prep_kernel(m_ref, fg_ref, cnt_ref):
+    queries = fg_ref.shape[1]
+    tile_rows = m_ref.shape[1] // queries
+    tile_cols = m_ref.shape[2]
+    acc = jnp.zeros((queries, tile_cols), jnp.float32)
+    for r in range(tile_rows):
+        rows = m_ref[0, pl.ds(r, queries, stride=tile_rows), :]
+        fg = (rows == 1).astype(jnp.float32)
+        acc = acc + fg
+        fg_ref[0, :, r * tile_cols : (r + 1) * tile_cols] = fg.astype(jnp.bfloat16)
+    cnt_ref[0] = jnp.sum(acc, axis=1, keepdims=True)
+
+
+def prep(masks):
+    images, queries, tile_rows, tile_cols = masks.shape
+    flat = masks.reshape(images, queries * tile_rows, tile_cols)
+    return pl.pallas_call(
+        prep_kernel,
+        grid=(images,),
+        in_specs=[pl.BlockSpec((1, queries * tile_rows, tile_cols), lambda i: (i, 0, 0))],
+        out_specs=[
+            pl.BlockSpec((1, queries, tile_rows * tile_cols), lambda i: (i, 0, 0)),
+            pl.BlockSpec((1, queries, 1), lambda i: (i, 0, 0)),
+        ],
+        out_shape=[
+            jax.ShapeDtypeStruct((images, queries, tile_rows * tile_cols), jnp.bfloat16),
+            jax.ShapeDtypeStruct((images, queries, 1), jnp.float32),
+        ],
+    )(flat)
+
+
+def attention_kernel(q_ref, k_ref, v_ref, fg_ref, zero_ref, top_ref, tot_ref, wv_ref, *, heads, scale):
+    queries = fg_ref.shape[1]
+    width = k_ref.shape[2]
+    head_size = width // heads
+    k = k_ref[0]
+    v = v_ref[0]
+    allowed = (fg_ref[0] != 0) | (zero_ref[0] != 0)
+    lane = lax.broadcasted_iota(jnp.int32, (queries, width), 1)
+    acc = jnp.zeros((queries, width), jnp.float32)
+    for h in range(heads):
+        q = q_ref[0, h * queries : (h + 1) * queries, :]
+        s = lax.dot_general(q, k, (((1,), (1,)), ((), ())), preferred_element_type=jnp.float32) * scale
+        top = jnp.max(jnp.where(allowed, s, NEG), axis=1, keepdims=True)
+        w = jnp.where(allowed, jnp.exp(s - top), 0.0).astype(jnp.bfloat16)
+        tot_ref[0, :, h : h + 1] = jnp.sum(w.astype(jnp.float32), axis=1, keepdims=True)
+        top_ref[0, :, h : h + 1] = top
+        r = jnp.dot(w, v, preferred_element_type=jnp.float32)
+        inside = (lane >= h * head_size) & (lane < (h + 1) * head_size)
+        acc = acc + jnp.where(inside, r, 0.0)
+    wv_ref[0] = acc
+
+
+def attention(qbd, keys, vals, fg, zero, heads, scale):
+    images, pixels, width = keys.shape
+    queries = fg.shape[1]
+    kernel = lambda *refs: attention_kernel(*refs, heads=heads, scale=scale)
     return pl.pallas_call(
         kernel,
-        grid=(images, heads),
+        grid=(images,),
         in_specs=[
-            pl.BlockSpec((1, 1, queries, hd), lambda i, h: (i, h, 0, 0)),
-            pl.BlockSpec((1, 1, pixels, hd), lambda i, h: (i, h, 0, 0)),
-            pl.BlockSpec((1, 1, pixels, hd), lambda i, h: (i, h, 0, 0)),
-            pl.BlockSpec((1, queries, pixels), lambda i, h: (i, 0, 0)),
+            pl.BlockSpec((1, heads * queries, width), lambda i: (i, 0, 0)),
+            pl.BlockSpec((1, pixels, width), lambda i: (i, 0, 0)),
+            pl.BlockSpec((1, pixels, width), lambda i: (i, 0, 0)),
+            pl.BlockSpec((1, queries, pixels), lambda i: (i, 0, 0)),
+            pl.BlockSpec((1, queries, 1), lambda i: (i, 0, 0)),
         ],
         out_specs=[
-            pl.BlockSpec((1, 1, queries, 1), lambda i, h: (i, h, 0, 0)),
-            pl.BlockSpec((1, 1, queries, 1), lambda i, h: (i, h, 0, 0)),
-            pl.BlockSpec((1, 1, queries, hd), lambda i, h: (i, h, 0, 0)),
+            pl.BlockSpec((1, queries, heads), lambda i: (i, 0, 0)),
+            pl.BlockSpec((1, queries, heads), lambda i: (i, 0, 0)),
+            pl.BlockSpec((1, queries, width), lambda i: (i, 0, 0)),
         ],
         out_shape=[
-            jax.ShapeDtypeStruct((images, heads, queries, 1), jnp.float32),
-            jax.ShapeDtypeStruct((images, heads, queries, 1), jnp.float32),
-            jax.ShapeDtypeStruct((images, heads, queries, hd), jnp.float32),
-        ],
-    )(qh, kh, vh, allowed)
+            jax.ShapeDtypeStruct((images, queries, heads), jnp.float32),
+            jax.ShapeDtypeStruct((images, queries, heads), jnp.float32),
+            jax.ShapeDtypeStruct((images, queries, width), jnp.float32),
+        ],
+    )(qbd, keys, vals, fg, zero)
 
 
 def on_device(
@@ -145,7 +187,7 @@
     head_size = width // heads
     pixels = tile_rows * tile_cols
     devices = lax.axis_size("rows") * lax.axis_size("cols")
-    local_count = jnp.sum(masks, axis=(2, 3)).astype(jnp.float32)
+    fg, local_count = prep(masks)
     padded = with_halo(features, (("rows", 1), ("cols", 2)), 1)
     conv = lax.conv_general_dilated(
         padded,
@@ -158,7 +200,7 @@
     grouped = conv.reshape(images, pixels, GROUPS, width // GROUPS)
     first_sum = jnp.sum(grouped, axis=(1, 3))
     second_sum = jnp.sum(grouped * grouped, axis=(1, 3))
-    stats = butterfly_sum(jnp.concatenate([local_count, first_sum, second_sum], axis=1))
+    stats = butterfly_sum(jnp.concatenate([local_count[..., 0], first_sum, second_sum], axis=1))
     count = stats[:, :query_count]
     first_sum = stats[:, query_count : query_count + GROUPS]
     second_sum = stats[:, query_count + GROUPS :]
@@ -174,19 +216,20 @@
     qproj = jnp.dot(
         queries.astype(jnp.bfloat16), query_weight, preferred_element_type=jnp.float32
     ).astype(jnp.bfloat16)
-    allowed = (
-        (masks.reshape(images, query_count, pixels) == 1) | (count == 0.0)[:, :, None]
-    ).astype(jnp.int32)
-    by_head = lambda x: x.reshape(images, -1, heads, head_size).transpose(0, 2, 1, 3)
-    top, total, weighted = attention(
-        by_head(qproj), by_head(keys), by_head(vals), allowed, 1.0 / head_size**0.5
-    )
+    zero = (count == 0.0).astype(jnp.float32)[:, :, None]
+    head_of_lane = jnp.arange(width) // head_size
+    qbd = jnp.where(
+        head_of_lane[None, None, None, :] == jnp.arange(heads)[None, :, None, None],
+        qproj[:, None, :, :],
+        jnp.zeros((), jnp.bfloat16),
+    ).reshape(images, heads * query_count, width)
+    top, total, weighted = attention(qbd, keys, vals, fg, zero, heads, 1.0 / head_size**0.5)
     span = images * query_count * width // devices
     packed = jnp.concatenate(
         [
-            weighted.transpose(0, 2, 1, 3).reshape(devices, span),
-            total[..., 0].transpose(0, 2, 1).reshape(devices, span // 32),
-            top[..., 0].transpose(0, 2, 1).reshape(devices, span // 32),
+            weighted.reshape(devices, span),
+            total.reshape(devices, span // 32),
+            top.reshape(devices, span // 32),
         ],
         axis=1,
     )

time: 255 us -> 234 us (0.918); the launches traced: 250 us -> 232 us
  other arithmetic: 36.5 us -> 23.9 us
  Pallas kernels: 32.3 us -> 25.6 us
  starting transfers between devices: 64.7 us -> 68 us
    reduce_sum x1 -> x0, other arithmetic: 16.1 us -> none  [on_device(): local_count = jnp.sum(masks, axis=(2, 3)).astype(jnp.float32)]
    reshape x6 -> x3, local copies, waits for them, and re-layouts: 20.7 us -> 4.85 us  [the longest x1 2.5 us: on_device(): weighted.reshape(devices, span)]
    reshape x12, local copies, waits for them, and re-layouts: 4.19 us -> 14.6 us  [merge(): w = wa * jnp.repeat(fa, 32, axis=1) + wb * jnp.repeat(fb, 32, axis=1)]
    pallas_call x1 -> x2, Pallas kernels: 32.3 us -> 25.6 us  [the longest x1 21.2 us: attention(): pl.pallas_call(kernel, grid=(images,), in_specs=[pl.BlockSpec((1, heads *...]
    broadcast_in_dim x16, local copies, waits for them, and re-layouts: 1.92 us -> 7.11 us  [merge(): w = wa * jnp.repeat(fa, 32, axis=1) + wb * jnp.repeat(fb, 32, axis=1)]
    pallas_call x2 -> x1, other arithmetic: 6.15 us -> 1.21 us  [prep(): pl.pallas_call(prep_kernel, grid=(images,), in_specs=[pl.BlockSpec((1, qu...]
    transpose x3 -> x0, local copies, waits for them, and re-layouts: 4.53 us -> none  [the longest x1 4.18 us: on_device(): weighted.transpose(0, 2, 1, 3).reshape(devices, span)]
    add x6, other arithmetic: 2.63 us -> 6.85 us  [merge(): w = wa * jnp.repeat(fa, 32, axis=1) + wb * jnp.repeat(fb, 32, axis=1)]
  transfers between devices with their start and end apart: 25 -> 25, of which waited for: 21 -> 22; matrix products, arithmetic and copies ran while one was open for 9% -> 2% of each run, Pallas kernels for 0% -> 2%
where the time goes in v2:
time: 234 us; the launch traced here: 232 us
  starting transfers between devices  68 us (29%)
  local copies, waits for them, and re-layouts  46.7 us (20%)
  waiting for transfers between devices  44 us (19%)
  Pallas kernels  25.6 us (11%)
  other arithmetic  23.9 us (10%)
  matrix products  22.8 us (10%)
    ppermute x7, starting transfers between devices, doubling_gather(): got = lax.ppermute(a, axis, [(i, i ^ k) for i in range(n)])  22.1 us
    pallas_call x1, Pallas kernels, attention(): pl.pallas_call(kernel, grid=(images,), in_specs=[pl.BlockSpec((1, heads *...  21.2 us
    ppermute x7, starting transfers between devices, halving_merge(): got = lax.ppermute(send, axis, [(i, i ^ k) for i in range(n)])  19.8 us
    ppermute x7, waiting for transfers between devices, halving_merge(): got = lax.ppermute(send, axis, [(i, i ^ k) for i in range(n)])  17.9 us
    reshape x12, local copies, waits for them, and re-layouts, merge(): w = wa * jnp.repeat(fa, 32, axis=1) + wb * jnp.repeat(fb, 32, axis=1)  14.6 us
    ppermute x7, starting transfers between devices, butterfly_sum(): got = lax.ppermute(x, axis, [(i, i ^ k) for i in range(n)])  13.8 us
    ppermute x7, waiting for transfers between devices, doubling_gather(): got = lax.ppermute(a, axis, [(i, i ^ k) for i in range(n)])  13.6 us
    conv_general_dilated x1, matrix products, on_device(): lax.conv_general_dilated(padded, conv_weight, (1, 1), 'VALID', dimension_...  12.6 us
  transfers between devices with their start and end apart: 25, of which 22 were waited for; matrix products, arithmetic and copies ran while one was open for 2% of the time, Pallas kernels for 2%

profile of v2, /device:TPU:1, one launch (start us, length us, event | category | flops | bytes accessed | tf_op | source)
XLA Modules:
  0.0 232.1 jit_solution(2285675316226732680)
XLA Ops:
  2.1 4.4 %collective-permute-start = (bf16[4,1,128,256]{3,0,2,1:T(4,128)(2,1)S(1)}, bf16[4,1,128,256]{3,0,2,1:T(4,128)(2,1)S(1)}, u32[]{:S(2)}, u32[]{:S(2)}) collective-permute-start(bf16[4,1,128,256]{3,0,2,1:T(4,128)(2,1)S(1)} %copy.42), channel_id=1, source_target_pairs={{0,8},{8,16},{16,24},{24,32},{32,40},{40,48},{48,56},{56,64},{64,7... | collective-permute-start | bytes 786440 | tf_op jit(solution)/shard_map/ppermute | solution.py:20
  8.0 3.4 %collective-permute-done = bf16[4,1,128,256]{3,0,2,1:T(4,128)(2,1)S(1)} collective-permute-done((bf16[4,1,128,256]{3,0,2,1:T(4,128)(2,1)S(1)}, bf16[4,1,128,256]{3,0,2,1:T(4,128)(2,1)S(1)}, u32[]{:S(2)}, u32[]{:S(2)}) %collective-permute-start) | collective-permute-done | bytes 262176 | tf_op jit(solution)/shard_map/ppermute | solution.py:20
  11.5 1.8 constant_dynamic-update-slice_fusion.1
  13.3 2.5 %collective-permute-done.1 = bf16[4,1,128,256]{3,0,2,1:T(4,128)(2,1)S(1)} collective-permute-done((bf16[4,1,128,256]{3,0,2,1:T(4,128)(2,1)S(1)}, bf16[4,1,128,256]{3,0,2,1:T(4,128)(2,1)S(1)}, u32[]{:S(2)}, u32[]{:S(2)}) %collective-permute-start.1) | collective-permute-done | bytes 262176 | tf_op jit(solution)/shard_map/ppermute | solution.py:22
  17.5 4.7 %collective-permute-start.2 = (bf16[4,10,1,256]{3,0,2,1:T(4,128)(2,1)S(1)}, bf16[4,10,1,256]{3,0,2,1:T(4,128)(2,1)S(1)}, u32[]{:S(2)}, u32[]{:S(2)}) collective-permute-start(bf16[4,10,1,256]{3,0,2,1:T(4,128)(2,1)S(1)} %get-tuple-element.38), channel_id=1, source_target_pairs={{0,1},{1,2},{2,3},{3,4},{4,5},{5,6},{6,7},{8,9},{9,10},{10,11},{11... | collective-permute-start | bytes 61448 | tf_op jit(solution)/shard_map/ppermute | solution.py:20
  22.2 1.9 collective-permute-start.3
  24.2 4.3 %shard_map.149 = (bf16[4,200,1024]{2,1,0:T(8,128)(2,1)}, f32[4,200,1]{2,1,0:T(8,128)}) custom-call(s32[4,1600,128]{2,1,0:T(8,128)} %bitcast.48), custom_call_target="tpu_custom_call" | custom-call | tf_op jit(solution)/shard_map/pallas_call | solution.py:104
  29.8 12.6 %fusion.46 = (f32[4,256]{1,0:T(4,128)S(1)}, f32[4,256]{1,0:T(4,128)S(1)}, f32[4,8,128,256]{3,0,2,1:T(4,128)}) fusion(bf16[3,3,256,256]{3,2,1,0:T(8,128)(2,1)S(1)} %copy-done, bf16[4,10,1,256]{3,0,2,1:T(4,128)(2,1)S(1)} %collective-permute-done.3, bf16[4,10,128,256]{3,0,2,1:T(4,128)(2,1)} %copy-done.13, bf16[4,10,1,256]{3,0,2,1:T(4,128)(2,1)S(1)} %collective-permute-done.2), kind=kOutput, calls=%fused_computation.141 | convolution fusion | flops 4842969088 | bytes 8044544 | tf_op jit(solution)/shard_map/conv_general_dilated | solution.py:192
  46.7 3.1 %collective-permute-start.6 = (f32[4,264]{1,0:T(4,128)S(1)}, f32[4,264]{1,0:T(4,128)S(1)}, u32[]{:S(2)}, u32[]{:S(2)}) collective-permute-start(f32[4,264]{1,0:T(4,128)S(1)} %add.151), channel_id=1, source_target_pairs={{0,4},{1,5},{2,6},{3,7},{4,0},{5,1},{6,2},{7,3},{8,12},{9,13},{10,... | collective-permute-start | bytes 12680 | tf_op jit(solution)/shard_map/ppermute | solution.py:37
  53.2 3.8 %collective-permute-start.8 = (f32[4,264]{1,0:T(4,128)S(1)}, f32[4,264]{1,0:T(4,128)S(1)}, u32[]{:S(2)}, u32[]{:S(2)}) collective-permute-start(f32[4,264]{1,0:T(4,128)S(1)} %add.153), channel_id=1, source_target_pairs={{0,16},{8,24},{16,0},{24,8},{32,48},{40,56},{48,32},{56,40},{64,80... | collective-permute-start | bytes 12680 | tf_op jit(solution)/shard_map/ppermute | solution.py:37
  60.8 2.7 %collective-permute-start.10 = (f32[4,264]{1,0:T(4,128)S(1)}, f32[4,264]{1,0:T(4,128)S(1)}, u32[]{:S(2)}, u32[]{:S(2)}) collective-permute-start(f32[4,264]{1,0:T(4,128)S(1)} %add.155), channel_id=1, source_target_pairs={{0,64},{8,72},{16,80},{24,88},{32,96},{40,104},{48,112},{56,120},{... | collective-permute-start | bytes 12680 | tf_op jit(solution)/shard_map/ppermute | solution.py:37
  63.7 2.2 bitcast_select_fusion.refs_0_
  66.4 3.2 %fusion.4 = bf16[4,1024,256]{2,1,0:T(8,128)(2,1)S(1)} fusion(f32[4,1024,256]{2,0,1:T(4,128)} %bitcast.47, f32[256]{0:T(256)S(1)} %copy-done.15, f32[256]{0:T(256)S(1)} %copy-done.16, f32[4,256]{1,0:T(4,128)S(1)} %div.109, f32[4,256]{1,0:T(4,128)S(1)} %sub.108), kind=kLoop, calls=%fused_computation.6 | loop fusion | flops 6291456 | bytes 6301696 | tf_op jit(solution)/shard_map/convert_element_type | solution.py:211
  69.5 2.0 convolution_convert_fusion.refs_2_
  71.6 2.1 convolution_convert_fusion.1.refs_1_
  74.6 21.2 %shard_map.150 = (f32[4,200,8]{2,1,0:T(8,128)}, f32[4,200,8]{2,1,0:T(8,128)}, f32[4,200,256]{2,1,0:T(8,128)}) custom-call(bf16[4,1600,256]{2,1,0:T(8,128)(2,1)} %bitcast_select_fusion.refs_0_, bf16[4,1024,256]{2,1,0:T(8,128)(2,1)} %convolution_convert_fusion.1.refs_1_, bf16[4,1024,256]{2,1,0:T(8,128)(2,1)} %convolution_convert_fusion.refs_2_, ...), custom_call_target="tpu_custom_call" | custom-call | tf_op jit(solution)/shard_map/pallas_call | solution.py:145
  95.9 2.5 %reshape.148 = f32[128,1600]{1,0:T(8,128)} reshape(f32[4,200,256]{2,1,0:T(8,128)} %get-tuple-element.9) | data formatting | bytes 1638400 | tf_op jit(solution)/shard_map/reshape | solution.py:230
  100.7 2.2 concatenate.75
  102.9 2.1 slice_select_fusion.1
  105.0 2.7 %collective-permute-start.11 = (f32[64,1700]{1,0:T(8,128)}, f32[64,1700]{1,0:T(8,128)}, u32[]{:S(2)}, u32[]{:S(2)}) collective-permute-start(f32[64,1700]{1,0:T(8,128)} %get-tuple-element.43), channel_id=1, source_target_pairs={{0,4},{1,5},{2,6},{3,7},{4,0},{5,1},{6,2},{7,3},{8,12},{9,13},{10,... | collective-permute-start | bytes 1305608 | tf_op jit(solution)/shard_map/ppermute | solution.py:69
  107.7 6.5 %collective-permute-done.11 = f32[64,1700]{1,0:T(8,128)} collective-permute-done((f32[64,1700]{1,0:T(8,128)}, f32[64,1700]{1,0:T(8,128)}, u32[]{:S(2)}, u32[]{:S(2)}) %collective-permute-start.11) | collective-permute-done | bytes 435232 | tf_op jit(solution)/shard_map/ppermute | solution.py:69
  116.3 2.2 copy.26
  119.5 2.2 copy.28
  121.7 2.2 fusion.12
  123.9 1.9 concatenate.76
  125.8 1.8 slice_select_fusion.3
  128.6 4.1 %collective-permute-done.12 = f32[32,1700]{1,0:T(8,128)} collective-permute-done((f32[32,1700]{1,0:T(8,128)}, f32[32,1700]{1,0:T(8,128)}, u32[]{:S(2)}, u32[]{:S(2)}) %collective-permute-start.12) | collective-permute-done | bytes 217632 | tf_op jit(solution)/shard_map/ppermute | solution.py:69
  134.8 2.1 reshape.153
  138.2 2.1 reshape.154
  140.3 1.9 fusion.15
  143.8 7.5 %collective-permute-start.13 = (f32[16,1700]{1,0:T(8,128)}, f32[16,1700]{1,0:T(8,128)S(1)}, u32[]{:S(2)}, u32[]{:S(2)}) collective-permute-start(f32[16,1700]{1,0:T(8,128)} %get-tuple-element.47), channel_id=1, source_target_pairs={{0,1},{1,0},{2,3},{3,2},{4,5},{5,4},{6,7},{7,6},{8,9},{9,8},{10,11... | collective-permute-start | bytes 326408 | tf_op jit(solution)/shard_map/ppermute | solution.py:69
  156.5 1.8 reshape.156
  159.4 2.9 %collective-permute-start.14 = (f32[8,1700]{1,0:T(8,128)S(1)}, f32[8,1700]{1,0:T(8,128)S(1)}, u32[]{:S(2)}, u32[]{:S(2)}) collective-permute-start(f32[8,1700]{1,0:T(8,128)S(1)} %get-tuple-element.49), channel_id=1, source_target_pairs={{0,64},{8,72},{16,80},{24,88},{32,96},{40,104},{48,112},{56,120},{... | collective-permute-start | bytes 163208 | tf_op jit(solution)/shard_map/ppermute | solution.py:69
  162.3 2.0 collective-permute-done.14
  168.7 1.7 collective-permute-done.15
  174.3 3.3 %collective-permute-start.16 = (f32[2,1700]{1,0:T(2,128)S(1)}, f32[2,1700]{1,0:T(2,128)S(1)}, u32[]{:S(2)}, u32[]{:S(2)}) collective-permute-start(f32[2,1700]{1,0:T(2,128)S(1)} %get-tuple-element.53), channel_id=1, source_target_pairs={{0,16},{8,24},{16,0},{24,8},{32,48},{40,56},{48,32},{56,40},{64,80... | collective-permute-start | bytes 40808 | tf_op jit(solution)/shard_map/ppermute | solution.py:69
  185.1 3.6 %collective-permute-start.19 = (bf16[2,1600]{1,0:T(2,128)(2,1)S(1)}, bf16[2,1600]{1,0:T(2,128)(2,1)S(1)}, u32[]{:S(2)}, u32[]{:S(2)}) collective-permute-start(bf16[2,1600]{1,0:T(2,128)(2,1)S(1)} %broadcast_select_fusion.4), channel_id=1, source_target_pairs={{0,16},{8,24},{16,0},{24,8},{32,48},{40,56},{48,32},{56,40},{64,80... | collective-permute-start | bytes 19208 | tf_op jit(solution)/shard_map/ppermute | solution.py:81
  192.4 2.6 %collective-permute-start.21 = (bf16[8,1600]{1,0:T(8,128)(2,1)S(1)}, bf16[8,1600]{1,0:T(8,128)(2,1)S(1)}, u32[]{:S(2)}, u32[]{:S(2)}) collective-permute-start(bf16[8,1600]{1,0:T(8,128)(2,1)S(1)} %maximum_select_fusion.4), channel_id=1, source_target_pairs={{0,64},{8,72},{16,80},{24,88},{32,96},{40,104},{48,112},{56,120},{... | collective-permute-start | bytes 76808 | tf_op jit(solution)/shard_map/ppermute | solution.py:81
  195.0 1.6 collective-permute-done.21
  196.7 8.8 %collective-permute-start.22 = (bf16[16,1600]{1,0:T(8,128)(2,1)S(1)}, bf16[16,1600]{1,0:T(8,128)(2,1)S(1)}, u32[]{:S(2)}, u32[]{:S(2)}) collective-permute-start(bf16[16,1600]{1,0:T(8,128)(2,1)S(1)} %maximum_select_fusion.3), channel_id=1, source_target_pairs={{0,1},{1,0},{2,3},{3,2},{4,5},{5,4},{6,7},{7,6},{8,9},{9,8},{10,11... | collective-permute-start | bytes 153608 | tf_op jit(solution)/shard_map/ppermute | solution.py:81
  206.4 1.7 collective-permute-start.23
  208.1 2.9 %collective-permute-done.23 = bf16[32,1600]{1,0:T(8,128)(2,1)S(1)} collective-permute-done((bf16[32,1600]{1,0:T(8,128)(2,1)S(1)}, bf16[32,1600]{1,0:T(8,128)(2,1)S(1)}, u32[]{:S(2)}, u32[]{:S(2)}) %collective-permute-start.23) | collective-permute-done | bytes 102432 | tf_op jit(solution)/shard_map/ppermute | solution.py:81
  211.1 3.0 %collective-permute-start.24 = (bf16[64,1600]{1,0:T(8,128)(2,1)S(1)}, bf16[64,1600]{1,0:T(8,128)(2,1)S(1)}, u32[]{:S(2)}, u32[]{:S(2)}) collective-permute-start(bf16[64,1600]{1,0:T(8,128)(2,1)S(1)} %maximum_select_fusion.1), channel_id=1, source_target_pairs={{0,4},{1,5},{2,6},{3,7},{4,0},{5,1},{6,2},{7,3},{8,12},{9,13},{10,... | collective-permute-start | bytes 614408 | tf_op jit(solution)/shard_map/ppermute | solution.py:81
  214.1 4.3 %collective-permute-done.24 = bf16[64,1600]{1,0:T(8,128)(2,1)S(1)} collective-permute-done((bf16[64,1600]{1,0:T(8,128)(2,1)S(1)}, bf16[64,1600]{1,0:T(8,128)(2,1)S(1)}, u32[]{:S(2)}, u32[]{:S(2)}) %collective-permute-start.24) | collective-permute-done | bytes 204832 | tf_op jit(solution)/shard_map/ppermute | solution.py:81
  219.2 2.4 %select_n.277 = bf16[4,200,256]{2,1,0:T(8,128)(2,1)} reshape(bf16[128,1600]{1,0:T(8,128)(2,1)} %maximum_select_fusion) | data formatting | bytes 819200 | tf_op jit(solution)/shard_map/jit(_where)/select_n | solution.py:83
  221.6 1.7 fusion.49
  226.0 3.1 %convolution_convert_fusion.2 = bf16[4,200,1024]{2,1,0:T(8,128)(2,1)} fusion(bf16[4,1024,256]{2,1,0:T(8,128)(2,1)S(1)} %fusion.4, bf16[4,200,256]{2,1,0:T(8,128)(2,1)} %fusion.11, bf16[256,256]{1,0:T(8,128)(2,1)S(1)} %copy-done.9), kind=kOutput, calls=%fused_computation.16 | convolution fusion | flops 525312000 | bytes 4276224 | tf_op jit(solution)/shard_map/bqc,bpc->bqp/dot_general | solution.py:248
  229.1 3.1 %copy.29 = bf16[100,8,8,128]{3,2,1,0:T(8,128)(2,1)} copy(bf16[100,8,8,128]{3,1,2,0:T(8,128)(2,1)} %bitcast.46) | data formatting | bytes 3276800
  (157 shorter events, 60.6 us)
Async XLA Ops:
  0.6 29.1 %copy-start = (bf16[3,3,256,256]{3,2,1,0:T(8,128)(2,1)S(1)}, bf16[3,3,256,256]{3,2,1,0:T(8,128)(2,1)}, u32[]{:S(2)}) copy-start(bf16[3,3,256,256]{3,2,1,0:T(8,128)(2,1)} %param.17) | copy-start | bytes 3538948
  0.6 10.9 %copy-start.1 = (bf16[4,8,128,256]{3,2,1,0:T(8,128)(2,1)S(1)}, bf16[4,8,128,256]{3,2,1,0:T(8,128)(2,1)}, u32[]{:S(2)}) copy-start(bf16[4,8,128,256]{3,2,1,0:T(8,128)(2,1)} %param.14) | copy-start | bytes 6291460
  2.1 9.3 %collective-permute-start = (bf16[4,1,128,256]{3,0,2,1:T(4,128)(2,1)S(1)}, bf16[4,1,128,256]{3,0,2,1:T(4,128)(2,1)S(1)}, u32[]{:S(2)}, u32[]{:S(2)}) collective-permute-start(bf16[4,1,128,256]{3,0,2,1:T(4,128)(2,1)S(1)} %copy.42), channel_id=1, source_target_pairs={{0,8},{8,16},{16,24},{24,32},{32,40},{40,48},{48,56},{56,64},{64,7... | collective-permute-start | bytes 786440 | tf_op jit(solution)/shard_map/ppermute | solution.py:20
  6.7 9.1 %collective-permute-start.1 = (bf16[4,1,128,256]{3,0,2,1:T(4,128)(2,1)S(1)}, bf16[4,1,128,256]{3,0,2,1:T(4,128)(2,1)S(1)}, u32[]{:S(2)}, u32[]{:S(2)}) collective-permute-start(bf16[4,1,128,256]{3,0,2,1:T(4,128)(2,1)S(1)} %copy.43), channel_id=1, source_target_pairs={{8,0},{16,8},{24,16},{32,24},{40,32},{48,40},{56,48},{64,56},{72,6... | collective-permute-start | bytes 786440 | tf_op jit(solution)/shard_map/ppermute | solution.py:22
  15.9 1.5 copy-start.13
  17.5 12.2 %collective-permute-start.2 = (bf16[4,10,1,256]{3,0,2,1:T(4,128)(2,1)S(1)}, bf16[4,10,1,256]{3,0,2,1:T(4,128)(2,1)S(1)}, u32[]{:S(2)}, u32[]{:S(2)}) collective-permute-start(bf16[4,10,1,256]{3,0,2,1:T(4,128)(2,1)S(1)} %get-tuple-element.38), channel_id=1, source_target_pairs={{0,1},{1,2},{2,3},{3,4},{4,5},{5,6},{6,7},{8,9},{9,10},{10,11},{11... | collective-permute-start | bytes 61448 | tf_op jit(solution)/shard_map/ppermute | solution.py:20
  22.2 7.5 %collective-permute-start.3 = (bf16[4,10,1,256]{3,0,2,1:T(4,128)(2,1)S(1)}, bf16[4,10,1,256]{3,0,2,1:T(4,128)(2,1)S(1)}, u32[]{:S(2)}, u32[]{:S(2)}) collective-permute-start(bf16[4,10,1,256]{3,0,2,1:T(4,128)(2,1)S(1)} %get-tuple-element.39), channel_id=1, source_target_pairs={{1,0},{2,1},{3,2},{4,3},{5,4},{6,5},{7,6},{9,8},{10,9},{11,10},{12... | collective-permute-start | bytes 61448 | tf_op jit(solution)/shard_map/ppermute | solution.py:22
  29.7 27.3 %copy-start.2 = (f32[4,200,256]{2,1,0:T(8,128)S(1)}, f32[4,200,256]{2,1,0:T(8,128)}, u32[]{:S(2)}) copy-start(f32[4,200,256]{2,1,0:T(8,128)} %param.16) | copy-start | bytes 2457604
  29.7 27.3 %copy-start.10 = (bf16[256,256]{1,0:T(8,128)(2,1)S(1)}, bf16[256,256]{1,0:T(8,128)(2,1)}, u32[]{:S(2)}) copy-start(bf16[256,256]{1,0:T(8,128)(2,1)} %param.20) | copy-start | bytes 393220
  42.9 1.2 collective-permute-start.4
  44.1 2.5 %collective-permute-start.5 = (f32[4,264]{1,0:T(4,128)S(1)}, f32[4,264]{1,0:T(4,128)S(1)}, u32[]{:S(2)}, u32[]{:S(2)}) collective-permute-start(f32[4,264]{1,0:T(4,128)S(1)} %fusion.56), channel_id=1, source_target_pairs={{0,2},{1,3},{2,0},{3,1},{4,6},{5,7},{6,4},{7,5},{8,10},{9,11},{10,... | collective-permute-start | bytes 12680 | tf_op jit(solution)/shard_map/ppermute | solution.py:37
  46.7 4.1 %collective-permute-start.6 = (f32[4,264]{1,0:T(4,128)S(1)}, f32[4,264]{1,0:T(4,128)S(1)}, u32[]{:S(2)}, u32[]{:S(2)}) collective-permute-start(f32[4,264]{1,0:T(4,128)S(1)} %add.151), channel_id=1, source_target_pairs={{0,4},{1,5},{2,6},{3,7},{4,0},{5,1},{6,2},{7,3},{8,12},{9,13},{10,... | collective-permute-start | bytes 12680 | tf_op jit(solution)/shard_map/ppermute | solution.py:37
  50.8 2.5 %collective-permute-start.7 = (f32[4,264]{1,0:T(4,128)S(1)}, f32[4,264]{1,0:T(4,128)S(1)}, u32[]{:S(2)}, u32[]{:S(2)}) collective-permute-start(f32[4,264]{1,0:T(4,128)S(1)} %add.152), channel_id=1, source_target_pairs={{0,8},{8,0},{16,24},{24,16},{32,40},{40,32},{48,56},{56,48},{64,72... | collective-permute-start | bytes 12680 | tf_op jit(solution)/shard_map/ppermute | solution.py:37
  53.2 4.8 %collective-permute-start.8 = (f32[4,264]{1,0:T(4,128)S(1)}, f32[4,264]{1,0:T(4,128)S(1)}, u32[]{:S(2)}, u32[]{:S(2)}) collective-permute-start(f32[4,264]{1,0:T(4,128)S(1)} %add.153), channel_id=1, source_target_pairs={{0,16},{8,24},{16,0},{24,8},{32,48},{40,56},{48,32},{56,40},{64,80... | collective-permute-start | bytes 12680 | tf_op jit(solution)/shard_map/ppermute | solution.py:37
  57.3 9.0 %copy-start.15 = (f32[256]{0:T(256)S(1)}, f32[256]{0:T(256)}, u32[]{:S(2)}) copy-start(f32[256]{0:T(256)} %param.19) | copy-start | bytes 3076
  57.3 9.0 %copy-start.16 = (f32[256]{0:T(256)S(1)}, f32[256]{0:T(256)}, u32[]{:S(2)}) copy-start(f32[256]{0:T(256)} %param.18) | copy-start | bytes 3076
  58.1 2.8 %collective-permute-start.9 = (f32[4,264]{1,0:T(4,128)S(1)}, f32[4,264]{1,0:T(4,128)S(1)}, u32[]{:S(2)}, u32[]{:S(2)}) collective-permute-start(f32[4,264]{1,0:T(4,128)S(1)} %add.154), channel_id=1, source_target_pairs={{0,32},{8,40},{16,48},{24,56},{32,0},{40,8},{48,16},{56,24},{64,96... | collective-permute-start | bytes 12680 | tf_op jit(solution)/shard_map/ppermute | solution.py:37
  60.8 5.0 %collective-permute-start.10 = (f32[4,264]{1,0:T(4,128)S(1)}, f32[4,264]{1,0:T(4,128)S(1)}, u32[]{:S(2)}, u32[]{:S(2)}) collective-permute-start(f32[4,264]{1,0:T(4,128)S(1)} %add.155), channel_id=1, source_target_pairs={{0,64},{8,72},{16,80},{24,88},{32,96},{40,104},{48,112},{56,120},{... | collective-permute-start | bytes 12680 | tf_op jit(solution)/shard_map/ppermute | solution.py:37
  66.3 3.2 %copy-start.6 = (bf16[256,256]{1,0:T(8,128)(2,1)S(1)}, bf16[256,256]{1,0:T(8,128)(2,1)}, u32[]{:S(2)}) copy-start(bf16[256,256]{1,0:T(8,128)(2,1)} %param.22) | copy-start | bytes 393220
  69.5 2.0 copy-start.7
  105.0 9.1 %collective-permute-start.11 = (f32[64,1700]{1,0:T(8,128)}, f32[64,1700]{1,0:T(8,128)}, u32[]{:S(2)}, u32[]{:S(2)}) collective-permute-start(f32[64,1700]{1,0:T(8,128)} %get-tuple-element.43), channel_id=1, source_target_pairs={{0,4},{1,5},{2,6},{3,7},{4,0},{5,1},{6,2},{7,3},{8,12},{9,13},{10,... | collective-permute-start | bytes 1305608 | tf_op jit(solution)/shard_map/ppermute | solution.py:69
  127.5 5.2 %collective-permute-start.12 = (f32[32,1700]{1,0:T(8,128)}, f32[32,1700]{1,0:T(8,128)}, u32[]{:S(2)}, u32[]{:S(2)}) collective-permute-start(f32[32,1700]{1,0:T(8,128)} %get-tuple-element.45), channel_id=1, source_target_pairs={{0,2},{1,3},{2,0},{3,1},{4,6},{5,7},{6,4},{7,5},{8,10},{9,11},{10,... | collective-permute-start | bytes 652808 | tf_op jit(solution)/shard_map/ppermute | solution.py:69
  143.8 8.7 %collective-permute-start.13 = (f32[16,1700]{1,0:T(8,128)}, f32[16,1700]{1,0:T(8,128)S(1)}, u32[]{:S(2)}, u32[]{:S(2)}) collective-permute-start(f32[16,1700]{1,0:T(8,128)} %get-tuple-element.47), channel_id=1, source_target_pairs={{0,1},{1,0},{2,3},{3,2},{4,5},{5,4},{6,7},{7,6},{8,9},{9,8},{10,11... | collective-permute-start | bytes 326408 | tf_op jit(solution)/shard_map/ppermute | solution.py:69
  152.6 0.9 copy-start.5
  159.4 4.9 %copy-start.4 = (f32[8,1700]{1,0:T(8,128)}, f32[8,1700]{1,0:T(8,128)S(1)}, u32[]{:S(2)}) copy-start(f32[8,1700]{1,0:T(8,128)S(1)} %get-tuple-element.48) | copy-start | bytes 163204
  159.4 4.8 %collective-permute-start.14 = (f32[8,1700]{1,0:T(8,128)S(1)}, f32[8,1700]{1,0:T(8,128)S(1)}, u32[]{:S(2)}, u32[]{:S(2)}) collective-permute-start(f32[8,1700]{1,0:T(8,128)S(1)} %get-tuple-element.49), channel_id=1, source_target_pairs={{0,64},{8,72},{16,80},{24,88},{32,96},{40,104},{48,112},{56,120},{... | collective-permute-start | bytes 163208 | tf_op jit(solution)/shard_map/ppermute | solution.py:69
  164.3 0.6 copy-start.12
  166.6 55.0 %copy-start.8 = (bf16[256,256]{1,0:T(8,128)(2,1)S(1)}, bf16[256,256]{1,0:T(8,128)(2,1)}, u32[]{:S(2)}) copy-start(bf16[256,256]{1,0:T(8,128)(2,1)} %param.23) | copy-start | bytes 393220
  167.6 2.8 %collective-permute-start.15 = (f32[4,1700]{1,0:T(4,128)S(1)}, f32[4,1700]{1,0:T(4,128)S(1)}, u32[]{:S(2)}, u32[]{:S(2)}) collective-permute-start(f32[4,1700]{1,0:T(4,128)S(1)} %get-tuple-element.51), channel_id=1, source_target_pairs={{0,32},{8,40},{16,48},{24,56},{32,0},{40,8},{48,16},{56,24},{64,96... | collective-permute-start | bytes 81608 | tf_op jit(solution)/shard_map/ppermute | solution.py:69
  170.4 0.7 copy-start.14
  174.3 4.4 %collective-permute-start.16 = (f32[2,1700]{1,0:T(2,128)S(1)}, f32[2,1700]{1,0:T(2,128)S(1)}, u32[]{:S(2)}, u32[]{:S(2)}) collective-permute-start(f32[2,1700]{1,0:T(2,128)S(1)} %get-tuple-element.53), channel_id=1, source_target_pairs={{0,16},{8,24},{16,0},{24,8},{32,48},{40,56},{48,32},{56,40},{64,80... | collective-permute-start | bytes 40808 | tf_op jit(solution)/shard_map/ppermute | solution.py:69
  179.3 2.6 %collective-permute-start.17 = (f32[1,1700]{1,0:T(1,128)S(1)}, f32[1,1700]{1,0:T(1,128)S(1)}, u32[]{:S(2)}, u32[]{:S(2)}) collective-permute-start(f32[1,1700]{1,0:T(1,128)S(1)} %get-tuple-element.58), channel_id=1, source_target_pairs={{0,8},{8,0},{16,24},{24,16},{32,40},{40,32},{48,56},{56,48},{64,72... | collective-permute-start | bytes 20408 | tf_op jit(solution)/shard_map/ppermute | solution.py:69
  182.5 2.6 %collective-permute-start.18 = (bf16[1,1600]{1,0:T(2,128)(2,1)S(1)}, bf16[1,1600]{1,0:T(2,128)(2,1)S(1)}, u32[]{:S(2)}, u32[]{:S(2)}) collective-permute-start(bf16[1,1600]{1,0:T(2,128)(2,1)S(1)} %fusion.32), channel_id=1, source_target_pairs={{0,8},{8,0},{16,24},{24,16},{32,40},{40,32},{48,56},{56,48},{64,72... | collective-permute-start | bytes 9608 | tf_op jit(solution)/shard_map/ppermute | solution.py:81
  185.1 4.6 %collective-permute-start.19 = (bf16[2,1600]{1,0:T(2,128)(2,1)S(1)}, bf16[2,1600]{1,0:T(2,128)(2,1)S(1)}, u32[]{:S(2)}, u32[]{:S(2)}) collective-permute-start(bf16[2,1600]{1,0:T(2,128)(2,1)S(1)} %broadcast_select_fusion.4), channel_id=1, source_target_pairs={{0,16},{8,24},{16,0},{24,8},{32,48},{40,56},{48,32},{56,40},{64,80... | collective-permute-start | bytes 19208 | tf_op jit(solution)/shard_map/ppermute | solution.py:81
  189.7 2.6 %collective-permute-start.20 = (bf16[4,1600]{1,0:T(4,128)(2,1)S(1)}, bf16[4,1600]{1,0:T(4,128)(2,1)S(1)}, u32[]{:S(2)}, u32[]{:S(2)}) collective-permute-start(bf16[4,1600]{1,0:T(4,128)(2,1)S(1)} %maximum_select_fusion.5), channel_id=1, source_target_pairs={{0,32},{8,40},{16,48},{24,56},{32,0},{40,8},{48,16},{56,24},{64,96... | collective-permute-start | bytes 38408 | tf_op jit(solution)/shard_map/ppermute | solution.py:81
  192.4 4.3 %collective-permute-start.21 = (bf16[8,1600]{1,0:T(8,128)(2,1)S(1)}, bf16[8,1600]{1,0:T(8,128)(2,1)S(1)}, u32[]{:S(2)}, u32[]{:S(2)}) collective-permute-start(bf16[8,1600]{1,0:T(8,128)(2,1)S(1)} %maximum_select_fusion.4), channel_id=1, source_target_pairs={{0,64},{8,72},{16,80},{24,88},{32,96},{40,104},{48,112},{56,120},{... | collective-permute-start | bytes 76808 | tf_op jit(solution)/shard_map/ppermute | solution.py:81
  196.7 9.7 %collective-permute-start.22 = (bf16[16,1600]{1,0:T(8,128)(2,1)S(1)}, bf16[16,1600]{1,0:T(8,128)(2,1)S(1)}, u32[]{:S(2)}, u32[]{:S(2)}) collective-permute-start(bf16[16,1600]{1,0:T(8,128)(2,1)S(1)} %maximum_select_fusion.3), channel_id=1, source_target_pairs={{0,1},{1,0},{2,3},{3,2},{4,5},{5,4},{6,7},{7,6},{8,9},{9,8},{10,11... | collective-permute-start | bytes 153608 | tf_op jit(solution)/shard_map/ppermute | solution.py:81
  206.4 17.3 %copy-start.17 = (f32[256]{0:T(256)S(1)}, f32[256]{0:T(256)}, u32[]{:S(2)}) copy-start(f32[256]{0:T(256)} %param.25) | copy-start | bytes 3076
  206.4 17.3 %copy-start.18 = (f32[256]{0:T(256)S(1)}, f32[256]{0:T(256)}, u32[]{:S(2)}) copy-start(f32[256]{0:T(256)} %param.24) | copy-start | bytes 3076
  206.4 4.6 %collective-permute-start.23 = (bf16[32,1600]{1,0:T(8,128)(2,1)S(1)}, bf16[32,1600]{1,0:T(8,128)(2,1)S(1)}, u32[]{:S(2)}, u32[]{:S(2)}) collective-permute-start(bf16[32,1600]{1,0:T(8,128)(2,1)S(1)} %maximum_select_fusion.2), channel_id=1, source_target_pairs={{0,2},{1,3},{2,0},{3,1},{4,6},{5,7},{6,4},{7,5},{8,10},{9,11},{10,... | collective-permute-start | bytes 307208 | tf_op jit(solution)/shard_map/ppermute | solution.py:81
  211.1 7.3 %collective-permute-start.24 = (bf16[64,1600]{1,0:T(8,128)(2,1)S(1)}, bf16[64,1600]{1,0:T(8,128)(2,1)S(1)}, u32[]{:S(2)}, u32[]{:S(2)}) collective-permute-start(bf16[64,1600]{1,0:T(8,128)(2,1)S(1)} %maximum_select_fusion.1), channel_id=1, source_target_pairs={{0,4},{1,5},{2,6},{3,7},{4,0},{5,1},{6,2},{7,3},{8,12},{9,13},{10,... | collective-permute-start | bytes 614408 | tf_op jit(solution)/shard_map/ppermute | solution.py:81
  221.6 3.3 %copy-start.11 = (bf16[256,256]{1,0:T(8,128)(2,1)S(1)}, bf16[256,256]{1,0:T(8,128)(2,1)}, u32[]{:S(2)}) copy-start(bf16[256,256]{1,0:T(8,128)(2,1)} %param.26) | copy-start | bytes 393220
  223.3 2.6 %copy-start.9 = (bf16[256,256]{1,0:T(8,128)(2,1)S(1)}, bf16[256,256]{1,0:T(8,128)(2,1)}, u32[]{:S(2)}) copy-start(bf16[256,256]{1,0:T(8,128)(2,1)} %param.27) | copy-start | bytes 393220
  224.1 0.9 copy-start.3

commit v3 on v2

--- a/solution.py
+++ b/solution.py
@@ -233,10 +233,16 @@
         ],
         axis=1,
     )
-    reduced = halving_merge(packed, span)
-    sums, totals, _ = split_parts(reduced, span)
+    parts = lax.all_to_all(packed, ("rows", "cols"), 0, 0, tiled=True)
+    sums, totals, tops = split_parts(parts, span)
+    highest = jnp.max(tops, axis=0, keepdims=True)
+    factor = jnp.exp(tops - highest)
+    totals = jnp.sum(totals * factor, axis=0, keepdims=True)
+    sums = jnp.sum(sums * jnp.repeat(factor, 32, axis=1), axis=0, keepdims=True)
     attn_block = (sums / jnp.repeat(totals, 32, axis=1)).astype(jnp.bfloat16)
-    attn = doubling_gather(attn_block).reshape(images, query_count, width)
+    attn = lax.all_to_all(
+        jnp.broadcast_to(attn_block, (devices, span)), ("rows", "cols"), 0, 0, tiled=True
+    ).reshape(images, query_count, width)
     mixed = queries + jnp.dot(attn, out_weight, preferred_element_type=jnp.float32)
     centre = jnp.mean(mixed, axis=2, keepdims=True)
     spread = jnp.mean((mixed - centre) ** 2, axis=2, keepdims=True)

time: 234 us -> 194 us (0.83)
  blocking collectives: 0 us -> 51.3 us
  starting transfers between devices: 68 us -> 26.1 us
  waiting for transfers between devices: 44 us -> 12.5 us
  local copies, waits for them, and re-layouts: 46.7 us -> 33.7 us
  other arithmetic: 23.9 us -> 20.4 us
    all_to_all x0 -> x2, blocking collectives: none -> 51.3 us  [the longest x1 33 us: on_device(): parts = lax.all_to_all(packed, ('rows', 'cols'), 0, 0, tiled=True)]
    ppermute x14 -> x0, starting transfers between devices: 41.9 us -> none  [the longest x7 22.1 us: doubling_gather(): got = lax.ppermute(a, axis, [(i, i ^ k) for i in range(n)])]
    ppermute x14 -> x0, waiting for transfers between devices: 31.5 us -> none  [the longest x7 17.9 us: halving_merge(): got = lax.ppermute(send, axis, [(i, i ^ k) for i in range(n)])]
    reshape x12 -> x1, local copies, waits for them, and re-layouts: 14.6 us -> 2.37 us  [on_device(): attn = lax.all_to_all(jnp.broadcast_to(attn_block, (devices, span)), ('ro...]
    add x12 -> x0, other arithmetic: 10.5 us -> none  [the longest x6 6.85 us: merge(): w = wa * jnp.repeat(fa, 32, axis=1) + wb * jnp.repeat(fb, 32, axis=1)]
    select_n x14 -> x0, other arithmetic: 5.66 us -> none  [the longest x7 4.65 us: halving_merge(): keep = jnp.where(upper, hi, lo)]
    unnamed x43 -> x37, local copies, waits for them, and re-layouts: 8.37 us -> 14 us
    all_to_all x0 -> x2, local copies, waits for them, and re-layouts: none -> 5.19 us  [on_device(): parts = lax.all_to_all(packed, ('rows', 'cols'), 0, 0, tiled=True)]
  transfers between devices with their start and end apart: 25 -> 11, of which waited for: 22 -> 8; matrix products, arithmetic and copies ran while one was open for 2% -> 3% of each run, Pallas kernels for 2% -> 2%
where the time goes in v3:
time: 194 us; the launch traced here: 193 us
  blocking collectives  51.3 us (26%)
  local copies, waits for them, and re-layouts  33.7 us (17%)
  starting transfers between devices  26.1 us (13%)
  Pallas kernels  25.6 us (13%)
  matrix products  22.8 us (12%)
  other arithmetic  20.4 us (11%)
  waiting for transfers between devices  12.5 us (6%)
    all_to_all x1, blocking collectives, on_device(): parts = lax.all_to_all(packed, ('rows', 'cols'), 0, 0, tiled=True)  33 us
    pallas_call x1, Pallas kernels, attention(): pl.pallas_call(kernel, grid=(images,), in_specs=[pl.BlockSpec((1, heads *...  21.2 us
    all_to_all x1, blocking collectives, on_device(): lax.all_to_all(jnp.broadcast_to(attn_block, (devices, span)), ('rows', 'c...  18.4 us
    unnamed x37, local copies, waits for them, and re-layouts  14 us
    ppermute x7, starting transfers between devices, butterfly_sum(): got = lax.ppermute(x, axis, [(i, i ^ k) for i in range(n)])  13.8 us
    conv_general_dilated x1, matrix products, on_device(): lax.conv_general_dilated(padded, conv_weight, (1, 1), 'VALID', dimension_...  12.6 us
    ppermute x2, starting transfers between devices, with_halo(): lax.ppermute(tail, axis, [(i, (i + 1) % count) for i in range(ends)])  9.11 us
    ppermute x7, waiting for transfers between devices, butterfly_sum(): got = lax.ppermute(x, axis, [(i, i ^ k) for i in range(n)])  6.5 us
  transfers between devices with their start and end apart: 11, of which 8 were waited for; matrix products, arithmetic and copies ran while one was open for 3% of the time, Pallas kernels for 2%

profile of v3, /device:TPU:1, one launch (start us, length us, event | category | flops | bytes accessed | tf_op | source)
XLA Modules:
  0.0 193.3 jit_solution(8372402584504528737)
XLA Ops:
  0.7 1.2 fusion.29
  2.1 4.4 %collective-permute-start = (bf16[4,1,128,256]{3,0,2,1:T(4,128)(2,1)S(1)}, bf16[4,1,128,256]{3,0,2,1:T(4,128)(2,1)S(1)}, u32[]{:S(2)}, u32[]{:S(2)}) collective-permute-start(bf16[4,1,128,256]{3,0,2,1:T(4,128)(2,1)S(1)} %copy.47), channel_id=1, source_target_pairs={{0,8},{8,16},{16,24},{24,32},{32,40},{40,48},{48,56},{56,64},{64,7... | collective-permute-start | bytes 786440 | tf_op jit(solution)/shard_map/ppermute | solution.py:20
  6.7 1.3 collective-permute-start.1
  8.0 3.4 %collective-permute-done = bf16[4,1,128,256]{3,0,2,1:T(4,128)(2,1)S(1)} collective-permute-done((bf16[4,1,128,256]{3,0,2,1:T(4,128)(2,1)S(1)}, bf16[4,1,128,256]{3,0,2,1:T(4,128)(2,1)S(1)}, u32[]{:S(2)}, u32[]{:S(2)}) %collective-permute-start) | collective-permute-done | bytes 262176 | tf_op jit(solution)/shard_map/ppermute | solution.py:20
  11.5 1.8 constant_dynamic-update-slice_fusion.1
  13.3 2.5 %collective-permute-done.1 = bf16[4,1,128,256]{3,0,2,1:T(4,128)(2,1)S(1)} collective-permute-done((bf16[4,1,128,256]{3,0,2,1:T(4,128)(2,1)S(1)}, bf16[4,1,128,256]{3,0,2,1:T(4,128)(2,1)S(1)}, u32[]{:S(2)}, u32[]{:S(2)}) %collective-permute-start.1) | collective-permute-done | bytes 262176 | tf_op jit(solution)/shard_map/ppermute | solution.py:22
  16.0 1.5 copy-done.10
  17.5 4.7 %collective-permute-start.2 = (bf16[4,10,1,256]{3,0,2,1:T(4,128)(2,1)S(1)}, bf16[4,10,1,256]{3,0,2,1:T(4,128)(2,1)S(1)}, u32[]{:S(2)}, u32[]{:S(2)}) collective-permute-start(bf16[4,10,1,256]{3,0,2,1:T(4,128)(2,1)S(1)} %get-tuple-element.16), channel_id=1, source_target_pairs={{0,1},{1,2},{2,3},{3,4},{4,5},{5,6},{6,7},{8,9},{9,10},{10,11},{11... | collective-permute-start | bytes 61448 | tf_op jit(solution)/shard_map/ppermute | solution.py:20
  22.2 1.9 collective-permute-start.3
  24.2 4.3 %shard_map.149 = (bf16[4,200,1024]{2,1,0:T(8,128)(2,1)}, f32[4,200,1]{2,1,0:T(8,128)}) custom-call(s32[4,1600,128]{2,1,0:T(8,128)} %bitcast.47), custom_call_target="tpu_custom_call" | custom-call | tf_op jit(solution)/shard_map/pallas_call | solution.py:104
  28.5 1.2 reduce.4
  29.8 12.6 %fusion.27 = (f32[4,256]{1,0:T(4,128)S(1)}, f32[4,256]{1,0:T(4,128)S(1)}, f32[4,8,128,256]{3,0,2,1:T(4,128)}) fusion(bf16[3,3,256,256]{3,2,1,0:T(8,128)(2,1)S(1)} %copy-done, bf16[4,10,1,256]{3,0,2,1:T(4,128)(2,1)S(1)} %collective-permute-done.3, bf16[4,10,128,256]{3,0,2,1:T(4,128)(2,1)} %copy-done.10, bf16[4,10,1,256]{3,0,2,1:T(4,128)(2,1)S(1)} %collective-permute-done.2), kind=kOutput, calls=%fused_computation.58 | convolution fusion | flops 4842969088 | bytes 8044544 | tf_op jit(solution)/shard_map/conv_general_dilated | solution.py:192
  42.9 1.2 collective-permute-done.4
  44.1 1.5 collective-permute-start.5
  45.6 1.0 collective-permute-done.5
  46.7 3.1 %collective-permute-start.6 = (f32[4,264]{1,0:T(4,128)S(1)}, f32[4,264]{1,0:T(4,128)S(1)}, u32[]{:S(2)}, u32[]{:S(2)}) collective-permute-start(f32[4,264]{1,0:T(4,128)S(1)} %add.64), channel_id=1, source_target_pairs={{0,4},{1,5},{2,6},{3,7},{4,0},{5,1},{6,2},{7,3},{8,12},{9,13},{10,... | collective-permute-start | bytes 12680 | tf_op jit(solution)/shard_map/ppermute | solution.py:37
  49.7 1.0 collective-permute-done.6
  50.8 1.5 collective-permute-start.7
  52.2 1.0 collective-permute-done.7
  53.2 3.8 %collective-permute-start.8 = (f32[4,264]{1,0:T(4,128)S(1)}, f32[4,264]{1,0:T(4,128)S(1)}, u32[]{:S(2)}, u32[]{:S(2)}) collective-permute-start(f32[4,264]{1,0:T(4,128)S(1)} %add.66), channel_id=1, source_target_pairs={{0,16},{8,24},{16,0},{24,8},{32,48},{40,56},{48,32},{56,40},{64,80... | collective-permute-start | bytes 12680 | tf_op jit(solution)/shard_map/ppermute | solution.py:37
  58.0 1.2 collective-permute-start.9
  59.3 1.6 collective-permute-done.9
  60.8 2.7 %collective-permute-start.10 = (f32[4,264]{1,0:T(4,128)S(1)}, f32[4,264]{1,0:T(4,128)S(1)}, u32[]{:S(2)}, u32[]{:S(2)}) collective-permute-start(f32[4,264]{1,0:T(4,128)S(1)} %add.68), channel_id=1, source_target_pairs={{0,64},{8,72},{16,80},{24,88},{32,96},{40,104},{48,112},{56,120},{... | collective-permute-start | bytes 12680 | tf_op jit(solution)/shard_map/ppermute | solution.py:37
  63.7 2.2 %bitcast_select_fusion.refs_0_ = bf16[4,1600,256]{2,1,0:T(8,128)(2,1)} fusion(pred[1600,256]{1,0:T(8,128)(4,1)S(1)} %bitcast.50, bf16[4,200,256]{2,1,0:T(8,128)(2,1)S(1)} %convolution_convert_fusion.4), kind=kLoop, calls=%fused_computation.7 | loop fusion | flops 1638400 | bytes 4096000 | tf_op jit(solution)/shard_map/jit(_where)/select_n | solution.py:221
  66.4 3.2 %fusion.4 = bf16[4,1024,256]{2,1,0:T(8,128)(2,1)S(1)} fusion(f32[4,1024,256]{2,0,1:T(4,128)} %bitcast.42, f32[256]{0:T(256)S(1)} %copy-done.11, f32[256]{0:T(256)S(1)} %copy-done.12, f32[4,256]{1,0:T(4,128)S(1)} %div.54, f32[4,256]{1,0:T(4,128)S(1)} %sub.44), kind=kLoop, calls=%fused_computation.6 | loop fusion | flops 6291456 | bytes 6301696 | tf_op jit(solution)/shard_map/convert_element_type | solution.py:211
  69.6 2.0 %convolution_convert_fusion.refs_2_ = bf16[4,1024,256]{2,1,0:T(8,128)(2,1)} fusion(bf16[4,1024,256]{2,1,0:T(8,128)(2,1)S(1)} %fusion.4, bf16[256,256]{1,0:T(8,128)(2,1)S(1)} %copy-done.4), kind=kOutput, calls=%fused_computation.14 | convolution fusion | flops 537919488 | bytes 4325376 | tf_op jit(solution)/shard_map/dot_general | solution.py:215
  71.6 2.1 %convolution_convert_fusion.1.refs_1_ = bf16[4,1024,256]{2,1,0:T(8,128)(2,1)} fusion(bf16[4,1024,256]{2,1,0:T(8,128)(2,1)S(1)} %fusion.4, bf16[256,256]{1,0:T(8,128)(2,1)S(1)} %copy-done.5), kind=kOutput, calls=%fused_computation.15 | convolution fusion | flops 537919488 | bytes 4325376 | tf_op jit(solution)/shard_map/dot_general | solution.py:214
  74.6 21.2 %shard_map.150 = (f32[4,200,8]{2,1,0:T(8,128)}, f32[4,200,8]{2,1,0:T(8,128)}, f32[4,200,256]{2,1,0:T(8,128)}) custom-call(bf16[4,1600,256]{2,1,0:T(8,128)(2,1)} %bitcast_select_fusion.refs_0_, bf16[4,1024,256]{2,1,0:T(8,128)(2,1)} %convolution_convert_fusion.1.refs_1_, bf16[4,1024,256]{2,1,0:T(8,128)(2,1)} %convolution_convert_fusion.refs_2_, ...), custom_call_target="tpu_custom_call" | custom-call | tf_op jit(solution)/shard_map/pallas_call | solution.py:145
  95.8 2.5 %reshape.123 = f32[128,1600]{1,0:T(8,128)} reshape(f32[4,200,256]{2,1,0:T(8,128)} %get-tuple-element.9) | data formatting | bytes 1638400 | tf_op jit(solution)/shard_map/reshape | solution.py:230
  98.3 1.2 reshape.124
  99.5 1.2 reshape.125
  100.7 2.2 %concatenate.15 = f32[128,1700]{1,0:T(8,128)} concatenate(f32[128,1600]{1,0:T(8,128)} %reshape.123, f32[128,50]{1,0:T(8,128)S(1)} %reshape.124, f32[128,50]{1,0:T(8,128)S(1)} %reshape.125), dimensions={1} | concatenate | bytes 1740800 | tf_op jit(solution)/shard_map/concatenate | solution.py:228
  102.9 2.1 %copy.32 = f32[128,1,1700]{2,1,0:T(1,128)S(1)} copy(f32[128,1,1700]{2,0,1:T(8,128)} %bitcast.43) | data formatting | bytes 1740800 | tf_op jit(solution)/shard_map/all_to_all | solution.py:236
  105.0 33.0 %all_to_all.18 = f32[128,1,1700]{2,1,0:T(1,128)} all-to-all(f32[128,1,1700]{2,1,0:T(1,128)S(1)} %copy.32), channel_id=1, replica_groups=mesh['rows'=16,'cols'=8] {'rows','cols'}, dimensions={0} | all-to-all | bytes 1740800 | tf_op jit(solution)/shard_map/all_to_all | solution.py:236
  138.0 3.1 %copy.33 = f32[128,1,1700]{0,2,1:T(8,128)} copy(f32[128,1,1700]{2,1,0:T(1,128)} %all_to_all.18) | data formatting | bytes 1740800 | tf_op jit(solution)/shard_map/all_to_all | solution.py:236
  141.9 1.0 fusion.22
  143.0 1.5 fusion.12
  144.6 1.4 broadcast_in_dim.69
  146.4 5.0 %reduce.6 = bf16[128,1600]{1,0:T(8,128)(2,1)} reduce(bf16[128,1,1600]{2,1,0:T(2,128)(2,1)} %broadcast_in_dim.69, bf16[]{:T(256)} %broadcast.105), dimensions={1}, to_apply=%broadcast_in_dim.69.reduce_sub_computation | reduce | bytes 819202 | tf_op jit(solution)/shard_map/broadcast_in_dim | solution.py:244
  151.5 2.3 %reshape.138 = bf16[128,2,800]{2,1,0:T(2,128)(2,1)} reshape(bf16[128,1600]{1,0:T(8,128)(2,1)} %reduce.6) | data formatting | bytes 819200
  153.7 18.4 %all_to_all.19 = bf16[128,2,800]{2,1,0:T(2,128)(2,1)} all-to-all(bf16[128,2,800]{2,1,0:T(2,128)(2,1)} %reshape.138), channel_id=1, replica_groups=mesh['rows'=16,'cols'=8] {'rows','cols'}, dimensions={0} | all-to-all | bytes 819200 | tf_op jit(solution)/shard_map/all_to_all | solution.py:243
  172.1 3.9 %reshape.139 = bf16[128,1,1600]{2,1,0:T(2,128)(2,1)} reshape(bf16[128,2,800]{2,1,0:T(2,128)(2,1)} %all_to_all.19) | data formatting | bytes 819200
  176.0 4.4 %reduce.5 = bf16[128,1600]{1,0:T(8,128)(2,1)} reduce(bf16[128,1,1600]{2,1,0:T(2,128)(2,1)} %reshape.139, bf16[]{:T(256)} %constant.43), dimensions={1}, to_apply=%all_to_all.15.reduce_sub_computation | reduce | bytes 819202 | tf_op jit(solution)/shard_map/all_to_all | solution.py:243
  180.4 2.4 %reshape.127 = bf16[4,200,256]{2,1,0:T(8,128)(2,1)} reshape(bf16[128,1600]{1,0:T(8,128)(2,1)} %reduce.5) | data formatting | bytes 819200 | tf_op jit(solution)/shard_map/reshape | solution.py:245
  182.8 1.7 fusion.30
  186.1 1.0 fusion.11
  187.1 3.1 %convolution_convert_fusion.2 = bf16[4,200,1024]{2,1,0:T(8,128)(2,1)} fusion(bf16[4,1024,256]{2,1,0:T(8,128)(2,1)S(1)} %fusion.4, bf16[4,200,256]{2,1,0:T(8,128)(2,1)} %fusion.11, bf16[256,256]{1,0:T(8,128)(2,1)S(1)} %copy-done.7), kind=kOutput, calls=%fused_computation.16 | convolution fusion | flops 525312000 | bytes 4276224 | tf_op jit(solution)/shard_map/bqc,bpc->bqp/dot_general | solution.py:254
  190.2 3.1 %copy.34 = bf16[100,8,8,128]{3,2,1,0:T(8,128)(2,1)} copy(bf16[100,8,8,128]{3,1,2,0:T(8,128)(2,1)} %bitcast.41) | data formatting | bytes 3276800
  (72 shorter events, 7.0 us)
Async XLA Ops:
  0.6 29.1 %copy-start = (bf16[3,3,256,256]{3,2,1,0:T(8,128)(2,1)S(1)}, bf16[3,3,256,256]{3,2,1,0:T(8,128)(2,1)}, u32[]{:S(2)}) copy-start(bf16[3,3,256,256]{3,2,1,0:T(8,128)(2,1)} %param.17) | copy-start | bytes 3538948
  0.6 10.9 %copy-start.1 = (bf16[4,8,128,256]{3,2,1,0:T(8,128)(2,1)S(1)}, bf16[4,8,128,256]{3,2,1,0:T(8,128)(2,1)}, u32[]{:S(2)}) copy-start(bf16[4,8,128,256]{3,2,1,0:T(8,128)(2,1)} %param.14) | copy-start | bytes 6291460
  2.1 9.3 %collective-permute-start = (bf16[4,1,128,256]{3,0,2,1:T(4,128)(2,1)S(1)}, bf16[4,1,128,256]{3,0,2,1:T(4,128)(2,1)S(1)}, u32[]{:S(2)}, u32[]{:S(2)}) collective-permute-start(bf16[4,1,128,256]{3,0,2,1:T(4,128)(2,1)S(1)} %copy.47), channel_id=1, source_target_pairs={{0,8},{8,16},{16,24},{24,32},{32,40},{40,48},{48,56},{56,64},{64,7... | collective-permute-start | bytes 786440 | tf_op jit(solution)/shard_map/ppermute | solution.py:20
  6.7 9.1 %collective-permute-start.1 = (bf16[4,1,128,256]{3,0,2,1:T(4,128)(2,1)S(1)}, bf16[4,1,128,256]{3,0,2,1:T(4,128)(2,1)S(1)}, u32[]{:S(2)}, u32[]{:S(2)}) collective-permute-start(bf16[4,1,128,256]{3,0,2,1:T(4,128)(2,1)S(1)} %copy.48), channel_id=1, source_target_pairs={{8,0},{16,8},{24,16},{32,24},{40,32},{48,40},{56,48},{64,56},{72,6... | collective-permute-start | bytes 786440 | tf_op jit(solution)/shard_map/ppermute | solution.py:22
  15.9 1.5 copy-start.10
  17.5 12.2 %collective-permute-start.2 = (bf16[4,10,1,256]{3,0,2,1:T(4,128)(2,1)S(1)}, bf16[4,10,1,256]{3,0,2,1:T(4,128)(2,1)S(1)}, u32[]{:S(2)}, u32[]{:S(2)}) collective-permute-start(bf16[4,10,1,256]{3,0,2,1:T(4,128)(2,1)S(1)} %get-tuple-element.16), channel_id=1, source_target_pairs={{0,1},{1,2},{2,3},{3,4},{4,5},{5,6},{6,7},{8,9},{9,10},{10,11},{11... | collective-permute-start | bytes 61448 | tf_op jit(solution)/shard_map/ppermute | solution.py:20
  22.2 7.5 %collective-permute-start.3 = (bf16[4,10,1,256]{3,0,2,1:T(4,128)(2,1)S(1)}, bf16[4,10,1,256]{3,0,2,1:T(4,128)(2,1)S(1)}, u32[]{:S(2)}, u32[]{:S(2)}) collective-permute-start(bf16[4,10,1,256]{3,0,2,1:T(4,128)(2,1)S(1)} %get-tuple-element.17), channel_id=1, source_target_pairs={{1,0},{2,1},{3,2},{4,3},{5,4},{6,5},{7,6},{9,8},{10,9},{11,10},{12... | collective-permute-start | bytes 61448 | tf_op jit(solution)/shard_map/ppermute | solution.py:22
  29.7 27.3 %copy-start.2 = (f32[4,200,256]{2,1,0:T(8,128)S(1)}, f32[4,200,256]{2,1,0:T(8,128)}, u32[]{:S(2)}) copy-start(f32[4,200,256]{2,1,0:T(8,128)} %param.16) | copy-start | bytes 2457604
  29.7 27.3 %copy-start.8 = (bf16[256,256]{1,0:T(8,128)(2,1)S(1)}, bf16[256,256]{1,0:T(8,128)(2,1)}, u32[]{:S(2)}) copy-start(bf16[256,256]{1,0:T(8,128)(2,1)} %param.20) | copy-start | bytes 393220
  42.8 1.2 collective-permute-start.4
  44.1 2.5 %collective-permute-start.5 = (f32[4,264]{1,0:T(4,128)S(1)}, f32[4,264]{1,0:T(4,128)S(1)}, u32[]{:S(2)}, u32[]{:S(2)}) collective-permute-start(f32[4,264]{1,0:T(4,128)S(1)} %fusion.37), channel_id=1, source_target_pairs={{0,2},{1,3},{2,0},{3,1},{4,6},{5,7},{6,4},{7,5},{8,10},{9,11},{10,... | collective-permute-start | bytes 12680 | tf_op jit(solution)/shard_map/ppermute | solution.py:37
  46.7 4.1 %collective-permute-start.6 = (f32[4,264]{1,0:T(4,128)S(1)}, f32[4,264]{1,0:T(4,128)S(1)}, u32[]{:S(2)}, u32[]{:S(2)}) collective-permute-start(f32[4,264]{1,0:T(4,128)S(1)} %add.64), channel_id=1, source_target_pairs={{0,4},{1,5},{2,6},{3,7},{4,0},{5,1},{6,2},{7,3},{8,12},{9,13},{10,... | collective-permute-start | bytes 12680 | tf_op jit(solution)/shard_map/ppermute | solution.py:37
  50.8 2.5 %collective-permute-start.7 = (f32[4,264]{1,0:T(4,128)S(1)}, f32[4,264]{1,0:T(4,128)S(1)}, u32[]{:S(2)}, u32[]{:S(2)}) collective-permute-start(f32[4,264]{1,0:T(4,128)S(1)} %add.65), channel_id=1, source_target_pairs={{0,8},{8,0},{16,24},{24,16},{32,40},{40,32},{48,56},{56,48},{64,72... | collective-permute-start | bytes 12680 | tf_op jit(solution)/shard_map/ppermute | solution.py:37
  53.2 4.8 %collective-permute-start.8 = (f32[4,264]{1,0:T(4,128)S(1)}, f32[4,264]{1,0:T(4,128)S(1)}, u32[]{:S(2)}, u32[]{:S(2)}) collective-permute-start(f32[4,264]{1,0:T(4,128)S(1)} %add.66), channel_id=1, source_target_pairs={{0,16},{8,24},{16,0},{24,8},{32,48},{40,56},{48,32},{56,40},{64,80... | collective-permute-start | bytes 12680 | tf_op jit(solution)/shard_map/ppermute | solution.py:37
  57.3 9.1 %copy-start.11 = (f32[256]{0:T(256)S(1)}, f32[256]{0:T(256)}, u32[]{:S(2)}) copy-start(f32[256]{0:T(256)} %param.19) | copy-start | bytes 3076
  57.3 9.1 %copy-start.12 = (f32[256]{0:T(256)S(1)}, f32[256]{0:T(256)}, u32[]{:S(2)}) copy-start(f32[256]{0:T(256)} %param.18) | copy-start | bytes 3076
  58.0 2.8 %collective-permute-start.9 = (f32[4,264]{1,0:T(4,128)S(1)}, f32[4,264]{1,0:T(4,128)S(1)}, u32[]{:S(2)}, u32[]{:S(2)}) collective-permute-start(f32[4,264]{1,0:T(4,128)S(1)} %add.67), channel_id=1, source_target_pairs={{0,32},{8,40},{16,48},{24,56},{32,0},{40,8},{48,16},{56,24},{64,96... | collective-permute-start | bytes 12680 | tf_op jit(solution)/shard_map/ppermute | solution.py:37
  60.8 5.1 %collective-permute-start.10 = (f32[4,264]{1,0:T(4,128)S(1)}, f32[4,264]{1,0:T(4,128)S(1)}, u32[]{:S(2)}, u32[]{:S(2)}) collective-permute-start(f32[4,264]{1,0:T(4,128)S(1)} %add.68), channel_id=1, source_target_pairs={{0,64},{8,72},{16,80},{24,88},{32,96},{40,104},{48,112},{56,120},{... | collective-permute-start | bytes 12680 | tf_op jit(solution)/shard_map/ppermute | solution.py:37
  66.4 3.2 %copy-start.4 = (bf16[256,256]{1,0:T(8,128)(2,1)S(1)}, bf16[256,256]{1,0:T(8,128)(2,1)}, u32[]{:S(2)}) copy-start(bf16[256,256]{1,0:T(8,128)(2,1)} %param.22) | copy-start | bytes 393220
  69.6 2.0 %copy-start.5 = (bf16[256,256]{1,0:T(8,128)(2,1)S(1)}, bf16[256,256]{1,0:T(8,128)(2,1)}, u32[]{:S(2)}) copy-start(bf16[256,256]{1,0:T(8,128)(2,1)} %param.21) | copy-start | bytes 393220
  151.5 31.3 %copy-start.6 = (bf16[256,256]{1,0:T(8,128)(2,1)S(1)}, bf16[256,256]{1,0:T(8,128)(2,1)}, u32[]{:S(2)}) copy-start(bf16[256,256]{1,0:T(8,128)(2,1)} %param.23) | copy-start | bytes 393220
  176.0 8.9 %copy-start.13 = (f32[256]{0:T(256)S(1)}, f32[256]{0:T(256)}, u32[]{:S(2)}) copy-start(f32[256]{0:T(256)} %param.25) | copy-start | bytes 3076
  176.0 8.9 %copy-start.14 = (f32[256]{0:T(256)S(1)}, f32[256]{0:T(256)}, u32[]{:S(2)}) copy-start(f32[256]{0:T(256)} %param.24) | copy-start | bytes 3076
  182.8 3.3 %copy-start.9 = (bf16[256,256]{1,0:T(8,128)(2,1)S(1)}, bf16[256,256]{1,0:T(8,128)(2,1)}, u32[]{:S(2)}) copy-start(bf16[256,256]{1,0:T(8,128)(2,1)} %param.26) | copy-start | bytes 393220
  182.8 4.4 %copy-start.7 = (bf16[256,256]{1,0:T(8,128)(2,1)S(1)}, bf16[256,256]{1,0:T(8,128)(2,1)}, u32[]{:S(2)}) copy-start(bf16[256,256]{1,0:T(8,128)(2,1)} %param.27) | copy-start | bytes 393220
  185.2 0.9 copy-start.3

commit v4 on v3

--- a/solution.py
+++ b/solution.py
@@ -200,7 +200,11 @@
     grouped = conv.reshape(images, pixels, GROUPS, width // GROUPS)
     first_sum = jnp.sum(grouped, axis=(1, 3))
     second_sum = jnp.sum(grouped * grouped, axis=(1, 3))
-    stats = butterfly_sum(jnp.concatenate([local_count[..., 0], first_sum, second_sum], axis=1))
+    stats = jnp.concatenate([local_count[..., 0], first_sum, second_sum], axis=1).reshape(1, -1)
+    stats = lax.all_to_all(
+        jnp.broadcast_to(stats, (devices, stats.shape[1])), ("rows", "cols"), 0, 0, tiled=True
+    )
+    stats = jnp.sum(stats, axis=0).reshape(images, -1)
     count = stats[:, :query_count]
     first_sum = stats[:, query_count : query_count + GROUPS]
     second_sum = stats[:, query_count + GROUPS :]

time: 194 us -> 188 us (0.969)
  blocking collectives: 51.3 us -> 40.7 us
  waiting for transfers between devices: 12.5 us -> 17.5 us
  starting transfers between devices: 26.1 us -> 23.2 us
    ppermute x7 -> x0, starting transfers between devices: 13.8 us -> none  [butterfly_sum(): got = lax.ppermute(x, axis, [(i, i ^ k) for i in range(n)])]
    all_to_all x0 -> x1, waiting for transfers between devices: none -> 11.5 us  [on_device(): lax.all_to_all(jnp.broadcast_to(stats, (devices, stats.shape[1])), ('rows...]
    all_to_all x0 -> x1, starting transfers between devices: none -> 10.9 us  [on_device(): lax.all_to_all(jnp.broadcast_to(stats, (devices, stats.shape[1])), ('rows...]
    all_to_all x1, blocking collectives: 33 us -> 22.4 us  [on_device(): parts = lax.all_to_all(packed, ('rows', 'cols'), 0, 0, tiled=True)]
    ppermute x7 -> x0, waiting for transfers between devices: 6.5 us -> none  [butterfly_sum(): got = lax.ppermute(x, axis, [(i, i ^ k) for i in range(n)])]
  transfers between devices with their start and end apart: 11 -> 5, of which waited for: 8 -> 3; matrix products, arithmetic and copies ran while one was open for 3% -> 3% of each run, Pallas kernels for 2% -> 2%
where the time goes in v4:
time: 188 us; the launch traced here: 186 us
  blocking collectives  40.7 us (22%)
  local copies, waits for them, and re-layouts  34.9 us (19%)
  Pallas kernels  25.6 us (14%)
  starting transfers between devices  23.2 us (12%)
  matrix products  22.7 us (12%)
  other arithmetic  20.7 us (11%)
  waiting for transfers between devices  17.5 us (9%)
    all_to_all x1, blocking collectives, on_device(): parts = lax.all_to_all(packed, ('rows', 'cols'), 0, 0, tiled=True)  22.4 us
    pallas_call x1, Pallas kernels, attention(): pl.pallas_call(kernel, grid=(images,), in_specs=[pl.BlockSpec((1, heads *...  21.2 us
    all_to_all x1, blocking collectives, on_device(): lax.all_to_all(jnp.broadcast_to(attn_block, (devices, span)), ('rows', 'c...  18.4 us
    unnamed x37, local copies, waits for them, and re-layouts  14 us
    conv_general_dilated x1, matrix products, on_device(): lax.conv_general_dilated(padded, conv_weight, (1, 1), 'VALID', dimension_...  12.6 us
    all_to_all x1, waiting for transfers between devices, on_device(): lax.all_to_all(jnp.broadcast_to(stats, (devices, stats.shape[1])), ('rows...  11.5 us
    all_to_all x1, starting transfers between devices, on_device(): lax.all_to_all(jnp.broadcast_to(stats, (devices, stats.shape[1])), ('rows...  10.9 us
    ppermute x2, starting transfers between devices, with_halo(): lax.ppermute(tail, axis, [(i, (i + 1) % count) for i in range(ends)])  9.11 us
  transfers between devices with their start and end apart: 5, of which 3 were waited for; matrix products, arithmetic and copies ran while one was open for 3% of the time, Pallas kernels for 2%

profile of v4, /device:TPU:1, one launch (start us, length us, event | category | flops | bytes accessed | tf_op | source)
XLA Modules:
  0.0 186.3 jit_solution(9461666641793476754)
XLA Ops:
  0.7 1.2 fusion.29
  2.1 4.4 %collective-permute-start = (bf16[4,1,128,256]{3,0,2,1:T(4,128)(2,1)S(1)}, bf16[4,1,128,256]{3,0,2,1:T(4,128)(2,1)S(1)}, u32[]{:S(2)}, u32[]{:S(2)}) collective-permute-start(bf16[4,1,128,256]{3,0,2,1:T(4,128)(2,1)S(1)} %copy.63), channel_id=1, source_target_pairs={{0,8},{8,16},{16,24},{24,32},{32,40},{40,48},{48,56},{56,64},{64,7... | collective-permute-start | bytes 786440 | tf_op jit(solution)/shard_map/ppermute | solution.py:20
  6.7 1.3 collective-permute-start.1
  8.0 3.4 %collective-permute-done = bf16[4,1,128,256]{3,0,2,1:T(4,128)(2,1)S(1)} collective-permute-done((bf16[4,1,128,256]{3,0,2,1:T(4,128)(2,1)S(1)}, bf16[4,1,128,256]{3,0,2,1:T(4,128)(2,1)S(1)}, u32[]{:S(2)}, u32[]{:S(2)}) %collective-permute-start) | collective-permute-done | bytes 262176 | tf_op jit(solution)/shard_map/ppermute | solution.py:20
  11.5 1.8 constant_dynamic-update-slice_fusion.1
  13.3 2.5 %collective-permute-done.1 = bf16[4,1,128,256]{3,0,2,1:T(4,128)(2,1)S(1)} collective-permute-done((bf16[4,1,128,256]{3,0,2,1:T(4,128)(2,1)S(1)}, bf16[4,1,128,256]{3,0,2,1:T(4,128)(2,1)S(1)}, u32[]{:S(2)}, u32[]{:S(2)}) %collective-permute-start.1) | collective-permute-done | bytes 262176 | tf_op jit(solution)/shard_map/ppermute | solution.py:22
  16.0 1.5 copy-done.10
  17.5 4.7 %collective-permute-start.2 = (bf16[4,10,1,256]{3,0,2,1:T(4,128)(2,1)S(1)}, bf16[4,10,1,256]{3,0,2,1:T(4,128)(2,1)S(1)}, u32[]{:S(2)}, u32[]{:S(2)}) collective-permute-start(bf16[4,10,1,256]{3,0,2,1:T(4,128)(2,1)S(1)} %get-tuple-element.16), channel_id=1, source_target_pairs={{0,1},{1,2},{2,3},{3,4},{4,5},{5,6},{6,7},{8,9},{9,10},{10,11},{11... | collective-permute-start | bytes 61448 | tf_op jit(solution)/shard_map/ppermute | solution.py:20
  22.2 1.9 %collective-permute-start.3 = (bf16[4,10,1,256]{3,0,2,1:T(4,128)(2,1)S(1)}, bf16[4,10,1,256]{3,0,2,1:T(4,128)(2,1)S(1)}, u32[]{:S(2)}, u32[]{:S(2)}) collective-permute-start(bf16[4,10,1,256]{3,0,2,1:T(4,128)(2,1)S(1)} %get-tuple-element.17), channel_id=1, source_target_pairs={{1,0},{2,1},{3,2},{4,3},{5,4},{6,5},{7,6},{9,8},{10,9},{11,10},{12... | collective-permute-start | bytes 61448 | tf_op jit(solution)/shard_map/ppermute | solution.py:22
  24.2 4.3 %shard_map.149 = (bf16[4,200,1024]{2,1,0:T(8,128)(2,1)}, f32[4,200,1]{2,1,0:T(8,128)}) custom-call(s32[4,1600,128]{2,1,0:T(8,128)} %bitcast.47), custom_call_target="tpu_custom_call" | custom-call | tf_op jit(solution)/shard_map/pallas_call | solution.py:104
  28.5 1.2 reduce.5
  29.8 12.6 %fusion.27 = (f32[4,256]{1,0:T(4,128)S(1)}, f32[4,256]{1,0:T(4,128)S(1)}, f32[4,8,128,256]{3,0,2,1:T(4,128)}) fusion(bf16[3,3,256,256]{3,2,1,0:T(8,128)(2,1)S(1)} %copy-done, bf16[4,10,1,256]{3,0,2,1:T(4,128)(2,1)S(1)} %collective-permute-done.3, bf16[4,10,128,256]{3,0,2,1:T(4,128)(2,1)} %copy-done.10, bf16[4,10,1,256]{3,0,2,1:T(4,128)(2,1)S(1)} %collective-permute-done.2), kind=kOutput, calls=%fused_computation.58 | convolution fusion | flops 4842969088 | bytes 8044544 | tf_op jit(solution)/shard_map/conv_general_dilated | solution.py:192
  42.9 1.1 broadcast_in_dim.72
  44.0 10.9 %all-to-all-start = ((f32[128,1,1056]{2,1,0:T(1,128)}), f32[128,1,1056]{2,1,0:T(1,128)S(1)}, u32[]{:S(2)}, u32[]{:S(2)}) async-start(f32[128,1,1056]{2,1,0:T(1,128)} %broadcast_in_dim.72), calls=%async_computation | async-start | bytes 1179648 | tf_op jit(solution)/shard_map/all_to_all | solution.py:204
  54.9 0.3 convolution_convert_fusion.4
  55.3 2.2 %bitcast_select_fusion.refs_0_ = bf16[4,1600,256]{2,1,0:T(8,128)(2,1)} fusion(pred[1600,256]{1,0:T(8,128)(4,1)S(1)} %bitcast.50, bf16[4,200,256]{2,1,0:T(8,128)(2,1)S(1)} %convolution_convert_fusion.4), kind=kLoop, calls=%fused_computation.7 | loop fusion | flops 1638400 | bytes 4096000 | tf_op jit(solution)/shard_map/jit(_where)/select_n | solution.py:225
  57.5 11.5 %all-to-all-done = f32[128,1,1056]{2,1,0:T(1,128)S(1)} async-done(((f32[128,1,1056]{2,1,0:T(1,128)}), f32[128,1,1056]{2,1,0:T(1,128)S(1)}, u32[]{:S(2)}, u32[]{:S(2)}) %all-to-all-start) | async-done | bytes 540704 | tf_op jit(solution)/shard_map/all_to_all | solution.py:204
  69.1 0.4 reduce_sum.83
  70.0 3.2 %fusion.4 = bf16[4,1024,256]{2,1,0:T(8,128)(2,1)S(1)} fusion(f32[4,1024,256]{2,0,1:T(4,128)} %bitcast.42, f32[256]{0:T(256)S(1)} %copy-done.11, f32[256]{0:T(256)S(1)} %copy-done.12, f32[4,256]{1,0:T(4,128)S(1)} %div.54, f32[4,256]{1,0:T(4,128)S(1)} %sub.44), kind=kLoop, calls=%fused_computation.6 | loop fusion | flops 6291456 | bytes 6301696 | tf_op jit(solution)/shard_map/convert_element_type | solution.py:215
  73.2 2.0 %convolution_convert_fusion.refs_2_ = bf16[4,1024,256]{2,1,0:T(8,128)(2,1)} fusion(bf16[4,1024,256]{2,1,0:T(8,128)(2,1)S(1)} %fusion.4, bf16[256,256]{1,0:T(8,128)(2,1)S(1)} %copy-done.4), kind=kOutput, calls=%fused_computation.14 | convolution fusion | flops 537919488 | bytes 4325376 | tf_op jit(solution)/shard_map/dot_general | solution.py:219
  75.2 2.1 %convolution_convert_fusion.1.refs_1_ = bf16[4,1024,256]{2,1,0:T(8,128)(2,1)} fusion(bf16[4,1024,256]{2,1,0:T(8,128)(2,1)S(1)} %fusion.4, bf16[256,256]{1,0:T(8,128)(2,1)S(1)} %copy-done.5), kind=kOutput, calls=%fused_computation.15 | convolution fusion | flops 537919488 | bytes 4325376 | tf_op jit(solution)/shard_map/dot_general | solution.py:218
  77.3 1.0 copy.46.refs_4_
  78.3 21.2 %shard_map.150 = (f32[4,200,8]{2,1,0:T(8,128)}, f32[4,200,8]{2,1,0:T(8,128)}, f32[4,200,256]{2,1,0:T(8,128)}) custom-call(bf16[4,1600,256]{2,1,0:T(8,128)(2,1)} %bitcast_select_fusion.refs_0_, bf16[4,1024,256]{2,1,0:T(8,128)(2,1)} %convolution_convert_fusion.1.refs_1_, bf16[4,1024,256]{2,1,0:T(8,128)(2,1)} %convolution_convert_fusion.refs_2_, ...), custom_call_target="tpu_custom_call" | custom-call | tf_op jit(solution)/shard_map/pallas_call | solution.py:145
  99.5 2.5 %reshape.136 = f32[128,1600]{1,0:T(8,128)} reshape(f32[4,200,256]{2,1,0:T(8,128)} %get-tuple-element.9) | data formatting | bytes 1638400 | tf_op jit(solution)/shard_map/reshape | solution.py:234
  102.0 1.2 reshape.137
  103.1 1.2 reshape.138
  104.3 2.2 %concatenate.15 = f32[128,1700]{1,0:T(8,128)} concatenate(f32[128,1600]{1,0:T(8,128)} %reshape.136, f32[128,50]{1,0:T(8,128)S(1)} %reshape.137, f32[128,50]{1,0:T(8,128)S(1)} %reshape.138), dimensions={1} | concatenate | bytes 1740800 | tf_op jit(solution)/shard_map/concatenate | solution.py:232
  106.5 2.1 %copy.47 = f32[128,1,1700]{2,1,0:T(1,128)S(1)} copy(f32[128,1,1700]{2,0,1:T(8,128)} %bitcast.43) | data formatting | bytes 1740800 | tf_op jit(solution)/shard_map/all_to_all | solution.py:240
  108.6 22.4 %all_to_all.24 = f32[128,1,1700]{2,1,0:T(1,128)} all-to-all(f32[128,1,1700]{2,1,0:T(1,128)S(1)} %copy.47), channel_id=1, replica_groups=mesh['rows'=16,'cols'=8] {'rows','cols'}, dimensions={0} | all-to-all | bytes 1740800 | tf_op jit(solution)/shard_map/all_to_all | solution.py:240
  131.0 3.1 %copy.48 = f32[128,1,1700]{0,2,1:T(8,128)} copy(f32[128,1,1700]{2,1,0:T(1,128)} %all_to_all.24) | data formatting | bytes 1740800 | tf_op jit(solution)/shard_map/all_to_all | solution.py:240
  134.1 0.9 slice_reduce_fusion
  134.9 1.0 fusion.22
  136.0 1.5 fusion.12
  137.6 1.4 broadcast_in_dim.78
  139.0 0.5 broadcast.108
  139.5 5.0 %reduce.7 = bf16[128,1600]{1,0:T(8,128)(2,1)} reduce(bf16[128,1,1600]{2,1,0:T(2,128)(2,1)} %broadcast_in_dim.78, bf16[]{:T(256)} %broadcast.108), dimensions={1}, to_apply=%broadcast_in_dim.78.reduce_sub_computation | reduce | bytes 819202 | tf_op jit(solution)/shard_map/broadcast_in_dim | solution.py:248
  144.5 2.3 %reshape.151 = bf16[128,2,800]{2,1,0:T(2,128)(2,1)} reshape(bf16[128,1600]{1,0:T(8,128)(2,1)} %reduce.7) | data formatting | bytes 819200
  146.8 18.4 %all_to_all.25 = bf16[128,2,800]{2,1,0:T(2,128)(2,1)} all-to-all(bf16[128,2,800]{2,1,0:T(2,128)(2,1)} %reshape.151), channel_id=1, replica_groups=mesh['rows'=16,'cols'=8] {'rows','cols'}, dimensions={0} | all-to-all | bytes 819200 | tf_op jit(solution)/shard_map/all_to_all | solution.py:247
  165.1 3.9 %reshape.152 = bf16[128,1,1600]{2,1,0:T(2,128)(2,1)} reshape(bf16[128,2,800]{2,1,0:T(2,128)(2,1)} %all_to_all.25) | data formatting | bytes 819200
  169.1 4.4 %reduce.6 = bf16[128,1600]{1,0:T(8,128)(2,1)} reduce(bf16[128,1,1600]{2,1,0:T(2,128)(2,1)} %reshape.152, bf16[]{:T(256)} %constant.43), dimensions={1}, to_apply=%all_to_all.20.reduce_sub_computation | reduce | bytes 819202 | tf_op jit(solution)/shard_map/all_to_all | solution.py:247
  173.4 2.4 %reshape.140 = bf16[4,200,256]{2,1,0:T(8,128)(2,1)} reshape(bf16[128,1600]{1,0:T(8,128)(2,1)} %reduce.6) | data formatting | bytes 819200 | tf_op jit(solution)/shard_map/reshape | solution.py:249
  175.8 1.7 fusion.30
  177.5 0.4 multiply_reduce_fusion.1
  177.9 0.3 multiply_add_fusion
  178.2 0.9 copy-done.3
  179.1 1.0 fusion.11
  180.2 3.1 %convolution_convert_fusion.2 = bf16[4,200,1024]{2,1,0:T(8,128)(2,1)} fusion(bf16[4,1024,256]{2,1,0:T(8,128)(2,1)S(1)} %fusion.4, bf16[4,200,256]{2,1,0:T(8,128)(2,1)} %fusion.11, bf16[256,256]{1,0:T(8,128)(2,1)S(1)} %copy-done.7), kind=kOutput, calls=%fused_computation.16 | convolution fusion | flops 525312000 | bytes 4276224 | tf_op jit(solution)/shard_map/bqc,bpc->bqp/dot_general | solution.py:258
  183.3 3.1 %copy.50 = bf16[100,8,8,128]{3,2,1,0:T(8,128)(2,1)} copy(bf16[100,8,8,128]{3,1,2,0:T(8,128)(2,1)} %bitcast.41) | data formatting | bytes 3276800
  (57 shorter events, 2.1 us)
Async XLA Ops:
  0.6 29.1 %copy-start = (bf16[3,3,256,256]{3,2,1,0:T(8,128)(2,1)S(1)}, bf16[3,3,256,256]{3,2,1,0:T(8,128)(2,1)}, u32[]{:S(2)}) copy-start(bf16[3,3,256,256]{3,2,1,0:T(8,128)(2,1)} %param.17) | copy-start | bytes 3538948
  0.6 10.9 %copy-start.1 = (bf16[4,8,128,256]{3,2,1,0:T(8,128)(2,1)S(1)}, bf16[4,8,128,256]{3,2,1,0:T(8,128)(2,1)}, u32[]{:S(2)}) copy-start(bf16[4,8,128,256]{3,2,1,0:T(8,128)(2,1)} %param.14) | copy-start | bytes 6291460
  2.1 9.3 %collective-permute-start = (bf16[4,1,128,256]{3,0,2,1:T(4,128)(2,1)S(1)}, bf16[4,1,128,256]{3,0,2,1:T(4,128)(2,1)S(1)}, u32[]{:S(2)}, u32[]{:S(2)}) collective-permute-start(bf16[4,1,128,256]{3,0,2,1:T(4,128)(2,1)S(1)} %copy.63), channel_id=1, source_target_pairs={{0,8},{8,16},{16,24},{24,32},{32,40},{40,48},{48,56},{56,64},{64,7... | collective-permute-start | bytes 786440 | tf_op jit(solution)/shard_map/ppermute | solution.py:20
  6.7 9.1 %collective-permute-start.1 = (bf16[4,1,128,256]{3,0,2,1:T(4,128)(2,1)S(1)}, bf16[4,1,128,256]{3,0,2,1:T(4,128)(2,1)S(1)}, u32[]{:S(2)}, u32[]{:S(2)}) collective-permute-start(bf16[4,1,128,256]{3,0,2,1:T(4,128)(2,1)S(1)} %copy.64), channel_id=1, source_target_pairs={{8,0},{16,8},{24,16},{32,24},{40,32},{48,40},{56,48},{64,56},{72,6... | collective-permute-start | bytes 786440 | tf_op jit(solution)/shard_map/ppermute | solution.py:22
  15.9 1.5 copy-start.10
  17.5 12.2 %collective-permute-start.2 = (bf16[4,10,1,256]{3,0,2,1:T(4,128)(2,1)S(1)}, bf16[4,10,1,256]{3,0,2,1:T(4,128)(2,1)S(1)}, u32[]{:S(2)}, u32[]{:S(2)}) collective-permute-start(bf16[4,10,1,256]{3,0,2,1:T(4,128)(2,1)S(1)} %get-tuple-element.16), channel_id=1, source_target_pairs={{0,1},{1,2},{2,3},{3,4},{4,5},{5,6},{6,7},{8,9},{9,10},{10,11},{11... | collective-permute-start | bytes 61448 | tf_op jit(solution)/shard_map/ppermute | solution.py:20
  22.2 7.5 %collective-permute-start.3 = (bf16[4,10,1,256]{3,0,2,1:T(4,128)(2,1)S(1)}, bf16[4,10,1,256]{3,0,2,1:T(4,128)(2,1)S(1)}, u32[]{:S(2)}, u32[]{:S(2)}) collective-permute-start(bf16[4,10,1,256]{3,0,2,1:T(4,128)(2,1)S(1)} %get-tuple-element.17), channel_id=1, source_target_pairs={{1,0},{2,1},{3,2},{4,3},{5,4},{6,5},{7,6},{9,8},{10,9},{11,10},{12... | collective-permute-start | bytes 61448 | tf_op jit(solution)/shard_map/ppermute | solution.py:22
  29.7 25.2 %copy-start.8 = (bf16[256,256]{1,0:T(8,128)(2,1)S(1)}, bf16[256,256]{1,0:T(8,128)(2,1)}, u32[]{:S(2)}) copy-start(bf16[256,256]{1,0:T(8,128)(2,1)} %param.20) | copy-start | bytes 393220
  42.3 12.6 %copy-start.2 = (f32[4,200,256]{2,1,0:T(8,128)S(1)}, f32[4,200,256]{2,1,0:T(8,128)}, u32[]{:S(2)}) copy-start(f32[4,200,256]{2,1,0:T(8,128)} %param.16) | copy-start | bytes 2457604
  44.0 25.1 %all-to-all-start = ((f32[128,1,1056]{2,1,0:T(1,128)}), f32[128,1,1056]{2,1,0:T(1,128)S(1)}, u32[]{:S(2)}, u32[]{:S(2)}) async-start(f32[128,1,1056]{2,1,0:T(1,128)} %broadcast_in_dim.72), calls=%async_computation | async-start | bytes 1179648 | tf_op jit(solution)/shard_map/all_to_all | solution.py:204
  55.2 14.8 %copy-start.11 = (f32[256]{0:T(256)S(1)}, f32[256]{0:T(256)}, u32[]{:S(2)}) copy-start(f32[256]{0:T(256)} %param.19) | copy-start | bytes 3076
  55.2 14.8 %copy-start.12 = (f32[256]{0:T(256)S(1)}, f32[256]{0:T(256)}, u32[]{:S(2)}) copy-start(f32[256]{0:T(256)} %param.18) | copy-start | bytes 3076
  70.0 3.2 %copy-start.4 = (bf16[256,256]{1,0:T(8,128)(2,1)S(1)}, bf16[256,256]{1,0:T(8,128)(2,1)}, u32[]{:S(2)}) copy-start(bf16[256,256]{1,0:T(8,128)(2,1)} %param.22) | copy-start | bytes 393220
  73.2 2.0 %copy-start.5 = (bf16[256,256]{1,0:T(8,128)(2,1)S(1)}, bf16[256,256]{1,0:T(8,128)(2,1)}, u32[]{:S(2)}) copy-start(bf16[256,256]{1,0:T(8,128)(2,1)} %param.21) | copy-start | bytes 393220
  144.5 31.3 %copy-start.6 = (bf16[256,256]{1,0:T(8,128)(2,1)S(1)}, bf16[256,256]{1,0:T(8,128)(2,1)}, u32[]{:S(2)}) copy-start(bf16[256,256]{1,0:T(8,128)(2,1)} %param.23) | copy-start | bytes 393220
  169.1 8.9 %copy-start.13 = (f32[256]{0:T(256)S(1)}, f32[256]{0:T(256)}, u32[]{:S(2)}) copy-start(f32[256]{0:T(256)} %param.25) | copy-start | bytes 3076
  169.1 8.9 %copy-start.14 = (f32[256]{0:T(256)S(1)}, f32[256]{0:T(256)}, u32[]{:S(2)}) copy-start(f32[256]{0:T(256)} %param.24) | copy-start | bytes 3076
  175.8 3.3 %copy-start.9 = (bf16[256,256]{1,0:T(8,128)(2,1)S(1)}, bf16[256,256]{1,0:T(8,128)(2,1)}, u32[]{:S(2)}) copy-start(bf16[256,256]{1,0:T(8,128)(2,1)} %param.26) | copy-start | bytes 393220
  175.8 4.4 %copy-start.7 = (bf16[256,256]{1,0:T(8,128)(2,1)S(1)}, bf16[256,256]{1,0:T(8,128)(2,1)}, u32[]{:S(2)}) copy-start(bf16[256,256]{1,0:T(8,128)(2,1)} %param.27) | copy-start | bytes 393220
  178.2 0.9 copy-start.3

commit v5 on v4

--- a/solution.py
+++ b/solution.py
@@ -123,13 +123,14 @@
     k = k_ref[0]
     v = v_ref[0]
     allowed = (fg_ref[0] != 0) | (zero_ref[0] != 0)
+    bias = jnp.where(allowed, 0.0, -jnp.inf)
     lane = lax.broadcasted_iota(jnp.int32, (queries, width), 1)
     acc = jnp.zeros((queries, width), jnp.float32)
     for h in range(heads):
         q = q_ref[0, h * queries : (h + 1) * queries, :]
         s = lax.dot_general(q, k, (((1,), (1,)), ((), ())), preferred_element_type=jnp.float32) * scale
-        top = jnp.max(jnp.where(allowed, s, NEG), axis=1, keepdims=True)
-        w = jnp.where(allowed, jnp.exp(s - top), 0.0).astype(jnp.bfloat16)
+        top = jnp.maximum(jnp.max(s + bias, axis=1, keepdims=True), NEG)
+        w = jnp.exp(s + bias - top).astype(jnp.bfloat16)
         tot_ref[0, :, h : h + 1] = jnp.sum(w.astype(jnp.float32), axis=1, keepdims=True)
         top_ref[0, :, h : h + 1] = top
         r = jnp.dot(w, v, preferred_element_type=jnp.float32)

time: 188 us -> 185 us (0.984)
  Pallas kernels: 25.6 us -> 23 us
    pallas_call x1, Pallas kernels: 21.2 us -> 18.7 us  [attention(): pl.pallas_call(kernel, grid=(images,), in_specs=[pl.BlockSpec((1, heads *...]
where the time goes in v5:
time: 185 us; the launch traced here: 184 us
  blocking collectives  40.7 us (22%)
  local copies, waits for them, and re-layouts  34.9 us (19%)
  starting transfers between devices  23.2 us (13%)
  Pallas kernels  23 us (12%)
  matrix products  22.7 us (12%)
  other arithmetic  20.7 us (11%)
  waiting for transfers between devices  17.5 us (9%)
    all_to_all x1, blocking collectives, on_device(): parts = lax.all_to_all(packed, ('rows', 'cols'), 0, 0, tiled=True)  22.4 us
    pallas_call x1, Pallas kernels, attention(): pl.pallas_call(kernel, grid=(images,), in_specs=[pl.BlockSpec((1, heads *...  18.7 us
    all_to_all x1, blocking collectives, on_device(): lax.all_to_all(jnp.broadcast_to(attn_block, (devices, span)), ('rows', 'c...  18.4 us
    unnamed x37, local copies, waits for them, and re-layouts  14 us
    conv_general_dilated x1, matrix products, on_device(): lax.conv_general_dilated(padded, conv_weight, (1, 1), 'VALID', dimension_...  12.6 us
    all_to_all x1, waiting for transfers between devices, on_device(): lax.all_to_all(jnp.broadcast_to(stats, (devices, stats.shape[1])), ('rows...  11.5 us
    all_to_all x1, starting transfers between devices, on_device(): lax.all_to_all(jnp.broadcast_to(stats, (devices, stats.shape[1])), ('rows...  10.9 us
    ppermute x2, starting transfers between devices, with_halo(): lax.ppermute(tail, axis, [(i, (i + 1) % count) for i in range(ends)])  9.11 us
  transfers between devices with their start and end apart: 5, of which 3 were waited for; matrix products, arithmetic and copies ran while one was open for 3% of the time, Pallas kernels for 2%

profile of v5, /device:TPU:1, one launch (start us, length us, event | category | flops | bytes accessed | tf_op | source)
XLA Modules:
  0.0 183.8 jit_solution(4364592653521923181)
XLA Ops:
  0.7 1.2 fusion.29
  2.1 4.4 %collective-permute-start = (bf16[4,1,128,256]{3,0,2,1:T(4,128)(2,1)S(1)}, bf16[4,1,128,256]{3,0,2,1:T(4,128)(2,1)S(1)}, u32[]{:S(2)}, u32[]{:S(2)}) collective-permute-start(bf16[4,1,128,256]{3,0,2,1:T(4,128)(2,1)S(1)} %copy.63), channel_id=1, source_target_pairs={{0,8},{8,16},{16,24},{24,32},{32,40},{40,48},{48,56},{56,64},{64,7... | collective-permute-start | bytes 786440 | tf_op jit(solution)/shard_map/ppermute | solution.py:20
  6.7 1.3 collective-permute-start.1
  8.0 3.4 %collective-permute-done = bf16[4,1,128,256]{3,0,2,1:T(4,128)(2,1)S(1)} collective-permute-done((bf16[4,1,128,256]{3,0,2,1:T(4,128)(2,1)S(1)}, bf16[4,1,128,256]{3,0,2,1:T(4,128)(2,1)S(1)}, u32[]{:S(2)}, u32[]{:S(2)}) %collective-permute-start) | collective-permute-done | bytes 262176 | tf_op jit(solution)/shard_map/ppermute | solution.py:20
  11.5 1.8 constant_dynamic-update-slice_fusion.1
  13.3 2.5 %collective-permute-done.1 = bf16[4,1,128,256]{3,0,2,1:T(4,128)(2,1)S(1)} collective-permute-done((bf16[4,1,128,256]{3,0,2,1:T(4,128)(2,1)S(1)}, bf16[4,1,128,256]{3,0,2,1:T(4,128)(2,1)S(1)}, u32[]{:S(2)}, u32[]{:S(2)}) %collective-permute-start.1) | collective-permute-done | bytes 262176 | tf_op jit(solution)/shard_map/ppermute | solution.py:22
  16.0 1.5 copy-done.10
  17.5 4.7 %collective-permute-start.2 = (bf16[4,10,1,256]{3,0,2,1:T(4,128)(2,1)S(1)}, bf16[4,10,1,256]{3,0,2,1:T(4,128)(2,1)S(1)}, u32[]{:S(2)}, u32[]{:S(2)}) collective-permute-start(bf16[4,10,1,256]{3,0,2,1:T(4,128)(2,1)S(1)} %get-tuple-element.16), channel_id=1, source_target_pairs={{0,1},{1,2},{2,3},{3,4},{4,5},{5,6},{6,7},{8,9},{9,10},{10,11},{11... | collective-permute-start | bytes 61448 | tf_op jit(solution)/shard_map/ppermute | solution.py:20
  22.2 1.9 %collective-permute-start.3 = (bf16[4,10,1,256]{3,0,2,1:T(4,128)(2,1)S(1)}, bf16[4,10,1,256]{3,0,2,1:T(4,128)(2,1)S(1)}, u32[]{:S(2)}, u32[]{:S(2)}) collective-permute-start(bf16[4,10,1,256]{3,0,2,1:T(4,128)(2,1)S(1)} %get-tuple-element.17), channel_id=1, source_target_pairs={{1,0},{2,1},{3,2},{4,3},{5,4},{6,5},{7,6},{9,8},{10,9},{11,10},{12... | collective-permute-start | bytes 61448 | tf_op jit(solution)/shard_map/ppermute | solution.py:22
  24.2 4.3 %shard_map.149 = (bf16[4,200,1024]{2,1,0:T(8,128)(2,1)}, f32[4,200,1]{2,1,0:T(8,128)}) custom-call(s32[4,1600,128]{2,1,0:T(8,128)} %bitcast.47), custom_call_target="tpu_custom_call" | custom-call | tf_op jit(solution)/shard_map/pallas_call | solution.py:104
  28.5 1.2 reduce.5
  29.8 12.6 %fusion.27 = (f32[4,256]{1,0:T(4,128)S(1)}, f32[4,256]{1,0:T(4,128)S(1)}, f32[4,8,128,256]{3,0,2,1:T(4,128)}) fusion(bf16[3,3,256,256]{3,2,1,0:T(8,128)(2,1)S(1)} %copy-done, bf16[4,10,1,256]{3,0,2,1:T(4,128)(2,1)S(1)} %collective-permute-done.3, bf16[4,10,128,256]{3,0,2,1:T(4,128)(2,1)} %copy-done.10, bf16[4,10,1,256]{3,0,2,1:T(4,128)(2,1)S(1)} %collective-permute-done.2), kind=kOutput, calls=%fused_computation.58 | convolution fusion | flops 4842969088 | bytes 8044544 | tf_op jit(solution)/shard_map/conv_general_dilated | solution.py:193
  42.9 1.1 broadcast_in_dim.72
  44.0 10.9 %all-to-all-start = ((f32[128,1,1056]{2,1,0:T(1,128)}), f32[128,1,1056]{2,1,0:T(1,128)S(1)}, u32[]{:S(2)}, u32[]{:S(2)}) async-start(f32[128,1,1056]{2,1,0:T(1,128)} %broadcast_in_dim.72), calls=%async_computation | async-start | bytes 1179648 | tf_op jit(solution)/shard_map/all_to_all | solution.py:205
  54.9 0.3 convolution_convert_fusion.4
  55.3 2.2 %bitcast_select_fusion.refs_0_ = bf16[4,1600,256]{2,1,0:T(8,128)(2,1)} fusion(pred[1600,256]{1,0:T(8,128)(4,1)S(1)} %bitcast.50, bf16[4,200,256]{2,1,0:T(8,128)(2,1)S(1)} %convolution_convert_fusion.4), kind=kLoop, calls=%fused_computation.7 | loop fusion | flops 1638400 | bytes 4096000 | tf_op jit(solution)/shard_map/jit(_where)/select_n | solution.py:226
  57.5 11.5 %all-to-all-done = f32[128,1,1056]{2,1,0:T(1,128)S(1)} async-done(((f32[128,1,1056]{2,1,0:T(1,128)}), f32[128,1,1056]{2,1,0:T(1,128)S(1)}, u32[]{:S(2)}, u32[]{:S(2)}) %all-to-all-start) | async-done | bytes 540704 | tf_op jit(solution)/shard_map/all_to_all | solution.py:205
  69.1 0.4 reduce_sum.83
  70.0 3.2 %fusion.4 = bf16[4,1024,256]{2,1,0:T(8,128)(2,1)S(1)} fusion(f32[4,1024,256]{2,0,1:T(4,128)} %bitcast.42, f32[256]{0:T(256)S(1)} %copy-done.11, f32[256]{0:T(256)S(1)} %copy-done.12, f32[4,256]{1,0:T(4,128)S(1)} %div.54, f32[4,256]{1,0:T(4,128)S(1)} %sub.44), kind=kLoop, calls=%fused_computation.6 | loop fusion | flops 6291456 | bytes 6301696 | tf_op jit(solution)/shard_map/convert_element_type | solution.py:216
  73.2 2.0 %convolution_convert_fusion.refs_2_ = bf16[4,1024,256]{2,1,0:T(8,128)(2,1)} fusion(bf16[4,1024,256]{2,1,0:T(8,128)(2,1)S(1)} %fusion.4, bf16[256,256]{1,0:T(8,128)(2,1)S(1)} %copy-done.4), kind=kOutput, calls=%fused_computation.14 | convolution fusion | flops 537919488 | bytes 4325376 | tf_op jit(solution)/shard_map/dot_general | solution.py:220
  75.2 2.1 %convolution_convert_fusion.1.refs_1_ = bf16[4,1024,256]{2,1,0:T(8,128)(2,1)} fusion(bf16[4,1024,256]{2,1,0:T(8,128)(2,1)S(1)} %fusion.4, bf16[256,256]{1,0:T(8,128)(2,1)S(1)} %copy-done.5), kind=kOutput, calls=%fused_computation.15 | convolution fusion | flops 537919488 | bytes 4325376 | tf_op jit(solution)/shard_map/dot_general | solution.py:219
  77.3 1.0 copy.46.refs_4_
  78.3 18.7 %shard_map.150 = (f32[4,200,8]{2,1,0:T(8,128)}, f32[4,200,8]{2,1,0:T(8,128)}, f32[4,200,256]{2,1,0:T(8,128)}) custom-call(bf16[4,1600,256]{2,1,0:T(8,128)(2,1)} %bitcast_select_fusion.refs_0_, bf16[4,1024,256]{2,1,0:T(8,128)(2,1)} %convolution_convert_fusion.1.refs_1_, bf16[4,1024,256]{2,1,0:T(8,128)(2,1)} %convolution_convert_fusion.refs_2_, ...), custom_call_target="tpu_custom_call" | custom-call | tf_op jit(solution)/shard_map/pallas_call | solution.py:146
  96.9 2.5 %reshape.136 = f32[128,1600]{1,0:T(8,128)} reshape(f32[4,200,256]{2,1,0:T(8,128)} %get-tuple-element.9) | data formatting | bytes 1638400 | tf_op jit(solution)/shard_map/reshape | solution.py:235
  99.4 1.2 reshape.137
  100.6 1.2 reshape.138
  101.8 2.2 %concatenate.15 = f32[128,1700]{1,0:T(8,128)} concatenate(f32[128,1600]{1,0:T(8,128)} %reshape.136, f32[128,50]{1,0:T(8,128)S(1)} %reshape.137, f32[128,50]{1,0:T(8,128)S(1)} %reshape.138), dimensions={1} | concatenate | bytes 1740800 | tf_op jit(solution)/shard_map/concatenate | solution.py:233
  104.0 2.1 %copy.47 = f32[128,1,1700]{2,1,0:T(1,128)S(1)} copy(f32[128,1,1700]{2,0,1:T(8,128)} %bitcast.43) | data formatting | bytes 1740800 | tf_op jit(solution)/shard_map/all_to_all | solution.py:241
  106.1 22.4 %all_to_all.24 = f32[128,1,1700]{2,1,0:T(1,128)} all-to-all(f32[128,1,1700]{2,1,0:T(1,128)S(1)} %copy.47), channel_id=1, replica_groups=mesh['rows'=16,'cols'=8] {'rows','cols'}, dimensions={0} | all-to-all | bytes 1740800 | tf_op jit(solution)/shard_map/all_to_all | solution.py:241
  128.4 3.1 %copy.48 = f32[128,1,1700]{0,2,1:T(8,128)} copy(f32[128,1,1700]{2,1,0:T(1,128)} %all_to_all.24) | data formatting | bytes 1740800 | tf_op jit(solution)/shard_map/all_to_all | solution.py:241
  131.5 0.9 slice_reduce_fusion
  132.4 1.0 fusion.22
  133.5 1.5 fusion.12
  135.1 1.4 broadcast_in_dim.78
  136.4 0.5 broadcast.108
  136.9 5.0 %reduce.7 = bf16[128,1600]{1,0:T(8,128)(2,1)} reduce(bf16[128,1,1600]{2,1,0:T(2,128)(2,1)} %broadcast_in_dim.78, bf16[]{:T(256)} %broadcast.108), dimensions={1}, to_apply=%broadcast_in_dim.78.reduce_sub_computation | reduce | bytes 819202 | tf_op jit(solution)/shard_map/broadcast_in_dim | solution.py:249
  141.9 2.3 %reshape.151 = bf16[128,2,800]{2,1,0:T(2,128)(2,1)} reshape(bf16[128,1600]{1,0:T(8,128)(2,1)} %reduce.7) | data formatting | bytes 819200
  144.2 18.4 %all_to_all.25 = bf16[128,2,800]{2,1,0:T(2,128)(2,1)} all-to-all(bf16[128,2,800]{2,1,0:T(2,128)(2,1)} %reshape.151), channel_id=1, replica_groups=mesh['rows'=16,'cols'=8] {'rows','cols'}, dimensions={0} | all-to-all | bytes 819200 | tf_op jit(solution)/shard_map/all_to_all | solution.py:248
  162.6 3.9 %reshape.152 = bf16[128,1,1600]{2,1,0:T(2,128)(2,1)} reshape(bf16[128,2,800]{2,1,0:T(2,128)(2,1)} %all_to_all.25) | data formatting | bytes 819200
  166.5 4.4 %reduce.6 = bf16[128,1600]{1,0:T(8,128)(2,1)} reduce(bf16[128,1,1600]{2,1,0:T(2,128)(2,1)} %reshape.152, bf16[]{:T(256)} %constant.43), dimensions={1}, to_apply=%all_to_all.20.reduce_sub_computation | reduce | bytes 819202 | tf_op jit(solution)/shard_map/all_to_all | solution.py:248
  170.9 2.4 %reshape.140 = bf16[4,200,256]{2,1,0:T(8,128)(2,1)} reshape(bf16[128,1600]{1,0:T(8,128)(2,1)} %reduce.6) | data formatting | bytes 819200 | tf_op jit(solution)/shard_map/reshape | solution.py:250
  173.3 1.7 fusion.30
  175.0 0.4 multiply_reduce_fusion.1
  175.4 0.3 multiply_add_fusion
  175.7 0.9 copy-done.3
  176.6 1.0 fusion.11
  177.6 3.1 %convolution_convert_fusion.2 = bf16[4,200,1024]{2,1,0:T(8,128)(2,1)} fusion(bf16[4,1024,256]{2,1,0:T(8,128)(2,1)S(1)} %fusion.4, bf16[4,200,256]{2,1,0:T(8,128)(2,1)} %fusion.11, bf16[256,256]{1,0:T(8,128)(2,1)S(1)} %copy-done.7), kind=kOutput, calls=%fused_computation.16 | convolution fusion | flops 525312000 | bytes 4276224 | tf_op jit(solution)/shard_map/bqc,bpc->bqp/dot_general | solution.py:259
  180.7 3.1 %copy.50 = bf16[100,8,8,128]{3,2,1,0:T(8,128)(2,1)} copy(bf16[100,8,8,128]{3,1,2,0:T(8,128)(2,1)} %bitcast.41) | data formatting | bytes 3276800
  (57 shorter events, 2.1 us)
Async XLA Ops:
  0.6 29.1 %copy-start = (bf16[3,3,256,256]{3,2,1,0:T(8,128)(2,1)S(1)}, bf16[3,3,256,256]{3,2,1,0:T(8,128)(2,1)}, u32[]{:S(2)}) copy-start(bf16[3,3,256,256]{3,2,1,0:T(8,128)(2,1)} %param.17) | copy-start | bytes 3538948
  0.6 10.9 %copy-start.1 = (bf16[4,8,128,256]{3,2,1,0:T(8,128)(2,1)S(1)}, bf16[4,8,128,256]{3,2,1,0:T(8,128)(2,1)}, u32[]{:S(2)}) copy-start(bf16[4,8,128,256]{3,2,1,0:T(8,128)(2,1)} %param.14) | copy-start | bytes 6291460
  2.1 9.3 %collective-permute-start = (bf16[4,1,128,256]{3,0,2,1:T(4,128)(2,1)S(1)}, bf16[4,1,128,256]{3,0,2,1:T(4,128)(2,1)S(1)}, u32[]{:S(2)}, u32[]{:S(2)}) collective-permute-start(bf16[4,1,128,256]{3,0,2,1:T(4,128)(2,1)S(1)} %copy.63), channel_id=1, source_target_pairs={{0,8},{8,16},{16,24},{24,32},{32,40},{40,48},{48,56},{56,64},{64,7... | collective-permute-start | bytes 786440 | tf_op jit(solution)/shard_map/ppermute | solution.py:20
  6.7 9.1 %collective-permute-start.1 = (bf16[4,1,128,256]{3,0,2,1:T(4,128)(2,1)S(1)}, bf16[4,1,128,256]{3,0,2,1:T(4,128)(2,1)S(1)}, u32[]{:S(2)}, u32[]{:S(2)}) collective-permute-start(bf16[4,1,128,256]{3,0,2,1:T(4,128)(2,1)S(1)} %copy.64), channel_id=1, source_target_pairs={{8,0},{16,8},{24,16},{32,24},{40,32},{48,40},{56,48},{64,56},{72,6... | collective-permute-start | bytes 786440 | tf_op jit(solution)/shard_map/ppermute | solution.py:22
  15.9 1.5 copy-start.10
  17.5 12.2 %collective-permute-start.2 = (bf16[4,10,1,256]{3,0,2,1:T(4,128)(2,1)S(1)}, bf16[4,10,1,256]{3,0,2,1:T(4,128)(2,1)S(1)}, u32[]{:S(2)}, u32[]{:S(2)}) collective-permute-start(bf16[4,10,1,256]{3,0,2,1:T(4,128)(2,1)S(1)} %get-tuple-element.16), channel_id=1, source_target_pairs={{0,1},{1,2},{2,3},{3,4},{4,5},{5,6},{6,7},{8,9},{9,10},{10,11},{11... | collective-permute-start | bytes 61448 | tf_op jit(solution)/shard_map/ppermute | solution.py:20
  22.2 7.5 %collective-permute-start.3 = (bf16[4,10,1,256]{3,0,2,1:T(4,128)(2,1)S(1)}, bf16[4,10,1,256]{3,0,2,1:T(4,128)(2,1)S(1)}, u32[]{:S(2)}, u32[]{:S(2)}) collective-permute-start(bf16[4,10,1,256]{3,0,2,1:T(4,128)(2,1)S(1)} %get-tuple-element.17), channel_id=1, source_target_pairs={{1,0},{2,1},{3,2},{4,3},{5,4},{6,5},{7,6},{9,8},{10,9},{11,10},{12... | collective-permute-start | bytes 61448 | tf_op jit(solution)/shard_map/ppermute | solution.py:22
  29.7 25.2 %copy-start.8 = (bf16[256,256]{1,0:T(8,128)(2,1)S(1)}, bf16[256,256]{1,0:T(8,128)(2,1)}, u32[]{:S(2)}) copy-start(bf16[256,256]{1,0:T(8,128)(2,1)} %param.20) | copy-start | bytes 393220
  42.3 12.6 %copy-start.2 = (f32[4,200,256]{2,1,0:T(8,128)S(1)}, f32[4,200,256]{2,1,0:T(8,128)}, u32[]{:S(2)}) copy-start(f32[4,200,256]{2,1,0:T(8,128)} %param.16) | copy-start | bytes 2457604
  44.0 25.1 %all-to-all-start = ((f32[128,1,1056]{2,1,0:T(1,128)}), f32[128,1,1056]{2,1,0:T(1,128)S(1)}, u32[]{:S(2)}, u32[]{:S(2)}) async-start(f32[128,1,1056]{2,1,0:T(1,128)} %broadcast_in_dim.72), calls=%async_computation | async-start | bytes 1179648 | tf_op jit(solution)/shard_map/all_to_all | solution.py:205
  55.2 14.8 %copy-start.11 = (f32[256]{0:T(256)S(1)}, f32[256]{0:T(256)}, u32[]{:S(2)}) copy-start(f32[256]{0:T(256)} %param.19) | copy-start | bytes 3076
  55.2 14.8 %copy-start.12 = (f32[256]{0:T(256)S(1)}, f32[256]{0:T(256)}, u32[]{:S(2)}) copy-start(f32[256]{0:T(256)} %param.18) | copy-start | bytes 3076
  70.0 3.2 %copy-start.4 = (bf16[256,256]{1,0:T(8,128)(2,1)S(1)}, bf16[256,256]{1,0:T(8,128)(2,1)}, u32[]{:S(2)}) copy-start(bf16[256,256]{1,0:T(8,128)(2,1)} %param.22) | copy-start | bytes 393220
  73.2 2.0 %copy-start.5 = (bf16[256,256]{1,0:T(8,128)(2,1)S(1)}, bf16[256,256]{1,0:T(8,128)(2,1)}, u32[]{:S(2)}) copy-start(bf16[256,256]{1,0:T(8,128)(2,1)} %param.21) | copy-start | bytes 393220
  141.9 31.3 %copy-start.6 = (bf16[256,256]{1,0:T(8,128)(2,1)S(1)}, bf16[256,256]{1,0:T(8,128)(2,1)}, u32[]{:S(2)}) copy-start(bf16[256,256]{1,0:T(8,128)(2,1)} %param.23) | copy-start | bytes 393220
  166.5 8.9 %copy-start.13 = (f32[256]{0:T(256)S(1)}, f32[256]{0:T(256)}, u32[]{:S(2)}) copy-start(f32[256]{0:T(256)} %param.25) | copy-start | bytes 3076
  166.5 8.9 %copy-start.14 = (f32[256]{0:T(256)S(1)}, f32[256]{0:T(256)}, u32[]{:S(2)}) copy-start(f32[256]{0:T(256)} %param.24) | copy-start | bytes 3076
  173.2 3.3 %copy-start.9 = (bf16[256,256]{1,0:T(8,128)(2,1)S(1)}, bf16[256,256]{1,0:T(8,128)(2,1)}, u32[]{:S(2)}) copy-start(bf16[256,256]{1,0:T(8,128)(2,1)} %param.26) | copy-start | bytes 393220
  173.3 4.4 %copy-start.7 = (bf16[256,256]{1,0:T(8,128)(2,1)S(1)}, bf16[256,256]{1,0:T(8,128)(2,1)}, u32[]{:S(2)}) copy-start(bf16[256,256]{1,0:T(8,128)(2,1)} %param.27) | copy-start | bytes 393220
  175.7 0.9 copy-start.3

commit v6 on v5

--- a/solution.py
+++ b/solution.py
@@ -2,6 +2,7 @@
 import jax.numpy as jnp
 from jax import lax
 from jax.experimental import pallas as pl
+from jax.experimental.pallas import tpu as pltpu
 from jax.sharding import PartitionSpec as P
 
 HEADS = 8
@@ -164,6 +165,34 @@
             jax.ShapeDtypeStruct((images, queries, width), jnp.float32),
         ],
     )(qbd, keys, vals, fg, zero)
+
+
+def logits_kernel(e_ref, f_ref, o_ref, acc_ref):
+    queries = e_ref.shape[1]
+    tile_cols = o_ref.shape[2]
+    tile_rows = o_ref.shape[1] // queries
+    e = e_ref[0]
+    for r in range(tile_rows):
+        f = f_ref[0, r * tile_cols : (r + 1) * tile_cols, :]
+        res = lax.dot_general(e, f, (((1,), (1,)), ((), ())), preferred_element_type=jnp.float32)
+        acc_ref[pl.ds(r, queries, stride=tile_rows), :] = res
+    o_ref[0] = acc_ref[...].astype(o_ref.dtype)
+
+
+def logits_of(embed, mask_feat, tile_rows, tile_cols):
+    images, queries, width = embed.shape
+    pixels = mask_feat.shape[1]
+    return pl.pallas_call(
+        logits_kernel,
+        grid=(images,),
+        in_specs=[
+            pl.BlockSpec((1, queries, width), lambda i: (i, 0, 0)),
+            pl.BlockSpec((1, pixels, width), lambda i: (i, 0, 0)),
+        ],
+        out_specs=pl.BlockSpec((1, queries * tile_rows, tile_cols), lambda i: (i, 0, 0)),
+        out_shape=jax.ShapeDtypeStruct((images, queries * tile_rows, tile_cols), jnp.bfloat16),
+        scratch_shapes=[pltpu.VMEM((queries * tile_rows, tile_cols), jnp.float32)],
+    )(embed, mask_feat)
 
 
 def on_device(
@@ -256,9 +285,7 @@
         jnp.dot(updated.astype(jnp.bfloat16), embed_one, preferred_element_type=jnp.float32)
     ).astype(jnp.bfloat16)
     embed = jnp.dot(hidden, embed_two, preferred_element_type=jnp.float32).astype(jnp.bfloat16)
-    logits = jnp.einsum(
-        "bqc,bpc->bqp", embed, mask_feat, preferred_element_type=jnp.float32
-    ).astype(jnp.bfloat16)
+    logits = logits_of(embed, mask_feat, tile_rows, tile_cols)
     return (updated, logits.reshape(images, query_count, tile_rows, tile_cols))
 
 

time: 185 us -> 160 us (0.86)
  local copies, waits for them, and re-layouts: 34.9 us -> 22.2 us
  other arithmetic: 20.7 us -> 14.4 us
  waiting for transfers between devices: 17.5 us -> 12.5 us
  Pallas kernels: 23 us -> 27.6 us
  matrix products: 22.7 us -> 18.6 us
    unnamed x37 -> x40, local copies, waits for them, and re-layouts: 14 us -> 5.8 us
    pallas_call x0 -> x1, Pallas kernels: none -> 4.56 us  [logits_of(): pl.pallas_call(logits_kernel, grid=(images,), in_specs=[pl.BlockSpec((1,...]
    all_to_all x1, waiting for transfers between devices: 11.5 us -> 8.4 us  [on_device(): lax.all_to_all(jnp.broadcast_to(stats, (devices, stats.shape[1])), ('rows...]
    all_to_all x2, local copies, waits for them, and re-layouts: 5.19 us -> 2.21 us  [on_device(): parts = lax.all_to_all(packed, ('rows', 'cols'), 0, 0, tiled=True)]
    dot_general x2 -> x1, matrix products: 4.13 us -> 1.25 us  [on_device(): jnp.dot(hidden, embed_two, preferred_element_type=jnp.float32)]
    conv_general_dilated x0 -> x1, local copies, waits for them, and re-layouts: none -> 2.68 us  [on_device(): lax.conv_general_dilated(padded, conv_weight, (1, 1), 'VALID', dimension_...]
    concatenate x1, local copies, waits for them, and re-layouts: 2.18 us -> 0.12 us  [on_device(): jnp.concatenate([weighted.reshape(devices, span), total.reshape(devices,...]
    ppermute x2, waiting for transfers between devices: 2.54 us -> 0.66 us  [with_halo(): lax.ppermute(head, axis, [((i + 1) % count, i) for i in range(ends)])]
  transfers between devices with their start and end apart: 5 -> 5, of which waited for: 3 -> 3; matrix products, arithmetic and copies ran while one was open for 3% -> 7% of each run, Pallas kernels for 2% -> 3%
where the time goes in v6:
time: 160 us; the launch traced here: 159 us
  blocking collectives  39.5 us (25%)
  Pallas kernels  27.6 us (17%)
  starting transfers between devices  23.2 us (14%)
  local copies, waits for them, and re-layouts  22.2 us (14%)
  matrix products  18.6 us (12%)
  other arithmetic  14.4 us (9%)
  waiting for transfers between devices  12.5 us (8%)
    all_to_all x1, blocking collectives, on_device(): parts = lax.all_to_all(packed, ('rows', 'cols'), 0, 0, tiled=True)  22.2 us
    pallas_call x1, Pallas kernels, attention(): pl.pallas_call(kernel, grid=(images,), in_specs=[pl.BlockSpec((1, heads *...  18.7 us
    all_to_all x1, blocking collectives, on_device(): lax.all_to_all(jnp.broadcast_to(attn_block, (devices, span)), ('rows', 'c...  17.3 us
    conv_general_dilated x1, matrix products, on_device(): lax.conv_general_dilated(padded, conv_weight, (1, 1), 'VALID', dimension_...  12.6 us
    all_to_all x1, starting transfers between devices, on_device(): lax.all_to_all(jnp.broadcast_to(stats, (devices, stats.shape[1])), ('rows...  10.9 us
    ppermute x2, starting transfers between devices, with_halo(): lax.ppermute(tail, axis, [(i, (i + 1) % count) for i in range(ends)])  9.11 us
    all_to_all x1, waiting for transfers between devices, on_device(): lax.all_to_all(jnp.broadcast_to(stats, (devices, stats.shape[1])), ('rows...  8.4 us
    unnamed x40, local copies, waits for them, and re-layouts  5.8 us
  transfers between devices with their start and end apart: 5, of which 3 were waited for; matrix products, arithmetic and copies ran while one was open for 7% of the time, Pallas kernels for 3%

profile of v6, /device:TPU:1, one launch (start us, length us, event | category | flops | bytes accessed | tf_op | source)
XLA Modules:
  0.0 159.0 jit_solution(2009840308545414349)
XLA Ops:
  0.7 1.2 fusion.32
  2.1 4.4 %collective-permute-start = (bf16[4,1,128,256]{3,0,2,1:T(4,128)(2,1)S(1)}, bf16[4,1,128,256]{3,0,2,1:T(4,128)(2,1)S(1)}, u32[]{:S(2)}, u32[]{:S(2)}) collective-permute-start(bf16[4,1,128,256]{3,0,2,1:T(4,128)(2,1)S(1)} %copy.51), channel_id=1, source_target_pairs={{0,8},{8,16},{16,24},{24,32},{32,40},{40,48},{48,56},{56,64},{64,7... | collective-permute-start | bytes 786440 | tf_op jit(solution)/shard_map/ppermute | solution.py:21
  6.5 0.2 copy.52
  6.7 1.3 collective-permute-start.1
  8.0 3.4 %collective-permute-done = bf16[4,1,128,256]{3,0,2,1:T(4,128)(2,1)S(1)} collective-permute-done((bf16[4,1,128,256]{3,0,2,1:T(4,128)(2,1)S(1)}, bf16[4,1,128,256]{3,0,2,1:T(4,128)(2,1)S(1)}, u32[]{:S(2)}, u32[]{:S(2)}) %collective-permute-start) | collective-permute-done | bytes 262176 | tf_op jit(solution)/shard_map/ppermute | solution.py:21
  11.4 0.8 constant_dynamic-update-slice_fusion.2
  12.2 3.0 %constant_dynamic-update-slice_fusion.1 = bf16[4,10,128,256]{3,0,2,1:T(4,128)(2,1)} fusion(bf16[4,10,128,256]{3,0,2,1:T(4,128)(2,1)} %constant_dynamic-update-slice_fusion.2, bf16[4,8,128,256]{3,2,1,0:T(8,128)(2,1)S(1)} %copy-done.4), kind=kLoop, calls=%fused_computation.39 | loop fusion | bytes 4194304
  15.2 0.7 collective-permute-done.1
  15.8 0.8 constant_dynamic-update-slice_fusion
  16.6 0.8 fusion.31
  17.4 4.7 %collective-permute-start.2 = (bf16[4,10,1,256]{3,0,2,1:T(4,128)(2,1)S(1)}, bf16[4,10,1,256]{3,0,2,1:T(4,128)(2,1)S(1)}, u32[]{:S(2)}, u32[]{:S(2)}) collective-permute-start(bf16[4,10,1,256]{3,0,2,1:T(4,128)(2,1)S(1)} %get-tuple-element.16), channel_id=1, source_target_pairs={{0,1},{1,2},{2,3},{3,4},{4,5},{5,6},{6,7},{8,9},{9,10},{10,11},{11... | collective-permute-start | bytes 61448 | tf_op jit(solution)/shard_map/ppermute | solution.py:21
  22.1 1.9 %collective-permute-start.3 = (bf16[4,10,1,256]{3,0,2,1:T(4,128)(2,1)S(1)}, bf16[4,10,1,256]{3,0,2,1:T(4,128)(2,1)S(1)}, u32[]{:S(2)}, u32[]{:S(2)}) collective-permute-start(bf16[4,10,1,256]{3,0,2,1:T(4,128)(2,1)S(1)} %get-tuple-element.17), channel_id=1, source_target_pairs={{1,0},{2,1},{3,2},{4,3},{5,4},{6,5},{7,6},{9,8},{10,9},{11,10},{12... | collective-permute-start | bytes 61448 | tf_op jit(solution)/shard_map/ppermute | solution.py:23
  24.1 4.3 %shard_map.149 = (bf16[4,200,1024]{2,1,0:T(8,128)(2,1)}, f32[4,200,1]{2,1,0:T(8,128)}) custom-call(s32[4,1600,128]{2,1,0:T(8,128)} %bitcast.51), custom_call_target="tpu_custom_call" | custom-call | tf_op jit(solution)/shard_map/pallas_call | solution.py:105
  28.4 1.2 reduce.5
  29.7 12.6 %fusion.30 = (f32[4,256]{1,0:T(4,128)S(1)}, f32[4,256]{1,0:T(4,128)S(1)}, f32[4,8,128,256]{3,0,2,1:T(4,128)}) fusion(bf16[3,3,256,256]{3,2,1,0:T(8,128)(2,1)S(1)} %copy-done, bf16[4,10,1,256]{3,0,2,1:T(4,128)(2,1)S(1)} %collective-permute-done.3, bf16[4,10,128,256]{3,0,2,1:T(4,128)(2,1)} %constant_dynamic-update-slice_fusion, ...), kind=kOutput, calls=%fused_computation.59 | convolution fusion | flops 4842969088 | bytes 8044544 | tf_op jit(solution)/shard_map/conv_general_dilated | solution.py:222
  42.8 1.1 broadcast_in_dim.72
  43.9 10.9 %all-to-all-start = ((f32[128,1,1056]{2,1,0:T(1,128)}), f32[128,1,1056]{2,1,0:T(1,128)S(1)}, u32[]{:S(2)}, u32[]{:S(2)}) async-start(f32[128,1,1056]{2,1,0:T(1,128)} %broadcast_in_dim.72), calls=%async_computation | async-start | bytes 1179648 | tf_op jit(solution)/shard_map/all_to_all | solution.py:234
  54.8 0.3 convolution_convert_fusion.3
  55.2 2.2 %bitcast_select_fusion.refs_0_ = bf16[4,1600,256]{2,1,0:T(8,128)(2,1)} fusion(pred[1600,256]{1,0:T(8,128)(4,1)S(1)} %bitcast.54, bf16[4,200,256]{2,1,0:T(8,128)(2,1)S(1)} %convolution_convert_fusion.3), kind=kLoop, calls=%fused_computation.7 | loop fusion | flops 1638400 | bytes 4096000 | tf_op jit(solution)/shard_map/jit(_where)/select_n | solution.py:255
  57.4 0.5 copy-done.2
  57.9 2.7 %copy.44 = f32[4,8,128,256]{3,2,1,0:T(8,128)} copy(f32[4,8,128,256]{3,0,2,1:T(4,128)S(1)} %copy-done.2) | data formatting | bytes 8388608 | tf_op jit(solution)/shard_map/conv_general_dilated | solution.py:222
  60.6 8.4 %all-to-all-done = f32[128,1,1056]{2,1,0:T(1,128)S(1)} async-done(((f32[128,1,1056]{2,1,0:T(1,128)}), f32[128,1,1056]{2,1,0:T(1,128)S(1)}, u32[]{:S(2)}, u32[]{:S(2)}) %all-to-all-start) | async-done | bytes 540704 | tf_op jit(solution)/shard_map/all_to_all | solution.py:234
  68.9 0.4 reduce_sum.83
  69.9 3.0 %fusion.4.f_ref = bf16[4,1024,256]{2,1,0:T(8,128)(2,1)S(1)} fusion(f32[4,8,128,256]{3,2,1,0:T(8,128)} %copy.44, f32[256]{0:T(256)S(1)} %copy-done.13, f32[256]{0:T(256)S(1)} %copy-done.14, f32[4,256]{1,0:T(4,128)S(1)} %div.54, f32[4,256]{1,0:T(4,128)S(1)} %sub.44), kind=kLoop, calls=%fused_computation.6 | loop fusion | flops 6291456 | bytes 6301696 | tf_op jit(solution)/shard_map/convert_element_type | solution.py:245
  72.9 2.1 %convolution_convert_fusion.refs_2_ = bf16[4,1024,256]{2,1,0:T(8,128)(2,1)} fusion(bf16[4,1024,256]{2,1,0:T(8,128)(2,1)S(1)} %fusion.4.f_ref, bf16[256,256]{1,0:T(8,128)(2,1)S(1)} %copy-done.7), kind=kOutput, calls=%fused_computation.14 | convolution fusion | flops 537919488 | bytes 4325376 | tf_op jit(solution)/shard_map/dot_general | solution.py:249
  75.0 2.0 %convolution_convert_fusion.1.refs_1_ = bf16[4,1024,256]{2,1,0:T(8,128)(2,1)} fusion(bf16[4,1024,256]{2,1,0:T(8,128)(2,1)S(1)} %fusion.4.f_ref, bf16[256,256]{1,0:T(8,128)(2,1)S(1)} %copy-done.8), kind=kOutput, calls=%fused_computation.15 | convolution fusion | flops 537919488 | bytes 4325376 | tf_op jit(solution)/shard_map/dot_general | solution.py:248
  77.0 1.0 copy.46.refs_4_
  78.0 18.7 %shard_map.150 = (f32[4,200,8]{2,1,0:T(8,128)}, f32[4,200,8]{2,1,0:T(8,128)}, f32[4,200,256]{2,1,0:T(8,128)}) custom-call(bf16[4,1600,256]{2,1,0:T(8,128)(2,1)} %bitcast_select_fusion.refs_0_, bf16[4,1024,256]{2,1,0:T(8,128)(2,1)} %convolution_convert_fusion.1.refs_1_, bf16[4,1024,256]{2,1,0:T(8,128)(2,1)} %convolution_convert_fusion.refs_2_, ...), custom_call_target="tpu_custom_call" | custom-call | tf_op jit(solution)/shard_map/pallas_call | solution.py:147
  96.7 1.6 reshape.136
  98.2 1.2 reshape.137
  99.4 1.2 reshape.138
  100.7 0.9 copy.47
  101.7 22.2 %all_to_all.24 = f32[128,1,1700]{2,1,0:T(1,128)S(1)} all-to-all(f32[128,1,1700]{2,1,0:T(1,128)S(1)} %copy.47), channel_id=1, replica_groups=mesh['rows'=16,'cols'=8] {'rows','cols'}, dimensions={0} | all-to-all | bytes 1740800 | tf_op jit(solution)/shard_map/all_to_all | solution.py:270
  123.9 1.3 copy.48
  125.5 0.3 fusion.12
  126.0 0.5 broadcast_in_dim.78
  126.5 0.5 broadcast.108
  127.0 3.3 %reduce.7 = bf16[128,1600]{1,0:T(8,128)(2,1)S(1)} reduce(bf16[128,1,1600]{2,1,0:T(2,128)(2,1)S(1)} %broadcast_in_dim.78, bf16[]{:T(256)} %broadcast.108), dimensions={1}, to_apply=%broadcast_in_dim.78.reduce_sub_computation | reduce | bytes 819202 | tf_op jit(solution)/shard_map/broadcast_in_dim | solution.py:278
  130.3 0.5 reshape.151
  130.8 17.3 %all_to_all.25 = bf16[128,2,800]{2,1,0:T(2,128)(2,1)S(1)} all-to-all(bf16[128,2,800]{2,1,0:T(2,128)(2,1)S(1)} %reshape.151), channel_id=1, replica_groups=mesh['rows'=16,'cols'=8] {'rows','cols'}, dimensions={0} | all-to-all | bytes 819200 | tf_op jit(solution)/shard_map/all_to_all | solution.py:277
  148.1 0.6 reshape.152
  148.7 2.7 %reduce.6 = bf16[128,1600]{1,0:T(8,128)(2,1)S(1)} reduce(bf16[128,1,1600]{2,1,0:T(2,128)(2,1)S(1)} %reshape.152, bf16[]{:T(256)} %constant.43), dimensions={1}, to_apply=%all_to_all.20.reduce_sub_computation | reduce | bytes 819202 | tf_op jit(solution)/shard_map/all_to_all | solution.py:277
  151.4 0.6 reshape.140
  152.1 0.4 fusion.33
  152.5 0.4 multiply_reduce_fusion.1
  152.9 0.3 multiply_add_fusion
  153.2 1.3 convolution_convert_fusion.2.e_ref
  154.5 4.6 %shard_map.151 = bf16[4,1600,128]{2,1,0:T(8,128)(2,1)} custom-call(bf16[4,200,256]{2,1,0:T(8,128)(2,1)} %convolution_convert_fusion.2.e_ref, bf16[4,1024,256]{2,1,0:T(8,128)(2,1)} %copy-done.1), custom_call_target="tpu_custom_call" | custom-call | tf_op jit(solution)/shard_map/pallas_call | solution.py:185
  (61 shorter events, 2.1 us)
Async XLA Ops:
  0.6 29.0 %copy-start = (bf16[3,3,256,256]{3,2,1,0:T(8,128)(2,1)S(1)}, bf16[3,3,256,256]{3,2,1,0:T(8,128)(2,1)}, u32[]{:S(2)}) copy-start(bf16[3,3,256,256]{3,2,1,0:T(8,128)(2,1)} %param.17) | copy-start | bytes 3538948
  0.6 11.6 %copy-start.4 = (bf16[4,8,128,256]{3,2,1,0:T(8,128)(2,1)S(1)}, bf16[4,8,128,256]{3,2,1,0:T(8,128)(2,1)}, u32[]{:S(2)}) copy-start(bf16[4,8,128,256]{3,2,1,0:T(8,128)(2,1)} %param.14) | copy-start | bytes 6291460
  2.1 9.3 %collective-permute-start = (bf16[4,1,128,256]{3,0,2,1:T(4,128)(2,1)S(1)}, bf16[4,1,128,256]{3,0,2,1:T(4,128)(2,1)S(1)}, u32[]{:S(2)}, u32[]{:S(2)}) collective-permute-start(bf16[4,1,128,256]{3,0,2,1:T(4,128)(2,1)S(1)} %copy.51), channel_id=1, source_target_pairs={{0,8},{8,16},{16,24},{24,32},{32,40},{40,48},{48,56},{56,64},{64,7... | collective-permute-start | bytes 786440 | tf_op jit(solution)/shard_map/ppermute | solution.py:21
  6.7 9.1 %collective-permute-start.1 = (bf16[4,1,128,256]{3,0,2,1:T(4,128)(2,1)S(1)}, bf16[4,1,128,256]{3,0,2,1:T(4,128)(2,1)S(1)}, u32[]{:S(2)}, u32[]{:S(2)}) collective-permute-start(bf16[4,1,128,256]{3,0,2,1:T(4,128)(2,1)S(1)} %copy.52), channel_id=1, source_target_pairs={{8,0},{16,8},{24,16},{32,24},{40,32},{48,40},{56,48},{64,56},{72,6... | collective-permute-start | bytes 786440 | tf_op jit(solution)/shard_map/ppermute | solution.py:23
  17.4 12.2 %collective-permute-start.2 = (bf16[4,10,1,256]{3,0,2,1:T(4,128)(2,1)S(1)}, bf16[4,10,1,256]{3,0,2,1:T(4,128)(2,1)S(1)}, u32[]{:S(2)}, u32[]{:S(2)}) collective-permute-start(bf16[4,10,1,256]{3,0,2,1:T(4,128)(2,1)S(1)} %get-tuple-element.16), channel_id=1, source_target_pairs={{0,1},{1,2},{2,3},{3,4},{4,5},{5,6},{6,7},{8,9},{9,10},{10,11},{11... | collective-permute-start | bytes 61448 | tf_op jit(solution)/shard_map/ppermute | solution.py:21
  22.1 7.5 %collective-permute-start.3 = (bf16[4,10,1,256]{3,0,2,1:T(4,128)(2,1)S(1)}, bf16[4,10,1,256]{3,0,2,1:T(4,128)(2,1)S(1)}, u32[]{:S(2)}, u32[]{:S(2)}) collective-permute-start(bf16[4,10,1,256]{3,0,2,1:T(4,128)(2,1)S(1)} %get-tuple-element.17), channel_id=1, source_target_pairs={{1,0},{2,1},{3,2},{4,3},{5,4},{6,5},{7,6},{9,8},{10,9},{11,10},{12... | collective-permute-start | bytes 61448 | tf_op jit(solution)/shard_map/ppermute | solution.py:23
  29.6 25.2 %copy-start.12 = (bf16[256,256]{1,0:T(8,128)(2,1)S(1)}, bf16[256,256]{1,0:T(8,128)(2,1)}, u32[]{:S(2)}) copy-start(bf16[256,256]{1,0:T(8,128)(2,1)} %param.20) | copy-start | bytes 393220
  42.2 12.6 %copy-start.5 = (f32[4,200,256]{2,1,0:T(8,128)S(1)}, f32[4,200,256]{2,1,0:T(8,128)}, u32[]{:S(2)}) copy-start(f32[4,200,256]{2,1,0:T(8,128)} %param.16) | copy-start | bytes 2457604
  43.9 25.1 %all-to-all-start = ((f32[128,1,1056]{2,1,0:T(1,128)}), f32[128,1,1056]{2,1,0:T(1,128)S(1)}, u32[]{:S(2)}, u32[]{:S(2)}) async-start(f32[128,1,1056]{2,1,0:T(1,128)} %broadcast_in_dim.72), calls=%async_computation | async-start | bytes 1179648 | tf_op jit(solution)/shard_map/all_to_all | solution.py:234
  54.8 3.1 %copy-start.2 = (f32[4,8,128,256]{3,0,2,1:T(4,128)S(1)}, f32[4,8,128,256]{3,0,2,1:T(4,128)}, u32[]{:S(2)}) copy-start(f32[4,8,128,256]{3,0,2,1:T(4,128)} %get-tuple-element.22) | copy-start | bytes 12582916
  57.9 12.0 %copy-start.13 = (f32[256]{0:T(256)S(1)}, f32[256]{0:T(256)}, u32[]{:S(2)}) copy-start(f32[256]{0:T(256)} %param.19) | copy-start | bytes 3076
  57.9 12.0 %copy-start.14 = (f32[256]{0:T(256)S(1)}, f32[256]{0:T(256)}, u32[]{:S(2)}) copy-start(f32[256]{0:T(256)} %param.18) | copy-start | bytes 3076
  69.9 3.0 %copy-start.7 = (bf16[256,256]{1,0:T(8,128)(2,1)S(1)}, bf16[256,256]{1,0:T(8,128)(2,1)}, u32[]{:S(2)}) copy-start(bf16[256,256]{1,0:T(8,128)(2,1)} %param.22) | copy-start | bytes 393220
  72.9 4.1 %copy-start.1 = (bf16[4,1024,256]{2,1,0:T(8,128)(2,1)}, bf16[4,1024,256]{2,1,0:T(8,128)(2,1)S(1)}, u32[]{:S(2)}) copy-start(bf16[4,1024,256]{2,1,0:T(8,128)(2,1)S(1)} %fusion.4.f_ref) | copy-start | bytes 6291460
  72.9 2.1 %copy-start.8 = (bf16[256,256]{1,0:T(8,128)(2,1)S(1)}, bf16[256,256]{1,0:T(8,128)(2,1)}, u32[]{:S(2)}) copy-start(bf16[256,256]{1,0:T(8,128)(2,1)} %param.21) | copy-start | bytes 393220
  130.3 21.7 %copy-start.6 = (f32[4,200,256]{2,1,0:T(8,128)S(1)}, f32[4,200,256]{2,1,0:T(8,128)}, u32[]{:S(2)}) copy-start(f32[4,200,256]{2,1,0:T(8,128)} %param.16) | copy-start | bytes 2457604
  130.3 21.7 %copy-start.9 = (bf16[256,256]{1,0:T(8,128)(2,1)S(1)}, bf16[256,256]{1,0:T(8,128)(2,1)}, u32[]{:S(2)}) copy-start(bf16[256,256]{1,0:T(8,128)(2,1)} %param.23) | copy-start | bytes 393220
  148.7 4.2 %copy-start.15 = (f32[256]{0:T(256)S(1)}, f32[256]{0:T(256)}, u32[]{:S(2)}) copy-start(f32[256]{0:T(256)} %param.25) | copy-start | bytes 3076
  148.7 4.2 %copy-start.16 = (f32[256]{0:T(256)S(1)}, f32[256]{0:T(256)}, u32[]{:S(2)}) copy-start(f32[256]{0:T(256)} %param.24) | copy-start | bytes 3076
  152.0 1.2 copy-start.10
  152.1 1.2 copy-start.11
  153.2 5.8 %copy-start.3 = (f32[4,200,256]{2,1,0:T(8,128)}, f32[4,200,256]{2,1,0:T(8,128)S(1)}, u32[]{:S(2)}) copy-start(f32[4,200,256]{2,1,0:T(8,128)S(1)} %multiply_add_fusion) | copy-start | bytes 2457604

commit v7 on v6

--- a/solution.py
+++ b/solution.py
@@ -193,6 +193,49 @@
         out_shape=jax.ShapeDtypeStruct((images, queries * tile_rows, tile_cols), jnp.bfloat16),
         scratch_shapes=[pltpu.VMEM((queries * tile_rows, tile_cols), jnp.float32)],
     )(embed, mask_feat)
+
+
+def conv_with_halo(features, weight):
+    images, tile_rows, tile_cols, width = features.shape
+    dims = ("NHWC", "HWIO", "NHWC")
+    conv = lambda x, w, pad: lax.conv_general_dilated(
+        x, w, (1, 1), pad, dimension_numbers=dims, preferred_element_type=jnp.float32
+    )
+    main = conv(features, weight, ((1, 1), (1, 1)))
+    rows = lax.axis_size("rows")
+    cols = lax.axis_size("cols")
+    down = [(i, i + 1) for i in range(rows - 1)]
+    up = [(i + 1, i) for i in range(rows - 1)]
+    rightward = [(i, i + 1) for i in range(cols - 1)]
+    leftward = [(i + 1, i) for i in range(cols - 1)]
+    above = lax.ppermute(features[:, -1:], "rows", down)
+    below = lax.ppermute(features[:, :1], "rows", up)
+    left = lax.ppermute(features[:, :, -1:], "cols", rightward)
+    right = lax.ppermute(features[:, :, :1], "cols", leftward)
+    edges = jnp.concatenate([above, below], axis=1)
+    west = lax.ppermute(edges[:, :, -1:], "cols", rightward)
+    east = lax.ppermute(edges[:, :, :1], "cols", leftward)
+    above = jnp.concatenate([west[:, :1], above, east[:, :1]], axis=2)
+    below = jnp.concatenate([west[:, 1:], below, east[:, 1:]], axis=2)
+    valid = ((0, 0), (0, 0))
+    column = ((1, 1), (0, 0))
+    row_terms = jnp.concatenate(
+        [
+            conv(above, weight[0:1], valid),
+            jnp.zeros((images, tile_rows - 2, tile_cols, width), jnp.float32),
+            conv(below, weight[2:3], valid),
+        ],
+        axis=1,
+    )
+    col_terms = jnp.concatenate(
+        [
+            conv(left, weight[:, 0:1], column),
+            jnp.zeros((images, tile_rows, tile_cols - 2, width), jnp.float32),
+            conv(right, weight[:, 2:3], column),
+        ],
+        axis=2,
+    )
+    return main + row_terms + col_terms
 
 
 def on_device(
@@ -218,15 +261,7 @@
     pixels = tile_rows * tile_cols
     devices = lax.axis_size("rows") * lax.axis_size("cols")
     fg, local_count = prep(masks)
-    padded = with_halo(features, (("rows", 1), ("cols", 2)), 1)
-    conv = lax.conv_general_dilated(
-        padded,
-        conv_weight,
-        (1, 1),
-        "VALID",
-        dimension_numbers=("NHWC", "HWIO", "NHWC"),
-        preferred_element_type=jnp.float32,
-    )
+    conv = conv_with_halo(features, conv_weight)
     grouped = conv.reshape(images, pixels, GROUPS, width // GROUPS)
     first_sum = jnp.sum(grouped, axis=(1, 3))
     second_sum = jnp.sum(grouped * grouped, axis=(1, 3))

time: 160 us -> 161 us (level)
  local copies, waits for them, and re-layouts: 22.2 us -> 18.1 us
  starting transfers between devices: 23.2 us -> 26.8 us
  matrix products: 18.6 us -> 21 us
    ppermute x4 -> x6, starting transfers between devices: 12.3 us -> 16.9 us  [the longest x1 4.38 us: conv_with_halo(): above = lax.ppermute(features[:, -1:], 'rows', down)]
    unnamed x40 -> x39, local copies, waits for them, and re-layouts: 5.8 us -> 2.01 us
    add x0 -> x1, local copies, waits for them, and re-layouts: none -> 2.68 us  [conv_with_halo(): return main + row_terms + col_terms]
    conv_general_dilated x1 -> x0, local copies, waits for them, and re-layouts: 2.68 us -> none  [on_device(): lax.conv_general_dilated(padded, conv_weight, (1, 1), 'VALID', dimension_...]
    conv_general_dilated x1 -> x5, matrix products: 12.6 us -> 15 us  [conv_with_halo(): lax.conv_general_dilated(x, w, (1, 1), pad, dimension_numbers=dims, prefe...]
    ppermute x4 -> x6, waiting for transfers between devices: 4.1 us -> 2.99 us  [the longest x1 2.97 us: conv_with_halo(): east = lax.ppermute(edges[:, :, :1], 'cols', leftward)]
  transfers between devices with their start and end apart: 5 -> 7, of which waited for: 3 -> 2; matrix products, arithmetic and copies ran while one was open for 7% -> 5% of each run, Pallas kernels for 3% -> 3%
where the time goes in v7:
time: 161 us; the launch traced here: 160 us
  blocking collectives  39.5 us (25%)
  Pallas kernels  27.6 us (17%)
  starting transfers between devices  26.8 us (17%)
  matrix products  21 us (13%)
  local copies, waits for them, and re-layouts  18.1 us (11%)
  other arithmetic  14.4 us (9%)
  waiting for transfers between devices  11.5 us (7%)
    all_to_all x1, blocking collectives, on_device(): parts = lax.all_to_all(packed, ('rows', 'cols'), 0, 0, tiled=True)  22.2 us
    pallas_call x1, Pallas kernels, attention(): pl.pallas_call(kernel, grid=(images,), in_specs=[pl.BlockSpec((1, heads *...  18.7 us
    all_to_all x1, blocking collectives, on_device(): lax.all_to_all(jnp.broadcast_to(attn_block, (devices, span)), ('rows', 'c...  17.3 us
    conv_general_dilated x5, matrix products, conv_with_halo(): lax.conv_general_dilated(x, w, (1, 1), pad, dimension_numbers=dims, prefe...  15 us
    all_to_all x1, starting transfers between devices, on_device(): lax.all_to_all(jnp.broadcast_to(stats, (devices, stats.shape[1])), ('rows...  9.84 us
    all_to_all x1, waiting for transfers between devices, on_device(): lax.all_to_all(jnp.broadcast_to(stats, (devices, stats.shape[1])), ('rows...  8.56 us
    pallas_call x1, Pallas kernels, logits_of(): pl.pallas_call(logits_kernel, grid=(images,), in_specs=[pl.BlockSpec((1,...  4.56 us
    ppermute x1, starting transfers between devices, conv_with_halo(): above = lax.ppermute(features[:, -1:], 'rows', down)  4.38 us
  transfers between devices with their start and end apart: 7, of which 2 were waited for; matrix products, arithmetic and copies ran while one was open for 5% of the time, Pallas kernels for 3%

profile of v7, /device:TPU:1, one launch (start us, length us, event | category | flops | bytes accessed | tf_op | source)
XLA Modules:
  0.0 160.1 jit_solution(18127850201805153276)
XLA Ops:
  0.7 1.2 fusion.47
  1.8 0.2 copy.62
  2.0 4.4 %collective-permute-start = (bf16[4,1,128,256]{3,0,2,1:T(4,128)(2,1)S(1)}, bf16[4,1,128,256]{3,0,2,1:T(4,128)(2,1)S(1)}, u32[]{:S(2)}, u32[]{:S(2)}) collective-permute-start(bf16[4,1,128,256]{3,0,2,1:T(4,128)(2,1)S(1)} %copy.62), channel_id=1, source_target_pairs={{0,8},{8,16},{16,24},{24,32},{32,40},{40,48},{48,56},{56,64},{64,7... | collective-permute-start | bytes 786440 | tf_op jit(solution)/shard_map/ppermute | solution.py:211
  6.4 1.0 fusion.46
  7.5 2.9 %collective-permute-start.5 = (bf16[4,8,1,256]{3,0,2,1:T(4,128)(2,1)S(1)}, bf16[4,8,1,256]{3,0,2,1:T(4,128)(2,1)S(1)}, u32[]{:S(2)}, u32[]{:S(2)}) collective-permute-start(bf16[4,8,1,256]{3,0,2,1:T(4,128)(2,1)S(1)} %copy.64), channel_id=1, source_target_pairs={{1,0},{2,1},{3,2},{4,3},{5,4},{6,5},{7,6},{9,8},{10,9},{11,10},{12... | collective-permute-start | bytes 49160 | tf_op jit(solution)/shard_map/ppermute | solution.py:214
  10.6 1.3 collective-permute-start.1
  11.9 3.1 %collective-permute-start.4 = (bf16[4,8,1,256]{3,0,2,1:T(4,128)(2,1)S(1)}, bf16[4,8,1,256]{3,0,2,1:T(4,128)(2,1)S(1)}, u32[]{:S(2)}, u32[]{:S(2)}) collective-permute-start(bf16[4,8,1,256]{3,0,2,1:T(4,128)(2,1)S(1)} %copy.65), channel_id=1, source_target_pairs={{0,1},{1,2},{2,3},{3,4},{4,5},{5,6},{6,7},{8,9},{9,10},{10,11},{11... | collective-permute-start | bytes 49160 | tf_op jit(solution)/shard_map/ppermute | solution.py:213
  15.2 4.3 %shard_map.149 = (bf16[4,200,1024]{2,1,0:T(8,128)(2,1)}, f32[4,200,1]{2,1,0:T(8,128)}) custom-call(s32[4,1600,128]{2,1,0:T(8,128)} %bitcast.53), custom_call_target="tpu_custom_call" | custom-call | tf_op jit(solution)/shard_map/pallas_call | solution.py:105
  19.5 1.2 reduce.5
  21.2 3.4 %collective-permute-start.2 = (bf16[4,2,1,256]{3,0,2,1:T(4,128)(2,1)S(1)}, bf16[4,2,1,256]{3,0,2,1:T(4,128)(2,1)S(1)}, u32[]{:S(2)}, u32[]{:S(2)}) collective-permute-start(bf16[4,2,1,256]{3,0,2,1:T(4,128)(2,1)S(1)} %get-tuple-element.20), channel_id=1, source_target_pairs={{0,1},{1,2},{2,3},{3,4},{4,5},{5,6},{6,7},{8,9},{9,10},{10,11},{11... | collective-permute-start | bytes 12296 | tf_op jit(solution)/shard_map/ppermute | solution.py:216
  24.8 1.9 %collective-permute-start.3 = (bf16[4,2,1,256]{3,0,2,1:T(4,128)(2,1)S(1)}, bf16[4,2,1,256]{3,0,2,1:T(4,128)(2,1)S(1)}, u32[]{:S(2)}, u32[]{:S(2)}) collective-permute-start(bf16[4,2,1,256]{3,0,2,1:T(4,128)(2,1)S(1)} %get-tuple-element.21), channel_id=1, source_target_pairs={{1,0},{2,1},{3,2},{4,3},{5,4},{6,5},{7,6},{9,8},{10,9},{11,10},{12... | collective-permute-start | bytes 12296 | tf_op jit(solution)/shard_map/ppermute | solution.py:217
  26.7 3.0 %collective-permute-done.3 = bf16[4,2,1,256]{3,0,2,1:T(4,128)(2,1)S(1)} collective-permute-done((bf16[4,2,1,256]{3,0,2,1:T(4,128)(2,1)S(1)}, bf16[4,2,1,256]{3,0,2,1:T(4,128)(2,1)S(1)}, u32[]{:S(2)}, u32[]{:S(2)}) %collective-permute-start.3) | collective-permute-done | bytes 4128 | tf_op jit(solution)/shard_map/ppermute | solution.py:217
  29.7 0.5 fusion.18
  30.2 0.5 fusion.16
  30.8 13.6 %fusion.45 = (f32[4,256]{1,0:T(4,128)S(1)}, f32[4,256]{1,0:T(4,128)S(1)}, f32[4,8,128,256]{3,0,2,1:T(4,128)}) fusion(f32[4,8,1,256]{3,0,2,1:T(4,128)S(1)} %fusion.12, f32[128]{0:T(128)S(1)} %pad.4.clone, f32[4,8,1,256]{3,0,2,1:T(4,128)S(1)} %fusion.14, f32[4,1,128,256]{3,0,2,1:T(4,128)S(1)} %fusion.16, f32[8]{0:T(128)S(1)} %pad.7.clone, ...), kind=kOutput, calls=%fused_computation.74 | convolution fusion | flops 4415551488 | bytes 8593952 | tf_op jit(solution)/shard_map/conv_general_dilated | solution.py:201
  44.9 1.1 broadcast_in_dim.80
  46.1 9.8 %all-to-all-start = ((f32[128,1,1056]{2,1,0:T(1,128)}), f32[128,1,1056]{2,1,0:T(1,128)S(1)}, u32[]{:S(2)}, u32[]{:S(2)}) async-start(f32[128,1,1056]{2,1,0:T(1,128)} %broadcast_in_dim.80), calls=%async_computation | async-start | bytes 1179648 | tf_op jit(solution)/shard_map/all_to_all | solution.py:269
  56.0 0.3 convolution_convert_fusion.3
  56.3 2.2 %bitcast_select_fusion.refs_0_ = bf16[4,1600,256]{2,1,0:T(8,128)(2,1)} fusion(pred[1600,256]{1,0:T(8,128)(4,1)S(1)} %bitcast.56, bf16[4,200,256]{2,1,0:T(8,128)(2,1)S(1)} %convolution_convert_fusion.3), kind=kLoop, calls=%fused_computation.9 | loop fusion | flops 1638400 | bytes 4096000 | tf_op jit(solution)/shard_map/jit(_where)/select_n | solution.py:290
  58.6 0.3 copy-done.2
  58.9 2.7 %copy.54 = f32[4,8,128,256]{3,2,1,0:T(8,128)} copy(f32[4,8,128,256]{3,0,2,1:T(4,128)S(1)} %copy-done.2) | data formatting | bytes 8388608 | tf_op jit(solution)/shard_map/add | solution.py:238
  61.5 8.6 %all-to-all-done = f32[128,1,1056]{2,1,0:T(1,128)S(1)} async-done(((f32[128,1,1056]{2,1,0:T(1,128)}), f32[128,1,1056]{2,1,0:T(1,128)S(1)}, u32[]{:S(2)}, u32[]{:S(2)}) %all-to-all-start) | async-done | bytes 540704 | tf_op jit(solution)/shard_map/all_to_all | solution.py:269
  70.1 0.4 reduce_sum.83
  71.0 3.0 %fusion.5.f_ref = bf16[4,1024,256]{2,1,0:T(8,128)(2,1)S(1)} fusion(f32[4,8,128,256]{3,2,1,0:T(8,128)} %copy.54, f32[256]{0:T(256)S(1)} %copy-done.12, f32[256]{0:T(256)S(1)} %copy-done.13, f32[4,256]{1,0:T(4,128)S(1)} %div.54, f32[4,256]{1,0:T(4,128)S(1)} %sub.44), kind=kLoop, calls=%fused_computation.8 | loop fusion | flops 6291456 | bytes 6301696 | tf_op jit(solution)/shard_map/convert_element_type | solution.py:280
  74.0 2.1 %convolution_convert_fusion.refs_2_ = bf16[4,1024,256]{2,1,0:T(8,128)(2,1)} fusion(bf16[4,1024,256]{2,1,0:T(8,128)(2,1)S(1)} %fusion.5.f_ref, bf16[256,256]{1,0:T(8,128)(2,1)S(1)} %copy-done), kind=kOutput, calls=%fused_computation.10 | convolution fusion | flops 537919488 | bytes 4325376 | tf_op jit(solution)/shard_map/dot_general | solution.py:284
  76.1 2.0 %convolution_convert_fusion.1.refs_1_ = bf16[4,1024,256]{2,1,0:T(8,128)(2,1)} fusion(bf16[4,1024,256]{2,1,0:T(8,128)(2,1)S(1)} %fusion.5.f_ref, bf16[256,256]{1,0:T(8,128)(2,1)S(1)} %copy-done.7), kind=kOutput, calls=%fused_computation.11 | convolution fusion | flops 537919488 | bytes 4325376 | tf_op jit(solution)/shard_map/dot_general | solution.py:283
  78.1 1.0 copy.56.refs_4_
  79.1 18.7 %shard_map.150 = (f32[4,200,8]{2,1,0:T(8,128)}, f32[4,200,8]{2,1,0:T(8,128)}, f32[4,200,256]{2,1,0:T(8,128)}) custom-call(bf16[4,1600,256]{2,1,0:T(8,128)(2,1)} %bitcast_select_fusion.refs_0_, bf16[4,1024,256]{2,1,0:T(8,128)(2,1)} %convolution_convert_fusion.1.refs_1_, bf16[4,1024,256]{2,1,0:T(8,128)(2,1)} %convolution_convert_fusion.refs_2_, ...), custom_call_target="tpu_custom_call" | custom-call | tf_op jit(solution)/shard_map/pallas_call | solution.py:147
  97.8 1.6 reshape.136
  99.3 1.2 reshape.137
  100.5 1.2 reshape.138
  101.8 0.9 copy.57
  102.8 22.2 %all_to_all.24 = f32[128,1,1700]{2,1,0:T(1,128)S(1)} all-to-all(f32[128,1,1700]{2,1,0:T(1,128)S(1)} %copy.57), channel_id=1, replica_groups=mesh['rows'=16,'cols'=8] {'rows','cols'}, dimensions={0} | all-to-all | bytes 1740800 | tf_op jit(solution)/shard_map/all_to_all | solution.py:305
  125.0 1.3 copy.58
  126.6 0.3 fusion.7
  127.1 0.5 broadcast_in_dim.86
  127.6 0.5 broadcast.112
  128.1 3.3 %reduce.7 = bf16[128,1600]{1,0:T(8,128)(2,1)S(1)} reduce(bf16[128,1,1600]{2,1,0:T(2,128)(2,1)S(1)} %broadcast_in_dim.86, bf16[]{:T(256)} %broadcast.112), dimensions={1}, to_apply=%broadcast_in_dim.86.reduce_sub_computation | reduce | bytes 819202 | tf_op jit(solution)/shard_map/broadcast_in_dim | solution.py:313
  131.4 0.5 reshape.151
  131.9 17.3 %all_to_all.25 = bf16[128,2,800]{2,1,0:T(2,128)(2,1)S(1)} all-to-all(bf16[128,2,800]{2,1,0:T(2,128)(2,1)S(1)} %reshape.151), channel_id=1, replica_groups=mesh['rows'=16,'cols'=8] {'rows','cols'}, dimensions={0} | all-to-all | bytes 819200 | tf_op jit(solution)/shard_map/all_to_all | solution.py:312
  149.1 0.6 reshape.152
  149.8 2.7 %reduce.6 = bf16[128,1600]{1,0:T(8,128)(2,1)S(1)} reduce(bf16[128,1,1600]{2,1,0:T(2,128)(2,1)S(1)} %reshape.152, bf16[]{:T(256)} %constant.45), dimensions={1}, to_apply=%all_to_all.20.reduce_sub_computation | reduce | bytes 819202 | tf_op jit(solution)/shard_map/all_to_all | solution.py:312
  152.5 0.6 reshape.140
  153.1 0.4 fusion.51
  153.5 0.4 multiply_reduce_fusion.1
  154.0 0.3 multiply_add_fusion
  154.3 1.3 convolution_convert_fusion.2.e_ref
  155.5 4.6 %shard_map.151 = bf16[4,1600,128]{2,1,0:T(8,128)(2,1)} custom-call(bf16[4,200,256]{2,1,0:T(8,128)(2,1)} %convolution_convert_fusion.2.e_ref, bf16[4,1024,256]{2,1,0:T(8,128)(2,1)} %copy-done.1), custom_call_target="tpu_custom_call" | custom-call | tf_op jit(solution)/shard_map/pallas_call | solution.py:185
  (75 shorter events, 2.9 us)
Async XLA Ops:
  0.6 73.4 %copy-start = (bf16[256,256]{1,0:T(8,128)(2,1)S(1)}, bf16[256,256]{1,0:T(8,128)(2,1)}, u32[]{:S(2)}) copy-start(bf16[256,256]{1,0:T(8,128)(2,1)} %param.22) | copy-start | bytes 393220
  0.6 20.1 %copy-start.5 = (bf16[3,3,256,256]{3,2,1,0:T(8,128)(2,1)S(1)}, bf16[3,3,256,256]{3,2,1,0:T(8,128)(2,1)}, u32[]{:S(2)}) copy-start(bf16[3,3,256,256]{3,2,1,0:T(8,128)(2,1)} %param.17) | copy-start | bytes 3538948
  2.0 18.9 %collective-permute-start = (bf16[4,1,128,256]{3,0,2,1:T(4,128)(2,1)S(1)}, bf16[4,1,128,256]{3,0,2,1:T(4,128)(2,1)S(1)}, u32[]{:S(2)}, u32[]{:S(2)}) collective-permute-start(bf16[4,1,128,256]{3,0,2,1:T(4,128)(2,1)S(1)} %copy.62), channel_id=1, source_target_pairs={{0,8},{8,16},{16,24},{24,32},{32,40},{40,48},{48,56},{56,64},{64,7... | collective-permute-start | bytes 786440 | tf_op jit(solution)/shard_map/ppermute | solution.py:211
  7.5 13.2 %collective-permute-start.5 = (bf16[4,8,1,256]{3,0,2,1:T(4,128)(2,1)S(1)}, bf16[4,8,1,256]{3,0,2,1:T(4,128)(2,1)S(1)}, u32[]{:S(2)}, u32[]{:S(2)}) collective-permute-start(bf16[4,8,1,256]{3,0,2,1:T(4,128)(2,1)S(1)} %copy.64), channel_id=1, source_target_pairs={{1,0},{2,1},{3,2},{4,3},{5,4},{6,5},{7,6},{9,8},{10,9},{11,10},{12... | collective-permute-start | bytes 49160 | tf_op jit(solution)/shard_map/ppermute | solution.py:214
  10.6 10.5 %collective-permute-start.1 = (bf16[4,1,128,256]{3,0,2,1:T(4,128)(2,1)S(1)}, bf16[4,1,128,256]{3,0,2,1:T(4,128)(2,1)S(1)}, u32[]{:S(2)}, u32[]{:S(2)}) collective-permute-start(bf16[4,1,128,256]{3,0,2,1:T(4,128)(2,1)S(1)} %copy.63), channel_id=1, source_target_pairs={{8,0},{16,8},{24,16},{32,24},{40,32},{48,40},{56,48},{64,56},{72,6... | collective-permute-start | bytes 786440 | tf_op jit(solution)/shard_map/ppermute | solution.py:212
  11.9 12.7 %collective-permute-start.4 = (bf16[4,8,1,256]{3,0,2,1:T(4,128)(2,1)S(1)}, bf16[4,8,1,256]{3,0,2,1:T(4,128)(2,1)S(1)}, u32[]{:S(2)}, u32[]{:S(2)}) collective-permute-start(bf16[4,8,1,256]{3,0,2,1:T(4,128)(2,1)S(1)} %copy.65), channel_id=1, source_target_pairs={{0,1},{1,2},{2,3},{3,4},{4,5},{5,6},{6,7},{8,9},{9,10},{10,11},{11... | collective-permute-start | bytes 49160 | tf_op jit(solution)/shard_map/ppermute | solution.py:213
  20.7 10.1 %copy-start.6 = (bf16[4,8,128,256]{3,2,1,0:T(8,128)(2,1)S(1)}, bf16[4,8,128,256]{3,2,1,0:T(8,128)(2,1)}, u32[]{:S(2)}) copy-start(bf16[4,8,128,256]{3,2,1,0:T(8,128)(2,1)} %param.14) | copy-start | bytes 6291460
  21.2 5.5 %collective-permute-start.2 = (bf16[4,2,1,256]{3,0,2,1:T(4,128)(2,1)S(1)}, bf16[4,2,1,256]{3,0,2,1:T(4,128)(2,1)S(1)}, u32[]{:S(2)}, u32[]{:S(2)}) collective-permute-start(bf16[4,2,1,256]{3,0,2,1:T(4,128)(2,1)S(1)} %get-tuple-element.20), channel_id=1, source_target_pairs={{0,1},{1,2},{2,3},{3,4},{4,5},{5,6},{6,7},{8,9},{9,10},{10,11},{11... | collective-permute-start | bytes 12296 | tf_op jit(solution)/shard_map/ppermute | solution.py:216
  24.8 4.9 %collective-permute-start.3 = (bf16[4,2,1,256]{3,0,2,1:T(4,128)(2,1)S(1)}, bf16[4,2,1,256]{3,0,2,1:T(4,128)(2,1)S(1)}, u32[]{:S(2)}, u32[]{:S(2)}) collective-permute-start(bf16[4,2,1,256]{3,0,2,1:T(4,128)(2,1)S(1)} %get-tuple-element.21), channel_id=1, source_target_pairs={{1,0},{2,1},{3,2},{4,3},{5,4},{6,5},{7,6},{9,8},{10,9},{11,10},{12... | collective-permute-start | bytes 12296 | tf_op jit(solution)/shard_map/ppermute | solution.py:217
  30.8 25.1 %copy-start.4 = (f32[4,200,256]{2,1,0:T(8,128)S(1)}, f32[4,200,256]{2,1,0:T(8,128)}, u32[]{:S(2)}) copy-start(f32[4,200,256]{2,1,0:T(8,128)} %param.16) | copy-start | bytes 2457604
  30.8 25.1 %copy-start.11 = (bf16[256,256]{1,0:T(8,128)(2,1)S(1)}, bf16[256,256]{1,0:T(8,128)(2,1)}, u32[]{:S(2)}) copy-start(bf16[256,256]{1,0:T(8,128)(2,1)} %param.20) | copy-start | bytes 393220
  46.1 24.0 %all-to-all-start = ((f32[128,1,1056]{2,1,0:T(1,128)}), f32[128,1,1056]{2,1,0:T(1,128)S(1)}, u32[]{:S(2)}, u32[]{:S(2)}) async-start(f32[128,1,1056]{2,1,0:T(1,128)} %broadcast_in_dim.80), calls=%async_computation | async-start | bytes 1179648 | tf_op jit(solution)/shard_map/all_to_all | solution.py:269
  55.9 2.9 %copy-start.2 = (f32[4,8,128,256]{3,0,2,1:T(4,128)S(1)}, f32[4,8,128,256]{3,0,2,1:T(4,128)}, u32[]{:S(2)}) copy-start(f32[4,8,128,256]{3,0,2,1:T(4,128)} %get-tuple-element.28) | copy-start | bytes 12582916
  58.8 12.2 %copy-start.12 = (f32[256]{0:T(256)S(1)}, f32[256]{0:T(256)}, u32[]{:S(2)}) copy-start(f32[256]{0:T(256)} %param.19) | copy-start | bytes 3076
  58.9 12.2 %copy-start.13 = (f32[256]{0:T(256)S(1)}, f32[256]{0:T(256)}, u32[]{:S(2)}) copy-start(f32[256]{0:T(256)} %param.18) | copy-start | bytes 3076
  74.0 4.1 %copy-start.1 = (bf16[4,1024,256]{2,1,0:T(8,128)(2,1)}, bf16[4,1024,256]{2,1,0:T(8,128)(2,1)S(1)}, u32[]{:S(2)}) copy-start(bf16[4,1024,256]{2,1,0:T(8,128)(2,1)S(1)} %fusion.5.f_ref) | copy-start | bytes 6291460
  74.0 2.1 %copy-start.7 = (bf16[256,256]{1,0:T(8,128)(2,1)S(1)}, bf16[256,256]{1,0:T(8,128)(2,1)}, u32[]{:S(2)}) copy-start(bf16[256,256]{1,0:T(8,128)(2,1)} %param.21) | copy-start | bytes 393220
  127.6 25.6 %copy-start.8 = (bf16[256,256]{1,0:T(8,128)(2,1)S(1)}, bf16[256,256]{1,0:T(8,128)(2,1)}, u32[]{:S(2)}) copy-start(bf16[256,256]{1,0:T(8,128)(2,1)} %param.23) | copy-start | bytes 393220
  149.1 4.8 %copy-start.14 = (f32[256]{0:T(256)S(1)}, f32[256]{0:T(256)}, u32[]{:S(2)}) copy-start(f32[256]{0:T(256)} %param.25) | copy-start | bytes 3076
  149.1 4.8 %copy-start.15 = (f32[256]{0:T(256)S(1)}, f32[256]{0:T(256)}, u32[]{:S(2)}) copy-start(f32[256]{0:T(256)} %param.24) | copy-start | bytes 3076
  149.8 4.5 %copy-start.9 = (bf16[256,256]{1,0:T(8,128)(2,1)S(1)}, bf16[256,256]{1,0:T(8,128)(2,1)}, u32[]{:S(2)}) copy-start(bf16[256,256]{1,0:T(8,128)(2,1)} %param.27) | copy-start | bytes 393220
  149.8 4.5 %copy-start.10 = (bf16[256,256]{1,0:T(8,128)(2,1)S(1)}, bf16[256,256]{1,0:T(8,128)(2,1)}, u32[]{:S(2)}) copy-start(bf16[256,256]{1,0:T(8,128)(2,1)} %param.26) | copy-start | bytes 393220
  154.3 5.8 %copy-start.3 = (f32[4,200,256]{2,1,0:T(8,128)}, f32[4,200,256]{2,1,0:T(8,128)S(1)}, u32[]{:S(2)}) copy-start(f32[4,200,256]{2,1,0:T(8,128)S(1)} %multiply_add_fusion) | copy-start | bytes 2457604

commit v8 on v7

--- a/solution.py
+++ b/solution.py
@@ -201,7 +201,7 @@
     conv = lambda x, w, pad: lax.conv_general_dilated(
         x, w, (1, 1), pad, dimension_numbers=dims, preferred_element_type=jnp.float32
     )
-    main = conv(features, weight, ((1, 1), (1, 1)))
+    main = lax.optimization_barrier(conv(features, weight, ((1, 1), (1, 1))))
     rows = lax.axis_size("rows")
     cols = lax.axis_size("cols")
     down = [(i, i + 1) for i in range(rows - 1)]

time: 161 us -> 164 us (1.019)
  other arithmetic: 14.4 us -> 19 us
  matrix products: 21 us -> 19.1 us
    reduce_sum x1 -> x2, other arithmetic: 0.09 us -> 4.71 us  [on_device(): first_sum = jnp.sum(grouped, axis=(1, 3))]
    conv_general_dilated x5, matrix products: 15 us -> 13.1 us  [conv_with_halo(): lax.conv_general_dilated(x, w, (1, 1), pad, dimension_numbers=dims, prefe...]
  transfers between devices with their start and end apart: 7 -> 7, of which waited for: 2 -> 2; matrix products, arithmetic and copies ran while one was open for 5% -> 12% of each run, Pallas kernels for 3% -> 3%
where the time goes in v8:
time: 164 us; the launch traced here: 163 us
  blocking collectives  39.5 us (24%)
  Pallas kernels  27.6 us (17%)
  starting transfers between devices  26.8 us (16%)
  matrix products  19.1 us (12%)
  other arithmetic  19 us (12%)
  local copies, waits for them, and re-layouts  18.1 us (11%)
  waiting for transfers between devices  11.5 us (7%)
    all_to_all x1, blocking collectives, on_device(): parts = lax.all_to_all(packed, ('rows', 'cols'), 0, 0, tiled=True)  22.2 us
    pallas_call x1, Pallas kernels, attention(): pl.pallas_call(kernel, grid=(images,), in_specs=[pl.BlockSpec((1, heads *...  18.7 us
    all_to_all x1, blocking collectives, on_device(): lax.all_to_all(jnp.broadcast_to(attn_block, (devices, span)), ('rows', 'c...  17.3 us
    conv_general_dilated x5, matrix products, conv_with_halo(): lax.conv_general_dilated(x, w, (1, 1), pad, dimension_numbers=dims, prefe...  13.1 us
    all_to_all x1, starting transfers between devices, on_device(): lax.all_to_all(jnp.broadcast_to(stats, (devices, stats.shape[1])), ('rows...  10.5 us
    all_to_all x1, waiting for transfers between devices, on_device(): lax.all_to_all(jnp.broadcast_to(stats, (devices, stats.shape[1])), ('rows...  8.56 us
    reduce_sum x2, other arithmetic, on_device(): first_sum = jnp.sum(grouped, axis=(1, 3))  4.71 us
    pallas_call x1, Pallas kernels, logits_of(): pl.pallas_call(logits_kernel, grid=(images,), in_specs=[pl.BlockSpec((1,...  4.56 us
  transfers between devices with their start and end apart: 7, of which 2 were waited for; matrix products, arithmetic and copies ran while one was open for 12% of the time, Pallas kernels for 3%

profile of v8, /device:TPU:1, one launch (start us, length us, event | category | flops | bytes accessed | tf_op | source)
XLA Modules:
  0.0 162.8 jit_solution(2712809645065418621)
XLA Ops:
  0.6 1.1 fusion.48
  2.0 4.4 %collective-permute-start = (bf16[4,1,128,256]{3,0,2,1:T(4,128)(2,1)S(1)}, bf16[4,1,128,256]{3,0,2,1:T(4,128)(2,1)S(1)}, u32[]{:S(2)}, u32[]{:S(2)}) collective-permute-start(bf16[4,1,128,256]{3,0,2,1:T(4,128)(2,1)S(1)} %copy.62), channel_id=1, source_target_pairs={{0,8},{8,16},{16,24},{24,32},{32,40},{40,48},{48,56},{56,64},{64,7... | collective-permute-start | bytes 786440 | tf_op jit(solution)/shard_map/ppermute | solution.py:211
  6.6 1.3 collective-permute-start.1
  7.9 1.0 fusion.49
  8.9 2.9 %collective-permute-start.5 = (bf16[4,8,1,256]{3,0,2,1:T(4,128)(2,1)S(1)}, bf16[4,8,1,256]{3,0,2,1:T(4,128)(2,1)S(1)}, u32[]{:S(2)}, u32[]{:S(2)}) collective-permute-start(bf16[4,8,1,256]{3,0,2,1:T(4,128)(2,1)S(1)} %copy.64), channel_id=1, source_target_pairs={{1,0},{2,1},{3,2},{4,3},{5,4},{6,5},{7,6},{9,8},{10,9},{11,10},{12... | collective-permute-start | bytes 49160 | tf_op jit(solution)/shard_map/ppermute | solution.py:214
  11.8 3.1 %collective-permute-start.4 = (bf16[4,8,1,256]{3,0,2,1:T(4,128)(2,1)S(1)}, bf16[4,8,1,256]{3,0,2,1:T(4,128)(2,1)S(1)}, u32[]{:S(2)}, u32[]{:S(2)}) collective-permute-start(bf16[4,8,1,256]{3,0,2,1:T(4,128)(2,1)S(1)} %copy.65), channel_id=1, source_target_pairs={{0,1},{1,2},{2,3},{3,4},{4,5},{5,6},{6,7},{8,9},{9,10},{10,11},{11... | collective-permute-start | bytes 49160 | tf_op jit(solution)/shard_map/ppermute | solution.py:213
  14.9 11.6 %fusion.44 = f32[4,8,128,256]{3,0,2,1:T(4,128)} fusion(bf16[3,3,256,256]{3,2,1,0:T(8,128)(2,1)} %param.17, bf16[4,8,128,256]{3,2,1,0:T(8,128)(2,1)} %param.14), kind=kOutput, calls=%fused_computation.73 | convolution fusion | flops 4406116352 | bytes 7471104 | tf_op jit(solution)/shard_map/conv_general_dilated | solution.py:201
  26.7 4.4 %shard_map.149 = (bf16[4,200,1024]{2,1,0:T(8,128)(2,1)}, f32[4,200,1]{2,1,0:T(8,128)}) custom-call(s32[4,1600,128]{2,1,0:T(8,128)} %bitcast.53), custom_call_target="tpu_custom_call" | custom-call | tf_op jit(solution)/shard_map/pallas_call | solution.py:105
  31.1 1.2 reduce.5
  32.8 2.7 %collective-permute-start.2 = (bf16[4,2,1,256]{3,0,2,1:T(4,128)(2,1)S(1)}, bf16[4,2,1,256]{3,0,2,1:T(4,128)(2,1)S(1)}, u32[]{:S(2)}, u32[]{:S(2)}) collective-permute-start(bf16[4,2,1,256]{3,0,2,1:T(4,128)(2,1)S(1)} %get-tuple-element.21), channel_id=1, source_target_pairs={{0,1},{1,2},{2,3},{3,4},{4,5},{5,6},{6,7},{8,9},{9,10},{10,11},{11... | collective-permute-start | bytes 12296 | tf_op jit(solution)/shard_map/ppermute | solution.py:216
  35.7 1.9 %collective-permute-start.3 = (bf16[4,2,1,256]{3,0,2,1:T(4,128)(2,1)S(1)}, bf16[4,2,1,256]{3,0,2,1:T(4,128)(2,1)S(1)}, u32[]{:S(2)}, u32[]{:S(2)}) collective-permute-start(bf16[4,2,1,256]{3,0,2,1:T(4,128)(2,1)S(1)} %get-tuple-element.22), channel_id=1, source_target_pairs={{1,0},{2,1},{3,2},{4,3},{5,4},{6,5},{7,6},{9,8},{10,9},{11,10},{12... | collective-permute-start | bytes 12296 | tf_op jit(solution)/shard_map/ppermute | solution.py:217
  37.7 3.0 %collective-permute-done.3 = bf16[4,2,1,256]{3,0,2,1:T(4,128)(2,1)S(1)} collective-permute-done((bf16[4,2,1,256]{3,0,2,1:T(4,128)(2,1)S(1)}, bf16[4,2,1,256]{3,0,2,1:T(4,128)(2,1)S(1)}, u32[]{:S(2)}, u32[]{:S(2)}) %collective-permute-start.3) | collective-permute-done | bytes 4128 | tf_op jit(solution)/shard_map/ppermute | solution.py:217
  40.6 0.5 fusion.16
  41.2 0.5 fusion.18
  41.7 4.6 %fusion.46 = (f32[4,256]{1,0:T(4,128)S(1)}, f32[4,256]{1,0:T(4,128)S(1)}, f32[4,8,128,256]{3,0,2,1:T(4,128)}) fusion(f32[4,8,1,256]{3,0,2,1:T(4,128)S(1)} %fusion.12, f32[128]{0:T(128)S(1)} %pad.4.clone, f32[4,8,1,256]{3,0,2,1:T(4,128)S(1)} %fusion.14, f32[4,8,128,256]{3,0,2,1:T(4,128)S(1)} %copy-done.3, f32[4,1,128,256]{3,0,2,1:T(4,128)S(1)} %fusion.16, ...), kind=kLoop, calls=%fused_computation.75 | loop fusion | flops 9435136 | bytes 9511456 | tf_op jit(solution)/shard_map/reduce_sum | solution.py:266
  46.9 1.1 broadcast_in_dim.80
  48.0 10.5 %all-to-all-start = ((f32[128,1,1056]{2,1,0:T(1,128)}), f32[128,1,1056]{2,1,0:T(1,128)S(1)}, u32[]{:S(2)}, u32[]{:S(2)}) async-start(f32[128,1,1056]{2,1,0:T(1,128)} %broadcast_in_dim.80), calls=%async_computation | async-start | bytes 1179648 | tf_op jit(solution)/shard_map/all_to_all | solution.py:269
  58.6 0.3 convolution_convert_fusion.3
  59.0 2.2 %bitcast_select_fusion.refs_0_ = bf16[4,1600,256]{2,1,0:T(8,128)(2,1)} fusion(pred[1600,256]{1,0:T(8,128)(4,1)S(1)} %bitcast.56, bf16[4,200,256]{2,1,0:T(8,128)(2,1)S(1)} %convolution_convert_fusion.3), kind=kLoop, calls=%fused_computation.9 | loop fusion | flops 1638400 | bytes 4096000 | tf_op jit(solution)/shard_map/jit(_where)/select_n | solution.py:290
  61.2 0.3 copy-done.2
  61.5 2.7 %copy.54 = f32[4,8,128,256]{3,2,1,0:T(8,128)} copy(f32[4,8,128,256]{3,0,2,1:T(4,128)S(1)} %copy-done.2) | data formatting | bytes 8388608 | tf_op jit(solution)/shard_map/add | solution.py:238
  64.2 8.6 %all-to-all-done = f32[128,1,1056]{2,1,0:T(1,128)S(1)} async-done(((f32[128,1,1056]{2,1,0:T(1,128)}), f32[128,1,1056]{2,1,0:T(1,128)S(1)}, u32[]{:S(2)}, u32[]{:S(2)}) %all-to-all-start) | async-done | bytes 540704 | tf_op jit(solution)/shard_map/all_to_all | solution.py:269
  72.8 0.4 reduce_sum.83
  73.7 3.0 %fusion.5.f_ref = bf16[4,1024,256]{2,1,0:T(8,128)(2,1)S(1)} fusion(f32[4,8,128,256]{3,2,1,0:T(8,128)} %copy.54, f32[256]{0:T(256)S(1)} %copy-done.12, f32[256]{0:T(256)S(1)} %copy-done.13, f32[4,256]{1,0:T(4,128)S(1)} %div.54, f32[4,256]{1,0:T(4,128)S(1)} %sub.44), kind=kLoop, calls=%fused_computation.8 | loop fusion | flops 6291456 | bytes 6301696 | tf_op jit(solution)/shard_map/convert_element_type | solution.py:280
  76.7 2.1 %convolution_convert_fusion.refs_2_ = bf16[4,1024,256]{2,1,0:T(8,128)(2,1)} fusion(bf16[4,1024,256]{2,1,0:T(8,128)(2,1)S(1)} %fusion.5.f_ref, bf16[256,256]{1,0:T(8,128)(2,1)S(1)} %copy-done), kind=kOutput, calls=%fused_computation.10 | convolution fusion | flops 537919488 | bytes 4325376 | tf_op jit(solution)/shard_map/dot_general | solution.py:284
  78.8 2.0 %convolution_convert_fusion.1.refs_1_ = bf16[4,1024,256]{2,1,0:T(8,128)(2,1)} fusion(bf16[4,1024,256]{2,1,0:T(8,128)(2,1)S(1)} %fusion.5.f_ref, bf16[256,256]{1,0:T(8,128)(2,1)S(1)} %copy-done.7), kind=kOutput, calls=%fused_computation.11 | convolution fusion | flops 537919488 | bytes 4325376 | tf_op jit(solution)/shard_map/dot_general | solution.py:283
  80.8 1.0 copy.56.refs_4_
  81.8 18.7 %shard_map.150 = (f32[4,200,8]{2,1,0:T(8,128)}, f32[4,200,8]{2,1,0:T(8,128)}, f32[4,200,256]{2,1,0:T(8,128)}) custom-call(bf16[4,1600,256]{2,1,0:T(8,128)(2,1)} %bitcast_select_fusion.refs_0_, bf16[4,1024,256]{2,1,0:T(8,128)(2,1)} %convolution_convert_fusion.1.refs_1_, bf16[4,1024,256]{2,1,0:T(8,128)(2,1)} %convolution_convert_fusion.refs_2_, ...), custom_call_target="tpu_custom_call" | custom-call | tf_op jit(solution)/shard_map/pallas_call | solution.py:147
  100.4 1.6 reshape.136
  102.0 1.2 reshape.137
  103.2 1.2 reshape.138
  104.5 0.9 copy.57
  105.5 22.2 %all_to_all.24 = f32[128,1,1700]{2,1,0:T(1,128)S(1)} all-to-all(f32[128,1,1700]{2,1,0:T(1,128)S(1)} %copy.57), channel_id=1, replica_groups=mesh['rows'=16,'cols'=8] {'rows','cols'}, dimensions={0} | all-to-all | bytes 1740800 | tf_op jit(solution)/shard_map/all_to_all | solution.py:305
  127.7 1.3 copy.58
  129.3 0.3 fusion.7
  129.8 0.5 broadcast_in_dim.86
  130.2 0.5 broadcast.114
  130.8 3.3 %reduce.7 = bf16[128,1600]{1,0:T(8,128)(2,1)S(1)} reduce(bf16[128,1,1600]{2,1,0:T(2,128)(2,1)S(1)} %broadcast_in_dim.86, bf16[]{:T(256)} %broadcast.114), dimensions={1}, to_apply=%broadcast_in_dim.86.reduce_sub_computation | reduce | bytes 819202 | tf_op jit(solution)/shard_map/broadcast_in_dim | solution.py:313
  134.1 0.5 reshape.151
  134.5 17.3 %all_to_all.25 = bf16[128,2,800]{2,1,0:T(2,128)(2,1)S(1)} all-to-all(bf16[128,2,800]{2,1,0:T(2,128)(2,1)S(1)} %reshape.151), channel_id=1, replica_groups=mesh['rows'=16,'cols'=8] {'rows','cols'}, dimensions={0} | all-to-all | bytes 819200 | tf_op jit(solution)/shard_map/all_to_all | solution.py:312
  151.8 0.6 reshape.152
  152.5 2.7 %reduce.6 = bf16[128,1600]{1,0:T(8,128)(2,1)S(1)} reduce(bf16[128,1,1600]{2,1,0:T(2,128)(2,1)S(1)} %reshape.152, bf16[]{:T(256)} %constant.45), dimensions={1}, to_apply=%all_to_all.20.reduce_sub_computation | reduce | bytes 819202 | tf_op jit(solution)/shard_map/all_to_all | solution.py:312
  155.2 0.6 reshape.140
  155.8 0.4 fusion.53
  156.2 0.4 multiply_reduce_fusion.1
  156.6 0.3 multiply_add_fusion
  156.9 1.3 convolution_convert_fusion.2.e_ref
  158.2 4.6 %shard_map.151 = bf16[4,1600,128]{2,1,0:T(8,128)(2,1)} custom-call(bf16[4,200,256]{2,1,0:T(8,128)(2,1)} %convolution_convert_fusion.2.e_ref, bf16[4,1024,256]{2,1,0:T(8,128)(2,1)} %copy-done.1), custom_call_target="tpu_custom_call" | custom-call | tf_op jit(solution)/shard_map/pallas_call | solution.py:185
  (76 shorter events, 3.1 us)
Async XLA Ops:
  0.6 76.1 %copy-start = (bf16[256,256]{1,0:T(8,128)(2,1)S(1)}, bf16[256,256]{1,0:T(8,128)(2,1)}, u32[]{:S(2)}) copy-start(bf16[256,256]{1,0:T(8,128)(2,1)} %param.22) | copy-start | bytes 393220
  2.0 30.6 %collective-permute-start = (bf16[4,1,128,256]{3,0,2,1:T(4,128)(2,1)S(1)}, bf16[4,1,128,256]{3,0,2,1:T(4,128)(2,1)S(1)}, u32[]{:S(2)}, u32[]{:S(2)}) collective-permute-start(bf16[4,1,128,256]{3,0,2,1:T(4,128)(2,1)S(1)} %copy.62), channel_id=1, source_target_pairs={{0,8},{8,16},{16,24},{24,32},{32,40},{40,48},{48,56},{56,64},{64,7... | collective-permute-start | bytes 786440 | tf_op jit(solution)/shard_map/ppermute | solution.py:211
  6.6 26.1 %collective-permute-start.1 = (bf16[4,1,128,256]{3,0,2,1:T(4,128)(2,1)S(1)}, bf16[4,1,128,256]{3,0,2,1:T(4,128)(2,1)S(1)}, u32[]{:S(2)}, u32[]{:S(2)}) collective-permute-start(bf16[4,1,128,256]{3,0,2,1:T(4,128)(2,1)S(1)} %copy.63), channel_id=1, source_target_pairs={{8,0},{16,8},{24,16},{32,24},{40,32},{48,40},{56,48},{64,56},{72,6... | collective-permute-start | bytes 786440 | tf_op jit(solution)/shard_map/ppermute | solution.py:212
  8.9 23.4 %collective-permute-start.5 = (bf16[4,8,1,256]{3,0,2,1:T(4,128)(2,1)S(1)}, bf16[4,8,1,256]{3,0,2,1:T(4,128)(2,1)S(1)}, u32[]{:S(2)}, u32[]{:S(2)}) collective-permute-start(bf16[4,8,1,256]{3,0,2,1:T(4,128)(2,1)S(1)} %copy.64), channel_id=1, source_target_pairs={{1,0},{2,1},{3,2},{4,3},{5,4},{6,5},{7,6},{9,8},{10,9},{11,10},{12... | collective-permute-start | bytes 49160 | tf_op jit(solution)/shard_map/ppermute | solution.py:214
  11.8 23.7 %collective-permute-start.4 = (bf16[4,8,1,256]{3,0,2,1:T(4,128)(2,1)S(1)}, bf16[4,8,1,256]{3,0,2,1:T(4,128)(2,1)S(1)}, u32[]{:S(2)}, u32[]{:S(2)}) collective-permute-start(bf16[4,8,1,256]{3,0,2,1:T(4,128)(2,1)S(1)} %copy.65), channel_id=1, source_target_pairs={{0,1},{1,2},{2,3},{3,4},{4,5},{5,6},{6,7},{8,9},{9,10},{10,11},{11... | collective-permute-start | bytes 49160 | tf_op jit(solution)/shard_map/ppermute | solution.py:213
  26.6 5.8 %copy-start.6 = (bf16[3,3,256,256]{3,2,1,0:T(8,128)(2,1)S(1)}, bf16[3,3,256,256]{3,2,1,0:T(8,128)(2,1)}, u32[]{:S(2)}) copy-start(bf16[3,3,256,256]{3,2,1,0:T(8,128)(2,1)} %param.17) | copy-start | bytes 3538948
  32.3 9.4 %copy-start.3 = (f32[4,8,128,256]{3,0,2,1:T(4,128)S(1)}, f32[4,8,128,256]{3,0,2,1:T(4,128)}, u32[]{:S(2)}) copy-start(f32[4,8,128,256]{3,0,2,1:T(4,128)} %fusion.44) | copy-start | bytes 12582916
  32.8 4.8 %collective-permute-start.2 = (bf16[4,2,1,256]{3,0,2,1:T(4,128)(2,1)S(1)}, bf16[4,2,1,256]{3,0,2,1:T(4,128)(2,1)S(1)}, u32[]{:S(2)}, u32[]{:S(2)}) collective-permute-start(bf16[4,2,1,256]{3,0,2,1:T(4,128)(2,1)S(1)} %get-tuple-element.21), channel_id=1, source_target_pairs={{0,1},{1,2},{2,3},{3,4},{4,5},{5,6},{6,7},{8,9},{9,10},{10,11},{11... | collective-permute-start | bytes 12296 | tf_op jit(solution)/shard_map/ppermute | solution.py:216
  35.7 4.9 %collective-permute-start.3 = (bf16[4,2,1,256]{3,0,2,1:T(4,128)(2,1)S(1)}, bf16[4,2,1,256]{3,0,2,1:T(4,128)(2,1)S(1)}, u32[]{:S(2)}, u32[]{:S(2)}) collective-permute-start(bf16[4,2,1,256]{3,0,2,1:T(4,128)(2,1)S(1)} %get-tuple-element.22), channel_id=1, source_target_pairs={{1,0},{2,1},{3,2},{4,3},{5,4},{6,5},{7,6},{9,8},{10,9},{11,10},{12... | collective-permute-start | bytes 12296 | tf_op jit(solution)/shard_map/ppermute | solution.py:217
  41.7 16.9 %copy-start.5 = (f32[4,200,256]{2,1,0:T(8,128)S(1)}, f32[4,200,256]{2,1,0:T(8,128)}, u32[]{:S(2)}) copy-start(f32[4,200,256]{2,1,0:T(8,128)} %param.16) | copy-start | bytes 2457604
  41.7 16.9 %copy-start.11 = (bf16[256,256]{1,0:T(8,128)(2,1)S(1)}, bf16[256,256]{1,0:T(8,128)(2,1)}, u32[]{:S(2)}) copy-start(bf16[256,256]{1,0:T(8,128)(2,1)} %param.20) | copy-start | bytes 393220
  48.0 24.7 %all-to-all-start = ((f32[128,1,1056]{2,1,0:T(1,128)}), f32[128,1,1056]{2,1,0:T(1,128)S(1)}, u32[]{:S(2)}, u32[]{:S(2)}) async-start(f32[128,1,1056]{2,1,0:T(1,128)} %broadcast_in_dim.80), calls=%async_computation | async-start | bytes 1179648 | tf_op jit(solution)/shard_map/all_to_all | solution.py:269
  58.6 2.9 %copy-start.2 = (f32[4,8,128,256]{3,0,2,1:T(4,128)S(1)}, f32[4,8,128,256]{3,0,2,1:T(4,128)}, u32[]{:S(2)}) copy-start(f32[4,8,128,256]{3,0,2,1:T(4,128)} %get-tuple-element.16) | copy-start | bytes 12582916
  61.5 12.2 %copy-start.12 = (f32[256]{0:T(256)S(1)}, f32[256]{0:T(256)}, u32[]{:S(2)}) copy-start(f32[256]{0:T(256)} %param.19) | copy-start | bytes 3076
  61.5 12.2 %copy-start.13 = (f32[256]{0:T(256)S(1)}, f32[256]{0:T(256)}, u32[]{:S(2)}) copy-start(f32[256]{0:T(256)} %param.18) | copy-start | bytes 3076
  76.7 4.1 %copy-start.1 = (bf16[4,1024,256]{2,1,0:T(8,128)(2,1)}, bf16[4,1024,256]{2,1,0:T(8,128)(2,1)S(1)}, u32[]{:S(2)}) copy-start(bf16[4,1024,256]{2,1,0:T(8,128)(2,1)S(1)} %fusion.5.f_ref) | copy-start | bytes 6291460
  76.7 2.1 %copy-start.7 = (bf16[256,256]{1,0:T(8,128)(2,1)S(1)}, bf16[256,256]{1,0:T(8,128)(2,1)}, u32[]{:S(2)}) copy-start(bf16[256,256]{1,0:T(8,128)(2,1)} %param.21) | copy-start | bytes 393220
  130.2 25.6 %copy-start.8 = (bf16[256,256]{1,0:T(8,128)(2,1)S(1)}, bf16[256,256]{1,0:T(8,128)(2,1)}, u32[]{:S(2)}) copy-start(bf16[256,256]{1,0:T(8,128)(2,1)} %param.23) | copy-start | bytes 393220
  151.8 4.8 %copy-start.14 = (f32[256]{0:T(256)S(1)}, f32[256]{0:T(256)}, u32[]{:S(2)}) copy-start(f32[256]{0:T(256)} %param.25) | copy-start | bytes 3076
  151.8 4.8 %copy-start.15 = (f32[256]{0:T(256)S(1)}, f32[256]{0:T(256)}, u32[]{:S(2)}) copy-start(f32[256]{0:T(256)} %param.24) | copy-start | bytes 3076
  152.5 4.5 %copy-start.9 = (bf16[256,256]{1,0:T(8,128)(2,1)S(1)}, bf16[256,256]{1,0:T(8,128)(2,1)}, u32[]{:S(2)}) copy-start(bf16[256,256]{1,0:T(8,128)(2,1)} %param.27) | copy-start | bytes 393220
  152.5 4.5 %copy-start.10 = (bf16[256,256]{1,0:T(8,128)(2,1)S(1)}, bf16[256,256]{1,0:T(8,128)(2,1)}, u32[]{:S(2)}) copy-start(bf16[256,256]{1,0:T(8,128)(2,1)} %param.26) | copy-start | bytes 393220
  156.9 5.8 %copy-start.4 = (f32[4,200,256]{2,1,0:T(8,128)}, f32[4,200,256]{2,1,0:T(8,128)S(1)}, u32[]{:S(2)}) copy-start(f32[4,200,256]{2,1,0:T(8,128)S(1)} %multiply_add_fusion) | copy-start | bytes 2457604

commit v9 on v6

--- a/solution.py
+++ b/solution.py
@@ -86,45 +86,39 @@
     return a
 
 
-def prep_kernel(m_ref, fg_ref, cnt_ref):
-    queries = fg_ref.shape[1]
+def count_kernel(m_ref, cnt_ref):
+    queries = cnt_ref.shape[1]
+    tile_rows = m_ref.shape[1] // queries
+    acc = jnp.zeros((queries, m_ref.shape[2]), jnp.float32)
+    for r in range(tile_rows):
+        acc = acc + (m_ref[0, pl.ds(r, queries, stride=tile_rows), :] == 1).astype(jnp.float32)
+    cnt_ref[0] = jnp.sum(acc, axis=1, keepdims=True)
+
+
+def count_of(flat, queries):
+    images, rows, tile_cols = flat.shape
+    return pl.pallas_call(
+        count_kernel,
+        grid=(images,),
+        in_specs=[pl.BlockSpec((1, rows, tile_cols), lambda i: (i, 0, 0))],
+        out_specs=pl.BlockSpec((1, queries, 1), lambda i: (i, 0, 0)),
+        out_shape=jax.ShapeDtypeStruct((images, queries, 1), jnp.float32),
+    )(flat)
+
+
+def attention_kernel(q_ref, k_ref, v_ref, m_ref, zero_ref, top_ref, tot_ref, wv_ref, bias_ref, *, heads, scale):
+    queries = zero_ref.shape[1]
+    width = k_ref.shape[2]
+    head_size = width // heads
     tile_rows = m_ref.shape[1] // queries
     tile_cols = m_ref.shape[2]
-    acc = jnp.zeros((queries, tile_cols), jnp.float32)
-    for r in range(tile_rows):
-        rows = m_ref[0, pl.ds(r, queries, stride=tile_rows), :]
-        fg = (rows == 1).astype(jnp.float32)
-        acc = acc + fg
-        fg_ref[0, :, r * tile_cols : (r + 1) * tile_cols] = fg.astype(jnp.bfloat16)
-    cnt_ref[0] = jnp.sum(acc, axis=1, keepdims=True)
-
-
-def prep(masks):
-    images, queries, tile_rows, tile_cols = masks.shape
-    flat = masks.reshape(images, queries * tile_rows, tile_cols)
-    return pl.pallas_call(
-        prep_kernel,
-        grid=(images,),
-        in_specs=[pl.BlockSpec((1, queries * tile_rows, tile_cols), lambda i: (i, 0, 0))],
-        out_specs=[
-            pl.BlockSpec((1, queries, tile_rows * tile_cols), lambda i: (i, 0, 0)),
-            pl.BlockSpec((1, queries, 1), lambda i: (i, 0, 0)),
-        ],
-        out_shape=[
-            jax.ShapeDtypeStruct((images, queries, tile_rows * tile_cols), jnp.bfloat16),
-            jax.ShapeDtypeStruct((images, queries, 1), jnp.float32),
-        ],
-    )(flat)
-
-
-def attention_kernel(q_ref, k_ref, v_ref, fg_ref, zero_ref, top_ref, tot_ref, wv_ref, *, heads, scale):
-    queries = fg_ref.shape[1]
-    width = k_ref.shape[2]
-    head_size = width // heads
     k = k_ref[0]
     v = v_ref[0]
-    allowed = (fg_ref[0] != 0) | (zero_ref[0] != 0)
-    bias = jnp.where(allowed, 0.0, -jnp.inf)
+    empty = zero_ref[0] != 0
+    for r in range(tile_rows):
+        allowed = (m_ref[0, pl.ds(r, queries, stride=tile_rows), :] == 1) | empty
+        bias_ref[:, r * tile_cols : (r + 1) * tile_cols] = jnp.where(allowed, 0.0, -jnp.inf)
+    bias = bias_ref[...]
     lane = lax.broadcasted_iota(jnp.int32, (queries, width), 1)
     acc = jnp.zeros((queries, width), jnp.float32)
     for h in range(heads):
@@ -140,9 +134,9 @@
     wv_ref[0] = acc
 
 
-def attention(qbd, keys, vals, fg, zero, heads, scale):
+def attention(qbd, keys, vals, flat, zero, heads, scale):
     images, pixels, width = keys.shape
-    queries = fg.shape[1]
+    queries = zero.shape[1]
     kernel = lambda *refs: attention_kernel(*refs, heads=heads, scale=scale)
     return pl.pallas_call(
         kernel,
@@ -151,7 +145,7 @@
             pl.BlockSpec((1, heads * queries, width), lambda i: (i, 0, 0)),
             pl.BlockSpec((1, pixels, width), lambda i: (i, 0, 0)),
             pl.BlockSpec((1, pixels, width), lambda i: (i, 0, 0)),
-            pl.BlockSpec((1, queries, pixels), lambda i: (i, 0, 0)),
+            pl.BlockSpec((1,) + flat.shape[1:], lambda i: (i, 0, 0)),
             pl.BlockSpec((1, queries, 1), lambda i: (i, 0, 0)),
         ],
         out_specs=[
@@ -164,7 +158,8 @@
             jax.ShapeDtypeStruct((images, queries, heads), jnp.float32),
             jax.ShapeDtypeStruct((images, queries, width), jnp.float32),
         ],
-    )(qbd, keys, vals, fg, zero)
+        scratch_shapes=[pltpu.VMEM((queries, pixels), jnp.float32)],
+    )(qbd, keys, vals, flat, zero)
 
 
 def logits_kernel(e_ref, f_ref, o_ref, acc_ref):
@@ -217,7 +212,8 @@
     head_size = width // heads
     pixels = tile_rows * tile_cols
     devices = lax.axis_size("rows") * lax.axis_size("cols")
-    fg, local_count = prep(masks)
+    flat_masks = masks.reshape(images, query_count * tile_rows, tile_cols)
+    local_count = count_of(flat_masks, query_count)
     padded = with_halo(features, (("rows", 1), ("cols", 2)), 1)
     conv = lax.conv_general_dilated(
         padded,
@@ -257,7 +253,7 @@
         qproj[:, None, :, :],
         jnp.zeros((), jnp.bfloat16),
     ).reshape(images, heads * query_count, width)
-    top, total, weighted = attention(qbd, keys, vals, fg, zero, heads, 1.0 / head_size**0.5)
+    top, total, weighted = attention(qbd, keys, vals, flat_masks, zero, heads, 1.0 / head_size**0.5)
     span = images * query_count * width // devices
     packed = jnp.concatenate(
         [

time: 160 us -> 160 us (level)
  no operation moved by 1% of the time
where the time goes in v9:
time: 160 us; the launch traced here: 159 us
  blocking collectives  39.5 us (25%)
  Pallas kernels  27.8 us (17%)
  starting transfers between devices  23.2 us (14%)
  local copies, waits for them, and re-layouts  22.2 us (14%)
  matrix products  18.6 us (12%)
  other arithmetic  14.4 us (9%)
  waiting for transfers between devices  12.5 us (8%)
    all_to_all x1, blocking collectives, on_device(): parts = lax.all_to_all(packed, ('rows', 'cols'), 0, 0, tiled=True)  22.2 us
    pallas_call x1, Pallas kernels, attention(): pl.pallas_call(kernel, grid=(images,), in_specs=[pl.BlockSpec((1, heads *...  19 us
    all_to_all x1, blocking collectives, on_device(): lax.all_to_all(jnp.broadcast_to(attn_block, (devices, span)), ('rows', 'c...  17.3 us
    conv_general_dilated x1, matrix products, on_device(): lax.conv_general_dilated(padded, conv_weight, (1, 1), 'VALID', dimension_...  12.6 us
    all_to_all x1, starting transfers between devices, on_device(): lax.all_to_all(jnp.broadcast_to(stats, (devices, stats.shape[1])), ('rows...  10.9 us
    ppermute x2, starting transfers between devices, with_halo(): lax.ppermute(tail, axis, [(i, (i + 1) % count) for i in range(ends)])  9.11 us
    all_to_all x1, waiting for transfers between devices, on_device(): lax.all_to_all(jnp.broadcast_to(stats, (devices, stats.shape[1])), ('rows...  8.4 us
    unnamed x40, local copies, waits for them, and re-layouts  5.8 us
  transfers between devices with their start and end apart: 5, of which 3 were waited for; matrix products, arithmetic and copies ran while one was open for 7% of the time, Pallas kernels for 3%

profile of v9, /device:TPU:1, one launch (start us, length us, event | category | flops | bytes accessed | tf_op | source)
XLA Modules:
  0.0 159.3 jit_solution(15140149359597412794)
XLA Ops:
  0.7 1.2 fusion.32
  1.9 0.2 copy.51
  2.1 4.4 %collective-permute-start = (bf16[4,1,128,256]{3,0,2,1:T(4,128)(2,1)S(1)}, bf16[4,1,128,256]{3,0,2,1:T(4,128)(2,1)S(1)}, u32[]{:S(2)}, u32[]{:S(2)}) collective-permute-start(bf16[4,1,128,256]{3,0,2,1:T(4,128)(2,1)S(1)} %copy.51), channel_id=1, source_target_pairs={{0,8},{8,16},{16,24},{24,32},{32,40},{40,48},{48,56},{56,64},{64,7... | collective-permute-start | bytes 786440 | tf_op jit(solution)/shard_map/ppermute | solution.py:21
  6.7 1.3 collective-permute-start.1
  8.0 3.4 %collective-permute-done = bf16[4,1,128,256]{3,0,2,1:T(4,128)(2,1)S(1)} collective-permute-done((bf16[4,1,128,256]{3,0,2,1:T(4,128)(2,1)S(1)}, bf16[4,1,128,256]{3,0,2,1:T(4,128)(2,1)S(1)}, u32[]{:S(2)}, u32[]{:S(2)}) %collective-permute-start) | collective-permute-done | bytes 262176 | tf_op jit(solution)/shard_map/ppermute | solution.py:21
  11.4 0.8 constant_dynamic-update-slice_fusion.2
  12.2 3.0 %constant_dynamic-update-slice_fusion.1 = bf16[4,10,128,256]{3,0,2,1:T(4,128)(2,1)} fusion(bf16[4,10,128,256]{3,0,2,1:T(4,128)(2,1)} %constant_dynamic-update-slice_fusion.2, bf16[4,8,128,256]{3,2,1,0:T(8,128)(2,1)S(1)} %copy-done.4), kind=kLoop, calls=%fused_computation.39 | loop fusion | bytes 4194304
  15.2 0.7 collective-permute-done.1
  15.8 0.8 constant_dynamic-update-slice_fusion
  16.6 0.8 fusion.31
  17.4 4.7 %collective-permute-start.2 = (bf16[4,10,1,256]{3,0,2,1:T(4,128)(2,1)S(1)}, bf16[4,10,1,256]{3,0,2,1:T(4,128)(2,1)S(1)}, u32[]{:S(2)}, u32[]{:S(2)}) collective-permute-start(bf16[4,10,1,256]{3,0,2,1:T(4,128)(2,1)S(1)} %get-tuple-element.12), channel_id=1, source_target_pairs={{0,1},{1,2},{2,3},{3,4},{4,5},{5,6},{6,7},{8,9},{9,10},{10,11},{11... | collective-permute-start | bytes 61448 | tf_op jit(solution)/shard_map/ppermute | solution.py:21
  22.1 1.9 %collective-permute-start.3 = (bf16[4,10,1,256]{3,0,2,1:T(4,128)(2,1)S(1)}, bf16[4,10,1,256]{3,0,2,1:T(4,128)(2,1)S(1)}, u32[]{:S(2)}, u32[]{:S(2)}) collective-permute-start(bf16[4,10,1,256]{3,0,2,1:T(4,128)(2,1)S(1)} %get-tuple-element.13), channel_id=1, source_target_pairs={{1,0},{2,1},{3,2},{4,3},{5,4},{6,5},{7,6},{9,8},{10,9},{11,10},{12... | collective-permute-start | bytes 61448 | tf_op jit(solution)/shard_map/ppermute | solution.py:23
  24.1 4.2 %shard_map.149 = f32[4,200,1]{2,1,0:T(8,128)} custom-call(s32[4,1600,128]{2,1,0:T(8,128)} %bitcast.47), custom_call_target="tpu_custom_call" | custom-call | tf_op jit(solution)/shard_map/pallas_call | solution.py:100
  28.3 1.2 reduce.5
  29.5 12.6 %fusion.30 = (f32[4,256]{1,0:T(4,128)S(1)}, f32[4,256]{1,0:T(4,128)S(1)}, f32[4,8,128,256]{3,0,2,1:T(4,128)}) fusion(bf16[3,3,256,256]{3,2,1,0:T(8,128)(2,1)S(1)} %copy-done, bf16[4,10,1,256]{3,0,2,1:T(4,128)(2,1)S(1)} %collective-permute-done.3, bf16[4,10,128,256]{3,0,2,1:T(4,128)(2,1)} %constant_dynamic-update-slice_fusion, ...), kind=kOutput, calls=%fused_computation.59 | convolution fusion | flops 4842969088 | bytes 8044544 | tf_op jit(solution)/shard_map/conv_general_dilated | solution.py:218
  42.6 1.1 broadcast_in_dim.72
  43.8 10.9 %all-to-all-start = ((f32[128,1,1056]{2,1,0:T(1,128)}), f32[128,1,1056]{2,1,0:T(1,128)S(1)}, u32[]{:S(2)}, u32[]{:S(2)}) async-start(f32[128,1,1056]{2,1,0:T(1,128)} %broadcast_in_dim.72), calls=%async_computation | async-start | bytes 1179648 | tf_op jit(solution)/shard_map/all_to_all | solution.py:230
  54.7 0.3 convolution_convert_fusion.3
  55.1 2.2 %bitcast_select_fusion.refs_0_ = bf16[4,1600,256]{2,1,0:T(8,128)(2,1)} fusion(pred[1600,256]{1,0:T(8,128)(4,1)S(1)} %bitcast.55, bf16[4,200,256]{2,1,0:T(8,128)(2,1)S(1)} %convolution_convert_fusion.3), kind=kLoop, calls=%fused_computation.7 | loop fusion | flops 1638400 | bytes 4096000 | tf_op jit(solution)/shard_map/jit(_where)/select_n | solution.py:251
  57.3 0.5 copy-done.2
  57.7 2.7 %copy.44 = f32[4,8,128,256]{3,2,1,0:T(8,128)} copy(f32[4,8,128,256]{3,0,2,1:T(4,128)S(1)} %copy-done.2) | data formatting | bytes 8388608 | tf_op jit(solution)/shard_map/conv_general_dilated | solution.py:218
  60.4 8.4 %all-to-all-done = f32[128,1,1056]{2,1,0:T(1,128)S(1)} async-done(((f32[128,1,1056]{2,1,0:T(1,128)}), f32[128,1,1056]{2,1,0:T(1,128)S(1)}, u32[]{:S(2)}, u32[]{:S(2)}) %all-to-all-start) | async-done | bytes 540704 | tf_op jit(solution)/shard_map/all_to_all | solution.py:230
  68.8 0.4 reduce_sum.83
  69.8 3.0 %fusion.4.f_ref = bf16[4,1024,256]{2,1,0:T(8,128)(2,1)S(1)} fusion(f32[4,8,128,256]{3,2,1,0:T(8,128)} %copy.44, f32[256]{0:T(256)S(1)} %copy-done.13, f32[256]{0:T(256)S(1)} %copy-done.14, f32[4,256]{1,0:T(4,128)S(1)} %div.54, f32[4,256]{1,0:T(4,128)S(1)} %sub.44), kind=kLoop, calls=%fused_computation.6 | loop fusion | flops 6291456 | bytes 6301696 | tf_op jit(solution)/shard_map/convert_element_type | solution.py:241
  72.8 2.1 %convolution_convert_fusion.refs_2_ = bf16[4,1024,256]{2,1,0:T(8,128)(2,1)} fusion(bf16[4,1024,256]{2,1,0:T(8,128)(2,1)S(1)} %fusion.4.f_ref, bf16[256,256]{1,0:T(8,128)(2,1)S(1)} %copy-done.7), kind=kOutput, calls=%fused_computation.14 | convolution fusion | flops 537919488 | bytes 4325376 | tf_op jit(solution)/shard_map/dot_general | solution.py:245
  74.9 2.0 %convolution_convert_fusion.1.refs_1_ = bf16[4,1024,256]{2,1,0:T(8,128)(2,1)} fusion(bf16[4,1024,256]{2,1,0:T(8,128)(2,1)S(1)} %fusion.4.f_ref, bf16[256,256]{1,0:T(8,128)(2,1)S(1)} %copy-done.8), kind=kOutput, calls=%fused_computation.15 | convolution fusion | flops 537919488 | bytes 4325376 | tf_op jit(solution)/shard_map/dot_general | solution.py:244
  76.9 1.0 copy.46.refs_4_
  77.9 19.0 %shard_map.150 = (f32[4,200,8]{2,1,0:T(8,128)}, f32[4,200,8]{2,1,0:T(8,128)}, f32[4,200,256]{2,1,0:T(8,128)}) custom-call(bf16[4,1600,256]{2,1,0:T(8,128)(2,1)} %bitcast_select_fusion.refs_0_, bf16[4,1024,256]{2,1,0:T(8,128)(2,1)} %convolution_convert_fusion.1.refs_1_, bf16[4,1024,256]{2,1,0:T(8,128)(2,1)} %convolution_convert_fusion.refs_2_, ...), custom_call_target="tpu_custom_call" | custom-call | tf_op jit(solution)/shard_map/pallas_call | solution.py:141
  96.9 1.6 reshape.136
  98.5 1.2 reshape.137
  99.7 1.2 reshape.138
  101.0 0.9 copy.47
  101.9 22.2 %all_to_all.24 = f32[128,1,1700]{2,1,0:T(1,128)S(1)} all-to-all(f32[128,1,1700]{2,1,0:T(1,128)S(1)} %copy.47), channel_id=1, replica_groups=mesh['rows'=16,'cols'=8] {'rows','cols'}, dimensions={0} | all-to-all | bytes 1740800 | tf_op jit(solution)/shard_map/all_to_all | solution.py:266
  124.1 1.3 copy.48
  125.8 0.3 fusion.12
  126.2 0.5 broadcast_in_dim.78
  126.7 0.5 broadcast.108
  127.2 3.3 %reduce.7 = bf16[128,1600]{1,0:T(8,128)(2,1)S(1)} reduce(bf16[128,1,1600]{2,1,0:T(2,128)(2,1)S(1)} %broadcast_in_dim.78, bf16[]{:T(256)} %broadcast.108), dimensions={1}, to_apply=%broadcast_in_dim.78.reduce_sub_computation | reduce | bytes 819202 | tf_op jit(solution)/shard_map/broadcast_in_dim | solution.py:274
  130.5 0.5 reshape.151
  131.0 17.3 %all_to_all.25 = bf16[128,2,800]{2,1,0:T(2,128)(2,1)S(1)} all-to-all(bf16[128,2,800]{2,1,0:T(2,128)(2,1)S(1)} %reshape.151), channel_id=1, replica_groups=mesh['rows'=16,'cols'=8] {'rows','cols'}, dimensions={0} | all-to-all | bytes 819200 | tf_op jit(solution)/shard_map/all_to_all | solution.py:273
  148.3 0.6 reshape.152
  148.9 2.7 %reduce.6 = bf16[128,1600]{1,0:T(8,128)(2,1)S(1)} reduce(bf16[128,1,1600]{2,1,0:T(2,128)(2,1)S(1)} %reshape.152, bf16[]{:T(256)} %constant.43), dimensions={1}, to_apply=%all_to_all.20.reduce_sub_computation | reduce | bytes 819202 | tf_op jit(solution)/shard_map/all_to_all | solution.py:273
  151.6 0.6 reshape.140
  152.3 0.4 fusion.33
  152.7 0.4 multiply_reduce_fusion.1
  153.1 0.3 multiply_add_fusion
  153.4 1.3 convolution_convert_fusion.2.e_ref
  154.7 4.6 %shard_map.151 = bf16[4,1600,128]{2,1,0:T(8,128)(2,1)} custom-call(bf16[4,200,256]{2,1,0:T(8,128)(2,1)} %convolution_convert_fusion.2.e_ref, bf16[4,1024,256]{2,1,0:T(8,128)(2,1)} %copy-done.1), custom_call_target="tpu_custom_call" | custom-call | tf_op jit(solution)/shard_map/pallas_call | solution.py:180
  (61 shorter events, 2.1 us)
Async XLA Ops:
  0.6 28.9 %copy-start = (bf16[3,3,256,256]{3,2,1,0:T(8,128)(2,1)S(1)}, bf16[3,3,256,256]{3,2,1,0:T(8,128)(2,1)}, u32[]{:S(2)}) copy-start(bf16[3,3,256,256]{3,2,1,0:T(8,128)(2,1)} %param.17) | copy-start | bytes 3538948
  0.6 11.6 %copy-start.4 = (bf16[4,8,128,256]{3,2,1,0:T(8,128)(2,1)S(1)}, bf16[4,8,128,256]{3,2,1,0:T(8,128)(2,1)}, u32[]{:S(2)}) copy-start(bf16[4,8,128,256]{3,2,1,0:T(8,128)(2,1)} %param.14) | copy-start | bytes 6291460
  2.1 9.3 %collective-permute-start = (bf16[4,1,128,256]{3,0,2,1:T(4,128)(2,1)S(1)}, bf16[4,1,128,256]{3,0,2,1:T(4,128)(2,1)S(1)}, u32[]{:S(2)}, u32[]{:S(2)}) collective-permute-start(bf16[4,1,128,256]{3,0,2,1:T(4,128)(2,1)S(1)} %copy.51), channel_id=1, source_target_pairs={{0,8},{8,16},{16,24},{24,32},{32,40},{40,48},{48,56},{56,64},{64,7... | collective-permute-start | bytes 786440 | tf_op jit(solution)/shard_map/ppermute | solution.py:21
  6.7 9.1 %collective-permute-start.1 = (bf16[4,1,128,256]{3,0,2,1:T(4,128)(2,1)S(1)}, bf16[4,1,128,256]{3,0,2,1:T(4,128)(2,1)S(1)}, u32[]{:S(2)}, u32[]{:S(2)}) collective-permute-start(bf16[4,1,128,256]{3,0,2,1:T(4,128)(2,1)S(1)} %copy.52), channel_id=1, source_target_pairs={{8,0},{16,8},{24,16},{32,24},{40,32},{48,40},{56,48},{64,56},{72,6... | collective-permute-start | bytes 786440 | tf_op jit(solution)/shard_map/ppermute | solution.py:23
  17.4 12.1 %collective-permute-start.2 = (bf16[4,10,1,256]{3,0,2,1:T(4,128)(2,1)S(1)}, bf16[4,10,1,256]{3,0,2,1:T(4,128)(2,1)S(1)}, u32[]{:S(2)}, u32[]{:S(2)}) collective-permute-start(bf16[4,10,1,256]{3,0,2,1:T(4,128)(2,1)S(1)} %get-tuple-element.12), channel_id=1, source_target_pairs={{0,1},{1,2},{2,3},{3,4},{4,5},{5,6},{6,7},{8,9},{9,10},{10,11},{11... | collective-permute-start | bytes 61448 | tf_op jit(solution)/shard_map/ppermute | solution.py:21
  22.1 7.4 %collective-permute-start.3 = (bf16[4,10,1,256]{3,0,2,1:T(4,128)(2,1)S(1)}, bf16[4,10,1,256]{3,0,2,1:T(4,128)(2,1)S(1)}, u32[]{:S(2)}, u32[]{:S(2)}) collective-permute-start(bf16[4,10,1,256]{3,0,2,1:T(4,128)(2,1)S(1)} %get-tuple-element.13), channel_id=1, source_target_pairs={{1,0},{2,1},{3,2},{4,3},{5,4},{6,5},{7,6},{9,8},{10,9},{11,10},{12... | collective-permute-start | bytes 61448 | tf_op jit(solution)/shard_map/ppermute | solution.py:23
  29.5 25.2 %copy-start.12 = (bf16[256,256]{1,0:T(8,128)(2,1)S(1)}, bf16[256,256]{1,0:T(8,128)(2,1)}, u32[]{:S(2)}) copy-start(bf16[256,256]{1,0:T(8,128)(2,1)} %param.20) | copy-start | bytes 393220
  42.1 12.6 %copy-start.5 = (f32[4,200,256]{2,1,0:T(8,128)S(1)}, f32[4,200,256]{2,1,0:T(8,128)}, u32[]{:S(2)}) copy-start(f32[4,200,256]{2,1,0:T(8,128)} %param.16) | copy-start | bytes 2457604
  43.8 25.1 %all-to-all-start = ((f32[128,1,1056]{2,1,0:T(1,128)}), f32[128,1,1056]{2,1,0:T(1,128)S(1)}, u32[]{:S(2)}, u32[]{:S(2)}) async-start(f32[128,1,1056]{2,1,0:T(1,128)} %broadcast_in_dim.72), calls=%async_computation | async-start | bytes 1179648 | tf_op jit(solution)/shard_map/all_to_all | solution.py:230
  54.7 3.1 %copy-start.2 = (f32[4,8,128,256]{3,0,2,1:T(4,128)S(1)}, f32[4,8,128,256]{3,0,2,1:T(4,128)}, u32[]{:S(2)}) copy-start(f32[4,8,128,256]{3,0,2,1:T(4,128)} %get-tuple-element.18) | copy-start | bytes 12582916
  57.7 12.0 %copy-start.13 = (f32[256]{0:T(256)S(1)}, f32[256]{0:T(256)}, u32[]{:S(2)}) copy-start(f32[256]{0:T(256)} %param.19) | copy-start | bytes 3076
  57.7 12.0 %copy-start.14 = (f32[256]{0:T(256)S(1)}, f32[256]{0:T(256)}, u32[]{:S(2)}) copy-start(f32[256]{0:T(256)} %param.18) | copy-start | bytes 3076
  69.8 3.0 %copy-start.7 = (bf16[256,256]{1,0:T(8,128)(2,1)S(1)}, bf16[256,256]{1,0:T(8,128)(2,1)}, u32[]{:S(2)}) copy-start(bf16[256,256]{1,0:T(8,128)(2,1)} %param.22) | copy-start | bytes 393220
  72.8 4.1 %copy-start.1 = (bf16[4,1024,256]{2,1,0:T(8,128)(2,1)}, bf16[4,1024,256]{2,1,0:T(8,128)(2,1)S(1)}, u32[]{:S(2)}) copy-start(bf16[4,1024,256]{2,1,0:T(8,128)(2,1)S(1)} %fusion.4.f_ref) | copy-start | bytes 6291460
  72.8 2.1 %copy-start.8 = (bf16[256,256]{1,0:T(8,128)(2,1)S(1)}, bf16[256,256]{1,0:T(8,128)(2,1)}, u32[]{:S(2)}) copy-start(bf16[256,256]{1,0:T(8,128)(2,1)} %param.21) | copy-start | bytes 393220
  130.5 21.7 %copy-start.6 = (f32[4,200,256]{2,1,0:T(8,128)S(1)}, f32[4,200,256]{2,1,0:T(8,128)}, u32[]{:S(2)}) copy-start(f32[4,200,256]{2,1,0:T(8,128)} %param.16) | copy-start | bytes 2457604
  130.5 21.7 %copy-start.9 = (bf16[256,256]{1,0:T(8,128)(2,1)S(1)}, bf16[256,256]{1,0:T(8,128)(2,1)}, u32[]{:S(2)}) copy-start(bf16[256,256]{1,0:T(8,128)(2,1)} %param.23) | copy-start | bytes 393220
  148.9 4.2 %copy-start.15 = (f32[256]{0:T(256)S(1)}, f32[256]{0:T(256)}, u32[]{:S(2)}) copy-start(f32[256]{0:T(256)} %param.25) | copy-start | bytes 3076
  148.9 4.2 %copy-start.16 = (f32[256]{0:T(256)S(1)}, f32[256]{0:T(256)}, u32[]{:S(2)}) copy-start(f32[256]{0:T(256)} %param.24) | copy-start | bytes 3076
  151.6 1.8 %copy-start.10 = (bf16[256,256]{1,0:T(8,128)(2,1)S(1)}, bf16[256,256]{1,0:T(8,128)(2,1)}, u32[]{:S(2)}) copy-start(bf16[256,256]{1,0:T(8,128)(2,1)} %param.27) | copy-start | bytes 393220
  151.6 1.8 %copy-start.11 = (bf16[256,256]{1,0:T(8,128)(2,1)S(1)}, bf16[256,256]{1,0:T(8,128)(2,1)}, u32[]{:S(2)}) copy-start(bf16[256,256]{1,0:T(8,128)(2,1)} %param.26) | copy-start | bytes 393220
  153.4 5.8 %copy-start.3 = (f32[4,200,256]{2,1,0:T(8,128)}, f32[4,200,256]{2,1,0:T(8,128)S(1)}, u32[]{:S(2)}) copy-start(f32[4,200,256]{2,1,0:T(8,128)S(1)} %multiply_add_fusion) | copy-start | bytes 2457604

commit v10 on v6

--- a/solution.py
+++ b/solution.py
@@ -140,8 +140,9 @@
     wv_ref[0] = acc
 
 
-def attention(qbd, keys, vals, fg, zero, heads, scale):
-    images, pixels, width = keys.shape
+def attention(qbd, keys_vals, fg, zero, heads, scale):
+    images, pixels, width = keys_vals.shape
+    width //= 2
     queries = fg.shape[1]
     kernel = lambda *refs: attention_kernel(*refs, heads=heads, scale=scale)
     return pl.pallas_call(
@@ -150,7 +151,7 @@
         in_specs=[
             pl.BlockSpec((1, heads * queries, width), lambda i: (i, 0, 0)),
             pl.BlockSpec((1, pixels, width), lambda i: (i, 0, 0)),
-            pl.BlockSpec((1, pixels, width), lambda i: (i, 0, 0)),
+            pl.BlockSpec((1, pixels, width), lambda i: (i, 0, 1)),
             pl.BlockSpec((1, queries, pixels), lambda i: (i, 0, 0)),
             pl.BlockSpec((1, queries, 1), lambda i: (i, 0, 0)),
         ],
@@ -164,7 +165,7 @@
             jax.ShapeDtypeStruct((images, queries, heads), jnp.float32),
             jax.ShapeDtypeStruct((images, queries, width), jnp.float32),
         ],
-    )(qbd, keys, vals, fg, zero)
+    )(qbd, keys_vals, keys_vals, fg, zero)
 
 
 def logits_kernel(e_ref, f_ref, o_ref, acc_ref):
@@ -245,8 +246,9 @@
     mask_feat = jax.nn.relu(normed.reshape(images, pixels, width) * gn_gain + gn_bias).astype(
         jnp.bfloat16
     )
-    keys = jnp.dot(mask_feat, key_weight, preferred_element_type=jnp.float32).astype(jnp.bfloat16)
-    vals = jnp.dot(mask_feat, value_weight, preferred_element_type=jnp.float32).astype(jnp.bfloat16)
+    keys_vals = jnp.dot(
+        mask_feat, jnp.concatenate([key_weight, value_weight], axis=1), preferred_element_type=jnp.float32
+    ).astype(jnp.bfloat16)
     qproj = jnp.dot(
         queries.astype(jnp.bfloat16), query_weight, preferred_element_type=jnp.float32
     ).astype(jnp.bfloat16)
@@ -257,7 +259,7 @@
         qproj[:, None, :, :],
         jnp.zeros((), jnp.bfloat16),
     ).reshape(images, heads * query_count, width)
-    top, total, weighted = attention(qbd, keys, vals, fg, zero, heads, 1.0 / head_size**0.5)
+    top, total, weighted = attention(qbd, keys_vals, fg, zero, heads, 1.0 / head_size**0.5)
     span = images * query_count * width // devices
     packed = jnp.concatenate(
         [

time: 160 us -> 159 us (level)
    dot_general x2 -> x1, matrix products: 4.08 us -> 3.18 us  [on_device(): jnp.dot(mask_feat, jnp.concatenate([key_weight, value_weight], axis=1), p...]
where the time goes in v10:
time: 159 us; the launch traced here: 158 us
  blocking collectives  39.5 us (25%)
  Pallas kernels  27.6 us (17%)
  starting transfers between devices  23.2 us (15%)
  local copies, waits for them, and re-layouts  22.2 us (14%)
  matrix products  17.7 us (11%)
  other arithmetic  14.5 us (9%)
  waiting for transfers between devices  12.5 us (8%)
    all_to_all x1, blocking collectives, on_device(): parts = lax.all_to_all(packed, ('rows', 'cols'), 0, 0, tiled=True)  22.2 us
    pallas_call x1, Pallas kernels, attention(): pl.pallas_call(kernel, grid=(images,), in_specs=[pl.BlockSpec((1, heads *...  18.7 us
    all_to_all x1, blocking collectives, on_device(): lax.all_to_all(jnp.broadcast_to(attn_block, (devices, span)), ('rows', 'c...  17.3 us
    conv_general_dilated x1, matrix products, on_device(): lax.conv_general_dilated(padded, conv_weight, (1, 1), 'VALID', dimension_...  12.6 us
    all_to_all x1, starting transfers between devices, on_device(): lax.all_to_all(jnp.broadcast_to(stats, (devices, stats.shape[1])), ('rows...  10.9 us
    ppermute x2, starting transfers between devices, with_halo(): lax.ppermute(tail, axis, [(i, (i + 1) % count) for i in range(ends)])  9.11 us
    all_to_all x1, waiting for transfers between devices, on_device(): lax.all_to_all(jnp.broadcast_to(stats, (devices, stats.shape[1])), ('rows...  8.4 us
    unnamed x40, local copies, waits for them, and re-layouts  5.8 us
  transfers between devices with their start and end apart: 5, of which 3 were waited for; matrix products, arithmetic and copies ran while one was open for 7% of the time, Pallas kernels for 3%

profile of v10, /device:TPU:1, one launch (start us, length us, event | category | flops | bytes accessed | tf_op | source)
XLA Modules:
  0.0 158.1 jit_solution(9177843299673664002)
XLA Ops:
  0.7 1.2 fusion.33
  1.9 0.2 copy.51
  2.1 4.4 %collective-permute-start = (bf16[4,1,128,256]{3,0,2,1:T(4,128)(2,1)S(1)}, bf16[4,1,128,256]{3,0,2,1:T(4,128)(2,1)S(1)}, u32[]{:S(2)}, u32[]{:S(2)}) collective-permute-start(bf16[4,1,128,256]{3,0,2,1:T(4,128)(2,1)S(1)} %copy.51), channel_id=1, source_target_pairs={{0,8},{8,16},{16,24},{24,32},{32,40},{40,48},{48,56},{56,64},{64,7... | collective-permute-start | bytes 786440 | tf_op jit(solution)/shard_map/ppermute | solution.py:21
  6.5 0.2 copy.52
  6.7 1.3 collective-permute-start.1
  8.0 3.4 %collective-permute-done = bf16[4,1,128,256]{3,0,2,1:T(4,128)(2,1)S(1)} collective-permute-done((bf16[4,1,128,256]{3,0,2,1:T(4,128)(2,1)S(1)}, bf16[4,1,128,256]{3,0,2,1:T(4,128)(2,1)S(1)}, u32[]{:S(2)}, u32[]{:S(2)}) %collective-permute-start) | collective-permute-done | bytes 262176 | tf_op jit(solution)/shard_map/ppermute | solution.py:21
  11.4 0.8 constant_dynamic-update-slice_fusion.2
  12.2 3.0 %constant_dynamic-update-slice_fusion.1 = bf16[4,10,128,256]{3,0,2,1:T(4,128)(2,1)} fusion(bf16[4,10,128,256]{3,0,2,1:T(4,128)(2,1)} %constant_dynamic-update-slice_fusion.2, bf16[4,8,128,256]{3,2,1,0:T(8,128)(2,1)S(1)} %copy-done.4), kind=kLoop, calls=%fused_computation.39 | loop fusion | bytes 4194304
  15.2 0.7 collective-permute-done.1
  15.8 0.8 constant_dynamic-update-slice_fusion
  16.6 0.8 fusion.32
  17.4 4.7 %collective-permute-start.2 = (bf16[4,10,1,256]{3,0,2,1:T(4,128)(2,1)S(1)}, bf16[4,10,1,256]{3,0,2,1:T(4,128)(2,1)S(1)}, u32[]{:S(2)}, u32[]{:S(2)}) collective-permute-start(bf16[4,10,1,256]{3,0,2,1:T(4,128)(2,1)S(1)} %get-tuple-element.16), channel_id=1, source_target_pairs={{0,1},{1,2},{2,3},{3,4},{4,5},{5,6},{6,7},{8,9},{9,10},{10,11},{11... | collective-permute-start | bytes 61448 | tf_op jit(solution)/shard_map/ppermute | solution.py:21
  22.1 1.9 %collective-permute-start.3 = (bf16[4,10,1,256]{3,0,2,1:T(4,128)(2,1)S(1)}, bf16[4,10,1,256]{3,0,2,1:T(4,128)(2,1)S(1)}, u32[]{:S(2)}, u32[]{:S(2)}) collective-permute-start(bf16[4,10,1,256]{3,0,2,1:T(4,128)(2,1)S(1)} %get-tuple-element.17), channel_id=1, source_target_pairs={{1,0},{2,1},{3,2},{4,3},{5,4},{6,5},{7,6},{9,8},{10,9},{11,10},{12... | collective-permute-start | bytes 61448 | tf_op jit(solution)/shard_map/ppermute | solution.py:23
  24.1 4.3 %shard_map.149 = (bf16[4,200,1024]{2,1,0:T(8,128)(2,1)}, f32[4,200,1]{2,1,0:T(8,128)}) custom-call(s32[4,1600,128]{2,1,0:T(8,128)} %bitcast.47), custom_call_target="tpu_custom_call" | custom-call | tf_op jit(solution)/shard_map/pallas_call | solution.py:105
  28.4 1.2 reduce.5
  29.7 12.6 %fusion.31 = (f32[4,256]{1,0:T(4,128)S(1)}, f32[4,256]{1,0:T(4,128)S(1)}, f32[4,8,128,256]{3,0,2,1:T(4,128)}) fusion(bf16[3,3,256,256]{3,2,1,0:T(8,128)(2,1)S(1)} %copy-done, bf16[4,10,1,256]{3,0,2,1:T(4,128)(2,1)S(1)} %collective-permute-done.3, bf16[4,10,128,256]{3,0,2,1:T(4,128)(2,1)} %constant_dynamic-update-slice_fusion, ...), kind=kOutput, calls=%fused_computation.60 | convolution fusion | flops 4842969088 | bytes 8044544 | tf_op jit(solution)/shard_map/conv_general_dilated | solution.py:223
  42.8 1.1 broadcast_in_dim.72
  43.9 10.9 %all-to-all-start = ((f32[128,1,1056]{2,1,0:T(1,128)}), f32[128,1,1056]{2,1,0:T(1,128)S(1)}, u32[]{:S(2)}, u32[]{:S(2)}) async-start(f32[128,1,1056]{2,1,0:T(1,128)} %broadcast_in_dim.72), calls=%async_computation | async-start | bytes 1179648 | tf_op jit(solution)/shard_map/all_to_all | solution.py:235
  54.9 0.3 convolution_convert_fusion.2
  55.2 2.2 %bitcast_select_fusion.refs_0_ = bf16[4,1600,256]{2,1,0:T(8,128)(2,1)} fusion(pred[1600,256]{1,0:T(8,128)(4,1)S(1)} %bitcast.50, bf16[4,200,256]{2,1,0:T(8,128)(2,1)S(1)} %convolution_convert_fusion.2), kind=kLoop, calls=%fused_computation.7 | loop fusion | flops 1638400 | bytes 4096000 | tf_op jit(solution)/shard_map/jit(_where)/select_n | solution.py:257
  57.5 0.5 copy-done.2
  57.9 2.7 %copy.44 = f32[4,8,128,256]{3,2,1,0:T(8,128)} copy(f32[4,8,128,256]{3,0,2,1:T(4,128)S(1)} %copy-done.2) | data formatting | bytes 8388608 | tf_op jit(solution)/shard_map/conv_general_dilated | solution.py:223
  60.6 8.4 %all-to-all-done = f32[128,1,1056]{2,1,0:T(1,128)S(1)} async-done(((f32[128,1,1056]{2,1,0:T(1,128)}), f32[128,1,1056]{2,1,0:T(1,128)S(1)}, u32[]{:S(2)}, u32[]{:S(2)}) %all-to-all-start) | async-done | bytes 540704 | tf_op jit(solution)/shard_map/all_to_all | solution.py:235
  69.0 0.4 reduce_sum.83
  69.9 1.0 copy.46.refs_4_
  70.9 3.0 %fusion.4.f_ref = bf16[4,1024,256]{2,1,0:T(8,128)(2,1)S(1)} fusion(f32[4,8,128,256]{3,2,1,0:T(8,128)} %copy.44, f32[256]{0:T(256)S(1)} %copy-done.13, f32[256]{0:T(256)S(1)} %copy-done.14, f32[4,256]{1,0:T(4,128)S(1)} %div.54, f32[4,256]{1,0:T(4,128)S(1)} %sub.44), kind=kLoop, calls=%fused_computation.6 | loop fusion | flops 6291456 | bytes 6301696 | tf_op jit(solution)/shard_map/convert_element_type | solution.py:246
  73.9 3.2 %convolution_convert_fusion.refs_1_.refs_2_ = bf16[4,1024,512]{2,1,0:T(8,128)(2,1)} fusion(bf16[4,1024,256]{2,1,0:T(8,128)(2,1)S(1)} %fusion.4.f_ref, bf16[256,256]{1,0:T(8,128)(2,1)S(1)} %copy-done.7, bf16[256,256]{1,0:T(8,128)(2,1)S(1)} %copy-done.8), kind=kOutput, calls=%fused_computation.8 | convolution fusion | flops 1076363264 | bytes 6553600 | tf_op jit(solution)/shard_map/dot_general | solution.py:249
  77.1 18.7 %shard_map.150 = (f32[4,200,8]{2,1,0:T(8,128)}, f32[4,200,8]{2,1,0:T(8,128)}, f32[4,200,256]{2,1,0:T(8,128)}) custom-call(bf16[4,1600,256]{2,1,0:T(8,128)(2,1)} %bitcast_select_fusion.refs_0_, bf16[4,1024,512]{2,1,0:T(8,128)(2,1)} %convolution_convert_fusion.refs_1_.refs_2_, bf16[4,1024,512]{2,1,0:T(8,128)(2,1)} %convolution_convert_fusion.refs_1_.refs_2_, ...), custom_call_target="tpu_custom_call" | custom-call | tf_op jit(solution)/shard_map/pallas_call | solution.py:148
  95.8 1.6 reshape.136
  97.4 1.2 reshape.137
  98.6 1.2 reshape.138
  99.9 0.9 copy.47
  100.8 22.2 %all_to_all.24 = f32[128,1,1700]{2,1,0:T(1,128)S(1)} all-to-all(f32[128,1,1700]{2,1,0:T(1,128)S(1)} %copy.47), channel_id=1, replica_groups=mesh['rows'=16,'cols'=8] {'rows','cols'}, dimensions={0} | all-to-all | bytes 1740800 | tf_op jit(solution)/shard_map/all_to_all | solution.py:272
  123.0 1.3 copy.48
  124.7 0.3 fusion.12
  125.1 0.5 broadcast_in_dim.78
  125.6 0.5 broadcast.108
  126.1 3.3 %reduce.7 = bf16[128,1600]{1,0:T(8,128)(2,1)S(1)} reduce(bf16[128,1,1600]{2,1,0:T(2,128)(2,1)S(1)} %broadcast_in_dim.78, bf16[]{:T(256)} %broadcast.108), dimensions={1}, to_apply=%broadcast_in_dim.78.reduce_sub_computation | reduce | bytes 819202 | tf_op jit(solution)/shard_map/broadcast_in_dim | solution.py:280
  129.5 0.5 reshape.150
  129.9 17.3 %all_to_all.25 = bf16[128,2,800]{2,1,0:T(2,128)(2,1)S(1)} all-to-all(bf16[128,2,800]{2,1,0:T(2,128)(2,1)S(1)} %reshape.150), channel_id=1, replica_groups=mesh['rows'=16,'cols'=8] {'rows','cols'}, dimensions={0} | all-to-all | bytes 819200 | tf_op jit(solution)/shard_map/all_to_all | solution.py:279
  147.2 0.6 reshape.151
  147.8 2.7 %reduce.6 = bf16[128,1600]{1,0:T(8,128)(2,1)S(1)} reduce(bf16[128,1,1600]{2,1,0:T(2,128)(2,1)S(1)} %reshape.151, bf16[]{:T(256)} %constant.43), dimensions={1}, to_apply=%all_to_all.20.reduce_sub_computation | reduce | bytes 819202 | tf_op jit(solution)/shard_map/all_to_all | solution.py:279
  150.5 0.6 reshape.140
  151.2 0.4 fusion.34
  151.6 0.4 multiply_reduce_fusion.1
  152.0 0.3 multiply_add_fusion
  152.4 1.2 convolution_convert_fusion.1.e_ref
  153.6 4.6 %shard_map.151 = bf16[4,1600,128]{2,1,0:T(8,128)(2,1)} custom-call(bf16[4,200,256]{2,1,0:T(8,128)(2,1)} %convolution_convert_fusion.1.e_ref, bf16[4,1024,256]{2,1,0:T(8,128)(2,1)} %copy-done.1), custom_call_target="tpu_custom_call" | custom-call | tf_op jit(solution)/shard_map/pallas_call | solution.py:186
  (60 shorter events, 1.9 us)
Async XLA Ops:
  0.6 29.0 %copy-start = (bf16[3,3,256,256]{3,2,1,0:T(8,128)(2,1)S(1)}, bf16[3,3,256,256]{3,2,1,0:T(8,128)(2,1)}, u32[]{:S(2)}) copy-start(bf16[3,3,256,256]{3,2,1,0:T(8,128)(2,1)} %param.17) | copy-start | bytes 3538948
  0.6 11.6 %copy-start.4 = (bf16[4,8,128,256]{3,2,1,0:T(8,128)(2,1)S(1)}, bf16[4,8,128,256]{3,2,1,0:T(8,128)(2,1)}, u32[]{:S(2)}) copy-start(bf16[4,8,128,256]{3,2,1,0:T(8,128)(2,1)} %param.14) | copy-start | bytes 6291460
  2.1 9.3 %collective-permute-start = (bf16[4,1,128,256]{3,0,2,1:T(4,128)(2,1)S(1)}, bf16[4,1,128,256]{3,0,2,1:T(4,128)(2,1)S(1)}, u32[]{:S(2)}, u32[]{:S(2)}) collective-permute-start(bf16[4,1,128,256]{3,0,2,1:T(4,128)(2,1)S(1)} %copy.51), channel_id=1, source_target_pairs={{0,8},{8,16},{16,24},{24,32},{32,40},{40,48},{48,56},{56,64},{64,7... | collective-permute-start | bytes 786440 | tf_op jit(solution)/shard_map/ppermute | solution.py:21
  6.7 9.1 %collective-permute-start.1 = (bf16[4,1,128,256]{3,0,2,1:T(4,128)(2,1)S(1)}, bf16[4,1,128,256]{3,0,2,1:T(4,128)(2,1)S(1)}, u32[]{:S(2)}, u32[]{:S(2)}) collective-permute-start(bf16[4,1,128,256]{3,0,2,1:T(4,128)(2,1)S(1)} %copy.52), channel_id=1, source_target_pairs={{8,0},{16,8},{24,16},{32,24},{40,32},{48,40},{56,48},{64,56},{72,6... | collective-permute-start | bytes 786440 | tf_op jit(solution)/shard_map/ppermute | solution.py:23
  17.4 12.2 %collective-permute-start.2 = (bf16[4,10,1,256]{3,0,2,1:T(4,128)(2,1)S(1)}, bf16[4,10,1,256]{3,0,2,1:T(4,128)(2,1)S(1)}, u32[]{:S(2)}, u32[]{:S(2)}) collective-permute-start(bf16[4,10,1,256]{3,0,2,1:T(4,128)(2,1)S(1)} %get-tuple-element.16), channel_id=1, source_target_pairs={{0,1},{1,2},{2,3},{3,4},{4,5},{5,6},{6,7},{8,9},{9,10},{10,11},{11... | collective-permute-start | bytes 61448 | tf_op jit(solution)/shard_map/ppermute | solution.py:21
  22.1 7.5 %collective-permute-start.3 = (bf16[4,10,1,256]{3,0,2,1:T(4,128)(2,1)S(1)}, bf16[4,10,1,256]{3,0,2,1:T(4,128)(2,1)S(1)}, u32[]{:S(2)}, u32[]{:S(2)}) collective-permute-start(bf16[4,10,1,256]{3,0,2,1:T(4,128)(2,1)S(1)} %get-tuple-element.17), channel_id=1, source_target_pairs={{1,0},{2,1},{3,2},{4,3},{5,4},{6,5},{7,6},{9,8},{10,9},{11,10},{12... | collective-permute-start | bytes 61448 | tf_op jit(solution)/shard_map/ppermute | solution.py:23
  29.6 25.2 %copy-start.5 = (f32[4,200,256]{2,1,0:T(8,128)S(1)}, f32[4,200,256]{2,1,0:T(8,128)}, u32[]{:S(2)}) copy-start(f32[4,200,256]{2,1,0:T(8,128)} %param.16) | copy-start | bytes 2457604
  29.6 25.2 %copy-start.12 = (bf16[256,256]{1,0:T(8,128)(2,1)S(1)}, bf16[256,256]{1,0:T(8,128)(2,1)}, u32[]{:S(2)}) copy-start(bf16[256,256]{1,0:T(8,128)(2,1)} %param.20) | copy-start | bytes 393220
  43.9 25.1 %all-to-all-start = ((f32[128,1,1056]{2,1,0:T(1,128)}), f32[128,1,1056]{2,1,0:T(1,128)S(1)}, u32[]{:S(2)}, u32[]{:S(2)}) async-start(f32[128,1,1056]{2,1,0:T(1,128)} %broadcast_in_dim.72), calls=%async_computation | async-start | bytes 1179648 | tf_op jit(solution)/shard_map/all_to_all | solution.py:235
  54.9 3.1 %copy-start.2 = (f32[4,8,128,256]{3,0,2,1:T(4,128)S(1)}, f32[4,8,128,256]{3,0,2,1:T(4,128)}, u32[]{:S(2)}) copy-start(f32[4,8,128,256]{3,0,2,1:T(4,128)} %get-tuple-element.22) | copy-start | bytes 12582916
  57.9 13.0 %copy-start.13 = (f32[256]{0:T(256)S(1)}, f32[256]{0:T(256)}, u32[]{:S(2)}) copy-start(f32[256]{0:T(256)} %param.19) | copy-start | bytes 3076
  57.9 13.0 %copy-start.14 = (f32[256]{0:T(256)S(1)}, f32[256]{0:T(256)}, u32[]{:S(2)}) copy-start(f32[256]{0:T(256)} %param.18) | copy-start | bytes 3076
  70.9 3.0 %copy-start.7 = (bf16[256,256]{1,0:T(8,128)(2,1)S(1)}, bf16[256,256]{1,0:T(8,128)(2,1)}, u32[]{:S(2)}) copy-start(bf16[256,256]{1,0:T(8,128)(2,1)} %param.22) | copy-start | bytes 393220
  70.9 3.0 %copy-start.8 = (bf16[256,256]{1,0:T(8,128)(2,1)S(1)}, bf16[256,256]{1,0:T(8,128)(2,1)}, u32[]{:S(2)}) copy-start(bf16[256,256]{1,0:T(8,128)(2,1)} %param.21) | copy-start | bytes 393220
  73.9 3.2 %copy-start.1 = (bf16[4,1024,256]{2,1,0:T(8,128)(2,1)}, bf16[4,1024,256]{2,1,0:T(8,128)(2,1)S(1)}, u32[]{:S(2)}) copy-start(bf16[4,1024,256]{2,1,0:T(8,128)(2,1)S(1)} %fusion.4.f_ref) | copy-start | bytes 6291460
  129.4 21.7 %copy-start.6 = (f32[4,200,256]{2,1,0:T(8,128)S(1)}, f32[4,200,256]{2,1,0:T(8,128)}, u32[]{:S(2)}) copy-start(f32[4,200,256]{2,1,0:T(8,128)} %param.16) | copy-start | bytes 2457604
  129.4 21.7 %copy-start.9 = (bf16[256,256]{1,0:T(8,128)(2,1)S(1)}, bf16[256,256]{1,0:T(8,128)(2,1)}, u32[]{:S(2)}) copy-start(bf16[256,256]{1,0:T(8,128)(2,1)} %param.23) | copy-start | bytes 393220
  147.8 4.2 %copy-start.15 = (f32[256]{0:T(256)S(1)}, f32[256]{0:T(256)}, u32[]{:S(2)}) copy-start(f32[256]{0:T(256)} %param.25) | copy-start | bytes 3076
  147.8 4.2 %copy-start.16 = (f32[256]{0:T(256)S(1)}, f32[256]{0:T(256)}, u32[]{:S(2)}) copy-start(f32[256]{0:T(256)} %param.24) | copy-start | bytes 3076
  151.2 1.2 copy-start.10
  151.2 1.2 copy-start.11
  152.3 5.8 %copy-start.3 = (f32[4,200,256]{2,1,0:T(8,128)}, f32[4,200,256]{2,1,0:T(8,128)S(1)}, u32[]{:S(2)}) copy-start(f32[4,200,256]{2,1,0:T(8,128)S(1)} %multiply_add_fusion) | copy-start | bytes 2457604

commit v11 on v10

--- a/solution.py
+++ b/solution.py
@@ -261,16 +261,23 @@
     ).reshape(images, heads * query_count, width)
     top, total, weighted = attention(qbd, keys_vals, fg, zero, heads, 1.0 / head_size**0.5)
     span = images * query_count * width // devices
+    groups = span // 32
+
+    def halves(x):
+        high = x.astype(jnp.bfloat16)
+        return [high, (x - high.astype(jnp.float32)).astype(jnp.bfloat16)]
+
     packed = jnp.concatenate(
-        [
-            weighted.reshape(devices, span),
-            total.reshape(devices, span // 32),
-            top.reshape(devices, span // 32),
-        ],
+        [weighted.reshape(devices, span).astype(jnp.bfloat16)]
+        + halves(total.reshape(devices, groups))
+        + halves(top.reshape(devices, groups)),
         axis=1,
     )
-    parts = lax.all_to_all(packed, ("rows", "cols"), 0, 0, tiled=True)
-    sums, totals, tops = split_parts(parts, span)
+    parts = lax.all_to_all(packed, ("rows", "cols"), 0, 0, tiled=True).astype(jnp.float32)
+    sums = parts[:, :span]
+    pieces = [parts[:, span + n * groups : span + (n + 1) * groups] for n in range(4)]
+    totals = pieces[0] + pieces[1]
+    tops = pieces[2] + pieces[3]
     highest = jnp.max(tops, axis=0, keepdims=True)
     factor = jnp.exp(tops - highest)
     totals = jnp.sum(totals * factor, axis=0, keepdims=True)

time: 159 us -> 156 us (0.981)
  blocking collectives: 39.5 us -> 35.3 us
  other arithmetic: 14.5 us -> 16.7 us
    all_to_all x1, blocking collectives: 22.2 us -> 18 us  [on_device(): lax.all_to_all(packed, ('rows', 'cols'), 0, 0, tiled=True)]
    reshape x3 -> x2, local copies, waits for them, and re-layouts: 3.93 us -> 2.35 us  [the longest x1 1.18 us: on_device(): top.reshape(devices, groups)]
where the time goes in v11:
time: 156 us; the launch traced here: 155 us
  blocking collectives  35.3 us (23%)
  Pallas kernels  27.6 us (18%)
  starting transfers between devices  23.2 us (15%)
  local copies, waits for them, and re-layouts  21.2 us (14%)
  matrix products  17.7 us (11%)
  other arithmetic  16.7 us (11%)
  waiting for transfers between devices  12.5 us (8%)
    pallas_call x1, Pallas kernels, attention(): pl.pallas_call(kernel, grid=(images,), in_specs=[pl.BlockSpec((1, heads *...  18.7 us
    all_to_all x1, blocking collectives, on_device(): lax.all_to_all(packed, ('rows', 'cols'), 0, 0, tiled=True)  18 us
    all_to_all x1, blocking collectives, on_device(): lax.all_to_all(jnp.broadcast_to(attn_block, (devices, span)), ('rows', 'c...  17.3 us
    conv_general_dilated x1, matrix products, on_device(): lax.conv_general_dilated(padded, conv_weight, (1, 1), 'VALID', dimension_...  12.6 us
    all_to_all x1, starting transfers between devices, on_device(): lax.all_to_all(jnp.broadcast_to(stats, (devices, stats.shape[1])), ('rows...  10.9 us
    ppermute x2, starting transfers between devices, with_halo(): lax.ppermute(tail, axis, [(i, (i + 1) % count) for i in range(ends)])  9.11 us
    all_to_all x1, waiting for transfers between devices, on_device(): lax.all_to_all(jnp.broadcast_to(stats, (devices, stats.shape[1])), ('rows...  8.4 us
    unnamed x40, local copies, waits for them, and re-layouts  7.1 us
  transfers between devices with their start and end apart: 5, of which 3 were waited for; matrix products, arithmetic and copies ran while one was open for 7% of the time, Pallas kernels for 3%

profile of v11, /device:TPU:1, one launch (start us, length us, event | category | flops | bytes accessed | tf_op | source)
XLA Modules:
  0.0 155.3 jit_solution(7015029494052512312)
XLA Ops:
  0.7 1.2 fusion.35
  2.1 4.4 %collective-permute-start = (bf16[4,1,128,256]{3,0,2,1:T(4,128)(2,1)S(1)}, bf16[4,1,128,256]{3,0,2,1:T(4,128)(2,1)S(1)}, u32[]{:S(2)}, u32[]{:S(2)}) collective-permute-start(bf16[4,1,128,256]{3,0,2,1:T(4,128)(2,1)S(1)} %copy.51), channel_id=1, source_target_pairs={{0,8},{8,16},{16,24},{24,32},{32,40},{40,48},{48,56},{56,64},{64,7... | collective-permute-start | bytes 786440 | tf_op jit(solution)/shard_map/ppermute | solution.py:21
  6.7 1.3 collective-permute-start.1
  8.0 3.4 %collective-permute-done = bf16[4,1,128,256]{3,0,2,1:T(4,128)(2,1)S(1)} collective-permute-done((bf16[4,1,128,256]{3,0,2,1:T(4,128)(2,1)S(1)}, bf16[4,1,128,256]{3,0,2,1:T(4,128)(2,1)S(1)}, u32[]{:S(2)}, u32[]{:S(2)}) %collective-permute-start) | collective-permute-done | bytes 262176 | tf_op jit(solution)/shard_map/ppermute | solution.py:21
  11.4 0.8 constant_dynamic-update-slice_fusion.2
  12.2 3.0 %constant_dynamic-update-slice_fusion.1 = bf16[4,10,128,256]{3,0,2,1:T(4,128)(2,1)} fusion(bf16[4,10,128,256]{3,0,2,1:T(4,128)(2,1)} %constant_dynamic-update-slice_fusion.2, bf16[4,8,128,256]{3,2,1,0:T(8,128)(2,1)S(1)} %copy-done.4), kind=kLoop, calls=%fused_computation.44 | loop fusion | bytes 4194304
  15.2 0.7 collective-permute-done.1
  15.8 0.8 constant_dynamic-update-slice_fusion
  16.6 0.8 fusion.34
  17.4 4.7 %collective-permute-start.2 = (bf16[4,10,1,256]{3,0,2,1:T(4,128)(2,1)S(1)}, bf16[4,10,1,256]{3,0,2,1:T(4,128)(2,1)S(1)}, u32[]{:S(2)}, u32[]{:S(2)}) collective-permute-start(bf16[4,10,1,256]{3,0,2,1:T(4,128)(2,1)S(1)} %get-tuple-element.20), channel_id=1, source_target_pairs={{0,1},{1,2},{2,3},{3,4},{4,5},{5,6},{6,7},{8,9},{9,10},{10,11},{11... | collective-permute-start | bytes 61448 | tf_op jit(solution)/shard_map/ppermute | solution.py:21
  22.1 1.9 %collective-permute-start.3 = (bf16[4,10,1,256]{3,0,2,1:T(4,128)(2,1)S(1)}, bf16[4,10,1,256]{3,0,2,1:T(4,128)(2,1)S(1)}, u32[]{:S(2)}, u32[]{:S(2)}) collective-permute-start(bf16[4,10,1,256]{3,0,2,1:T(4,128)(2,1)S(1)} %get-tuple-element.21), channel_id=1, source_target_pairs={{1,0},{2,1},{3,2},{4,3},{5,4},{6,5},{7,6},{9,8},{10,9},{11,10},{12... | collective-permute-start | bytes 61448 | tf_op jit(solution)/shard_map/ppermute | solution.py:23
  24.1 4.3 %shard_map.149 = (bf16[4,200,1024]{2,1,0:T(8,128)(2,1)}, f32[4,200,1]{2,1,0:T(8,128)}) custom-call(s32[4,1600,128]{2,1,0:T(8,128)} %bitcast.45), custom_call_target="tpu_custom_call" | custom-call | tf_op jit(solution)/shard_map/pallas_call | solution.py:105
  28.4 1.2 reduce.5
  29.7 12.6 %fusion.33 = (f32[4,256]{1,0:T(4,128)S(1)}, f32[4,256]{1,0:T(4,128)S(1)}, f32[4,8,128,256]{3,0,2,1:T(4,128)}) fusion(bf16[3,3,256,256]{3,2,1,0:T(8,128)(2,1)S(1)} %copy-done, bf16[4,10,1,256]{3,0,2,1:T(4,128)(2,1)S(1)} %collective-permute-done.3, bf16[4,10,128,256]{3,0,2,1:T(4,128)(2,1)} %constant_dynamic-update-slice_fusion, ...), kind=kOutput, calls=%fused_computation.65 | convolution fusion | flops 4842969088 | bytes 8044544 | tf_op jit(solution)/shard_map/conv_general_dilated | solution.py:223
  42.8 1.1 broadcast_in_dim.72
  43.9 10.9 %all-to-all-start = ((f32[128,1,1056]{2,1,0:T(1,128)}), f32[128,1,1056]{2,1,0:T(1,128)S(1)}, u32[]{:S(2)}, u32[]{:S(2)}) async-start(f32[128,1,1056]{2,1,0:T(1,128)} %broadcast_in_dim.72), calls=%async_computation | async-start | bytes 1179648 | tf_op jit(solution)/shard_map/all_to_all | solution.py:235
  55.2 2.2 %bitcast_select_fusion.refs_0_ = bf16[4,1600,256]{2,1,0:T(8,128)(2,1)} fusion(pred[1600,256]{1,0:T(8,128)(4,1)S(1)} %bitcast.49, bf16[4,200,256]{2,1,0:T(8,128)(2,1)S(1)} %convolution_convert_fusion.2), kind=kLoop, calls=%fused_computation.7 | loop fusion | flops 1638400 | bytes 4096000 | tf_op jit(solution)/shard_map/jit(_where)/select_n | solution.py:257
  57.5 0.5 copy-done.2
  57.9 2.7 %copy.44 = f32[4,8,128,256]{3,2,1,0:T(8,128)} copy(f32[4,8,128,256]{3,0,2,1:T(4,128)S(1)} %copy-done.2) | data formatting | bytes 8388608 | tf_op jit(solution)/shard_map/conv_general_dilated | solution.py:223
  60.6 8.4 %all-to-all-done = f32[128,1,1056]{2,1,0:T(1,128)S(1)} async-done(((f32[128,1,1056]{2,1,0:T(1,128)}), f32[128,1,1056]{2,1,0:T(1,128)S(1)}, u32[]{:S(2)}, u32[]{:S(2)}) %all-to-all-start) | async-done | bytes 540704 | tf_op jit(solution)/shard_map/all_to_all | solution.py:235
  69.0 0.4 reduce_sum.83
  69.9 1.0 copy.46.refs_4_
  70.9 3.0 %fusion.4.f_ref = bf16[4,1024,256]{2,1,0:T(8,128)(2,1)S(1)} fusion(f32[4,8,128,256]{3,2,1,0:T(8,128)} %copy.44, f32[256]{0:T(256)S(1)} %copy-done.12, f32[256]{0:T(256)S(1)} %copy-done.13, f32[4,256]{1,0:T(4,128)S(1)} %div.54, f32[4,256]{1,0:T(4,128)S(1)} %sub.50), kind=kLoop, calls=%fused_computation.6 | loop fusion | flops 6291456 | bytes 6301696 | tf_op jit(solution)/shard_map/convert_element_type | solution.py:246
  73.9 3.2 %convolution_convert_fusion.refs_1_.refs_2_ = bf16[4,1024,512]{2,1,0:T(8,128)(2,1)} fusion(bf16[4,1024,256]{2,1,0:T(8,128)(2,1)S(1)} %fusion.4.f_ref, bf16[256,256]{1,0:T(8,128)(2,1)S(1)} %copy-done.6, bf16[256,256]{1,0:T(8,128)(2,1)S(1)} %copy-done.7), kind=kOutput, calls=%fused_computation.8 | convolution fusion | flops 1076363264 | bytes 6553600 | tf_op jit(solution)/shard_map/dot_general | solution.py:249
  77.1 18.7 %shard_map.150 = (f32[4,200,8]{2,1,0:T(8,128)}, f32[4,200,8]{2,1,0:T(8,128)}, f32[4,200,256]{2,1,0:T(8,128)}) custom-call(bf16[4,1600,256]{2,1,0:T(8,128)(2,1)} %bitcast_select_fusion.refs_0_, bf16[4,1024,512]{2,1,0:T(8,128)(2,1)} %convolution_convert_fusion.refs_1_.refs_2_, bf16[4,1024,512]{2,1,0:T(8,128)(2,1)} %convolution_convert_fusion.refs_1_.refs_2_, ...), custom_call_target="tpu_custom_call" | custom-call | tf_op jit(solution)/shard_map/pallas_call | solution.py:148
  95.8 1.2 reshape.137
  97.0 1.2 reshape.138
  98.2 1.2 convert_element_type.64
  99.4 0.5 convert_element_type.65
  100.1 0.5 broadcast.108
  100.6 0.9 reduce.7
  101.5 0.6 reshape.151
  102.1 18.0 %all_to_all.21 = bf16[128,2,900]{2,1,0:T(2,128)(2,1)S(1)} all-to-all(bf16[128,2,900]{2,1,0:T(2,128)(2,1)S(1)} %reshape.151), channel_id=1, replica_groups=mesh['rows'=16,'cols'=8] {'rows','cols'}, dimensions={0} | all-to-all | bytes 921600 | tf_op jit(solution)/shard_map/all_to_all | solution.py:276
  120.2 0.7 reshape.152
  120.9 0.9 copy.48
  122.3 0.3 fusion.12
  122.7 0.5 broadcast_in_dim.78
  123.2 3.3 %reduce.8 = bf16[128,1600]{1,0:T(8,128)(2,1)S(1)} reduce(bf16[128,1,1600]{2,1,0:T(2,128)(2,1)S(1)} %broadcast_in_dim.78, bf16[]{:T(256)} %broadcast.108), dimensions={1}, to_apply=%broadcast_in_dim.78.reduce_sub_computation | reduce | bytes 819202 | tf_op jit(solution)/shard_map/broadcast_in_dim | solution.py:287
  126.5 0.5 reshape.153
  127.0 17.3 %all_to_all.22 = bf16[128,2,800]{2,1,0:T(2,128)(2,1)S(1)} all-to-all(bf16[128,2,800]{2,1,0:T(2,128)(2,1)S(1)} %reshape.153), channel_id=1, replica_groups=mesh['rows'=16,'cols'=8] {'rows','cols'}, dimensions={0} | all-to-all | bytes 819200 | tf_op jit(solution)/shard_map/all_to_all | solution.py:286
  144.3 0.6 reshape.154
  145.0 2.7 %reduce.6 = bf16[128,1600]{1,0:T(8,128)(2,1)S(1)} reduce(bf16[128,1,1600]{2,1,0:T(2,128)(2,1)S(1)} %reshape.154, bf16[]{:T(256)} %constant.43), dimensions={1}, to_apply=%all_to_all.17.reduce_sub_computation | reduce | bytes 819202 | tf_op jit(solution)/shard_map/all_to_all | solution.py:286
  147.7 0.6 reshape.140
  148.3 0.4 fusion.36
  148.7 0.4 multiply_reduce_fusion.1
  149.1 0.3 multiply_add_fusion
  149.5 1.2 convolution_convert_fusion.1.e_ref
  150.7 4.6 %shard_map.151 = bf16[4,1600,128]{2,1,0:T(8,128)(2,1)} custom-call(bf16[4,200,256]{2,1,0:T(8,128)(2,1)} %convolution_convert_fusion.1.e_ref, bf16[4,1024,256]{2,1,0:T(8,128)(2,1)} %copy-done.1), custom_call_target="tpu_custom_call" | custom-call | tf_op jit(solution)/shard_map/pallas_call | solution.py:186
  (63 shorter events, 2.7 us)
Async XLA Ops:
  0.6 29.0 %copy-start = (bf16[3,3,256,256]{3,2,1,0:T(8,128)(2,1)S(1)}, bf16[3,3,256,256]{3,2,1,0:T(8,128)(2,1)}, u32[]{:S(2)}) copy-start(bf16[3,3,256,256]{3,2,1,0:T(8,128)(2,1)} %param.17) | copy-start | bytes 3538948
  0.6 11.6 %copy-start.4 = (bf16[4,8,128,256]{3,2,1,0:T(8,128)(2,1)S(1)}, bf16[4,8,128,256]{3,2,1,0:T(8,128)(2,1)}, u32[]{:S(2)}) copy-start(bf16[4,8,128,256]{3,2,1,0:T(8,128)(2,1)} %param.14) | copy-start | bytes 6291460
  2.1 9.3 %collective-permute-start = (bf16[4,1,128,256]{3,0,2,1:T(4,128)(2,1)S(1)}, bf16[4,1,128,256]{3,0,2,1:T(4,128)(2,1)S(1)}, u32[]{:S(2)}, u32[]{:S(2)}) collective-permute-start(bf16[4,1,128,256]{3,0,2,1:T(4,128)(2,1)S(1)} %copy.51), channel_id=1, source_target_pairs={{0,8},{8,16},{16,24},{24,32},{32,40},{40,48},{48,56},{56,64},{64,7... | collective-permute-start | bytes 786440 | tf_op jit(solution)/shard_map/ppermute | solution.py:21
  6.7 9.1 %collective-permute-start.1 = (bf16[4,1,128,256]{3,0,2,1:T(4,128)(2,1)S(1)}, bf16[4,1,128,256]{3,0,2,1:T(4,128)(2,1)S(1)}, u32[]{:S(2)}, u32[]{:S(2)}) collective-permute-start(bf16[4,1,128,256]{3,0,2,1:T(4,128)(2,1)S(1)} %copy.52), channel_id=1, source_target_pairs={{8,0},{16,8},{24,16},{32,24},{40,32},{48,40},{56,48},{64,56},{72,6... | collective-permute-start | bytes 786440 | tf_op jit(solution)/shard_map/ppermute | solution.py:23
  17.4 12.2 %collective-permute-start.2 = (bf16[4,10,1,256]{3,0,2,1:T(4,128)(2,1)S(1)}, bf16[4,10,1,256]{3,0,2,1:T(4,128)(2,1)S(1)}, u32[]{:S(2)}, u32[]{:S(2)}) collective-permute-start(bf16[4,10,1,256]{3,0,2,1:T(4,128)(2,1)S(1)} %get-tuple-element.20), channel_id=1, source_target_pairs={{0,1},{1,2},{2,3},{3,4},{4,5},{5,6},{6,7},{8,9},{9,10},{10,11},{11... | collective-permute-start | bytes 61448 | tf_op jit(solution)/shard_map/ppermute | solution.py:21
  22.1 7.5 %collective-permute-start.3 = (bf16[4,10,1,256]{3,0,2,1:T(4,128)(2,1)S(1)}, bf16[4,10,1,256]{3,0,2,1:T(4,128)(2,1)S(1)}, u32[]{:S(2)}, u32[]{:S(2)}) collective-permute-start(bf16[4,10,1,256]{3,0,2,1:T(4,128)(2,1)S(1)} %get-tuple-element.21), channel_id=1, source_target_pairs={{1,0},{2,1},{3,2},{4,3},{5,4},{6,5},{7,6},{9,8},{10,9},{11,10},{12... | collective-permute-start | bytes 61448 | tf_op jit(solution)/shard_map/ppermute | solution.py:23
  29.6 25.2 %copy-start.5 = (f32[4,200,256]{2,1,0:T(8,128)S(1)}, f32[4,200,256]{2,1,0:T(8,128)}, u32[]{:S(2)}) copy-start(f32[4,200,256]{2,1,0:T(8,128)} %param.16) | copy-start | bytes 2457604
  29.6 25.2 %copy-start.11 = (bf16[256,256]{1,0:T(8,128)(2,1)S(1)}, bf16[256,256]{1,0:T(8,128)(2,1)}, u32[]{:S(2)}) copy-start(bf16[256,256]{1,0:T(8,128)(2,1)} %param.20) | copy-start | bytes 393220
  43.9 25.1 %all-to-all-start = ((f32[128,1,1056]{2,1,0:T(1,128)}), f32[128,1,1056]{2,1,0:T(1,128)S(1)}, u32[]{:S(2)}, u32[]{:S(2)}) async-start(f32[128,1,1056]{2,1,0:T(1,128)} %broadcast_in_dim.72), calls=%async_computation | async-start | bytes 1179648 | tf_op jit(solution)/shard_map/all_to_all | solution.py:235
  54.9 3.1 %copy-start.2 = (f32[4,8,128,256]{3,0,2,1:T(4,128)S(1)}, f32[4,8,128,256]{3,0,2,1:T(4,128)}, u32[]{:S(2)}) copy-start(f32[4,8,128,256]{3,0,2,1:T(4,128)} %get-tuple-element.26) | copy-start | bytes 12582916
  57.9 13.0 %copy-start.12 = (f32[256]{0:T(256)S(1)}, f32[256]{0:T(256)}, u32[]{:S(2)}) copy-start(f32[256]{0:T(256)} %param.19) | copy-start | bytes 3076
  57.9 13.0 %copy-start.13 = (f32[256]{0:T(256)S(1)}, f32[256]{0:T(256)}, u32[]{:S(2)}) copy-start(f32[256]{0:T(256)} %param.18) | copy-start | bytes 3076
  70.9 3.0 %copy-start.6 = (bf16[256,256]{1,0:T(8,128)(2,1)S(1)}, bf16[256,256]{1,0:T(8,128)(2,1)}, u32[]{:S(2)}) copy-start(bf16[256,256]{1,0:T(8,128)(2,1)} %param.22) | copy-start | bytes 393220
  70.9 3.0 %copy-start.7 = (bf16[256,256]{1,0:T(8,128)(2,1)S(1)}, bf16[256,256]{1,0:T(8,128)(2,1)}, u32[]{:S(2)}) copy-start(bf16[256,256]{1,0:T(8,128)(2,1)} %param.21) | copy-start | bytes 393220
  73.9 3.2 %copy-start.1 = (bf16[4,1024,256]{2,1,0:T(8,128)(2,1)}, bf16[4,1024,256]{2,1,0:T(8,128)(2,1)S(1)}, u32[]{:S(2)}) copy-start(bf16[4,1024,256]{2,1,0:T(8,128)(2,1)S(1)} %fusion.4.f_ref) | copy-start | bytes 6291460
  126.5 21.8 %copy-start.8 = (bf16[256,256]{1,0:T(8,128)(2,1)S(1)}, bf16[256,256]{1,0:T(8,128)(2,1)}, u32[]{:S(2)}) copy-start(bf16[256,256]{1,0:T(8,128)(2,1)} %param.23) | copy-start | bytes 393220
  145.0 4.2 %copy-start.14 = (f32[256]{0:T(256)S(1)}, f32[256]{0:T(256)}, u32[]{:S(2)}) copy-start(f32[256]{0:T(256)} %param.25) | copy-start | bytes 3076
  145.0 4.2 %copy-start.15 = (f32[256]{0:T(256)S(1)}, f32[256]{0:T(256)}, u32[]{:S(2)}) copy-start(f32[256]{0:T(256)} %param.24) | copy-start | bytes 3076
  147.7 1.8 %copy-start.9 = (bf16[256,256]{1,0:T(8,128)(2,1)S(1)}, bf16[256,256]{1,0:T(8,128)(2,1)}, u32[]{:S(2)}) copy-start(bf16[256,256]{1,0:T(8,128)(2,1)} %param.27) | copy-start | bytes 393220
  147.7 1.8 %copy-start.10 = (bf16[256,256]{1,0:T(8,128)(2,1)S(1)}, bf16[256,256]{1,0:T(8,128)(2,1)}, u32[]{:S(2)}) copy-start(bf16[256,256]{1,0:T(8,128)(2,1)} %param.26) | copy-start | bytes 393220
  149.5 5.8 %copy-start.3 = (f32[4,200,256]{2,1,0:T(8,128)}, f32[4,200,256]{2,1,0:T(8,128)S(1)}, u32[]{:S(2)}) copy-start(f32[4,200,256]{2,1,0:T(8,128)S(1)} %multiply_add_fusion) | copy-start | bytes 2457604

commit v12 on v11

--- a/solution.py
+++ b/solution.py
@@ -231,14 +231,24 @@
     grouped = conv.reshape(images, pixels, GROUPS, width // GROUPS)
     first_sum = jnp.sum(grouped, axis=(1, 3))
     second_sum = jnp.sum(grouped * grouped, axis=(1, 3))
-    stats = jnp.concatenate([local_count[..., 0], first_sum, second_sum], axis=1).reshape(1, -1)
+    present = jnp.minimum(local_count[..., 0], 1.0).reshape(1, -1)
+    sums = jnp.concatenate([first_sum, second_sum], axis=1).reshape(1, -1)
+    high = sums.astype(jnp.bfloat16)
+    rest = sums - high.astype(jnp.float32)
+    middle = rest.astype(jnp.bfloat16)
+    low = (rest - middle.astype(jnp.float32)).astype(jnp.bfloat16)
+    stats = jnp.concatenate([present.astype(jnp.bfloat16), high, middle, low], axis=1)
     stats = lax.all_to_all(
         jnp.broadcast_to(stats, (devices, stats.shape[1])), ("rows", "cols"), 0, 0, tiled=True
-    )
-    stats = jnp.sum(stats, axis=0).reshape(images, -1)
-    count = stats[:, :query_count]
-    first_sum = stats[:, query_count : query_count + GROUPS]
-    second_sum = stats[:, query_count + GROUPS :]
+    ).astype(jnp.float32)
+    flags = images * query_count
+    count = jnp.sum(stats[:, :flags], axis=0).reshape(images, query_count)
+    parts = stats[:, flags:]
+    width_sums = parts.shape[1] // 3
+    parts = parts[:, :width_sums] + parts[:, width_sums : 2 * width_sums] + parts[:, 2 * width_sums :]
+    sums = jnp.sum(parts, axis=0).reshape(images, 2 * GROUPS)
+    first_sum = sums[:, :GROUPS]
+    second_sum = sums[:, GROUPS:]
     number = devices * pixels * (width // GROUPS)
     mean = first_sum / number
     var = second_sum / number - mean * mean

time: 156 us -> 162 us (1.038)
  local copies, waits for them, and re-layouts: 21.2 us -> 26.4 us
  other arithmetic: 16.7 us -> 19.9 us
  waiting for transfers between devices: 12.5 us -> 10 us
    unnamed x40 -> x42, local copies, waits for them, and re-layouts: 7.1 us -> 10.6 us
    ppermute x2, waiting for transfers between devices: 3.45 us -> 0.01 us  [with_halo(): lax.ppermute(tail, axis, [(i, (i + 1) % count) for i in range(ends)])]
    broadcast_in_dim x1, other arithmetic: 0.01 us -> 3.29 us  [on_device(): jnp.broadcast_to(stats, (devices, stats.shape[1]))]
    ppermute x2, waiting for transfers between devices: 0.66 us -> 3.06 us  [with_halo(): lax.ppermute(head, axis, [((i + 1) % count, i) for i in range(ends)])]
  transfers between devices with their start and end apart: 5 -> 5, of which waited for: 3 -> 2; matrix products, arithmetic and copies ran while one was open for 7% -> 7% of each run, Pallas kernels for 3% -> 3%
where the time goes in v12:
time: 162 us; the launch traced here: 161 us
  blocking collectives  35.4 us (22%)
  Pallas kernels  27.6 us (17%)
  local copies, waits for them, and re-layouts  26.4 us (16%)
  starting transfers between devices  22.6 us (14%)
  other arithmetic  19.9 us (12%)
  matrix products  17.6 us (11%)
  waiting for transfers between devices  10 us (6%)
    pallas_call x1, Pallas kernels, attention(): pl.pallas_call(kernel, grid=(images,), in_specs=[pl.BlockSpec((1, heads *...  18.7 us
    all_to_all x1, blocking collectives, on_device(): lax.all_to_all(packed, ('rows', 'cols'), 0, 0, tiled=True)  18.1 us
    all_to_all x1, blocking collectives, on_device(): lax.all_to_all(jnp.broadcast_to(attn_block, (devices, span)), ('rows', 'c...  17.3 us
    conv_general_dilated x1, matrix products, on_device(): lax.conv_general_dilated(padded, conv_weight, (1, 1), 'VALID', dimension_...  12.5 us
    unnamed x42, local copies, waits for them, and re-layouts  10.6 us
    all_to_all x1, starting transfers between devices, on_device(): lax.all_to_all(jnp.broadcast_to(stats, (devices, stats.shape[1])), ('rows...  10.3 us
    ppermute x2, starting transfers between devices, with_halo(): lax.ppermute(tail, axis, [(i, (i + 1) % count) for i in range(ends)])  9.1 us
    all_to_all x1, waiting for transfers between devices, on_device(): lax.all_to_all(jnp.broadcast_to(stats, (devices, stats.shape[1])), ('rows...  6.98 us
  transfers between devices with their start and end apart: 5, of which 2 were waited for; matrix products, arithmetic and copies ran while one was open for 7% of the time, Pallas kernels for 3%

profile of v12, /device:TPU:1, one launch (start us, length us, event | category | flops | bytes accessed | tf_op | source)
XLA Modules:
  0.0 160.7 jit_solution(8473098493449697755)
XLA Ops:
  0.6 1.2 fusion.35
  1.8 0.9 copy.36
  2.7 5.1 %collective-permute-start = (bf16[4,1,128,256]{3,0,2,1:T(4,128)(2,1)}, bf16[4,1,128,256]{3,0,2,1:T(4,128)(2,1)}, u32[]{:S(2)}, u32[]{:S(2)}) collective-permute-start(bf16[4,1,128,256]{3,0,2,1:T(4,128)(2,1)} %copy.36), channel_id=1, source_target_pairs={{0,8},{8,16},{16,24},{24,32},{32,40},{40,48},{48,56},{56,64},{64,7... | collective-permute-start | bytes 786440 | tf_op jit(solution)/shard_map/ppermute | solution.py:21
  8.0 1.3 collective-permute-start.1
  9.3 4.3 %shard_map.149 = (bf16[4,200,1024]{2,1,0:T(8,128)(2,1)}, f32[4,200,1]{2,1,0:T(8,128)}) custom-call(s32[4,1600,128]{2,1,0:T(8,128)} %bitcast.46), custom_call_target="tpu_custom_call" | custom-call | tf_op jit(solution)/shard_map/pallas_call | solution.py:105
  13.6 1.2 fusion.19
  14.9 1.7 %constant_dynamic-update-slice_fusion.2 = bf16[4,10,128,256]{3,0,2,1:T(4,128)(2,1)} fusion(bf16[4,1,128,256]{3,0,2,1:T(4,128)(2,1)} %collective-permute-done), kind=kLoop, calls=%fused_computation.52 | loop fusion | bytes 524288
  16.6 3.0 %constant_dynamic-update-slice_fusion.1 = bf16[4,10,128,256]{3,0,2,1:T(4,128)(2,1)} fusion(bf16[4,10,128,256]{3,0,2,1:T(4,128)(2,1)} %constant_dynamic-update-slice_fusion.2, bf16[4,8,128,256]{3,2,1,0:T(8,128)(2,1)S(1)} %copy-done.4), kind=kLoop, calls=%fused_computation.51 | loop fusion | bytes 4194304
  19.6 1.7 %constant_dynamic-update-slice_fusion = bf16[4,10,128,256]{3,0,2,1:T(4,128)(2,1)} fusion(bf16[4,10,128,256]{3,0,2,1:T(4,128)(2,1)} %constant_dynamic-update-slice_fusion.1, bf16[4,1,128,256]{3,0,2,1:T(4,128)(2,1)} %collective-permute-done.1), kind=kLoop, calls=%fused_computation.50 | loop fusion | bytes 524288 | tf_op jit(solution)/shard_map/concatenate | solution.py:19
  21.3 0.8 fusion.34
  22.1 4.0 %collective-permute-start.2 = (bf16[4,10,1,256]{3,0,2,1:T(4,128)(2,1)S(1)}, bf16[4,10,1,256]{3,0,2,1:T(4,128)(2,1)S(1)}, u32[]{:S(2)}, u32[]{:S(2)}) collective-permute-start(bf16[4,10,1,256]{3,0,2,1:T(4,128)(2,1)S(1)} %get-tuple-element.20), channel_id=1, source_target_pairs={{0,1},{1,2},{2,3},{3,4},{4,5},{5,6},{6,7},{8,9},{9,10},{10,11},{11... | collective-permute-start | bytes 61448 | tf_op jit(solution)/shard_map/ppermute | solution.py:21
  26.1 1.9 %collective-permute-start.3 = (bf16[4,10,1,256]{3,0,2,1:T(4,128)(2,1)S(1)}, bf16[4,10,1,256]{3,0,2,1:T(4,128)(2,1)S(1)}, u32[]{:S(2)}, u32[]{:S(2)}) collective-permute-start(bf16[4,10,1,256]{3,0,2,1:T(4,128)(2,1)S(1)} %get-tuple-element.21), channel_id=1, source_target_pairs={{1,0},{2,1},{3,2},{4,3},{5,4},{6,5},{7,6},{9,8},{10,9},{11,10},{12... | collective-permute-start | bytes 61448 | tf_op jit(solution)/shard_map/ppermute | solution.py:23
  28.2 3.1 %collective-permute-done.3 = bf16[4,10,1,256]{3,0,2,1:T(4,128)(2,1)S(1)} collective-permute-done((bf16[4,10,1,256]{3,0,2,1:T(4,128)(2,1)S(1)}, bf16[4,10,1,256]{3,0,2,1:T(4,128)(2,1)S(1)}, u32[]{:S(2)}, u32[]{:S(2)}) %collective-permute-start.3) | collective-permute-done | bytes 20512 | tf_op jit(solution)/shard_map/ppermute | solution.py:23
  31.2 12.5 %fusion.33 = (f32[4,256]{1,0:T(4,128)S(1)}, f32[4,256]{1,0:T(4,128)S(1)}, f32[4,8,128,256]{3,0,2,1:T(4,128)}) fusion(bf16[3,3,256,256]{3,2,1,0:T(8,128)(2,1)S(1)} %copy-done, bf16[4,10,1,256]{3,0,2,1:T(4,128)(2,1)S(1)} %collective-permute-done.3, bf16[4,10,128,256]{3,0,2,1:T(4,128)(2,1)} %constant_dynamic-update-slice_fusion, ...), kind=kOutput, calls=%fused_computation.71 | convolution fusion | flops 4842969088 | bytes 8044544 | tf_op jit(solution)/shard_map/conv_general_dilated | solution.py:223
  44.4 0.4 broadcast_in_dim.65
  44.9 0.6 broadcast.129
  45.5 3.3 %reduce.8 = bf16[128,1568]{1,0:T(8,128)(2,1)S(1)} reduce(bf16[128,1,1568]{2,1,0:T(2,128)(2,1)S(1)} %broadcast_in_dim.65, bf16[]{:T(256)} %broadcast.129), dimensions={1}, to_apply=%broadcast_in_dim.65.reduce_sub_computation | reduce | bytes 802818 | tf_op jit(solution)/shard_map/broadcast_in_dim | solution.py:242
  48.8 1.2 reshape.251
  50.0 10.3 %all-to-all-start = ((bf16[128,2,784]{2,1,0:T(2,128)(2,1)}), bf16[128,2,784]{2,1,0:T(2,128)(2,1)S(1)}, u32[]{:S(2)}, u32[]{:S(2)}) async-start(bf16[128,2,784]{2,1,0:T(2,128)(2,1)} %reshape.251), calls=%async_computation | async-start | bytes 917504 | tf_op jit(solution)/shard_map/all_to_all | solution.py:241
  60.7 2.2 %bitcast_select_fusion.refs_0_ = bf16[4,1600,256]{2,1,0:T(8,128)(2,1)} fusion(pred[1600,256]{1,0:T(8,128)(4,1)S(1)} %bitcast.50, bf16[4,200,256]{2,1,0:T(8,128)(2,1)S(1)} %convolution_convert_fusion.2), kind=kLoop, calls=%fused_computation.7 | loop fusion | flops 1638400 | bytes 4096000 | tf_op jit(solution)/shard_map/jit(_where)/select_n | solution.py:267
  62.9 0.4 copy-done.2
  63.3 2.7 %copy.30 = f32[4,8,128,256]{3,2,1,0:T(8,128)} copy(f32[4,8,128,256]{3,0,2,1:T(4,128)S(1)} %copy-done.2) | data formatting | bytes 8388608 | tf_op jit(solution)/shard_map/conv_general_dilated | solution.py:223
  66.0 7.0 %all-to-all-done = bf16[128,2,784]{2,1,0:T(2,128)(2,1)S(1)} async-done(((bf16[128,2,784]{2,1,0:T(2,128)(2,1)}), bf16[128,2,784]{2,1,0:T(2,128)(2,1)S(1)}, u32[]{:S(2)}, u32[]{:S(2)}) %all-to-all-start) | async-done | bytes 401440 | tf_op jit(solution)/shard_map/all_to_all | solution.py:241
  73.0 0.6 reshape.252
  73.6 1.2 copy.31
  75.8 1.0 reshape.247.refs_4_
  76.8 3.0 %fusion.4.f_ref = bf16[4,1024,256]{2,1,0:T(8,128)(2,1)S(1)} fusion(f32[4,8,128,256]{3,2,1,0:T(8,128)} %copy.30, f32[256]{0:T(256)S(1)} %copy-done.12, f32[256]{0:T(256)S(1)} %copy-done.13, f32[4,256]{1,0:T(4,128)S(1)} %div.54, f32[4,256]{1,0:T(4,128)S(1)} %sub.78), kind=kLoop, calls=%fused_computation.6 | loop fusion | flops 6291456 | bytes 6301696 | tf_op jit(solution)/shard_map/convert_element_type | solution.py:256
  79.9 3.2 %convolution_convert_fusion.refs_1_.refs_2_ = bf16[4,1024,512]{2,1,0:T(8,128)(2,1)} fusion(bf16[4,1024,256]{2,1,0:T(8,128)(2,1)S(1)} %fusion.4.f_ref, bf16[256,256]{1,0:T(8,128)(2,1)S(1)} %copy-done.6, bf16[256,256]{1,0:T(8,128)(2,1)S(1)} %copy-done.7), kind=kOutput, calls=%fused_computation.8 | convolution fusion | flops 1076363264 | bytes 6553600 | tf_op jit(solution)/shard_map/dot_general | solution.py:259
  83.1 18.7 %shard_map.150 = (f32[4,200,8]{2,1,0:T(8,128)}, f32[4,200,8]{2,1,0:T(8,128)}, f32[4,200,256]{2,1,0:T(8,128)}) custom-call(bf16[4,1600,256]{2,1,0:T(8,128)(2,1)} %bitcast_select_fusion.refs_0_, bf16[4,1024,512]{2,1,0:T(8,128)(2,1)} %convolution_convert_fusion.refs_1_.refs_2_, bf16[4,1024,512]{2,1,0:T(8,128)(2,1)} %convolution_convert_fusion.refs_1_.refs_2_, ...), custom_call_target="tpu_custom_call" | custom-call | tf_op jit(solution)/shard_map/pallas_call | solution.py:148
  101.7 1.2 reshape.234
  102.9 1.2 reshape.235
  104.1 1.2 convert_element_type.178
  105.3 0.5 convert_element_type.179
  106.0 0.9 reduce.9
  106.9 0.6 reshape.253
  107.5 18.1 %all_to_all.21 = bf16[128,2,900]{2,1,0:T(2,128)(2,1)S(1)} all-to-all(bf16[128,2,900]{2,1,0:T(2,128)(2,1)S(1)} %reshape.253), channel_id=1, replica_groups=mesh['rows'=16,'cols'=8] {'rows','cols'}, dimensions={0} | all-to-all | bytes 921600 | tf_op jit(solution)/shard_map/all_to_all | solution.py:286
  125.6 0.7 reshape.254
  126.4 0.9 copy.34
  128.2 0.5 broadcast_in_dim.69
  128.7 3.3 %reduce.10 = bf16[128,1600]{1,0:T(8,128)(2,1)S(1)} reduce(bf16[128,1,1600]{2,1,0:T(2,128)(2,1)S(1)} %broadcast_in_dim.69, bf16[]{:T(256)} %broadcast.129), dimensions={1}, to_apply=%broadcast_in_dim.69.reduce_sub_computation | reduce | bytes 819202 | tf_op jit(solution)/shard_map/broadcast_in_dim | solution.py:297
  132.0 0.5 reshape.255
  132.4 17.3 %all_to_all.22 = bf16[128,2,800]{2,1,0:T(2,128)(2,1)S(1)} all-to-all(bf16[128,2,800]{2,1,0:T(2,128)(2,1)S(1)} %reshape.255), channel_id=1, replica_groups=mesh['rows'=16,'cols'=8] {'rows','cols'}, dimensions={0} | all-to-all | bytes 819200 | tf_op jit(solution)/shard_map/all_to_all | solution.py:296
  149.8 0.6 reshape.256
  150.4 2.7 %reduce.6 = bf16[128,1600]{1,0:T(8,128)(2,1)S(1)} reduce(bf16[128,1,1600]{2,1,0:T(2,128)(2,1)S(1)} %reshape.256, bf16[]{:T(256)} %constant.44), dimensions={1}, to_apply=%all_to_all.17.reduce_sub_computation | reduce | bytes 819202 | tf_op jit(solution)/shard_map/all_to_all | solution.py:296
  153.1 0.6 reshape.237
  153.8 0.4 fusion.36
  154.9 1.2 convolution_convert_fusion.1.e_ref
  156.2 4.6 %shard_map.151 = bf16[4,1600,128]{2,1,0:T(8,128)(2,1)} custom-call(bf16[4,200,256]{2,1,0:T(8,128)(2,1)} %convolution_convert_fusion.1.e_ref, bf16[4,1024,256]{2,1,0:T(8,128)(2,1)} %copy-done.1), custom_call_target="tpu_custom_call" | custom-call | tf_op jit(solution)/shard_map/pallas_call | solution.py:186
  (73 shorter events, 4.1 us)
Async XLA Ops:
  0.6 30.6 %copy-start = (bf16[3,3,256,256]{3,2,1,0:T(8,128)(2,1)S(1)}, bf16[3,3,256,256]{3,2,1,0:T(8,128)(2,1)}, u32[]{:S(2)}) copy-start(bf16[3,3,256,256]{3,2,1,0:T(8,128)(2,1)} %param.17) | copy-start | bytes 3538948
  1.8 14.8 %copy-start.4 = (bf16[4,8,128,256]{3,2,1,0:T(8,128)(2,1)S(1)}, bf16[4,8,128,256]{3,2,1,0:T(8,128)(2,1)}, u32[]{:S(2)}) copy-start(bf16[4,8,128,256]{3,2,1,0:T(8,128)(2,1)} %param.14) | copy-start | bytes 6291460
  2.7 12.1 %collective-permute-start = (bf16[4,1,128,256]{3,0,2,1:T(4,128)(2,1)}, bf16[4,1,128,256]{3,0,2,1:T(4,128)(2,1)}, u32[]{:S(2)}, u32[]{:S(2)}) collective-permute-start(bf16[4,1,128,256]{3,0,2,1:T(4,128)(2,1)} %copy.36), channel_id=1, source_target_pairs={{0,8},{8,16},{16,24},{24,32},{32,40},{40,48},{48,56},{56,64},{64,7... | collective-permute-start | bytes 786440 | tf_op jit(solution)/shard_map/ppermute | solution.py:21
  8.0 11.6 %collective-permute-start.1 = (bf16[4,1,128,256]{3,0,2,1:T(4,128)(2,1)S(1)}, bf16[4,1,128,256]{3,0,2,1:T(4,128)(2,1)}, u32[]{:S(2)}, u32[]{:S(2)}) collective-permute-start(bf16[4,1,128,256]{3,0,2,1:T(4,128)(2,1)S(1)} %copy.37), channel_id=1, source_target_pairs={{8,0},{16,8},{24,16},{32,24},{40,32},{48,40},{56,48},{64,56},{72,6... | collective-permute-start | bytes 786440 | tf_op jit(solution)/shard_map/ppermute | solution.py:23
  22.1 6.1 %collective-permute-start.2 = (bf16[4,10,1,256]{3,0,2,1:T(4,128)(2,1)S(1)}, bf16[4,10,1,256]{3,0,2,1:T(4,128)(2,1)S(1)}, u32[]{:S(2)}, u32[]{:S(2)}) collective-permute-start(bf16[4,10,1,256]{3,0,2,1:T(4,128)(2,1)S(1)} %get-tuple-element.20), channel_id=1, source_target_pairs={{0,1},{1,2},{2,3},{3,4},{4,5},{5,6},{6,7},{8,9},{9,10},{10,11},{11... | collective-permute-start | bytes 61448 | tf_op jit(solution)/shard_map/ppermute | solution.py:21
  26.1 5.1 %collective-permute-start.3 = (bf16[4,10,1,256]{3,0,2,1:T(4,128)(2,1)S(1)}, bf16[4,10,1,256]{3,0,2,1:T(4,128)(2,1)S(1)}, u32[]{:S(2)}, u32[]{:S(2)}) collective-permute-start(bf16[4,10,1,256]{3,0,2,1:T(4,128)(2,1)S(1)} %get-tuple-element.21), channel_id=1, source_target_pairs={{1,0},{2,1},{3,2},{4,3},{5,4},{6,5},{7,6},{9,8},{10,9},{11,10},{12... | collective-permute-start | bytes 61448 | tf_op jit(solution)/shard_map/ppermute | solution.py:23
  43.7 16.5 %copy-start.5 = (f32[4,200,256]{2,1,0:T(8,128)S(1)}, f32[4,200,256]{2,1,0:T(8,128)}, u32[]{:S(2)}) copy-start(f32[4,200,256]{2,1,0:T(8,128)} %param.16) | copy-start | bytes 2457604
  43.7 16.5 %copy-start.11 = (bf16[256,256]{1,0:T(8,128)(2,1)S(1)}, bf16[256,256]{1,0:T(8,128)(2,1)}, u32[]{:S(2)}) copy-start(bf16[256,256]{1,0:T(8,128)(2,1)} %param.20) | copy-start | bytes 393220
  50.0 23.0 %all-to-all-start = ((bf16[128,2,784]{2,1,0:T(2,128)(2,1)}), bf16[128,2,784]{2,1,0:T(2,128)(2,1)S(1)}, u32[]{:S(2)}, u32[]{:S(2)}) async-start(bf16[128,2,784]{2,1,0:T(2,128)(2,1)} %reshape.251), calls=%async_computation | async-start | bytes 917504 | tf_op jit(solution)/shard_map/all_to_all | solution.py:241
  60.3 3.0 %copy-start.2 = (f32[4,8,128,256]{3,0,2,1:T(4,128)S(1)}, f32[4,8,128,256]{3,0,2,1:T(4,128)}, u32[]{:S(2)}) copy-start(f32[4,8,128,256]{3,0,2,1:T(4,128)} %get-tuple-element.29) | copy-start | bytes 12582916
  66.0 10.8 %copy-start.12 = (f32[256]{0:T(256)S(1)}, f32[256]{0:T(256)}, u32[]{:S(2)}) copy-start(f32[256]{0:T(256)} %param.19) | copy-start | bytes 3076
  66.0 10.8 %copy-start.13 = (f32[256]{0:T(256)S(1)}, f32[256]{0:T(256)}, u32[]{:S(2)}) copy-start(f32[256]{0:T(256)} %param.18) | copy-start | bytes 3076
  76.8 3.0 %copy-start.6 = (bf16[256,256]{1,0:T(8,128)(2,1)S(1)}, bf16[256,256]{1,0:T(8,128)(2,1)}, u32[]{:S(2)}) copy-start(bf16[256,256]{1,0:T(8,128)(2,1)} %param.22) | copy-start | bytes 393220
  76.8 3.0 %copy-start.7 = (bf16[256,256]{1,0:T(8,128)(2,1)S(1)}, bf16[256,256]{1,0:T(8,128)(2,1)}, u32[]{:S(2)}) copy-start(bf16[256,256]{1,0:T(8,128)(2,1)} %param.21) | copy-start | bytes 393220
  79.9 3.2 %copy-start.1 = (bf16[4,1024,256]{2,1,0:T(8,128)(2,1)}, bf16[4,1024,256]{2,1,0:T(8,128)(2,1)S(1)}, u32[]{:S(2)}) copy-start(bf16[4,1024,256]{2,1,0:T(8,128)(2,1)S(1)} %fusion.4.f_ref) | copy-start | bytes 6291460
  132.0 21.8 %copy-start.8 = (bf16[256,256]{1,0:T(8,128)(2,1)S(1)}, bf16[256,256]{1,0:T(8,128)(2,1)}, u32[]{:S(2)}) copy-start(bf16[256,256]{1,0:T(8,128)(2,1)} %param.23) | copy-start | bytes 393220
  150.4 4.2 %copy-start.14 = (f32[256]{0:T(256)S(1)}, f32[256]{0:T(256)}, u32[]{:S(2)}) copy-start(f32[256]{0:T(256)} %param.25) | copy-start | bytes 3076
  150.4 4.2 %copy-start.15 = (f32[256]{0:T(256)S(1)}, f32[256]{0:T(256)}, u32[]{:S(2)}) copy-start(f32[256]{0:T(256)} %param.24) | copy-start | bytes 3076
  153.1 1.8 %copy-start.9 = (bf16[256,256]{1,0:T(8,128)(2,1)S(1)}, bf16[256,256]{1,0:T(8,128)(2,1)}, u32[]{:S(2)}) copy-start(bf16[256,256]{1,0:T(8,128)(2,1)} %param.27) | copy-start | bytes 393220
  153.8 1.2 copy-start.10
  154.9 5.8 %copy-start.3 = (f32[4,200,256]{2,1,0:T(8,128)}, f32[4,200,256]{2,1,0:T(8,128)S(1)}, u32[]{:S(2)}) copy-start(f32[4,200,256]{2,1,0:T(8,128)S(1)} %multiply_add_fusion) | copy-start | bytes 2457604

commit v13 on v11

--- a/solution.py
+++ b/solution.py
@@ -125,8 +125,6 @@
     v = v_ref[0]
     allowed = (fg_ref[0] != 0) | (zero_ref[0] != 0)
     bias = jnp.where(allowed, 0.0, -jnp.inf)
-    lane = lax.broadcasted_iota(jnp.int32, (queries, width), 1)
-    acc = jnp.zeros((queries, width), jnp.float32)
     for h in range(heads):
         q = q_ref[0, h * queries : (h + 1) * queries, :]
         s = lax.dot_general(q, k, (((1,), (1,)), ((), ())), preferred_element_type=jnp.float32) * scale
@@ -135,9 +133,7 @@
         tot_ref[0, :, h : h + 1] = jnp.sum(w.astype(jnp.float32), axis=1, keepdims=True)
         top_ref[0, :, h : h + 1] = top
         r = jnp.dot(w, v, preferred_element_type=jnp.float32)
-        inside = (lane >= h * head_size) & (lane < (h + 1) * head_size)
-        acc = acc + jnp.where(inside, r, 0.0)
-    wv_ref[0] = acc
+        wv_ref[0, :, h * head_size : (h + 1) * head_size] = r[:, h * head_size : (h + 1) * head_size]
 
 
 def attention(qbd, keys_vals, fg, zero, heads, scale):

time: 156 us -> 156 us (level)
  no operation moved by 1% of the time
where the time goes in v13:
time: 156 us; the launch traced here: 155 us
  blocking collectives  35.3 us (23%)
  Pallas kernels  27.5 us (18%)
  starting transfers between devices  23.2 us (15%)
  local copies, waits for them, and re-layouts  21.2 us (14%)
  matrix products  17.7 us (11%)
  other arithmetic  16.7 us (11%)
  waiting for transfers between devices  12.5 us (8%)
    pallas_call x1, Pallas kernels, attention(): pl.pallas_call(kernel, grid=(images,), in_specs=[pl.BlockSpec((1, heads *...  18.6 us
    all_to_all x1, blocking collectives, on_device(): lax.all_to_all(packed, ('rows', 'cols'), 0, 0, tiled=True)  18 us
    all_to_all x1, blocking collectives, on_device(): lax.all_to_all(jnp.broadcast_to(attn_block, (devices, span)), ('rows', 'c...  17.3 us
    conv_general_dilated x1, matrix products, on_device(): lax.conv_general_dilated(padded, conv_weight, (1, 1), 'VALID', dimension_...  12.6 us
    all_to_all x1, starting transfers between devices, on_device(): lax.all_to_all(jnp.broadcast_to(stats, (devices, stats.shape[1])), ('rows...  10.9 us
    ppermute x2, starting transfers between devices, with_halo(): lax.ppermute(tail, axis, [(i, (i + 1) % count) for i in range(ends)])  9.11 us
    all_to_all x1, waiting for transfers between devices, on_device(): lax.all_to_all(jnp.broadcast_to(stats, (devices, stats.shape[1])), ('rows...  8.4 us
    unnamed x40, local copies, waits for them, and re-layouts  7.1 us
  transfers between devices with their start and end apart: 5, of which 3 were waited for; matrix products, arithmetic and copies ran while one was open for 7% of the time, Pallas kernels for 3%

profile of v13, /device:TPU:1, one launch (start us, length us, event | category | flops | bytes accessed | tf_op | source)
XLA Modules:
  0.0 155.2 jit_solution(1259398959851122744)
XLA Ops:
  0.7 1.2 fusion.35
  2.1 4.4 %collective-permute-start = (bf16[4,1,128,256]{3,0,2,1:T(4,128)(2,1)S(1)}, bf16[4,1,128,256]{3,0,2,1:T(4,128)(2,1)S(1)}, u32[]{:S(2)}, u32[]{:S(2)}) collective-permute-start(bf16[4,1,128,256]{3,0,2,1:T(4,128)(2,1)S(1)} %copy.51), channel_id=1, source_target_pairs={{0,8},{8,16},{16,24},{24,32},{32,40},{40,48},{48,56},{56,64},{64,7... | collective-permute-start | bytes 786440 | tf_op jit(solution)/shard_map/ppermute | solution.py:21
  6.7 1.3 collective-permute-start.1
  8.0 3.4 %collective-permute-done = bf16[4,1,128,256]{3,0,2,1:T(4,128)(2,1)S(1)} collective-permute-done((bf16[4,1,128,256]{3,0,2,1:T(4,128)(2,1)S(1)}, bf16[4,1,128,256]{3,0,2,1:T(4,128)(2,1)S(1)}, u32[]{:S(2)}, u32[]{:S(2)}) %collective-permute-start) | collective-permute-done | bytes 262176 | tf_op jit(solution)/shard_map/ppermute | solution.py:21
  11.4 0.8 constant_dynamic-update-slice_fusion.2
  12.2 3.0 %constant_dynamic-update-slice_fusion.1 = bf16[4,10,128,256]{3,0,2,1:T(4,128)(2,1)} fusion(bf16[4,10,128,256]{3,0,2,1:T(4,128)(2,1)} %constant_dynamic-update-slice_fusion.2, bf16[4,8,128,256]{3,2,1,0:T(8,128)(2,1)S(1)} %copy-done.4), kind=kLoop, calls=%fused_computation.44 | loop fusion | bytes 4194304
  15.2 0.7 collective-permute-done.1
  15.8 0.8 constant_dynamic-update-slice_fusion
  16.6 0.8 fusion.34
  17.4 4.7 %collective-permute-start.2 = (bf16[4,10,1,256]{3,0,2,1:T(4,128)(2,1)S(1)}, bf16[4,10,1,256]{3,0,2,1:T(4,128)(2,1)S(1)}, u32[]{:S(2)}, u32[]{:S(2)}) collective-permute-start(bf16[4,10,1,256]{3,0,2,1:T(4,128)(2,1)S(1)} %get-tuple-element.20), channel_id=1, source_target_pairs={{0,1},{1,2},{2,3},{3,4},{4,5},{5,6},{6,7},{8,9},{9,10},{10,11},{11... | collective-permute-start | bytes 61448 | tf_op jit(solution)/shard_map/ppermute | solution.py:21
  22.1 1.9 %collective-permute-start.3 = (bf16[4,10,1,256]{3,0,2,1:T(4,128)(2,1)S(1)}, bf16[4,10,1,256]{3,0,2,1:T(4,128)(2,1)S(1)}, u32[]{:S(2)}, u32[]{:S(2)}) collective-permute-start(bf16[4,10,1,256]{3,0,2,1:T(4,128)(2,1)S(1)} %get-tuple-element.21), channel_id=1, source_target_pairs={{1,0},{2,1},{3,2},{4,3},{5,4},{6,5},{7,6},{9,8},{10,9},{11,10},{12... | collective-permute-start | bytes 61448 | tf_op jit(solution)/shard_map/ppermute | solution.py:23
  24.1 4.3 %shard_map.149 = (bf16[4,200,1024]{2,1,0:T(8,128)(2,1)}, f32[4,200,1]{2,1,0:T(8,128)}) custom-call(s32[4,1600,128]{2,1,0:T(8,128)} %bitcast.45), custom_call_target="tpu_custom_call" | custom-call | tf_op jit(solution)/shard_map/pallas_call | solution.py:105
  28.4 1.2 reduce.5
  29.7 12.6 %fusion.33 = (f32[4,256]{1,0:T(4,128)S(1)}, f32[4,256]{1,0:T(4,128)S(1)}, f32[4,8,128,256]{3,0,2,1:T(4,128)}) fusion(bf16[3,3,256,256]{3,2,1,0:T(8,128)(2,1)S(1)} %copy-done, bf16[4,10,1,256]{3,0,2,1:T(4,128)(2,1)S(1)} %collective-permute-done.3, bf16[4,10,128,256]{3,0,2,1:T(4,128)(2,1)} %constant_dynamic-update-slice_fusion, ...), kind=kOutput, calls=%fused_computation.65 | convolution fusion | flops 4842969088 | bytes 8044544 | tf_op jit(solution)/shard_map/conv_general_dilated | solution.py:219
  42.8 1.1 broadcast_in_dim.72
  43.9 10.9 %all-to-all-start = ((f32[128,1,1056]{2,1,0:T(1,128)}), f32[128,1,1056]{2,1,0:T(1,128)S(1)}, u32[]{:S(2)}, u32[]{:S(2)}) async-start(f32[128,1,1056]{2,1,0:T(1,128)} %broadcast_in_dim.72), calls=%async_computation | async-start | bytes 1179648 | tf_op jit(solution)/shard_map/all_to_all | solution.py:231
  55.2 2.2 %bitcast_select_fusion.refs_0_ = bf16[4,1600,256]{2,1,0:T(8,128)(2,1)} fusion(pred[1600,256]{1,0:T(8,128)(4,1)S(1)} %bitcast.49, bf16[4,200,256]{2,1,0:T(8,128)(2,1)S(1)} %convolution_convert_fusion.2), kind=kLoop, calls=%fused_computation.7 | loop fusion | flops 1638400 | bytes 4096000 | tf_op jit(solution)/shard_map/jit(_where)/select_n | solution.py:253
  57.5 0.5 copy-done.2
  57.9 2.7 %copy.44 = f32[4,8,128,256]{3,2,1,0:T(8,128)} copy(f32[4,8,128,256]{3,0,2,1:T(4,128)S(1)} %copy-done.2) | data formatting | bytes 8388608 | tf_op jit(solution)/shard_map/conv_general_dilated | solution.py:219
  60.6 8.4 %all-to-all-done = f32[128,1,1056]{2,1,0:T(1,128)S(1)} async-done(((f32[128,1,1056]{2,1,0:T(1,128)}), f32[128,1,1056]{2,1,0:T(1,128)S(1)}, u32[]{:S(2)}, u32[]{:S(2)}) %all-to-all-start) | async-done | bytes 540704 | tf_op jit(solution)/shard_map/all_to_all | solution.py:231
  69.0 0.4 reduce_sum.83
  69.9 1.0 copy.46.refs_4_
  70.9 3.0 %fusion.4.f_ref = bf16[4,1024,256]{2,1,0:T(8,128)(2,1)S(1)} fusion(f32[4,8,128,256]{3,2,1,0:T(8,128)} %copy.44, f32[256]{0:T(256)S(1)} %copy-done.12, f32[256]{0:T(256)S(1)} %copy-done.13, f32[4,256]{1,0:T(4,128)S(1)} %div.54, f32[4,256]{1,0:T(4,128)S(1)} %sub.50), kind=kLoop, calls=%fused_computation.6 | loop fusion | flops 6291456 | bytes 6301696 | tf_op jit(solution)/shard_map/convert_element_type | solution.py:242
  73.9 3.2 %convolution_convert_fusion.refs_1_.refs_2_ = bf16[4,1024,512]{2,1,0:T(8,128)(2,1)} fusion(bf16[4,1024,256]{2,1,0:T(8,128)(2,1)S(1)} %fusion.4.f_ref, bf16[256,256]{1,0:T(8,128)(2,1)S(1)} %copy-done.6, bf16[256,256]{1,0:T(8,128)(2,1)S(1)} %copy-done.7), kind=kOutput, calls=%fused_computation.8 | convolution fusion | flops 1076363264 | bytes 6553600 | tf_op jit(solution)/shard_map/dot_general | solution.py:245
  77.1 18.6 %shard_map.150 = (f32[4,200,8]{2,1,0:T(8,128)}, f32[4,200,8]{2,1,0:T(8,128)}, f32[4,200,256]{2,1,0:T(8,128)}) custom-call(bf16[4,1600,256]{2,1,0:T(8,128)(2,1)} %bitcast_select_fusion.refs_0_, bf16[4,1024,512]{2,1,0:T(8,128)(2,1)} %convolution_convert_fusion.refs_1_.refs_2_, bf16[4,1024,512]{2,1,0:T(8,128)(2,1)} %convolution_convert_fusion.refs_1_.refs_2_, ...), custom_call_target="tpu_custom_call" | custom-call | tf_op jit(solution)/shard_map/pallas_call | solution.py:144
  95.7 1.2 reshape.137
  96.9 1.2 reshape.138
  98.1 1.2 convert_element_type.64
  99.3 0.5 convert_element_type.65
  100.0 0.5 broadcast.108
  100.5 0.9 reduce.7
  101.4 0.6 reshape.151
  102.0 18.0 %all_to_all.21 = bf16[128,2,900]{2,1,0:T(2,128)(2,1)S(1)} all-to-all(bf16[128,2,900]{2,1,0:T(2,128)(2,1)S(1)} %reshape.151), channel_id=1, replica_groups=mesh['rows'=16,'cols'=8] {'rows','cols'}, dimensions={0} | all-to-all | bytes 921600 | tf_op jit(solution)/shard_map/all_to_all | solution.py:272
  120.1 0.7 reshape.152
  120.8 0.9 copy.48
  122.2 0.3 fusion.12
  122.6 0.5 broadcast_in_dim.78
  123.1 3.3 %reduce.8 = bf16[128,1600]{1,0:T(8,128)(2,1)S(1)} reduce(bf16[128,1,1600]{2,1,0:T(2,128)(2,1)S(1)} %broadcast_in_dim.78, bf16[]{:T(256)} %broadcast.108), dimensions={1}, to_apply=%broadcast_in_dim.78.reduce_sub_computation | reduce | bytes 819202 | tf_op jit(solution)/shard_map/broadcast_in_dim | solution.py:283
  126.4 0.5 reshape.153
  126.9 17.3 %all_to_all.22 = bf16[128,2,800]{2,1,0:T(2,128)(2,1)S(1)} all-to-all(bf16[128,2,800]{2,1,0:T(2,128)(2,1)S(1)} %reshape.153), channel_id=1, replica_groups=mesh['rows'=16,'cols'=8] {'rows','cols'}, dimensions={0} | all-to-all | bytes 819200 | tf_op jit(solution)/shard_map/all_to_all | solution.py:282
  144.2 0.6 reshape.154
  144.9 2.7 %reduce.6 = bf16[128,1600]{1,0:T(8,128)(2,1)S(1)} reduce(bf16[128,1,1600]{2,1,0:T(2,128)(2,1)S(1)} %reshape.154, bf16[]{:T(256)} %constant.43), dimensions={1}, to_apply=%all_to_all.17.reduce_sub_computation | reduce | bytes 819202 | tf_op jit(solution)/shard_map/all_to_all | solution.py:282
  147.6 0.6 reshape.140
  148.2 0.4 fusion.36
  148.7 0.4 multiply_reduce_fusion.1
  149.1 0.3 multiply_add_fusion
  149.4 1.2 convolution_convert_fusion.1.e_ref
  150.6 4.6 %shard_map.151 = bf16[4,1600,128]{2,1,0:T(8,128)(2,1)} custom-call(bf16[4,200,256]{2,1,0:T(8,128)(2,1)} %convolution_convert_fusion.1.e_ref, bf16[4,1024,256]{2,1,0:T(8,128)(2,1)} %copy-done.1), custom_call_target="tpu_custom_call" | custom-call | tf_op jit(solution)/shard_map/pallas_call | solution.py:182
  (63 shorter events, 2.7 us)
Async XLA Ops:
  0.6 29.0 %copy-start = (bf16[3,3,256,256]{3,2,1,0:T(8,128)(2,1)S(1)}, bf16[3,3,256,256]{3,2,1,0:T(8,128)(2,1)}, u32[]{:S(2)}) copy-start(bf16[3,3,256,256]{3,2,1,0:T(8,128)(2,1)} %param.17) | copy-start | bytes 3538948
  0.6 11.6 %copy-start.4 = (bf16[4,8,128,256]{3,2,1,0:T(8,128)(2,1)S(1)}, bf16[4,8,128,256]{3,2,1,0:T(8,128)(2,1)}, u32[]{:S(2)}) copy-start(bf16[4,8,128,256]{3,2,1,0:T(8,128)(2,1)} %param.14) | copy-start | bytes 6291460
  2.1 9.3 %collective-permute-start = (bf16[4,1,128,256]{3,0,2,1:T(4,128)(2,1)S(1)}, bf16[4,1,128,256]{3,0,2,1:T(4,128)(2,1)S(1)}, u32[]{:S(2)}, u32[]{:S(2)}) collective-permute-start(bf16[4,1,128,256]{3,0,2,1:T(4,128)(2,1)S(1)} %copy.51), channel_id=1, source_target_pairs={{0,8},{8,16},{16,24},{24,32},{32,40},{40,48},{48,56},{56,64},{64,7... | collective-permute-start | bytes 786440 | tf_op jit(solution)/shard_map/ppermute | solution.py:21
  6.7 9.1 %collective-permute-start.1 = (bf16[4,1,128,256]{3,0,2,1:T(4,128)(2,1)S(1)}, bf16[4,1,128,256]{3,0,2,1:T(4,128)(2,1)S(1)}, u32[]{:S(2)}, u32[]{:S(2)}) collective-permute-start(bf16[4,1,128,256]{3,0,2,1:T(4,128)(2,1)S(1)} %copy.52), channel_id=1, source_target_pairs={{8,0},{16,8},{24,16},{32,24},{40,32},{48,40},{56,48},{64,56},{72,6... | collective-permute-start | bytes 786440 | tf_op jit(solution)/shard_map/ppermute | solution.py:23
  17.4 12.2 %collective-permute-start.2 = (bf16[4,10,1,256]{3,0,2,1:T(4,128)(2,1)S(1)}, bf16[4,10,1,256]{3,0,2,1:T(4,128)(2,1)S(1)}, u32[]{:S(2)}, u32[]{:S(2)}) collective-permute-start(bf16[4,10,1,256]{3,0,2,1:T(4,128)(2,1)S(1)} %get-tuple-element.20), channel_id=1, source_target_pairs={{0,1},{1,2},{2,3},{3,4},{4,5},{5,6},{6,7},{8,9},{9,10},{10,11},{11... | collective-permute-start | bytes 61448 | tf_op jit(solution)/shard_map/ppermute | solution.py:21
  22.1 7.5 %collective-permute-start.3 = (bf16[4,10,1,256]{3,0,2,1:T(4,128)(2,1)S(1)}, bf16[4,10,1,256]{3,0,2,1:T(4,128)(2,1)S(1)}, u32[]{:S(2)}, u32[]{:S(2)}) collective-permute-start(bf16[4,10,1,256]{3,0,2,1:T(4,128)(2,1)S(1)} %get-tuple-element.21), channel_id=1, source_target_pairs={{1,0},{2,1},{3,2},{4,3},{5,4},{6,5},{7,6},{9,8},{10,9},{11,10},{12... | collective-permute-start | bytes 61448 | tf_op jit(solution)/shard_map/ppermute | solution.py:23
  29.6 25.2 %copy-start.5 = (f32[4,200,256]{2,1,0:T(8,128)S(1)}, f32[4,200,256]{2,1,0:T(8,128)}, u32[]{:S(2)}) copy-start(f32[4,200,256]{2,1,0:T(8,128)} %param.16) | copy-start | bytes 2457604
  29.6 25.2 %copy-start.11 = (bf16[256,256]{1,0:T(8,128)(2,1)S(1)}, bf16[256,256]{1,0:T(8,128)(2,1)}, u32[]{:S(2)}) copy-start(bf16[256,256]{1,0:T(8,128)(2,1)} %param.20) | copy-start | bytes 393220
  43.9 25.1 %all-to-all-start = ((f32[128,1,1056]{2,1,0:T(1,128)}), f32[128,1,1056]{2,1,0:T(1,128)S(1)}, u32[]{:S(2)}, u32[]{:S(2)}) async-start(f32[128,1,1056]{2,1,0:T(1,128)} %broadcast_in_dim.72), calls=%async_computation | async-start | bytes 1179648 | tf_op jit(solution)/shard_map/all_to_all | solution.py:231
  54.9 3.1 %copy-start.2 = (f32[4,8,128,256]{3,0,2,1:T(4,128)S(1)}, f32[4,8,128,256]{3,0,2,1:T(4,128)}, u32[]{:S(2)}) copy-start(f32[4,8,128,256]{3,0,2,1:T(4,128)} %get-tuple-element.26) | copy-start | bytes 12582916
  57.9 13.0 %copy-start.12 = (f32[256]{0:T(256)S(1)}, f32[256]{0:T(256)}, u32[]{:S(2)}) copy-start(f32[256]{0:T(256)} %param.19) | copy-start | bytes 3076
  57.9 13.0 %copy-start.13 = (f32[256]{0:T(256)S(1)}, f32[256]{0:T(256)}, u32[]{:S(2)}) copy-start(f32[256]{0:T(256)} %param.18) | copy-start | bytes 3076
  70.9 3.0 %copy-start.6 = (bf16[256,256]{1,0:T(8,128)(2,1)S(1)}, bf16[256,256]{1,0:T(8,128)(2,1)}, u32[]{:S(2)}) copy-start(bf16[256,256]{1,0:T(8,128)(2,1)} %param.22) | copy-start | bytes 393220
  70.9 3.0 %copy-start.7 = (bf16[256,256]{1,0:T(8,128)(2,1)S(1)}, bf16[256,256]{1,0:T(8,128)(2,1)}, u32[]{:S(2)}) copy-start(bf16[256,256]{1,0:T(8,128)(2,1)} %param.21) | copy-start | bytes 393220
  73.9 3.2 %copy-start.1 = (bf16[4,1024,256]{2,1,0:T(8,128)(2,1)}, bf16[4,1024,256]{2,1,0:T(8,128)(2,1)S(1)}, u32[]{:S(2)}) copy-start(bf16[4,1024,256]{2,1,0:T(8,128)(2,1)S(1)} %fusion.4.f_ref) | copy-start | bytes 6291460
  126.4 21.8 %copy-start.8 = (bf16[256,256]{1,0:T(8,128)(2,1)S(1)}, bf16[256,256]{1,0:T(8,128)(2,1)}, u32[]{:S(2)}) copy-start(bf16[256,256]{1,0:T(8,128)(2,1)} %param.23) | copy-start | bytes 393220
  144.9 4.2 %copy-start.14 = (f32[256]{0:T(256)S(1)}, f32[256]{0:T(256)}, u32[]{:S(2)}) copy-start(f32[256]{0:T(256)} %param.25) | copy-start | bytes 3076
  144.9 4.2 %copy-start.15 = (f32[256]{0:T(256)S(1)}, f32[256]{0:T(256)}, u32[]{:S(2)}) copy-start(f32[256]{0:T(256)} %param.24) | copy-start | bytes 3076
  147.6 1.8 %copy-start.9 = (bf16[256,256]{1,0:T(8,128)(2,1)S(1)}, bf16[256,256]{1,0:T(8,128)(2,1)}, u32[]{:S(2)}) copy-start(bf16[256,256]{1,0:T(8,128)(2,1)} %param.27) | copy-start | bytes 393220
  147.6 1.8 %copy-start.10 = (bf16[256,256]{1,0:T(8,128)(2,1)S(1)}, bf16[256,256]{1,0:T(8,128)(2,1)}, u32[]{:S(2)}) copy-start(bf16[256,256]{1,0:T(8,128)(2,1)} %param.26) | copy-start | bytes 393220
  149.4 5.8 %copy-start.3 = (f32[4,200,256]{2,1,0:T(8,128)}, f32[4,200,256]{2,1,0:T(8,128)S(1)}, u32[]{:S(2)}) copy-start(f32[4,200,256]{2,1,0:T(8,128)S(1)} %multiply_add_fusion) | copy-start | bytes 2457604

commit v14 on v13

--- a/solution.py
+++ b/solution.py
@@ -125,14 +125,16 @@
     v = v_ref[0]
     allowed = (fg_ref[0] != 0) | (zero_ref[0] != 0)
     bias = jnp.where(allowed, 0.0, -jnp.inf)
+    lane = lax.broadcasted_iota(jnp.int32, v.shape, 1)
     for h in range(heads):
         q = q_ref[0, h * queries : (h + 1) * queries, :]
         s = lax.dot_general(q, k, (((1,), (1,)), ((), ())), preferred_element_type=jnp.float32) * scale
         top = jnp.maximum(jnp.max(s + bias, axis=1, keepdims=True), NEG)
         w = jnp.exp(s + bias - top).astype(jnp.bfloat16)
-        tot_ref[0, :, h : h + 1] = jnp.sum(w.astype(jnp.float32), axis=1, keepdims=True)
         top_ref[0, :, h : h + 1] = top
-        r = jnp.dot(w, v, preferred_element_type=jnp.float32)
+        spare = ((h + 1) % heads) * head_size
+        r = jnp.dot(w, jnp.where(lane == spare, jnp.ones((), v.dtype), v), preferred_element_type=jnp.float32)
+        tot_ref[0, :, h : h + 1] = r[:, spare : spare + 1]
         wv_ref[0, :, h * head_size : (h + 1) * head_size] = r[:, h * head_size : (h + 1) * head_size]
 
 

time: 156 us -> 156 us (level)
  no operation moved by 1% of the time
where the time goes in v14:
time: 156 us
  blocking collectives  35.3 us (23%)
  Pallas kernels  27.9 us (18%)
  starting transfers between devices  23.2 us (15%)
  local copies, waits for them, and re-layouts  21.2 us (14%)
  matrix products  17.7 us (11%)
  other arithmetic  16.7 us (11%)
  waiting for transfers between devices  12.5 us (8%)
    pallas_call x1, Pallas kernels, attention(): pl.pallas_call(kernel, grid=(images,), in_specs=[pl.BlockSpec((1, heads *...  19 us
    all_to_all x1, blocking collectives, on_device(): lax.all_to_all(packed, ('rows', 'cols'), 0, 0, tiled=True)  18 us
    all_to_all x1, blocking collectives, on_device(): lax.all_to_all(jnp.broadcast_to(attn_block, (devices, span)), ('rows', 'c...  17.3 us
    conv_general_dilated x1, matrix products, on_device(): lax.conv_general_dilated(padded, conv_weight, (1, 1), 'VALID', dimension_...  12.6 us
    all_to_all x1, starting transfers between devices, on_device(): lax.all_to_all(jnp.broadcast_to(stats, (devices, stats.shape[1])), ('rows...  10.9 us
    ppermute x2, starting transfers between devices, with_halo(): lax.ppermute(tail, axis, [(i, (i + 1) % count) for i in range(ends)])  9.11 us
    all_to_all x1, waiting for transfers between devices, on_device(): lax.all_to_all(jnp.broadcast_to(stats, (devices, stats.shape[1])), ('rows...  8.4 us
    unnamed x40, local copies, waits for them, and re-layouts  7.1 us
  transfers between devices with their start and end apart: 5, of which 3 were waited for; matrix products, arithmetic and copies ran while one was open for 7% of the time, Pallas kernels for 3%

profile of v14, /device:TPU:1, one launch (start us, length us, event | category | flops | bytes accessed | tf_op | source)
XLA Modules:
  0.0 155.6 jit_solution(12954894671239073082)
XLA Ops:
  0.7 1.2 fusion.35
  2.1 4.4 %collective-permute-start = (bf16[4,1,128,256]{3,0,2,1:T(4,128)(2,1)S(1)}, bf16[4,1,128,256]{3,0,2,1:T(4,128)(2,1)S(1)}, u32[]{:S(2)}, u32[]{:S(2)}) collective-permute-start(bf16[4,1,128,256]{3,0,2,1:T(4,128)(2,1)S(1)} %copy.51), channel_id=1, source_target_pairs={{0,8},{8,16},{16,24},{24,32},{32,40},{40,48},{48,56},{56,64},{64,7... | collective-permute-start | bytes 786440 | tf_op jit(solution)/shard_map/ppermute | solution.py:21
  6.7 1.3 collective-permute-start.1
  8.0 3.4 %collective-permute-done = bf16[4,1,128,256]{3,0,2,1:T(4,128)(2,1)S(1)} collective-permute-done((bf16[4,1,128,256]{3,0,2,1:T(4,128)(2,1)S(1)}, bf16[4,1,128,256]{3,0,2,1:T(4,128)(2,1)S(1)}, u32[]{:S(2)}, u32[]{:S(2)}) %collective-permute-start) | collective-permute-done | bytes 262176 | tf_op jit(solution)/shard_map/ppermute | solution.py:21
  11.4 0.8 constant_dynamic-update-slice_fusion.2
  12.2 3.0 %constant_dynamic-update-slice_fusion.1 = bf16[4,10,128,256]{3,0,2,1:T(4,128)(2,1)} fusion(bf16[4,10,128,256]{3,0,2,1:T(4,128)(2,1)} %constant_dynamic-update-slice_fusion.2, bf16[4,8,128,256]{3,2,1,0:T(8,128)(2,1)S(1)} %copy-done.4), kind=kLoop, calls=%fused_computation.44 | loop fusion | bytes 4194304
  15.2 0.7 collective-permute-done.1
  15.8 0.8 constant_dynamic-update-slice_fusion
  16.6 0.8 fusion.34
  17.4 4.7 %collective-permute-start.2 = (bf16[4,10,1,256]{3,0,2,1:T(4,128)(2,1)S(1)}, bf16[4,10,1,256]{3,0,2,1:T(4,128)(2,1)S(1)}, u32[]{:S(2)}, u32[]{:S(2)}) collective-permute-start(bf16[4,10,1,256]{3,0,2,1:T(4,128)(2,1)S(1)} %get-tuple-element.20), channel_id=1, source_target_pairs={{0,1},{1,2},{2,3},{3,4},{4,5},{5,6},{6,7},{8,9},{9,10},{10,11},{11... | collective-permute-start | bytes 61448 | tf_op jit(solution)/shard_map/ppermute | solution.py:21
  22.1 1.9 %collective-permute-start.3 = (bf16[4,10,1,256]{3,0,2,1:T(4,128)(2,1)S(1)}, bf16[4,10,1,256]{3,0,2,1:T(4,128)(2,1)S(1)}, u32[]{:S(2)}, u32[]{:S(2)}) collective-permute-start(bf16[4,10,1,256]{3,0,2,1:T(4,128)(2,1)S(1)} %get-tuple-element.21), channel_id=1, source_target_pairs={{1,0},{2,1},{3,2},{4,3},{5,4},{6,5},{7,6},{9,8},{10,9},{11,10},{12... | collective-permute-start | bytes 61448 | tf_op jit(solution)/shard_map/ppermute | solution.py:23
  24.1 4.3 %shard_map.149 = (bf16[4,200,1024]{2,1,0:T(8,128)(2,1)}, f32[4,200,1]{2,1,0:T(8,128)}) custom-call(s32[4,1600,128]{2,1,0:T(8,128)} %bitcast.45), custom_call_target="tpu_custom_call" | custom-call | tf_op jit(solution)/shard_map/pallas_call | solution.py:105
  28.4 1.2 reduce.5
  29.7 12.6 %fusion.33 = (f32[4,256]{1,0:T(4,128)S(1)}, f32[4,256]{1,0:T(4,128)S(1)}, f32[4,8,128,256]{3,0,2,1:T(4,128)}) fusion(bf16[3,3,256,256]{3,2,1,0:T(8,128)(2,1)S(1)} %copy-done, bf16[4,10,1,256]{3,0,2,1:T(4,128)(2,1)S(1)} %collective-permute-done.3, bf16[4,10,128,256]{3,0,2,1:T(4,128)(2,1)} %constant_dynamic-update-slice_fusion, ...), kind=kOutput, calls=%fused_computation.65 | convolution fusion | flops 4842969088 | bytes 8044544 | tf_op jit(solution)/shard_map/conv_general_dilated | solution.py:221
  42.8 1.1 broadcast_in_dim.72
  43.9 10.9 %all-to-all-start = ((f32[128,1,1056]{2,1,0:T(1,128)}), f32[128,1,1056]{2,1,0:T(1,128)S(1)}, u32[]{:S(2)}, u32[]{:S(2)}) async-start(f32[128,1,1056]{2,1,0:T(1,128)} %broadcast_in_dim.72), calls=%async_computation | async-start | bytes 1179648 | tf_op jit(solution)/shard_map/all_to_all | solution.py:233
  55.2 2.2 %bitcast_select_fusion.refs_0_ = bf16[4,1600,256]{2,1,0:T(8,128)(2,1)} fusion(pred[1600,256]{1,0:T(8,128)(4,1)S(1)} %bitcast.49, bf16[4,200,256]{2,1,0:T(8,128)(2,1)S(1)} %convolution_convert_fusion.2), kind=kLoop, calls=%fused_computation.7 | loop fusion | flops 1638400 | bytes 4096000 | tf_op jit(solution)/shard_map/jit(_where)/select_n | solution.py:255
  57.5 0.5 copy-done.2
  57.9 2.7 %copy.44 = f32[4,8,128,256]{3,2,1,0:T(8,128)} copy(f32[4,8,128,256]{3,0,2,1:T(4,128)S(1)} %copy-done.2) | data formatting | bytes 8388608 | tf_op jit(solution)/shard_map/conv_general_dilated | solution.py:221
  60.6 8.4 %all-to-all-done = f32[128,1,1056]{2,1,0:T(1,128)S(1)} async-done(((f32[128,1,1056]{2,1,0:T(1,128)}), f32[128,1,1056]{2,1,0:T(1,128)S(1)}, u32[]{:S(2)}, u32[]{:S(2)}) %all-to-all-start) | async-done | bytes 540704 | tf_op jit(solution)/shard_map/all_to_all | solution.py:233
  69.0 0.4 reduce_sum.83
  69.9 1.0 copy.46.refs_4_
  70.9 3.0 %fusion.4.f_ref = bf16[4,1024,256]{2,1,0:T(8,128)(2,1)S(1)} fusion(f32[4,8,128,256]{3,2,1,0:T(8,128)} %copy.44, f32[256]{0:T(256)S(1)} %copy-done.12, f32[256]{0:T(256)S(1)} %copy-done.13, f32[4,256]{1,0:T(4,128)S(1)} %div.54, f32[4,256]{1,0:T(4,128)S(1)} %sub.50), kind=kLoop, calls=%fused_computation.6 | loop fusion | flops 6291456 | bytes 6301696 | tf_op jit(solution)/shard_map/convert_element_type | solution.py:244
  73.9 3.2 %convolution_convert_fusion.refs_1_.refs_2_ = bf16[4,1024,512]{2,1,0:T(8,128)(2,1)} fusion(bf16[4,1024,256]{2,1,0:T(8,128)(2,1)S(1)} %fusion.4.f_ref, bf16[256,256]{1,0:T(8,128)(2,1)S(1)} %copy-done.6, bf16[256,256]{1,0:T(8,128)(2,1)S(1)} %copy-done.7), kind=kOutput, calls=%fused_computation.8 | convolution fusion | flops 1076363264 | bytes 6553600 | tf_op jit(solution)/shard_map/dot_general | solution.py:247
  77.1 19.0 %shard_map.150 = (f32[4,200,8]{2,1,0:T(8,128)}, f32[4,200,8]{2,1,0:T(8,128)}, f32[4,200,256]{2,1,0:T(8,128)}) custom-call(bf16[4,1600,256]{2,1,0:T(8,128)(2,1)} %bitcast_select_fusion.refs_0_, bf16[4,1024,512]{2,1,0:T(8,128)(2,1)} %convolution_convert_fusion.refs_1_.refs_2_, bf16[4,1024,512]{2,1,0:T(8,128)(2,1)} %convolution_convert_fusion.refs_1_.refs_2_, ...), custom_call_target="tpu_custom_call" | custom-call | tf_op jit(solution)/shard_map/pallas_call | solution.py:146
  96.1 1.2 reshape.137
  97.3 1.2 reshape.138
  98.5 1.2 convert_element_type.64
  99.7 0.5 convert_element_type.65
  100.4 0.5 broadcast.108
  100.9 0.9 reduce.7
  101.9 0.6 reshape.151
  102.5 18.0 %all_to_all.21 = bf16[128,2,900]{2,1,0:T(2,128)(2,1)S(1)} all-to-all(bf16[128,2,900]{2,1,0:T(2,128)(2,1)S(1)} %reshape.151), channel_id=1, replica_groups=mesh['rows'=16,'cols'=8] {'rows','cols'}, dimensions={0} | all-to-all | bytes 921600 | tf_op jit(solution)/shard_map/all_to_all | solution.py:274
  120.5 0.7 reshape.152
  121.2 0.9 copy.48
  122.6 0.3 fusion.12
  123.1 0.5 broadcast_in_dim.78
  123.5 3.3 %reduce.8 = bf16[128,1600]{1,0:T(8,128)(2,1)S(1)} reduce(bf16[128,1,1600]{2,1,0:T(2,128)(2,1)S(1)} %broadcast_in_dim.78, bf16[]{:T(256)} %broadcast.108), dimensions={1}, to_apply=%broadcast_in_dim.78.reduce_sub_computation | reduce | bytes 819202 | tf_op jit(solution)/shard_map/broadcast_in_dim | solution.py:285
  126.9 0.5 reshape.153
  127.3 17.3 %all_to_all.22 = bf16[128,2,800]{2,1,0:T(2,128)(2,1)S(1)} all-to-all(bf16[128,2,800]{2,1,0:T(2,128)(2,1)S(1)} %reshape.153), channel_id=1, replica_groups=mesh['rows'=16,'cols'=8] {'rows','cols'}, dimensions={0} | all-to-all | bytes 819200 | tf_op jit(solution)/shard_map/all_to_all | solution.py:284
  144.6 0.6 reshape.154
  145.3 2.7 %reduce.6 = bf16[128,1600]{1,0:T(8,128)(2,1)S(1)} reduce(bf16[128,1,1600]{2,1,0:T(2,128)(2,1)S(1)} %reshape.154, bf16[]{:T(256)} %constant.43), dimensions={1}, to_apply=%all_to_all.17.reduce_sub_computation | reduce | bytes 819202 | tf_op jit(solution)/shard_map/all_to_all | solution.py:284
  148.0 0.6 reshape.140
  148.6 0.4 fusion.36
  149.1 0.4 multiply_reduce_fusion.1
  149.5 0.3 multiply_add_fusion
  149.8 1.2 convolution_convert_fusion.1.e_ref
  151.0 4.6 %shard_map.151 = bf16[4,1600,128]{2,1,0:T(8,128)(2,1)} custom-call(bf16[4,200,256]{2,1,0:T(8,128)(2,1)} %convolution_convert_fusion.1.e_ref, bf16[4,1024,256]{2,1,0:T(8,128)(2,1)} %copy-done.1), custom_call_target="tpu_custom_call" | custom-call | tf_op jit(solution)/shard_map/pallas_call | solution.py:184
  (63 shorter events, 2.7 us)
Async XLA Ops:
  0.6 29.0 %copy-start = (bf16[3,3,256,256]{3,2,1,0:T(8,128)(2,1)S(1)}, bf16[3,3,256,256]{3,2,1,0:T(8,128)(2,1)}, u32[]{:S(2)}) copy-start(bf16[3,3,256,256]{3,2,1,0:T(8,128)(2,1)} %param.17) | copy-start | bytes 3538948
  0.6 11.6 %copy-start.4 = (bf16[4,8,128,256]{3,2,1,0:T(8,128)(2,1)S(1)}, bf16[4,8,128,256]{3,2,1,0:T(8,128)(2,1)}, u32[]{:S(2)}) copy-start(bf16[4,8,128,256]{3,2,1,0:T(8,128)(2,1)} %param.14) | copy-start | bytes 6291460
  2.1 9.3 %collective-permute-start = (bf16[4,1,128,256]{3,0,2,1:T(4,128)(2,1)S(1)}, bf16[4,1,128,256]{3,0,2,1:T(4,128)(2,1)S(1)}, u32[]{:S(2)}, u32[]{:S(2)}) collective-permute-start(bf16[4,1,128,256]{3,0,2,1:T(4,128)(2,1)S(1)} %copy.51), channel_id=1, source_target_pairs={{0,8},{8,16},{16,24},{24,32},{32,40},{40,48},{48,56},{56,64},{64,7... | collective-permute-start | bytes 786440 | tf_op jit(solution)/shard_map/ppermute | solution.py:21
  6.7 9.1 %collective-permute-start.1 = (bf16[4,1,128,256]{3,0,2,1:T(4,128)(2,1)S(1)}, bf16[4,1,128,256]{3,0,2,1:T(4,128)(2,1)S(1)}, u32[]{:S(2)}, u32[]{:S(2)}) collective-permute-start(bf16[4,1,128,256]{3,0,2,1:T(4,128)(2,1)S(1)} %copy.52), channel_id=1, source_target_pairs={{8,0},{16,8},{24,16},{32,24},{40,32},{48,40},{56,48},{64,56},{72,6... | collective-permute-start | bytes 786440 | tf_op jit(solution)/shard_map/ppermute | solution.py:23
  17.4 12.2 %collective-permute-start.2 = (bf16[4,10,1,256]{3,0,2,1:T(4,128)(2,1)S(1)}, bf16[4,10,1,256]{3,0,2,1:T(4,128)(2,1)S(1)}, u32[]{:S(2)}, u32[]{:S(2)}) collective-permute-start(bf16[4,10,1,256]{3,0,2,1:T(4,128)(2,1)S(1)} %get-tuple-element.20), channel_id=1, source_target_pairs={{0,1},{1,2},{2,3},{3,4},{4,5},{5,6},{6,7},{8,9},{9,10},{10,11},{11... | collective-permute-start | bytes 61448 | tf_op jit(solution)/shard_map/ppermute | solution.py:21
  22.1 7.5 %collective-permute-start.3 = (bf16[4,10,1,256]{3,0,2,1:T(4,128)(2,1)S(1)}, bf16[4,10,1,256]{3,0,2,1:T(4,128)(2,1)S(1)}, u32[]{:S(2)}, u32[]{:S(2)}) collective-permute-start(bf16[4,10,1,256]{3,0,2,1:T(4,128)(2,1)S(1)} %get-tuple-element.21), channel_id=1, source_target_pairs={{1,0},{2,1},{3,2},{4,3},{5,4},{6,5},{7,6},{9,8},{10,9},{11,10},{12... | collective-permute-start | bytes 61448 | tf_op jit(solution)/shard_map/ppermute | solution.py:23
  29.6 25.2 %copy-start.5 = (f32[4,200,256]{2,1,0:T(8,128)S(1)}, f32[4,200,256]{2,1,0:T(8,128)}, u32[]{:S(2)}) copy-start(f32[4,200,256]{2,1,0:T(8,128)} %param.16) | copy-start | bytes 2457604
  29.6 25.2 %copy-start.11 = (bf16[256,256]{1,0:T(8,128)(2,1)S(1)}, bf16[256,256]{1,0:T(8,128)(2,1)}, u32[]{:S(2)}) copy-start(bf16[256,256]{1,0:T(8,128)(2,1)} %param.20) | copy-start | bytes 393220
  43.9 25.1 %all-to-all-start = ((f32[128,1,1056]{2,1,0:T(1,128)}), f32[128,1,1056]{2,1,0:T(1,128)S(1)}, u32[]{:S(2)}, u32[]{:S(2)}) async-start(f32[128,1,1056]{2,1,0:T(1,128)} %broadcast_in_dim.72), calls=%async_computation | async-start | bytes 1179648 | tf_op jit(solution)/shard_map/all_to_all | solution.py:233
  54.9 3.1 %copy-start.2 = (f32[4,8,128,256]{3,0,2,1:T(4,128)S(1)}, f32[4,8,128,256]{3,0,2,1:T(4,128)}, u32[]{:S(2)}) copy-start(f32[4,8,128,256]{3,0,2,1:T(4,128)} %get-tuple-element.26) | copy-start | bytes 12582916
  57.9 13.0 %copy-start.12 = (f32[256]{0:T(256)S(1)}, f32[256]{0:T(256)}, u32[]{:S(2)}) copy-start(f32[256]{0:T(256)} %param.19) | copy-start | bytes 3076
  57.9 13.0 %copy-start.13 = (f32[256]{0:T(256)S(1)}, f32[256]{0:T(256)}, u32[]{:S(2)}) copy-start(f32[256]{0:T(256)} %param.18) | copy-start | bytes 3076
  70.9 3.0 %copy-start.6 = (bf16[256,256]{1,0:T(8,128)(2,1)S(1)}, bf16[256,256]{1,0:T(8,128)(2,1)}, u32[]{:S(2)}) copy-start(bf16[256,256]{1,0:T(8,128)(2,1)} %param.22) | copy-start | bytes 393220
  70.9 3.0 %copy-start.7 = (bf16[256,256]{1,0:T(8,128)(2,1)S(1)}, bf16[256,256]{1,0:T(8,128)(2,1)}, u32[]{:S(2)}) copy-start(bf16[256,256]{1,0:T(8,128)(2,1)} %param.21) | copy-start | bytes 393220
  73.9 3.2 %copy-start.1 = (bf16[4,1024,256]{2,1,0:T(8,128)(2,1)}, bf16[4,1024,256]{2,1,0:T(8,128)(2,1)S(1)}, u32[]{:S(2)}) copy-start(bf16[4,1024,256]{2,1,0:T(8,128)(2,1)S(1)} %fusion.4.f_ref) | copy-start | bytes 6291460
  126.8 21.8 %copy-start.8 = (bf16[256,256]{1,0:T(8,128)(2,1)S(1)}, bf16[256,256]{1,0:T(8,128)(2,1)}, u32[]{:S(2)}) copy-start(bf16[256,256]{1,0:T(8,128)(2,1)} %param.23) | copy-start | bytes 393220
  145.3 4.2 %copy-start.14 = (f32[256]{0:T(256)S(1)}, f32[256]{0:T(256)}, u32[]{:S(2)}) copy-start(f32[256]{0:T(256)} %param.25) | copy-start | bytes 3076
  145.3 4.2 %copy-start.15 = (f32[256]{0:T(256)S(1)}, f32[256]{0:T(256)}, u32[]{:S(2)}) copy-start(f32[256]{0:T(256)} %param.24) | copy-start | bytes 3076
  148.0 1.8 %copy-start.9 = (bf16[256,256]{1,0:T(8,128)(2,1)S(1)}, bf16[256,256]{1,0:T(8,128)(2,1)}, u32[]{:S(2)}) copy-start(bf16[256,256]{1,0:T(8,128)(2,1)} %param.27) | copy-start | bytes 393220
  148.0 1.8 %copy-start.10 = (bf16[256,256]{1,0:T(8,128)(2,1)S(1)}, bf16[256,256]{1,0:T(8,128)(2,1)}, u32[]{:S(2)}) copy-start(bf16[256,256]{1,0:T(8,128)(2,1)} %param.26) | copy-start | bytes 393220
  149.8 5.8 %copy-start.3 = (f32[4,200,256]{2,1,0:T(8,128)}, f32[4,200,256]{2,1,0:T(8,128)S(1)}, u32[]{:S(2)}) copy-start(f32[4,200,256]{2,1,0:T(8,128)S(1)} %multiply_add_fusion) | copy-start | bytes 2457604

commit v15 on v13

--- a/solution.py
+++ b/solution.py
@@ -95,7 +95,7 @@
         rows = m_ref[0, pl.ds(r, queries, stride=tile_rows), :]
         fg = (rows == 1).astype(jnp.float32)
         acc = acc + fg
-        fg_ref[0, :, r * tile_cols : (r + 1) * tile_cols] = fg.astype(jnp.bfloat16)
+        fg_ref[0, :, r * tile_cols : (r + 1) * tile_cols] = fg.astype(jnp.int8)
     cnt_ref[0] = jnp.sum(acc, axis=1, keepdims=True)
 
 
@@ -111,7 +111,7 @@
             pl.BlockSpec((1, queries, 1), lambda i: (i, 0, 0)),
         ],
         out_shape=[
-            jax.ShapeDtypeStruct((images, queries, tile_rows * tile_cols), jnp.bfloat16),
+            jax.ShapeDtypeStruct((images, queries, tile_rows * tile_cols), jnp.int8),
             jax.ShapeDtypeStruct((images, queries, 1), jnp.float32),
         ],
     )(flat)

time: 156 us -> 156 us (level)
  no operation moved by 1% of the time
where the time goes in v15:
time: 156 us; the launch traced here: 155 us
  blocking collectives  35.4 us (23%)
  Pallas kernels  27.3 us (18%)
  starting transfers between devices  23.2 us (15%)
  local copies, waits for them, and re-layouts  21.2 us (14%)
  matrix products  17.7 us (11%)
  other arithmetic  16.7 us (11%)
  waiting for transfers between devices  12.5 us (8%)
    pallas_call x1, Pallas kernels, attention(): pl.pallas_call(kernel, grid=(images,), in_specs=[pl.BlockSpec((1, heads *...  18.4 us
    all_to_all x1, blocking collectives, on_device(): lax.all_to_all(packed, ('rows', 'cols'), 0, 0, tiled=True)  18 us
    all_to_all x1, blocking collectives, on_device(): lax.all_to_all(jnp.broadcast_to(attn_block, (devices, span)), ('rows', 'c...  17.3 us
    conv_general_dilated x1, matrix products, on_device(): lax.conv_general_dilated(padded, conv_weight, (1, 1), 'VALID', dimension_...  12.6 us
    all_to_all x1, starting transfers between devices, on_device(): lax.all_to_all(jnp.broadcast_to(stats, (devices, stats.shape[1])), ('rows...  10.9 us
    ppermute x2, starting transfers between devices, with_halo(): lax.ppermute(tail, axis, [(i, (i + 1) % count) for i in range(ends)])  9.11 us
    all_to_all x1, waiting for transfers between devices, on_device(): lax.all_to_all(jnp.broadcast_to(stats, (devices, stats.shape[1])), ('rows...  8.4 us
    unnamed x40, local copies, waits for them, and re-layouts  7.09 us
  transfers between devices with their start and end apart: 5, of which 3 were waited for; matrix products, arithmetic and copies ran while one was open for 7% of the time, Pallas kernels for 3%

profile of v15, /device:TPU:1, one launch (start us, length us, event | category | flops | bytes accessed | tf_op | source)
XLA Modules:
  0.0 155.0 jit_solution(15237341858098460560)
XLA Ops:
  0.7 1.2 fusion.35
  2.1 4.4 %collective-permute-start = (bf16[4,1,128,256]{3,0,2,1:T(4,128)(2,1)S(1)}, bf16[4,1,128,256]{3,0,2,1:T(4,128)(2,1)S(1)}, u32[]{:S(2)}, u32[]{:S(2)}) collective-permute-start(bf16[4,1,128,256]{3,0,2,1:T(4,128)(2,1)S(1)} %copy.51), channel_id=1, source_target_pairs={{0,8},{8,16},{16,24},{24,32},{32,40},{40,48},{48,56},{56,64},{64,7... | collective-permute-start | bytes 786440 | tf_op jit(solution)/shard_map/ppermute | solution.py:21
  6.7 1.3 collective-permute-start.1
  8.0 3.4 %collective-permute-done = bf16[4,1,128,256]{3,0,2,1:T(4,128)(2,1)S(1)} collective-permute-done((bf16[4,1,128,256]{3,0,2,1:T(4,128)(2,1)S(1)}, bf16[4,1,128,256]{3,0,2,1:T(4,128)(2,1)S(1)}, u32[]{:S(2)}, u32[]{:S(2)}) %collective-permute-start) | collective-permute-done | bytes 262176 | tf_op jit(solution)/shard_map/ppermute | solution.py:21
  11.4 0.8 constant_dynamic-update-slice_fusion.2
  12.2 3.0 %constant_dynamic-update-slice_fusion.1 = bf16[4,10,128,256]{3,0,2,1:T(4,128)(2,1)} fusion(bf16[4,10,128,256]{3,0,2,1:T(4,128)(2,1)} %constant_dynamic-update-slice_fusion.2, bf16[4,8,128,256]{3,2,1,0:T(8,128)(2,1)S(1)} %copy-done.4), kind=kLoop, calls=%fused_computation.44 | loop fusion | bytes 4194304
  15.2 0.7 collective-permute-done.1
  15.8 0.8 constant_dynamic-update-slice_fusion
  16.6 0.8 fusion.34
  17.4 4.7 %collective-permute-start.2 = (bf16[4,10,1,256]{3,0,2,1:T(4,128)(2,1)S(1)}, bf16[4,10,1,256]{3,0,2,1:T(4,128)(2,1)S(1)}, u32[]{:S(2)}, u32[]{:S(2)}) collective-permute-start(bf16[4,10,1,256]{3,0,2,1:T(4,128)(2,1)S(1)} %get-tuple-element.20), channel_id=1, source_target_pairs={{0,1},{1,2},{2,3},{3,4},{4,5},{5,6},{6,7},{8,9},{9,10},{10,11},{11... | collective-permute-start | bytes 61448 | tf_op jit(solution)/shard_map/ppermute | solution.py:21
  22.1 1.9 %collective-permute-start.3 = (bf16[4,10,1,256]{3,0,2,1:T(4,128)(2,1)S(1)}, bf16[4,10,1,256]{3,0,2,1:T(4,128)(2,1)S(1)}, u32[]{:S(2)}, u32[]{:S(2)}) collective-permute-start(bf16[4,10,1,256]{3,0,2,1:T(4,128)(2,1)S(1)} %get-tuple-element.21), channel_id=1, source_target_pairs={{1,0},{2,1},{3,2},{4,3},{5,4},{6,5},{7,6},{9,8},{10,9},{11,10},{12... | collective-permute-start | bytes 61448 | tf_op jit(solution)/shard_map/ppermute | solution.py:23
  24.1 4.3 %shard_map.149 = (s8[4,200,1024]{2,1,0:T(8,128)(4,1)}, f32[4,200,1]{2,1,0:T(8,128)}) custom-call(s32[4,1600,128]{2,1,0:T(8,128)} %bitcast.45), custom_call_target="tpu_custom_call" | custom-call | tf_op jit(solution)/shard_map/pallas_call | solution.py:105
  28.3 1.2 reduce.5
  29.6 12.6 %fusion.33 = (f32[4,256]{1,0:T(4,128)S(1)}, f32[4,256]{1,0:T(4,128)S(1)}, f32[4,8,128,256]{3,0,2,1:T(4,128)}) fusion(bf16[3,3,256,256]{3,2,1,0:T(8,128)(2,1)S(1)} %copy-done, bf16[4,10,1,256]{3,0,2,1:T(4,128)(2,1)S(1)} %collective-permute-done.3, bf16[4,10,128,256]{3,0,2,1:T(4,128)(2,1)} %constant_dynamic-update-slice_fusion, ...), kind=kOutput, calls=%fused_computation.65 | convolution fusion | flops 4842969088 | bytes 8044544 | tf_op jit(solution)/shard_map/conv_general_dilated | solution.py:219
  42.8 1.1 broadcast_in_dim.72
  43.9 10.9 %all-to-all-start = ((f32[128,1,1056]{2,1,0:T(1,128)}), f32[128,1,1056]{2,1,0:T(1,128)S(1)}, u32[]{:S(2)}, u32[]{:S(2)}) async-start(f32[128,1,1056]{2,1,0:T(1,128)} %broadcast_in_dim.72), calls=%async_computation | async-start | bytes 1179648 | tf_op jit(solution)/shard_map/all_to_all | solution.py:231
  55.2 2.2 %bitcast_select_fusion.refs_0_ = bf16[4,1600,256]{2,1,0:T(8,128)(2,1)} fusion(pred[1600,256]{1,0:T(8,128)(4,1)S(1)} %bitcast.49, bf16[4,200,256]{2,1,0:T(8,128)(2,1)S(1)} %convolution_convert_fusion.2), kind=kLoop, calls=%fused_computation.7 | loop fusion | flops 1638400 | bytes 4096000 | tf_op jit(solution)/shard_map/jit(_where)/select_n | solution.py:253
  57.4 0.5 copy-done.2
  57.9 2.7 %copy.44 = f32[4,8,128,256]{3,2,1,0:T(8,128)} copy(f32[4,8,128,256]{3,0,2,1:T(4,128)S(1)} %copy-done.2) | data formatting | bytes 8388608 | tf_op jit(solution)/shard_map/conv_general_dilated | solution.py:219
  60.5 8.4 %all-to-all-done = f32[128,1,1056]{2,1,0:T(1,128)S(1)} async-done(((f32[128,1,1056]{2,1,0:T(1,128)}), f32[128,1,1056]{2,1,0:T(1,128)S(1)}, u32[]{:S(2)}, u32[]{:S(2)}) %all-to-all-start) | async-done | bytes 540704 | tf_op jit(solution)/shard_map/all_to_all | solution.py:231
  68.9 0.4 reduce_sum.83
  69.9 1.0 copy.46.refs_4_
  70.9 3.0 %fusion.4.f_ref = bf16[4,1024,256]{2,1,0:T(8,128)(2,1)S(1)} fusion(f32[4,8,128,256]{3,2,1,0:T(8,128)} %copy.44, f32[256]{0:T(256)S(1)} %copy-done.12, f32[256]{0:T(256)S(1)} %copy-done.13, f32[4,256]{1,0:T(4,128)S(1)} %div.54, f32[4,256]{1,0:T(4,128)S(1)} %sub.50), kind=kLoop, calls=%fused_computation.6 | loop fusion | flops 6291456 | bytes 6301696 | tf_op jit(solution)/shard_map/convert_element_type | solution.py:242
  73.9 3.2 %convolution_convert_fusion.refs_1_.refs_2_ = bf16[4,1024,512]{2,1,0:T(8,128)(2,1)} fusion(bf16[4,1024,256]{2,1,0:T(8,128)(2,1)S(1)} %fusion.4.f_ref, bf16[256,256]{1,0:T(8,128)(2,1)S(1)} %copy-done.6, bf16[256,256]{1,0:T(8,128)(2,1)S(1)} %copy-done.7), kind=kOutput, calls=%fused_computation.8 | convolution fusion | flops 1076363264 | bytes 6553600 | tf_op jit(solution)/shard_map/dot_general | solution.py:245
  77.1 18.4 %shard_map.150 = (f32[4,200,8]{2,1,0:T(8,128)}, f32[4,200,8]{2,1,0:T(8,128)}, f32[4,200,256]{2,1,0:T(8,128)}) custom-call(bf16[4,1600,256]{2,1,0:T(8,128)(2,1)} %bitcast_select_fusion.refs_0_, bf16[4,1024,512]{2,1,0:T(8,128)(2,1)} %convolution_convert_fusion.refs_1_.refs_2_, bf16[4,1024,512]{2,1,0:T(8,128)(2,1)} %convolution_convert_fusion.refs_1_.refs_2_, ...), custom_call_target="tpu_custom_call" | custom-call | tf_op jit(solution)/shard_map/pallas_call | solution.py:144
  95.5 1.2 reshape.137
  96.7 1.2 reshape.138
  97.9 1.2 convert_element_type.64
  99.1 0.5 convert_element_type.65
  99.8 0.5 broadcast.108
  100.3 0.9 reduce.7
  101.2 0.6 reshape.151
  101.8 18.0 %all_to_all.21 = bf16[128,2,900]{2,1,0:T(2,128)(2,1)S(1)} all-to-all(bf16[128,2,900]{2,1,0:T(2,128)(2,1)S(1)} %reshape.151), channel_id=1, replica_groups=mesh['rows'=16,'cols'=8] {'rows','cols'}, dimensions={0} | all-to-all | bytes 921600 | tf_op jit(solution)/shard_map/all_to_all | solution.py:272
  119.9 0.7 reshape.152
  120.6 0.9 copy.48
  122.0 0.3 fusion.12
  122.5 0.5 broadcast_in_dim.78
  122.9 3.3 %reduce.8 = bf16[128,1600]{1,0:T(8,128)(2,1)S(1)} reduce(bf16[128,1,1600]{2,1,0:T(2,128)(2,1)S(1)} %broadcast_in_dim.78, bf16[]{:T(256)} %broadcast.108), dimensions={1}, to_apply=%broadcast_in_dim.78.reduce_sub_computation | reduce | bytes 819202 | tf_op jit(solution)/shard_map/broadcast_in_dim | solution.py:283
  126.3 0.5 reshape.153
  126.7 17.3 %all_to_all.22 = bf16[128,2,800]{2,1,0:T(2,128)(2,1)S(1)} all-to-all(bf16[128,2,800]{2,1,0:T(2,128)(2,1)S(1)} %reshape.153), channel_id=1, replica_groups=mesh['rows'=16,'cols'=8] {'rows','cols'}, dimensions={0} | all-to-all | bytes 819200 | tf_op jit(solution)/shard_map/all_to_all | solution.py:282
  144.0 0.6 reshape.154
  144.7 2.7 %reduce.6 = bf16[128,1600]{1,0:T(8,128)(2,1)S(1)} reduce(bf16[128,1,1600]{2,1,0:T(2,128)(2,1)S(1)} %reshape.154, bf16[]{:T(256)} %constant.43), dimensions={1}, to_apply=%all_to_all.17.reduce_sub_computation | reduce | bytes 819202 | tf_op jit(solution)/shard_map/all_to_all | solution.py:282
  147.4 0.6 reshape.140
  148.0 0.4 fusion.36
  148.5 0.4 multiply_reduce_fusion.1
  148.9 0.3 multiply_add_fusion
  149.2 1.2 convolution_convert_fusion.1.e_ref
  150.4 4.6 %shard_map.151 = bf16[4,1600,128]{2,1,0:T(8,128)(2,1)} custom-call(bf16[4,200,256]{2,1,0:T(8,128)(2,1)} %convolution_convert_fusion.1.e_ref, bf16[4,1024,256]{2,1,0:T(8,128)(2,1)} %copy-done.1), custom_call_target="tpu_custom_call" | custom-call | tf_op jit(solution)/shard_map/pallas_call | solution.py:182
  (63 shorter events, 2.7 us)
Async XLA Ops:
  0.6 29.0 %copy-start = (bf16[3,3,256,256]{3,2,1,0:T(8,128)(2,1)S(1)}, bf16[3,3,256,256]{3,2,1,0:T(8,128)(2,1)}, u32[]{:S(2)}) copy-start(bf16[3,3,256,256]{3,2,1,0:T(8,128)(2,1)} %param.17) | copy-start | bytes 3538948
  0.6 11.6 %copy-start.4 = (bf16[4,8,128,256]{3,2,1,0:T(8,128)(2,1)S(1)}, bf16[4,8,128,256]{3,2,1,0:T(8,128)(2,1)}, u32[]{:S(2)}) copy-start(bf16[4,8,128,256]{3,2,1,0:T(8,128)(2,1)} %param.14) | copy-start | bytes 6291460
  2.1 9.3 %collective-permute-start = (bf16[4,1,128,256]{3,0,2,1:T(4,128)(2,1)S(1)}, bf16[4,1,128,256]{3,0,2,1:T(4,128)(2,1)S(1)}, u32[]{:S(2)}, u32[]{:S(2)}) collective-permute-start(bf16[4,1,128,256]{3,0,2,1:T(4,128)(2,1)S(1)} %copy.51), channel_id=1, source_target_pairs={{0,8},{8,16},{16,24},{24,32},{32,40},{40,48},{48,56},{56,64},{64,7... | collective-permute-start | bytes 786440 | tf_op jit(solution)/shard_map/ppermute | solution.py:21
  6.7 9.1 %collective-permute-start.1 = (bf16[4,1,128,256]{3,0,2,1:T(4,128)(2,1)S(1)}, bf16[4,1,128,256]{3,0,2,1:T(4,128)(2,1)S(1)}, u32[]{:S(2)}, u32[]{:S(2)}) collective-permute-start(bf16[4,1,128,256]{3,0,2,1:T(4,128)(2,1)S(1)} %copy.52), channel_id=1, source_target_pairs={{8,0},{16,8},{24,16},{32,24},{40,32},{48,40},{56,48},{64,56},{72,6... | collective-permute-start | bytes 786440 | tf_op jit(solution)/shard_map/ppermute | solution.py:23
  17.4 12.2 %collective-permute-start.2 = (bf16[4,10,1,256]{3,0,2,1:T(4,128)(2,1)S(1)}, bf16[4,10,1,256]{3,0,2,1:T(4,128)(2,1)S(1)}, u32[]{:S(2)}, u32[]{:S(2)}) collective-permute-start(bf16[4,10,1,256]{3,0,2,1:T(4,128)(2,1)S(1)} %get-tuple-element.20), channel_id=1, source_target_pairs={{0,1},{1,2},{2,3},{3,4},{4,5},{5,6},{6,7},{8,9},{9,10},{10,11},{11... | collective-permute-start | bytes 61448 | tf_op jit(solution)/shard_map/ppermute | solution.py:21
  22.1 7.5 %collective-permute-start.3 = (bf16[4,10,1,256]{3,0,2,1:T(4,128)(2,1)S(1)}, bf16[4,10,1,256]{3,0,2,1:T(4,128)(2,1)S(1)}, u32[]{:S(2)}, u32[]{:S(2)}) collective-permute-start(bf16[4,10,1,256]{3,0,2,1:T(4,128)(2,1)S(1)} %get-tuple-element.21), channel_id=1, source_target_pairs={{1,0},{2,1},{3,2},{4,3},{5,4},{6,5},{7,6},{9,8},{10,9},{11,10},{12... | collective-permute-start | bytes 61448 | tf_op jit(solution)/shard_map/ppermute | solution.py:23
  29.6 25.2 %copy-start.5 = (f32[4,200,256]{2,1,0:T(8,128)S(1)}, f32[4,200,256]{2,1,0:T(8,128)}, u32[]{:S(2)}) copy-start(f32[4,200,256]{2,1,0:T(8,128)} %param.16) | copy-start | bytes 2457604
  29.6 25.2 %copy-start.11 = (bf16[256,256]{1,0:T(8,128)(2,1)S(1)}, bf16[256,256]{1,0:T(8,128)(2,1)}, u32[]{:S(2)}) copy-start(bf16[256,256]{1,0:T(8,128)(2,1)} %param.20) | copy-start | bytes 393220
  43.9 25.1 %all-to-all-start = ((f32[128,1,1056]{2,1,0:T(1,128)}), f32[128,1,1056]{2,1,0:T(1,128)S(1)}, u32[]{:S(2)}, u32[]{:S(2)}) async-start(f32[128,1,1056]{2,1,0:T(1,128)} %broadcast_in_dim.72), calls=%async_computation | async-start | bytes 1179648 | tf_op jit(solution)/shard_map/all_to_all | solution.py:231
  54.8 3.1 %copy-start.2 = (f32[4,8,128,256]{3,0,2,1:T(4,128)S(1)}, f32[4,8,128,256]{3,0,2,1:T(4,128)}, u32[]{:S(2)}) copy-start(f32[4,8,128,256]{3,0,2,1:T(4,128)} %get-tuple-element.26) | copy-start | bytes 12582916
  57.9 13.0 %copy-start.12 = (f32[256]{0:T(256)S(1)}, f32[256]{0:T(256)}, u32[]{:S(2)}) copy-start(f32[256]{0:T(256)} %param.19) | copy-start | bytes 3076
  57.9 13.0 %copy-start.13 = (f32[256]{0:T(256)S(1)}, f32[256]{0:T(256)}, u32[]{:S(2)}) copy-start(f32[256]{0:T(256)} %param.18) | copy-start | bytes 3076
  70.9 3.0 %copy-start.6 = (bf16[256,256]{1,0:T(8,128)(2,1)S(1)}, bf16[256,256]{1,0:T(8,128)(2,1)}, u32[]{:S(2)}) copy-start(bf16[256,256]{1,0:T(8,128)(2,1)} %param.22) | copy-start | bytes 393220
  70.9 3.0 %copy-start.7 = (bf16[256,256]{1,0:T(8,128)(2,1)S(1)}, bf16[256,256]{1,0:T(8,128)(2,1)}, u32[]{:S(2)}) copy-start(bf16[256,256]{1,0:T(8,128)(2,1)} %param.21) | copy-start | bytes 393220
  73.9 3.2 %copy-start.1 = (bf16[4,1024,256]{2,1,0:T(8,128)(2,1)}, bf16[4,1024,256]{2,1,0:T(8,128)(2,1)S(1)}, u32[]{:S(2)}) copy-start(bf16[4,1024,256]{2,1,0:T(8,128)(2,1)S(1)} %fusion.4.f_ref) | copy-start | bytes 6291460
  126.3 21.8 %copy-start.8 = (bf16[256,256]{1,0:T(8,128)(2,1)S(1)}, bf16[256,256]{1,0:T(8,128)(2,1)}, u32[]{:S(2)}) copy-start(bf16[256,256]{1,0:T(8,128)(2,1)} %param.23) | copy-start | bytes 393220
  144.7 4.2 %copy-start.14 = (f32[256]{0:T(256)S(1)}, f32[256]{0:T(256)}, u32[]{:S(2)}) copy-start(f32[256]{0:T(256)} %param.25) | copy-start | bytes 3076
  144.7 4.2 %copy-start.15 = (f32[256]{0:T(256)S(1)}, f32[256]{0:T(256)}, u32[]{:S(2)}) copy-start(f32[256]{0:T(256)} %param.24) | copy-start | bytes 3076
  147.4 1.8 %copy-start.9 = (bf16[256,256]{1,0:T(8,128)(2,1)S(1)}, bf16[256,256]{1,0:T(8,128)(2,1)}, u32[]{:S(2)}) copy-start(bf16[256,256]{1,0:T(8,128)(2,1)} %param.27) | copy-start | bytes 393220
  147.4 1.8 %copy-start.10 = (bf16[256,256]{1,0:T(8,128)(2,1)S(1)}, bf16[256,256]{1,0:T(8,128)(2,1)}, u32[]{:S(2)}) copy-start(bf16[256,256]{1,0:T(8,128)(2,1)} %param.26) | copy-start | bytes 393220
  149.2 5.8 %copy-start.3 = (f32[4,200,256]{2,1,0:T(8,128)}, f32[4,200,256]{2,1,0:T(8,128)S(1)}, u32[]{:S(2)}) copy-start(f32[4,200,256]{2,1,0:T(8,128)S(1)} %multiply_add_fusion) | copy-start | bytes 2457604
